TPU v7x, 32 devices: a whole 2x2x4 slice. The times are simulated.
32 devices in a mesh: rows: 4 (over y, x), cols: 8 (over z, core).
Axes of the slice: x: 2, y: 2, z: 4, core: 2. Of those that a mesh axis runs over, the one named last changes fastest.
Arguments:
- direct: float32 [49152, 1536], P(('rows', 'cols')), may hold values from -6 to 6
- adjoint: float32 [49152, 1536], P(('rows', 'cols')), may hold values from -6 to 6
- probes: float32 [1536, 256], replicated, may hold values from -6 to 6
Outputs:
- direct_modes: float32 [49152, 256], P(('rows', 'cols'))
- adjoint_modes: float32 [49152, 256], P(('rows', 'cols'))
All inputs are finite; a program needn't handle non-finite values.
Results may differ from a plain program's by a relative error of at most 0.00013.
Values sent between devices are 32-bit elements; how exact they have to be, the bound alone decides.
No kernel may reach another device: no remote copies, remote signals or barrier semaphores. Data moves between devices by JAX's collectives and lax.ppermute only.
A program may use at most 128 MiB of HBM per device.

v0:
```python
import math

import jax
import jax.numpy as jnp
from jax import lax
from jax.sharding import PartitionSpec as P


def shards(direct, adjoint, probes):
    high = lax.Precision.HIGHEST
    row_count = lax.axis_size("rows")
    col_count = lax.axis_size("cols")
    snap_count = direct.shape[1]
    tile_rows = snap_count // row_count
    tile_cols = snap_count // col_count
    scale = 1.0 / math.sqrt(direct.shape[0] * row_count * col_count * snap_count)
    norm_factor = 1.0 / math.sqrt(snap_count)
    partial_hankel = (
        jnp.dot(adjoint.T, direct, precision=high, preferred_element_type=jnp.float32) * scale
    )
    ordered = partial_hankel.reshape(row_count, tile_rows, col_count, tile_cols)
    ordered = ordered.transpose(0, 2, 1, 3).reshape(row_count * col_count * tile_rows, tile_cols)
    tile = lax.psum_scatter(ordered, ("rows", "cols"), scatter_dimension=0, tiled=True)
    col_index = lax.axis_index("cols")
    coef_d = lax.dynamic_slice_in_dim(probes, col_index * tile_cols, tile_cols, 0)
    coef_a = jnp.zeros((tile_rows, probes.shape[1]), jnp.float32)
    for rnd in range(2):
        coef_a = lax.psum(
            jnp.dot(tile, coef_d, precision=high, preferred_element_type=jnp.float32), "cols"
        )
        coef_d = lax.psum(
            jnp.dot(tile.T, coef_a, precision=high, preferred_element_type=jnp.float32), "rows"
        )
    columns = direct
    direct_sum = jnp.dot(
        columns,
        lax.all_gather(coef_d, "cols", axis=0, tiled=True),
        precision=high,
        preferred_element_type=jnp.float32,
    )
    columns = adjoint
    adjoint_sum = jnp.dot(
        columns,
        lax.all_gather(coef_a, "rows", axis=0, tiled=True),
        precision=high,
        preferred_element_type=jnp.float32,
    )
    return (direct_sum * norm_factor, adjoint_sum * norm_factor)


def solution(mesh):
    placed = (P(("rows", "cols"), None), P(("rows", "cols"), None), P())
    return jax.shard_map(
        shards,
        mesh=mesh,
        in_specs=placed,
        out_specs=(P(("rows", "cols"), None), P(("rows", "cols"), None)),
        check_vma=False,
    )
```

profile of v0, /device:TPU:0, one launch (start us, length us, event | category | flops | bytes accessed | tf_op | source)
XLA Modules:
  0.0 542.0 jit_solution(3329419538630469028)
XLA Ops:
  7.2 52.5 %convolution_multiply_fusion = f32[1536,1536]{1,0:T(8,128)} fusion(f32[1536,1536]{1,0:T(8,128)} %param.4, f32[1536,1536]{1,0:T(8,128)} %param.3), kind=kOutput, calls=%fused_computation | convolution fusion | flops 43488903168 | bytes 28311552 | tf_op jit(solution)/shard_map/dot_general | solution.py:19
  59.7 9.6 %copy.7 = f32[1536,1536]{0,1:T(8,128)} copy(f32[1536,1536]{1,0:T(8,128)} %convolution_multiply_fusion) | data formatting | bytes 18874368 | tf_op jit(solution)/shard_map/mul | solution.py:19
  69.3 11.7 %reshape.10 = f32[4,384,8,192]{1,0,3,2:T(4,128)} reshape(f32[1536,1536]{0,1:T(8,128)} %copy.7) | data formatting | bytes 18874368 | tf_op jit(solution)/shard_map/reshape | solution.py:21
  81.0 9.1 %copy.8 = f32[4,8,384,192]{2,1,0,3:T(8,128)S(1)} copy(f32[4,8,384,192]{2,0,3,1:T(4,128)} %bitcast.26) | data formatting | bytes 18874368 | tf_op jit(solution)/shard_map/transpose | solution.py:22
  90.1 21.1 %copy.11 = f32[24,8,32,384]{3,1,2,0:T(8,128)} copy(f32[24,8,32,384]{3,2,1,0:T(8,128)S(1)} %bitcast.27) | data formatting | bytes 18874368
  111.3 0.0 all-reduce.5.cloned.1.call-start
  111.3 138.4 %reduce-scatter.2.cloned.1.call-done = f32[384,192]{0,1:T(8,128)} async-done(((f32[12288,192]{0,1:T(8,128)}), f32[384,192]{0,1:T(8,128)}) %reduce-scatter.2.cloned.1.call-update) | async-done | bytes 294928 | tf_op jit(solution)/shard_map/reduce_scatter | solution.py:23
  249.8 2.6 fusion.2
  252.4 54.9 %all-reduce.5.cloned.1.call-done = f32[384,256]{1,0:T(8,128)} async-done(((f32[384,256]{1,0:T(8,128)}), f32[384,256]{1,0:T(8,128)}) %all-reduce.5.cloned.1.call-update) | async-done | bytes 393232 | tf_op jit(solution)/shard_map/psum | solution.py:28
  307.3 2.3 fusion.5
  309.6 0.0 all-reduce.9.cloned.1.call-start
  309.6 42.6 %all-reduce.7.cloned.1.call-done = f32[192,256]{1,0:T(8,128)} async-done(((f32[192,256]{1,0:T(8,128)}), f32[192,256]{1,0:T(8,128)}) %all-reduce.7.cloned.1.call-update) | async-done | bytes 196624 | tf_op jit(solution)/shard_map/psum | solution.py:31
  352.2 2.6 fusion.6
  354.9 0.0 all-reduce.11.cloned.1.call-start
  354.9 55.7 %all-reduce.9.cloned.1.call-done = f32[384,256]{1,0:T(8,128)} async-done(((f32[384,256]{1,0:T(8,128)}), f32[384,256]{1,0:T(8,128)}) %all-reduce.9.cloned.1.call-update) | async-done | bytes 393232 | tf_op jit(solution)/shard_map/psum | solution.py:28
  410.6 2.3 fusion.7
  412.9 0.5 all-gather.5.cloned.1.call-update
  413.5 41.9 %all-reduce.11.cloned.1.call-done = f32[192,256]{1,0:T(8,128)} async-done(((f32[192,256]{1,0:T(8,128)}), f32[192,256]{1,0:T(8,128)}) %all-reduce.11.cloned.1.call-update) | async-done | bytes 196624 | tf_op jit(solution)/shard_map/psum | solution.py:31
  455.4 32.8 %all-gather.5.cloned.1.call-done = f32[1536,256]{1,0:T(8,128)} async-done(((f32[384,256]{1,0:T(8,128)}), f32[1536,256]{1,0:T(8,128)}) %all-gather.5.cloned.1.call-update) | async-done | bytes 1572880 | tf_op jit(solution)/shard_map/all_gather | solution.py:44
  488.2 18.0 %fusion.1 = f32[1536,256]{0,1:T(8,128)S(1)} fusion(f32[1536,256]{1,0:T(8,128)} %all-gather.5.cloned.1.call-done, f32[1536,1536]{1,0:T(8,128)} %param.4), kind=kOutput, calls=%fused_computation.4 | convolution fusion | flops 7248150528 | bytes 12582912 | tf_op jit(solution)/shard_map/dot_general | solution.py:42
  506.3 1.6 copy.10
  507.9 7.2 %all-gather.3.cloned.1.call-done = f32[1536,256]{1,0:T(8,128)} async-done(((f32[192,256]{1,0:T(8,128)}), f32[1536,256]{1,0:T(8,128)}) %all-gather.3.cloned.1.call-update) | async-done | bytes 1572880 | tf_op jit(solution)/shard_map/all_gather | solution.py:37
  515.0 18.2 %fusion = f32[1536,256]{0,1:T(8,128)S(1)} fusion(f32[1536,256]{1,0:T(8,128)} %all-gather.3.cloned.1.call-done, f32[1536,1536]{1,0:T(8,128)} %param.3), kind=kOutput, calls=%fused_computation.3 | convolution fusion | flops 7248150528 | bytes 12582912 | tf_op jit(solution)/shard_map/dot_general | solution.py:35
  533.3 1.6 copy.9
  (12 shorter events, 0.3 us)
Async XLA Ops:
  7.2 242.6 %copy-start = (f32[1536,256]{1,0:T(8,128)S(1)}, f32[1536,256]{1,0:T(8,128)}, u32[]{:S(2)}) copy-start(f32[1536,256]{1,0:T(8,128)} %param.5) | copy-start | bytes 4718596
  7.2 242.6 %reduce-scatter.2.cloned.1.call-start = ((), (), s32[]{:S(2)}) async-start(), calls=%async_computation.1 | async-start | bytes 9732096 | tf_op jit(solution)/shard_map/reduce_scatter | solution.py:23
  111.3 196.0 %all-reduce.5.cloned.1.call-start = ((), (), s32[]{:S(2)}) async-start(), calls=%async_computation.2 | async-start | bytes 786432 | tf_op jit(solution)/shard_map/psum | solution.py:28
  252.4 99.9 %all-reduce.7.cloned.1.call-start = ((), (), s32[]{:S(2)}) async-start(), calls=%async_computation.3 | async-start | bytes 393216 | tf_op jit(solution)/shard_map/psum | solution.py:31
  309.6 101.0 %all-reduce.9.cloned.1.call-start = ((), (), s32[]{:S(2)}) async-start(), calls=%async_computation.4 | async-start | bytes 786432 | tf_op jit(solution)/shard_map/psum | solution.py:28
  354.9 100.5 %all-reduce.11.cloned.1.call-start = ((), (), s32[]{:S(2)}) async-start(), calls=%async_computation.5 | async-start | bytes 393216 | tf_op jit(solution)/shard_map/psum | solution.py:31
  412.9 75.3 %all-gather.5.cloned.1.call-start = ((), (), s32[]{:S(2)}) async-start(), calls=%async_computation.7 | async-start | bytes 1966080 | tf_op jit(solution)/shard_map/all_gather | solution.py:44
  413.5 101.6 %all-gather.3.cloned.1.call-start = ((), (), s32[]{:S(2)}) async-start(), calls=%async_computation.6 | async-start | bytes 1769472 | tf_op jit(solution)/shard_map/all_gather | solution.py:37
Sparse Core Ops, SparseCore 0:
  111.4 138.3 reduce-scatter.1
  252.8 54.4 all-reduce.4
  310.8 41.4 all-reduce.6
  355.1 55.4 all-reduce.8
  413.9 41.4 all-reduce.10
  457.2 30.9 all-gather.4
  490.0 25.0 all-gather.2
where the time goes:
time: 547 us; the launch traced here: 542 us
  waiting for transfers between devices  374 us (68%)
  matrix products  98.4 us (18%)
  local copies, waits for them, and re-layouts  54.8 us (10%)
  between operations  14.4 us (3%)
    reduce_scatter x1, waiting for transfers between devices, shards(): lax.psum_scatter(ordered, ('rows', 'cols'), scatter_dimension=0, tiled=True)  138 us
    psum x2, waiting for transfers between devices, shards(): lax.psum(jnp.dot(tile, coef_d, precision=high, preferred_element_type=jnp...  111 us
    psum x2, waiting for transfers between devices, shards(): lax.psum(jnp.dot(tile.T, coef_a, precision=high, preferred_element_type=j...  84.5 us
    dot_general x1, matrix products, shards(): jnp.dot(adjoint.T, direct, precision=high, preferred_element_type=jnp.flo...  52.5 us
    all_gather x1, waiting for transfers between devices, shards(): lax.all_gather(coef_a, 'rows', axis=0, tiled=True)  32.8 us
    unnamed x5, local copies, waits for them, and re-layouts  24.4 us
    dot_general x1, matrix products, shards(): jnp.dot(columns, lax.all_gather(coef_d, 'cols', axis=0, tiled=True), prec...  18.2 us
    dot_general x1, matrix products, shards(): jnp.dot(columns, lax.all_gather(coef_a, 'rows', axis=0, tiled=True), prec...  18 us
  transfers between devices with their start and end apart: 7, of which 7 were waited for; matrix products, arithmetic and copies ran while one was open for 4% of the time, Pallas kernels for 0%

commit v1 on v0

v1 whole, which is shorter than its diff:
```python
import math

import jax
import jax.numpy as jnp
from jax import lax
from jax.sharding import PartitionSpec as P


def doubling_sum(x, axis):
    count = lax.axis_size(axis)
    step = 1
    while step < count:
        x = x + lax.ppermute(x, axis, [(i, i ^ step) for i in range(count)])
        step *= 2
    return x


def shards(direct, adjoint, probes):
    high = lax.Precision.HIGHEST
    fast = lax.Precision.HIGH
    row_count = lax.axis_size("rows")
    col_count = lax.axis_size("cols")
    state_rows, snap_count = direct.shape
    tile_rows = snap_count // row_count
    tile_cols = snap_count // col_count
    scale = 1.0 / math.sqrt(state_rows * row_count * col_count * snap_count)
    norm_factor = 1.0 / math.sqrt(snap_count)
    ordered = jnp.einsum(
        "nri,ncj->rcij",
        adjoint.reshape(state_rows, row_count, tile_rows),
        direct.reshape(state_rows, col_count, tile_cols),
        precision=fast,
        preferred_element_type=jnp.float32,
    ) * scale
    ordered = ordered.reshape(row_count * col_count * tile_rows, tile_cols)
    tile = lax.psum_scatter(ordered, ("rows", "cols"), scatter_dimension=0, tiled=True)
    col_index = lax.axis_index("cols")
    coef_d = lax.dynamic_slice_in_dim(probes, col_index * tile_cols, tile_cols, 0)
    coef_a = jnp.zeros((tile_rows, probes.shape[1]), jnp.float32)
    for rnd in range(2):
        coef_a = doubling_sum(
            jnp.dot(tile, coef_d, precision=high, preferred_element_type=jnp.float32), "cols"
        )
        coef_d = doubling_sum(
            jnp.dot(tile.T, coef_a, precision=high, preferred_element_type=jnp.float32), "rows"
        )
    direct_sum = jnp.dot(
        direct,
        lax.all_gather(coef_d, "cols", axis=0, tiled=True),
        precision=fast,
        preferred_element_type=jnp.float32,
    )
    adjoint_sum = jnp.dot(
        adjoint,
        lax.all_gather(coef_a, "rows", axis=0, tiled=True),
        precision=fast,
        preferred_element_type=jnp.float32,
    )
    return (direct_sum * norm_factor, adjoint_sum * norm_factor)


def solution(mesh):
    placed = (P(("rows", "cols"), None), P(("rows", "cols"), None), P())
    return jax.shard_map(
        shards,
        mesh=mesh,
        in_specs=placed,
        out_specs=(P(("rows", "cols"), None), P(("rows", "cols"), None)),
        check_vma=False,
    )
```

time: 547 us -> 370 us (0.68)
  waiting for transfers between devices: 374 us -> 252 us
  matrix products: 98.4 us -> 57.3 us
  local copies, waits for them, and re-layouts: 54.8 us -> 34.1 us
  starting transfers between devices: 0.29 us -> 11.3 us
    psum x4 -> x0, waiting for transfers between devices: 195 us -> none  [the longest x2 111 us: shards(): lax.psum(jnp.dot(tile, coef_d, precision=high, preferred_element_type=jnp...]
    ppermute x0 -> x10, waiting for transfers between devices: none -> 82.2 us  [doubling_sum(): x = x + lax.ppermute(x, axis, [(i, i ^ step) for i in range(count)])]
    dot_general x3, matrix products: 88.7 us -> 50.6 us  [the longest x1 29.3 us: shards(): jnp.einsum('nri,ncj->rcij', adjoint.reshape(state_rows, row_count, tile_r...]
    all_gather x1, waiting for transfers between devices: 32.8 us -> 16 us  [shards(): lax.all_gather(coef_a, 'rows', axis=0, tiled=True)]
    reshape x1 -> x0, local copies, waits for them, and re-layouts: 11.7 us -> none  [shards(): ordered = partial_hankel.reshape(row_count, tile_rows, col_count, tile_cols)]
    ppermute x0 -> x10, starting transfers between devices: none -> 11.2 us  [doubling_sum(): x = x + lax.ppermute(x, axis, [(i, i ^ step) for i in range(count)])]
    transpose x1 -> x0, local copies, waits for them, and re-layouts: 9.14 us -> none  [shards(): ordered.transpose(0, 2, 1, 3)]
    all_gather x1, waiting for transfers between devices: 7.16 us -> 15.1 us  [shards(): lax.all_gather(coef_d, 'cols', axis=0, tiled=True)]
  transfers between devices with their start and end apart: 7 -> 13, of which waited for: 7 -> 13; matrix products, arithmetic and copies ran while one was open for 4% -> 4% of each run, Pallas kernels for 0% -> 0%
where the time goes in v1:
time: 370 us
  waiting for transfers between devices  252 us (68%)
  matrix products  57.3 us (15%)
  local copies, waits for them, and re-layouts  34.1 us (9%)
  between operations  13.9 us (4%)
  starting transfers between devices  11.3 us (3%)
    reduce_scatter x1, waiting for transfers between devices, shards(): lax.psum_scatter(ordered, ('rows', 'cols'), scatter_dimension=0, tiled=True)  138 us
    ppermute x10, waiting for transfers between devices, doubling_sum(): x = x + lax.ppermute(x, axis, [(i, i ^ step) for i in range(count)])  82.2 us
    dot_general x1, matrix products, shards(): jnp.einsum('nri,ncj->rcij', adjoint.reshape(state_rows, row_count, tile_r...  29.3 us
    unnamed x8, local copies, waits for them, and re-layouts  25 us
    all_gather x1, waiting for transfers between devices, shards(): lax.all_gather(coef_a, 'rows', axis=0, tiled=True)  16 us
    all_gather x1, waiting for transfers between devices, shards(): lax.all_gather(coef_d, 'cols', axis=0, tiled=True)  15.1 us
    ppermute x10, starting transfers between devices, doubling_sum(): x = x + lax.ppermute(x, axis, [(i, i ^ step) for i in range(count)])  11.2 us
    dot_general x1, matrix products, shards(): jnp.dot(adjoint, lax.all_gather(coef_a, 'rows', axis=0, tiled=True), prec...  10.6 us
  transfers between devices with their start and end apart: 13, of which 13 were waited for; matrix products, arithmetic and copies ran while one was open for 4% of the time, Pallas kernels for 0%

profile of v1, /device:TPU:0, one launch (start us, length us, event | category | flops | bytes accessed | tf_op | source)
XLA Modules:
  0.0 370.1 jit_solution(17735093671254014787)
XLA Ops:
  7.2 9.7 %copy.9 = f32[1536,1536]{0,1:T(8,128)} copy(f32[1536,1536]{1,0:T(8,128)} %param.3) | data formatting | bytes 18874368 | tf_op args[0]
  17.0 29.3 %multiply_bitcast_fusion = f32[4,8,384,192]{2,3,0,1:T(8,128)} fusion(f32[1536,8,192,1]{0,2,3,1:T(8,128)} %bitcast.40, f32[192,4,8,384]{3,2,1,0:T(8,128)} %bitcast.39), kind=kOutput, calls=%fused_computation.3 | convolution fusion | flops 21745631232 | bytes 28311552 | tf_op jit(solution)/shard_map/nri,ncj->rcij/dot_general | solution.py:28
  46.3 9.1 %copy.11 = f32[4,8,384,192]{2,1,0,3:T(8,128)S(1)} copy(f32[4,8,384,192]{2,3,0,1:T(8,128)} %multiply_bitcast_fusion) | data formatting | bytes 18874368 | tf_op jit(solution)/shard_map/mul | solution.py:28
  55.4 12.0 %copy.16 = f32[24,8,32,384]{3,1,2,0:T(8,128)} copy(f32[24,8,32,384]{3,2,1,0:T(8,128)S(1)} %bitcast.38) | data formatting | bytes 18874368
  67.5 138.4 %reduce-scatter.2.cloned.1.call-done = f32[384,192]{0,1:T(8,128)} async-done(((f32[12288,192]{0,1:T(8,128)}), f32[384,192]{0,1:T(8,128)}) %reduce-scatter.2.cloned.1.call-update) | async-done | bytes 294928 | tf_op jit(solution)/shard_map/reduce_scatter | solution.py:36
  205.9 1.9 fusion.8
  207.9 1.7 collective-permute-done
  210.9 10.0 %collective-permute-done.1 = f32[384,256]{1,0:T(8,128)S(1)} collective-permute-done((f32[384,256]{1,0:T(8,128)S(1)}, f32[384,256]{1,0:T(8,128)S(1)}, u32[]{:S(2)}, u32[]{:S(2)}) %collective-permute-start.1) | collective-permute-done | bytes 393248 | tf_op jit(solution)/shard_map/ppermute | solution.py:13
  222.4 18.2 %collective-permute-done.2 = f32[384,256]{1,0:T(8,128)S(1)} collective-permute-done((f32[384,256]{1,0:T(8,128)S(1)}, f32[384,256]{1,0:T(8,128)S(1)}, u32[]{:S(2)}, u32[]{:S(2)}) %collective-permute-start.2) | collective-permute-done | bytes 393248 | tf_op jit(solution)/shard_map/ppermute | solution.py:13
  243.4 4.9 %collective-permute-done.3 = f32[192,256]{1,0:T(8,128)S(1)} collective-permute-done((f32[192,256]{1,0:T(8,128)S(1)}, f32[192,256]{1,0:T(8,128)S(1)}, u32[]{:S(2)}, u32[]{:S(2)}) %collective-permute-start.3) | collective-permute-done | bytes 196640 | tf_op jit(solution)/shard_map/ppermute | solution.py:13
  249.8 4.2 %collective-permute-done.4 = f32[192,256]{1,0:T(8,128)S(1)} collective-permute-done((f32[192,256]{1,0:T(8,128)S(1)}, f32[192,256]{1,0:T(8,128)S(1)}, u32[]{:S(2)}, u32[]{:S(2)}) %collective-permute-start.4) | collective-permute-done | bytes 196640 | tf_op jit(solution)/shard_map/ppermute | solution.py:13
  254.0 1.8 fusion.6
  256.0 1.7 collective-permute-done.5
  258.1 10.9 %collective-permute-done.6 = f32[384,256]{1,0:T(8,128)S(1)} collective-permute-done((f32[384,256]{1,0:T(8,128)S(1)}, f32[384,256]{1,0:T(8,128)S(1)}, u32[]{:S(2)}, u32[]{:S(2)}) %collective-permute-start.6) | collective-permute-done | bytes 393248 | tf_op jit(solution)/shard_map/ppermute | solution.py:13
  269.0 2.0 collective-permute-start.7
  271.0 17.8 %collective-permute-done.7 = f32[384,256]{1,0:T(8,128)S(1)} collective-permute-done((f32[384,256]{1,0:T(8,128)S(1)}, f32[384,256]{1,0:T(8,128)S(1)}, u32[]{:S(2)}, u32[]{:S(2)}) %collective-permute-start.7) | collective-permute-done | bytes 393248 | tf_op jit(solution)/shard_map/ppermute | solution.py:13
  292.6 4.8 %collective-permute-done.8 = f32[192,256]{1,0:T(8,128)S(1)} collective-permute-done((f32[192,256]{1,0:T(8,128)S(1)}, f32[192,256]{1,0:T(8,128)S(1)}, u32[]{:S(2)}, u32[]{:S(2)}) %collective-permute-start.8) | collective-permute-done | bytes 196640 | tf_op jit(solution)/shard_map/ppermute | solution.py:13
  297.5 1.6 collective-permute-start.9
  299.1 8.1 %collective-permute-done.9 = f32[192,256]{1,0:T(8,128)S(1)} collective-permute-done((f32[192,256]{1,0:T(8,128)S(1)}, f32[192,256]{1,0:T(8,128)S(1)}, u32[]{:S(2)}, u32[]{:S(2)}) %collective-permute-start.9) | collective-permute-done | bytes 196640 | tf_op jit(solution)/shard_map/ppermute | solution.py:13
  307.9 16.0 %all-gather.5.cloned.1.call-done = f32[1536,256]{1,0:T(8,128)} async-done(((f32[384,256]{1,0:T(8,128)}), f32[1536,256]{1,0:T(8,128)}) %all-gather.5.cloned.1.call-update) | async-done | bytes 1572880 | tf_op jit(solution)/shard_map/all_gather | solution.py:55
  323.9 10.6 %fusion.3 = f32[1536,256]{0,1:T(8,128)S(1)} fusion(f32[1536,256]{1,0:T(8,128)} %all-gather.5.cloned.1.call-done, f32[1536,1536]{1,0:T(8,128)} %param.4), kind=kOutput, calls=%fused_computation.7 | convolution fusion | flops 3624271872 | bytes 12582912 | tf_op jit(solution)/shard_map/dot_general | solution.py:53
  336.1 15.1 %all-gather.3.cloned.1.call-done = f32[1536,256]{1,0:T(8,128)} async-done(((f32[192,256]{1,0:T(8,128)}), f32[1536,256]{1,0:T(8,128)}) %all-gather.3.cloned.1.call-update) | async-done | bytes 1572880 | tf_op jit(solution)/shard_map/all_gather | solution.py:49
  351.3 10.6 %fusion.2 = f32[1536,256]{0,1:T(8,128)S(1)} fusion(f32[1536,256]{1,0:T(8,128)} %all-gather.3.cloned.1.call-done, f32[1536,1536]{1,0:T(8,128)} %param.3), kind=kOutput, calls=%fused_computation.6 | convolution fusion | flops 3624271872 | bytes 12582912 | tf_op jit(solution)/shard_map/dot_general | solution.py:47
  361.9 1.6 copy.12
  (29 shorter events, 14.1 us)
Async XLA Ops:
  7.2 198.7 %copy-start = (f32[1536,256]{1,0:T(8,128)S(1)}, f32[1536,256]{1,0:T(8,128)}, u32[]{:S(2)}) copy-start(f32[1536,256]{1,0:T(8,128)} %param.5) | copy-start | bytes 4718596
  7.2 198.7 %reduce-scatter.2.cloned.1.call-start = ((), (), s32[]{:S(2)}) async-start(), calls=%async_computation.1 | async-start | bytes 9732096 | tf_op jit(solution)/shard_map/reduce_scatter | solution.py:36
  67.4 256.4 %all-gather.5.cloned.1.call-start = ((), (), s32[]{:S(2)}) async-start(), calls=%async_computation.3 | async-start | bytes 1966080 | tf_op jit(solution)/shard_map/all_gather | solution.py:55
  205.9 83.7 %copy-start.1 = (f32[384,192]{0,1:T(8,128)S(1)}, f32[384,192]{0,1:T(8,128)}, u32[]{:S(2)}) copy-start(f32[384,192]{0,1:T(8,128)} %reduce-scatter.2.cloned.1.call-done) | copy-start | bytes 884740
  207.8 1.8 collective-permute-start
  209.6 11.2 %collective-permute-start.1 = (f32[384,256]{1,0:T(8,128)S(1)}, f32[384,256]{1,0:T(8,128)S(1)}, u32[]{:S(2)}, u32[]{:S(2)}) collective-permute-start(f32[384,256]{1,0:T(8,128)S(1)} %add.36), channel_id=1, source_target_pairs={{0,2},{1,3},{2,0},{3,1},{4,6},{5,7},{6,4},{7,5},{8,10},{9,11},{10,... | collective-permute-start | bytes 1179656 | tf_op jit(solution)/shard_map/ppermute | solution.py:13
  220.9 19.7 %collective-permute-start.2 = (f32[384,256]{1,0:T(8,128)S(1)}, f32[384,256]{1,0:T(8,128)S(1)}, u32[]{:S(2)}, u32[]{:S(2)}) collective-permute-start(f32[384,256]{1,0:T(8,128)S(1)} %add.37), channel_id=1, source_target_pairs={{0,4},{1,5},{2,6},{3,7},{4,0},{5,1},{6,2},{7,3},{8,12},{9,13},{10,... | collective-permute-start | bytes 1179656 | tf_op jit(solution)/shard_map/ppermute | solution.py:13
  242.1 6.2 %collective-permute-start.3 = (f32[192,256]{1,0:T(8,128)S(1)}, f32[192,256]{1,0:T(8,128)S(1)}, u32[]{:S(2)}, u32[]{:S(2)}) collective-permute-start(f32[192,256]{1,0:T(8,128)S(1)} %fusion.4), channel_id=1, source_target_pairs={{0,8},{8,0},{16,24},{24,16},{1,9},{9,1},{17,25},{25,17},{2,10},{10... | collective-permute-start | bytes 589832 | tf_op jit(solution)/shard_map/ppermute | solution.py:13
  248.3 5.7 %collective-permute-start.4 = (f32[192,256]{1,0:T(8,128)S(1)}, f32[192,256]{1,0:T(8,128)S(1)}, u32[]{:S(2)}, u32[]{:S(2)}) collective-permute-start(f32[192,256]{1,0:T(8,128)S(1)} %add.39), channel_id=1, source_target_pairs={{0,16},{8,24},{16,0},{24,8},{1,17},{9,25},{17,1},{25,9},{2,18},{10... | collective-permute-start | bytes 589832 | tf_op jit(solution)/shard_map/ppermute | solution.py:13
  255.9 1.8 collective-permute-start.5
  257.7 11.2 %collective-permute-start.6 = (f32[384,256]{1,0:T(8,128)S(1)}, f32[384,256]{1,0:T(8,128)S(1)}, u32[]{:S(2)}, u32[]{:S(2)}) collective-permute-start(f32[384,256]{1,0:T(8,128)S(1)} %add.41), channel_id=1, source_target_pairs={{0,2},{1,3},{2,0},{3,1},{4,6},{5,7},{6,4},{7,5},{8,10},{9,11},{10,... | collective-permute-start | bytes 1179656 | tf_op jit(solution)/shard_map/ppermute | solution.py:13
  269.0 19.7 %collective-permute-start.7 = (f32[384,256]{1,0:T(8,128)S(1)}, f32[384,256]{1,0:T(8,128)S(1)}, u32[]{:S(2)}, u32[]{:S(2)}) collective-permute-start(f32[384,256]{1,0:T(8,128)S(1)} %add.42), channel_id=1, source_target_pairs={{0,4},{1,5},{2,6},{3,7},{4,0},{5,1},{6,2},{7,3},{8,12},{9,13},{10,... | collective-permute-start | bytes 1179656 | tf_op jit(solution)/shard_map/ppermute | solution.py:13
  289.5 61.7 %all-gather.3.cloned.1.call-start = ((), (), s32[]{:S(2)}) async-start(), calls=%async_computation.2 | async-start | bytes 1769472 | tf_op jit(solution)/shard_map/all_gather | solution.py:49
  291.1 6.4 %collective-permute-start.8 = (f32[192,256]{1,0:T(8,128)S(1)}, f32[192,256]{1,0:T(8,128)S(1)}, u32[]{:S(2)}, u32[]{:S(2)}) collective-permute-start(f32[192,256]{1,0:T(8,128)S(1)} %fusion.11), channel_id=1, source_target_pairs={{0,8},{8,0},{16,24},{24,16},{1,9},{9,1},{17,25},{25,17},{2,10},{10... | collective-permute-start | bytes 589832 | tf_op jit(solution)/shard_map/ppermute | solution.py:13
  297.5 9.7 %collective-permute-start.9 = (f32[192,256]{1,0:T(8,128)S(1)}, f32[192,256]{1,0:T(8,128)S(1)}, u32[]{:S(2)}, u32[]{:S(2)}) collective-permute-start(f32[192,256]{1,0:T(8,128)S(1)} %add.44), channel_id=1, source_target_pairs={{0,16},{8,24},{16,0},{24,8},{1,17},{9,25},{17,1},{25,9},{2,18},{10... | collective-permute-start | bytes 589832 | tf_op jit(solution)/shard_map/ppermute | solution.py:13
Sparse Core Ops, SparseCore 0:
  67.6 138.2 reduce-scatter.1
  289.7 34.1 all-gather.4
  326.2 25.0 all-gather.2

commit v2 on v1

v2 whole, which is shorter than its diff:
```python
import math

import jax
import jax.numpy as jnp
from jax import lax
from jax.sharding import PartitionSpec as P


def doubling_sum(x, axis, first, last):
    count = lax.axis_size(axis)
    step = first
    while step < last:
        x = x + lax.ppermute(x, axis, [(i, i ^ step) for i in range(count)])
        step *= 2
    return x


def shards(direct, adjoint, probes):
    high = lax.Precision.HIGHEST
    fast = lax.Precision.HIGH
    row_count = lax.axis_size("rows")
    col_count = lax.axis_size("cols")
    chip_count = col_count // 2
    state_rows, snap_count = direct.shape
    probe_half = probes.shape[1] // 2
    tile_rows = snap_count // row_count
    chip_cols = snap_count // chip_count
    scale = 1.0 / math.sqrt(state_rows * row_count * col_count * snap_count)
    norm_factor = 1.0 / math.sqrt(snap_count)
    partial_hankel = (
        jnp.dot(adjoint.T, direct, precision=fast, preferred_element_type=jnp.float32) * scale
    )
    strip = lax.psum_scatter(partial_hankel, "rows", scatter_dimension=0, tiled=True)
    tile = lax.psum_scatter(strip, "cols", scatter_dimension=1, tiled=True)
    col_index = lax.axis_index("cols")
    core = col_index % 2
    chip = col_index // 2
    other = lax.ppermute(tile, "cols", [(i, i ^ 1) for i in range(col_count)])
    first = core == 0
    chip_tile = jnp.concatenate(
        [jnp.where(first, tile, other), jnp.where(first, other, tile)], axis=1
    )
    own_probes = lax.dynamic_slice_in_dim(probes, core * probe_half, probe_half, 1)
    coef_d = lax.dynamic_slice_in_dim(own_probes, chip * chip_cols, chip_cols, 0)
    coef_a = jnp.zeros((tile_rows, probe_half), jnp.float32)
    for rnd in range(2):
        coef_a = doubling_sum(
            jnp.dot(chip_tile, coef_d, precision=high, preferred_element_type=jnp.float32),
            "cols", 2, col_count,
        )
        coef_d = doubling_sum(
            jnp.dot(chip_tile.T, coef_a, precision=high, preferred_element_type=jnp.float32),
            "rows", 1, row_count,
        )
    half_a = lax.all_gather(coef_a, "rows", axis=0, tiled=True)
    other_a = lax.ppermute(half_a, "cols", [(i, i ^ 1) for i in range(col_count)])
    full_a = jnp.concatenate(
        [jnp.where(first, half_a, other_a), jnp.where(first, other_a, half_a)], axis=1
    )
    gathered_d = lax.all_gather(coef_d, "cols", axis=0, tiled=False)
    full_d = (
        gathered_d.reshape(chip_count, 2, chip_cols, probe_half)
        .transpose(0, 2, 1, 3)
        .reshape(snap_count, 2 * probe_half)
    )
    direct_sum = jnp.dot(direct, full_d, precision=fast, preferred_element_type=jnp.float32)
    adjoint_sum = jnp.dot(adjoint, full_a, precision=fast, preferred_element_type=jnp.float32)
    return (direct_sum * norm_factor, adjoint_sum * norm_factor)


def solution(mesh):
    placed = (P(("rows", "cols"), None), P(("rows", "cols"), None), P())
    return jax.shard_map(
        shards,
        mesh=mesh,
        in_specs=placed,
        out_specs=(P(("rows", "cols"), None), P(("rows", "cols"), None)),
        check_vma=False,
    )
```

time: 370 us -> 287 us (0.78)
  waiting for transfers between devices: 252 us -> 188 us
  local copies, waits for them, and re-layouts: 34.1 us -> 10.1 us
  blocking collectives: 0 us -> 11.4 us
  starting transfers between devices: 11.3 us -> 7.46 us
    reduce_scatter x1, waiting for transfers between devices: 138 us -> 97.8 us  [shards(): lax.psum_scatter(partial_hankel, 'rows', scatter_dimension=0, tiled=True)]
    unnamed x3 -> x4, waiting for transfers between devices: 0.05 us -> 36.4 us
    ppermute x10 -> x8, waiting for transfers between devices: 82.2 us -> 50 us  [doubling_sum(): x = x + lax.ppermute(x, axis, [(i, i ^ step) for i in range(count)])]
    all_gather x2 -> x1, waiting for transfers between devices: 31.1 us -> 0.01 us  [shards(): gathered_d = lax.all_gather(coef_d, 'cols', axis=0, tiled=False)]
    unnamed x8 -> x6, local copies, waits for them, and re-layouts: 25 us -> 7.44 us
    all_gather x0 -> x1, blocking collectives: none -> 11.4 us  [shards(): half_a = lax.all_gather(coef_a, 'rows', axis=0, tiled=True)]
    mul x1 -> x0, local copies, waits for them, and re-layouts: 9.14 us -> none  [shards(): jnp.einsum('nri,ncj->rcij', adjoint.reshape(state_rows, row_count, tile_r...]
    ppermute x10 -> x8, starting transfers between devices: 11.2 us -> 7.08 us  [doubling_sum(): x = x + lax.ppermute(x, axis, [(i, i ^ step) for i in range(count)])]
  transfers between devices with their start and end apart: 13 -> 13, of which waited for: 13 -> 12; matrix products, arithmetic and copies ran while one was open for 4% -> 4% of each run, Pallas kernels for 0% -> 0%
where the time goes in v2:
time: 287 us
  waiting for transfers between devices  188 us (66%)
  matrix products  54.9 us (19%)
  between operations  13.9 us (5%)
  blocking collectives  11.4 us (4%)
  local copies, waits for them, and re-layouts  10.1 us (4%)
  starting transfers between devices  7.46 us (3%)
    reduce_scatter x1, waiting for transfers between devices, shards(): lax.psum_scatter(partial_hankel, 'rows', scatter_dimension=0, tiled=True)  97.8 us
    ppermute x8, waiting for transfers between devices, doubling_sum(): x = x + lax.ppermute(x, axis, [(i, i ^ step) for i in range(count)])  50 us
    unnamed x4, waiting for transfers between devices  36.4 us
    dot_general x1, matrix products, shards(): jnp.dot(adjoint.T, direct, precision=fast, preferred_element_type=jnp.flo...  29.3 us
    all_gather x1, blocking collectives, shards(): half_a = lax.all_gather(coef_a, 'rows', axis=0, tiled=True)  11.4 us
    dot_general x1, matrix products, shards(): jnp.dot(direct, full_d, precision=fast, preferred_element_type=jnp.float32)  10.9 us
    dot_general x1, matrix products, shards(): jnp.dot(adjoint, full_a, precision=fast, preferred_element_type=jnp.float32)  10.7 us
    unnamed x6, local copies, waits for them, and re-layouts  7.44 us
  transfers between devices with their start and end apart: 13, of which 12 were waited for; matrix products, arithmetic and copies ran while one was open for 4% of the time, Pallas kernels for 0%

profile of v2, /device:TPU:0, one launch (start us, length us, event | category | flops | bytes accessed | tf_op | source)
XLA Modules:
  0.0 286.9 jit_solution(9315340995842665224)
XLA Ops:
  7.2 29.3 %convolution_multiply_fusion = f32[1536,1536]{1,0:T(8,128)} fusion(f32[1536,1536]{1,0:T(8,128)} %param.4, f32[1536,1536]{1,0:T(8,128)} %param.3), kind=kOutput, calls=%fused_computation | convolution fusion | flops 21745631232 | bytes 28311552 | tf_op jit(solution)/shard_map/dot_general | solution.py:31
  36.6 97.8 %reduce-scatter.5.cloned.1.call-done = f32[384,1536]{1,0:T(8,128)} async-done(((f32[1536,1536]{1,0:T(8,128)}), f32[384,1536]{1,0:T(8,128)}) %reduce-scatter.5.cloned.1.call-update) | async-done | bytes 2359312 | tf_op jit(solution)/shard_map/reduce_scatter | solution.py:33
  134.5 3.1 %copy.13 = f32[384,1536]{0,1:T(8,128)} copy(f32[384,1536]{1,0:T(8,128)} %reduce-scatter.5.cloned.1.call-done) | data formatting | bytes 4718592
  137.8 36.3 %reduce-scatter.7.cloned.1.call-done = f32[192,384]{1,0:T(8,128)} async-done(((f32[1536,384]{1,0:T(8,128)}), f32[192,384]{1,0:T(8,128)}) %reduce-scatter.7.cloned.1.call-update) | async-done | bytes 294928
  175.4 1.7 collective-permute-done
  178.0 6.9 %collective-permute-done.1 = f32[384,128]{1,0:T(8,128)S(1)} collective-permute-done((f32[384,128]{1,0:T(8,128)S(1)}, f32[384,128]{1,0:T(8,128)S(1)}, u32[]{:S(2)}, u32[]{:S(2)}) %collective-permute-start.1) | collective-permute-done | bytes 196640 | tf_op jit(solution)/shard_map/ppermute | solution.py:13
  185.5 10.7 %collective-permute-done.2 = f32[384,128]{1,0:T(8,128)S(1)} collective-permute-done((f32[384,128]{1,0:T(8,128)S(1)}, f32[384,128]{1,0:T(8,128)S(1)}, u32[]{:S(2)}, u32[]{:S(2)}) %collective-permute-start.2) | collective-permute-done | bytes 196640 | tf_op jit(solution)/shard_map/ppermute | solution.py:13
  197.5 1.4 collective-permute-start.3
  198.9 5.4 %collective-permute-done.3 = f32[384,128]{1,0:T(8,128)S(1)} collective-permute-done((f32[384,128]{1,0:T(8,128)S(1)}, f32[384,128]{1,0:T(8,128)S(1)}, u32[]{:S(2)}, u32[]{:S(2)}) %collective-permute-start.3) | collective-permute-done | bytes 196640 | tf_op jit(solution)/shard_map/ppermute | solution.py:13
  204.4 1.4 collective-permute-start.4
  205.8 4.6 %collective-permute-done.4 = f32[384,128]{1,0:T(8,128)S(1)} collective-permute-done((f32[384,128]{1,0:T(8,128)S(1)}, f32[384,128]{1,0:T(8,128)S(1)}, u32[]{:S(2)}, u32[]{:S(2)}) %collective-permute-start.4) | collective-permute-done | bytes 196640 | tf_op jit(solution)/shard_map/ppermute | solution.py:13
  211.1 5.7 %collective-permute-done.5 = f32[384,128]{1,0:T(8,128)S(1)} collective-permute-done((f32[384,128]{1,0:T(8,128)S(1)}, f32[384,128]{1,0:T(8,128)S(1)}, u32[]{:S(2)}, u32[]{:S(2)}) %collective-permute-start.5) | collective-permute-done | bytes 196640 | tf_op jit(solution)/shard_map/ppermute | solution.py:13
  217.4 8.1 %collective-permute-done.6 = f32[384,128]{1,0:T(8,128)S(1)} collective-permute-done((f32[384,128]{1,0:T(8,128)S(1)}, f32[384,128]{1,0:T(8,128)S(1)}, u32[]{:S(2)}, u32[]{:S(2)}) %collective-permute-start.6) | collective-permute-done | bytes 196640 | tf_op jit(solution)/shard_map/ppermute | solution.py:13
  226.9 1.4 collective-permute-start.7
  228.3 4.3 %collective-permute-done.7 = f32[384,128]{1,0:T(8,128)S(1)} collective-permute-done((f32[384,128]{1,0:T(8,128)S(1)}, f32[384,128]{1,0:T(8,128)S(1)}, u32[]{:S(2)}, u32[]{:S(2)}) %collective-permute-start.7) | collective-permute-done | bytes 196640 | tf_op jit(solution)/shard_map/ppermute | solution.py:13
  232.6 1.4 collective-permute-start.8
  234.1 4.3 %collective-permute-done.8 = f32[384,128]{1,0:T(8,128)S(1)} collective-permute-done((f32[384,128]{1,0:T(8,128)S(1)}, f32[384,128]{1,0:T(8,128)S(1)}, u32[]{:S(2)}, u32[]{:S(2)}) %collective-permute-start.8) | collective-permute-done | bytes 196640 | tf_op jit(solution)/shard_map/ppermute | solution.py:13
  239.1 11.4 %all_gather.11 = f32[1536,128]{1,0:T(8,128)S(1)} all-gather(f32[384,128]{1,0:T(8,128)S(1)} %add.49), channel_id=1, replica_groups=mesh['rows'=4,'cols'=8] {'rows'}, dimensions={0}, use_global_device_ids=true | all-gather | bytes 983040 | tf_op jit(solution)/shard_map/all_gather | solution.py:55
  250.5 2.3 collective-permute-done.9
  252.9 10.7 %fusion.1 = f32[1536,256]{0,1:T(8,128)S(1)} fusion(f32[1536,1536]{1,0:T(8,128)} %param.4, f32[1536,128]{1,0:T(8,128)S(1)} %get-tuple-element.9, f32[1536,128]{1,0:T(8,128)S(1)} %get-tuple-element.8), kind=kOutput, calls=%fused_computation.4 | convolution fusion | flops 3624665088 | bytes 12582912 | tf_op jit(solution)/shard_map/dot_general | solution.py:67
  263.6 1.6 copy.12
  265.2 2.6 copy.10
  267.8 10.9 %fusion = f32[1536,256]{0,1:T(8,128)S(1)} fusion(f32[1536,1536]{1,0:T(8,128)} %param.3, f32[192,8,2,128]{3,2,1,0:T(2,128)S(1)} %bitcast.19), kind=kOutput, calls=%fused_computation.3 | convolution fusion | flops 3624271872 | bytes 12582912 | tf_op jit(solution)/shard_map/dot_general | solution.py:66
  278.7 1.6 copy.11
  (28 shorter events, 7.9 us)
Async XLA Ops:
  7.2 169.9 %copy-start = (f32[1536,256]{1,0:T(8,128)S(1)}, f32[1536,256]{1,0:T(8,128)}, u32[]{:S(2)}) copy-start(f32[1536,256]{1,0:T(8,128)} %param.5) | copy-start | bytes 4718596
  7.2 127.3 %reduce-scatter.5.cloned.1.call-start = ((), (), s32[]{:S(2)}) async-start(), calls=%async_computation.2 | async-start | bytes 11796480 | tf_op jit(solution)/shard_map/reduce_scatter | solution.py:33
  36.6 137.6 %reduce-scatter.7.cloned.1.call-start = ((), (), s32[]{:S(2)}) async-start(), calls=%async_computation.4 | async-start | bytes 2654208
  137.6 127.7 %all-gather.3.cloned.1.call-start = ((), (), s32[]{:S(2)}) async-start(), calls=%async_computation.3 | async-start | bytes 1769472 | tf_op jit(solution)/shard_map/all_gather | solution.py:60
  175.3 1.8 collective-permute-start
  177.9 7.0 %collective-permute-start.1 = (f32[384,128]{1,0:T(8,128)S(1)}, f32[384,128]{1,0:T(8,128)S(1)}, u32[]{:S(2)}, u32[]{:S(2)}) collective-permute-start(f32[384,128]{1,0:T(8,128)S(1)} %fusion.11), channel_id=1, source_target_pairs={{0,2},{1,3},{2,0},{3,1},{4,6},{5,7},{6,4},{7,5},{8,10},{9,11},{10,... | collective-permute-start | bytes 589832 | tf_op jit(solution)/shard_map/ppermute | solution.py:13
  184.9 11.3 %collective-permute-start.2 = (f32[384,128]{1,0:T(8,128)S(1)}, f32[384,128]{1,0:T(8,128)S(1)}, u32[]{:S(2)}, u32[]{:S(2)}) collective-permute-start(f32[384,128]{1,0:T(8,128)S(1)} %add.44), channel_id=1, source_target_pairs={{0,4},{1,5},{2,6},{3,7},{4,0},{5,1},{6,2},{7,3},{8,12},{9,13},{10,... | collective-permute-start | bytes 589832 | tf_op jit(solution)/shard_map/ppermute | solution.py:13
  197.5 6.8 %collective-permute-start.3 = (f32[384,128]{1,0:T(8,128)S(1)}, f32[384,128]{1,0:T(8,128)S(1)}, u32[]{:S(2)}, u32[]{:S(2)}) collective-permute-start(f32[384,128]{1,0:T(8,128)S(1)} %fusion.9), channel_id=1, source_target_pairs={{0,8},{8,0},{16,24},{24,16},{1,9},{9,1},{17,25},{25,17},{2,10},{10... | collective-permute-start | bytes 589832 | tf_op jit(solution)/shard_map/ppermute | solution.py:13
  204.4 6.0 %collective-permute-start.4 = (f32[384,128]{1,0:T(8,128)S(1)}, f32[384,128]{1,0:T(8,128)S(1)}, u32[]{:S(2)}, u32[]{:S(2)}) collective-permute-start(f32[384,128]{1,0:T(8,128)S(1)} %add.46), channel_id=1, source_target_pairs={{0,16},{8,24},{16,0},{24,8},{1,17},{9,25},{17,1},{25,9},{2,18},{10... | collective-permute-start | bytes 589832 | tf_op jit(solution)/shard_map/ppermute | solution.py:13
  211.1 5.7 %collective-permute-start.5 = (f32[384,128]{1,0:T(8,128)S(1)}, f32[384,128]{1,0:T(8,128)S(1)}, u32[]{:S(2)}, u32[]{:S(2)}) collective-permute-start(f32[384,128]{1,0:T(8,128)S(1)} %fusion.7), channel_id=1, source_target_pairs={{0,2},{1,3},{2,0},{3,1},{4,6},{5,7},{6,4},{7,5},{8,10},{9,11},{10,... | collective-permute-start | bytes 589832 | tf_op jit(solution)/shard_map/ppermute | solution.py:13
  216.8 8.8 %collective-permute-start.6 = (f32[384,128]{1,0:T(8,128)S(1)}, f32[384,128]{1,0:T(8,128)S(1)}, u32[]{:S(2)}, u32[]{:S(2)}) collective-permute-start(f32[384,128]{1,0:T(8,128)S(1)} %add.48), channel_id=1, source_target_pairs={{0,4},{1,5},{2,6},{3,7},{4,0},{5,1},{6,2},{7,3},{8,12},{9,13},{10,... | collective-permute-start | bytes 589832 | tf_op jit(solution)/shard_map/ppermute | solution.py:13
  226.9 5.7 %collective-permute-start.7 = (f32[384,128]{1,0:T(8,128)S(1)}, f32[384,128]{1,0:T(8,128)S(1)}, u32[]{:S(2)}, u32[]{:S(2)}) collective-permute-start(f32[384,128]{1,0:T(8,128)S(1)} %fusion.14), channel_id=1, source_target_pairs={{0,8},{8,0},{16,24},{24,16},{1,9},{9,1},{17,25},{25,17},{2,10},{10... | collective-permute-start | bytes 589832 | tf_op jit(solution)/shard_map/ppermute | solution.py:13
  232.6 5.7 %collective-permute-start.8 = (f32[384,128]{1,0:T(8,128)S(1)}, f32[384,128]{1,0:T(8,128)S(1)}, u32[]{:S(2)}, u32[]{:S(2)}) collective-permute-start(f32[384,128]{1,0:T(8,128)S(1)} %add.50), channel_id=1, source_target_pairs={{0,16},{8,24},{16,0},{24,8},{1,17},{9,25},{17,1},{25,9},{2,18},{10... | collective-permute-start | bytes 589832 | tf_op jit(solution)/shard_map/ppermute | solution.py:13
  250.5 2.3 collective-permute-start.9
Sparse Core Ops, SparseCore 0:
  36.7 97.7 reduce-scatter.4
  137.7 36.4 reduce-scatter.6
  239.2 24.6 all-gather.2

commit v3 on v2

v3 whole, which is shorter than its diff:
```python
import math

import jax
import jax.numpy as jnp
from jax import lax
from jax.sharding import PartitionSpec as P


def exchange(x, axis, step):
    count = lax.axis_size(axis)
    return lax.ppermute(x, axis, [(i, i ^ step) for i in range(count)])


def doubling_sum(x, axis, first, last):
    step = first
    while step < last:
        x = x + exchange(x, axis, step)
        step *= 2
    return x


def in_order(first, mine, theirs, axis):
    return jnp.concatenate(
        [jnp.where(first, mine, theirs), jnp.where(first, theirs, mine)], axis=axis
    )


def shards(direct, adjoint, probes):
    high = lax.Precision.HIGHEST
    fast = lax.Precision.HIGH
    row_count = lax.axis_size("rows")
    col_count = lax.axis_size("cols")
    chip_count = col_count // 2
    state_rows, snap_count = direct.shape
    probe_half = probes.shape[1] // 2
    half_rows = snap_count // 2
    part_rows = half_rows // row_count
    chip_cols = snap_count // chip_count
    scale = 1.0 / math.sqrt(state_rows * row_count * col_count * snap_count)
    norm_factor = 1.0 / math.sqrt(snap_count)
    col_index = lax.axis_index("cols")
    core = col_index % 2
    chip = col_index // 2
    first = core == 0
    partial_hankel = (
        jnp.dot(adjoint.T, direct, precision=fast, preferred_element_type=jnp.float32) * scale
    )
    keep = lax.dynamic_slice_in_dim(partial_hankel, core * half_rows, half_rows, 0)
    send = lax.dynamic_slice_in_dim(partial_hankel, (1 - core) * half_rows, half_rows, 0)
    chip_sum = keep + exchange(send, "cols", 1)
    strip = lax.psum_scatter(chip_sum, "rows", scatter_dimension=0, tiled=True)
    bits = chip_count.bit_length() - 1
    strip = strip.reshape((part_rows,) + (2,) * bits + (chip_cols,))
    for bit in range(bits):
        mine = (chip >> bit) % 2
        kept = lax.dynamic_index_in_dim(strip, mine, axis=strip.ndim - 2, keepdims=False)
        sent = lax.dynamic_index_in_dim(strip, 1 - mine, axis=strip.ndim - 2, keepdims=False)
        strip = kept + exchange(sent, "cols", 2 << bit)
    tile = strip
    chip_tile = in_order(first, tile, exchange(tile, "cols", 1), 0)
    own_probes = lax.dynamic_slice_in_dim(probes, core * probe_half, probe_half, 1)
    coef_d = lax.dynamic_slice_in_dim(own_probes, chip * chip_cols, chip_cols, 0)
    coef_a = jnp.zeros((2 * part_rows, probe_half), jnp.float32)
    for rnd in range(2):
        coef_a = doubling_sum(
            jnp.dot(chip_tile, coef_d, precision=high, preferred_element_type=jnp.float32),
            "cols", 2, col_count,
        )
        coef_d = doubling_sum(
            jnp.dot(chip_tile.T, coef_a, precision=high, preferred_element_type=jnp.float32),
            "rows", 1, row_count,
        )
    gathered_a = lax.all_gather(coef_a, "rows", axis=0, tiled=False)
    half_a = (
        gathered_a.reshape(row_count, 2, part_rows, probe_half)
        .transpose(1, 0, 2, 3)
        .reshape(snap_count, probe_half)
    )
    full_a = in_order(first, half_a, exchange(half_a, "cols", 1), 1)
    gathered_d = lax.all_gather(coef_d, "cols", axis=0, tiled=False)
    full_d = (
        gathered_d.reshape(chip_count, 2, chip_cols, probe_half)
        .transpose(0, 2, 1, 3)
        .reshape(snap_count, 2 * probe_half)
    )
    direct_sum = jnp.dot(direct, full_d, precision=fast, preferred_element_type=jnp.float32)
    adjoint_sum = jnp.dot(adjoint, full_a, precision=fast, preferred_element_type=jnp.float32)
    return (direct_sum * norm_factor, adjoint_sum * norm_factor)


def solution(mesh):
    placed = (P(("rows", "cols"), None), P(("rows", "cols"), None), P())
    return jax.shard_map(
        shards,
        mesh=mesh,
        in_specs=placed,
        out_specs=(P(("rows", "cols"), None), P(("rows", "cols"), None)),
        check_vma=False,
    )
```

time: 287 us -> 267 us (0.930)
  waiting for transfers between devices: 188 us -> 142 us
  starting transfers between devices: 7.46 us -> 17.6 us
  other arithmetic: 0.96 us -> 8.27 us
  local copies, waits for them, and re-layouts: 10.1 us -> 14.9 us
  matrix products: 54.9 us -> 57.9 us
    reduce_scatter x1, waiting for transfers between devices: 97.8 us -> 59.6 us  [shards(): strip = lax.psum_scatter(chip_sum, 'rows', scatter_dimension=0, tiled=True)]
    unnamed x4 -> x2, waiting for transfers between devices: 36.4 us -> 0.03 us
    ppermute x10 -> x13, waiting for transfers between devices: 53.9 us -> 82.8 us  [exchange(): return lax.ppermute(x, axis, [(i, i ^ step) for i in range(count)])]
    ppermute x10 -> x13, starting transfers between devices: 7.15 us -> 17.3 us  [exchange(): return lax.ppermute(x, axis, [(i, i ^ step) for i in range(count)])]
    add x6 -> x9, other arithmetic: 0.81 us -> 8.12 us  [the longest x1 6.88 us: shards(): chip_sum = keep + exchange(send, 'cols', 1)]
    dynamic_slice x0 -> x3, local copies, waits for them, and re-layouts: none -> 4.22 us  [the longest x1 2.69 us: shards(): lax.dynamic_slice_in_dim(partial_hankel, (1 - core) * half_rows, half_row...]
    dot_general x1, matrix products: 29.3 us -> 32.6 us  [shards(): jnp.dot(adjoint.T, direct, precision=fast, preferred_element_type=jnp.flo...]
    unnamed x6 -> x8, local copies, waits for them, and re-layouts: 7.44 us -> 5.95 us
  transfers between devices with their start and end apart: 13 -> 15, of which waited for: 12 -> 14; matrix products, arithmetic and copies ran while one was open for 4% -> 5% of each run, Pallas kernels for 0% -> 0%
where the time goes in v3:
time: 267 us
  waiting for transfers between devices  142 us (53%)
  matrix products  57.9 us (22%)
  starting transfers between devices  17.6 us (7%)
  local copies, waits for them, and re-layouts  14.9 us (6%)
  between operations  14.3 us (5%)
  blocking collectives  11.2 us (4%)
  other arithmetic  8.27 us (3%)
    ppermute x13, waiting for transfers between devices, exchange(): return lax.ppermute(x, axis, [(i, i ^ step) for i in range(count)])  82.8 us
    reduce_scatter x1, waiting for transfers between devices, shards(): strip = lax.psum_scatter(chip_sum, 'rows', scatter_dimension=0, tiled=True)  59.6 us
    dot_general x1, matrix products, shards(): jnp.dot(adjoint.T, direct, precision=fast, preferred_element_type=jnp.flo...  32.6 us
    ppermute x13, starting transfers between devices, exchange(): return lax.ppermute(x, axis, [(i, i ^ step) for i in range(count)])  17.3 us
    all_gather x1, blocking collectives, shards(): gathered_a = lax.all_gather(coef_a, 'rows', axis=0, tiled=False)  11.2 us
    dot_general x1, matrix products, shards(): jnp.dot(direct, full_d, precision=fast, preferred_element_type=jnp.float32)  10.9 us
    dot_general x1, matrix products, shards(): jnp.dot(adjoint, full_a, precision=fast, preferred_element_type=jnp.float32)  10.7 us
    add x1, other arithmetic, shards(): chip_sum = keep + exchange(send, 'cols', 1)  6.88 us
  transfers between devices with their start and end apart: 15, of which 14 were waited for; matrix products, arithmetic and copies ran while one was open for 5% of the time, Pallas kernels for 0%

profile of v3, /device:TPU:0, one launch (start us, length us, event | category | flops | bytes accessed | tf_op | source)
XLA Modules:
  0.0 266.6 jit_solution(16534227849287177902)
XLA Ops:
  7.2 32.6 %convolution_multiply_fusion = f32[1536,1536]{1,0:T(8,128)S(1)} fusion(f32[1536,1536]{1,0:T(8,128)} %param.4, f32[1536,1536]{1,0:T(8,128)} %param.3), kind=kOutput, calls=%fused_computation | convolution fusion | flops 21745631232 | bytes 28311552 | tf_op jit(solution)/shard_map/dot_general | solution.py:46
  39.8 2.7 %constant_dynamic-slice_fusion.4 = f32[768,1536]{1,0:T(8,128)} fusion(f32[1536,1536]{1,0:T(8,128)S(1)} %convolution_multiply_fusion, s32[]{:T(128)S(6)} %select_n.76), kind=kLoop, calls=%fused_computation.31 | loop fusion | bytes 9437188 | tf_op jit(solution)/shard_map/dynamic_slice | solution.py:49
  42.5 2.4 copy-done.1
  45.4 7.9 %collective-permute-done = f32[768,1536]{1,0:T(8,128)} collective-permute-done((f32[768,1536]{1,0:T(8,128)}, f32[768,1536]{1,0:T(8,128)}, u32[]{:S(2)}, u32[]{:S(2)}) %collective-permute-start) | collective-permute-done | bytes 4718624 | tf_op jit(solution)/shard_map/ppermute | solution.py:11
  53.2 6.9 %dynamic-slice_add_fusion = f32[768,1536]{1,0:T(8,128)} fusion(f32[768,1536]{1,0:T(8,128)} %collective-permute-done, f32[1536,1536]{1,0:T(8,128)} %copy-done.1, s32[]{:T(128)S(6)} %select_n.75), kind=kLoop, calls=%fused_computation.1 | loop fusion | flops 1179648 | bytes 14155780 | tf_op jit(solution)/shard_map/add | solution.py:50
  60.4 59.6 %reduce-scatter.2.cloned.1.call-done = f32[192,1536]{1,0:T(8,128)} async-done(((f32[768,1536]{1,0:T(8,128)}), f32[192,1536]{1,0:T(8,128)}) %reduce-scatter.2.cloned.1.call-update) | async-done | bytes 1179664 | tf_op jit(solution)/shard_map/reduce_scatter | solution.py:51
  125.0 13.6 %collective-permute-done.1 = f32[192,2,384]{2,1,0:T(2,128)S(1)} collective-permute-done((f32[192,2,384]{2,1,0:T(2,128)S(1)}, f32[192,2,384]{2,1,0:T(2,128)S(1)}, u32[]{:S(2)}, u32[]{:S(2)}) %collective-permute-start.1) | collective-permute-done | bytes 589856 | tf_op jit(solution)/shard_map/ppermute | solution.py:11
  139.5 2.5 collective-permute-start.2
  142.0 12.7 %collective-permute-done.2 = f32[192,384]{1,0:T(8,128)S(1)} collective-permute-done((f32[192,384]{1,0:T(8,128)S(1)}, f32[192,384]{1,0:T(8,128)S(1)}, u32[]{:S(2)}, u32[]{:S(2)}) %collective-permute-start.2) | collective-permute-done | bytes 294944 | tf_op jit(solution)/shard_map/ppermute | solution.py:11
  157.7 6.5 %collective-permute-done.4 = f32[384,128]{1,0:T(8,128)S(1)} collective-permute-done((f32[384,128]{1,0:T(8,128)S(1)}, f32[384,128]{1,0:T(8,128)S(1)}, u32[]{:S(2)}, u32[]{:S(2)}) %collective-permute-start.4) | collective-permute-done | bytes 196640 | tf_op jit(solution)/shard_map/ppermute | solution.py:11
  164.2 2.2 collective-permute-start.5
  166.4 9.1 %collective-permute-done.5 = f32[384,128]{1,0:T(8,128)S(1)} collective-permute-done((f32[384,128]{1,0:T(8,128)S(1)}, f32[384,128]{1,0:T(8,128)S(1)}, u32[]{:S(2)}, u32[]{:S(2)}) %collective-permute-start.5) | collective-permute-done | bytes 196640 | tf_op jit(solution)/shard_map/ppermute | solution.py:11
  178.0 4.8 %collective-permute-done.6 = f32[384,128]{1,0:T(8,128)S(1)} collective-permute-done((f32[384,128]{1,0:T(8,128)S(1)}, f32[384,128]{1,0:T(8,128)S(1)}, u32[]{:S(2)}, u32[]{:S(2)}) %collective-permute-start.6) | collective-permute-done | bytes 196640 | tf_op jit(solution)/shard_map/ppermute | solution.py:11
  184.2 4.3 %collective-permute-done.7 = f32[384,128]{1,0:T(8,128)S(1)} collective-permute-done((f32[384,128]{1,0:T(8,128)S(1)}, f32[384,128]{1,0:T(8,128)S(1)}, u32[]{:S(2)}, u32[]{:S(2)}) %collective-permute-start.7) | collective-permute-done | bytes 196640 | tf_op jit(solution)/shard_map/ppermute | solution.py:11
  190.7 4.3 %collective-permute-done.8 = f32[384,128]{1,0:T(8,128)S(1)} collective-permute-done((f32[384,128]{1,0:T(8,128)S(1)}, f32[384,128]{1,0:T(8,128)S(1)}, u32[]{:S(2)}, u32[]{:S(2)}) %collective-permute-start.8) | collective-permute-done | bytes 196640 | tf_op jit(solution)/shard_map/ppermute | solution.py:11
  195.0 2.8 %collective-permute-start.9 = (f32[384,128]{1,0:T(8,128)S(1)}, f32[384,128]{1,0:T(8,128)S(1)}, u32[]{:S(2)}, u32[]{:S(2)}) collective-permute-start(f32[384,128]{1,0:T(8,128)S(1)} %add.94), channel_id=1, source_target_pairs={{0,4},{1,5},{2,6},{3,7},{4,0},{5,1},{6,2},{7,3},{8,12},{9,13},{10,... | collective-permute-start | bytes 589832 | tf_op jit(solution)/shard_map/ppermute | solution.py:11
  197.8 6.6 %collective-permute-done.9 = f32[384,128]{1,0:T(8,128)S(1)} collective-permute-done((f32[384,128]{1,0:T(8,128)S(1)}, f32[384,128]{1,0:T(8,128)S(1)}, u32[]{:S(2)}, u32[]{:S(2)}) %collective-permute-start.9) | collective-permute-done | bytes 196640 | tf_op jit(solution)/shard_map/ppermute | solution.py:11
  207.0 4.3 %collective-permute-done.10 = f32[384,128]{1,0:T(8,128)S(1)} collective-permute-done((f32[384,128]{1,0:T(8,128)S(1)}, f32[384,128]{1,0:T(8,128)S(1)}, u32[]{:S(2)}, u32[]{:S(2)}) %collective-permute-start.10) | collective-permute-done | bytes 196640 | tf_op jit(solution)/shard_map/ppermute | solution.py:11
  212.7 5.1 %collective-permute-done.11 = f32[384,128]{1,0:T(8,128)S(1)} collective-permute-done((f32[384,128]{1,0:T(8,128)S(1)}, f32[384,128]{1,0:T(8,128)S(1)}, u32[]{:S(2)}, u32[]{:S(2)}) %collective-permute-start.11) | collective-permute-done | bytes 196640 | tf_op jit(solution)/shard_map/ppermute | solution.py:11
  218.5 11.2 %all-gather.1 = f32[1536,128]{1,0:T(8,128)S(1)} all-gather(f32[384,128]{1,0:T(8,128)S(1)} %add.95), channel_id=3, replica_groups=mesh['rows'=4,'cols'=8] {'rows'}, dimensions={0}, use_global_device_ids=true | all-gather | bytes 983040 | tf_op jit(solution)/shard_map/all_gather | solution.py:73
  229.9 2.3 collective-permute-done.12
  232.2 10.7 %fusion.1 = f32[1536,256]{0,1:T(8,128)S(1)} fusion(f32[1536,1536]{1,0:T(8,128)} %param.4, f32[1536,128]{1,0:T(8,128)S(1)} %get-tuple-element.7, f32[1536,128]{1,0:T(8,128)S(1)} %get-tuple-element.6), kind=kOutput, calls=%fused_computation.5 | convolution fusion | flops 3624665088 | bytes 12582912 | tf_op jit(solution)/shard_map/dot_general | solution.py:87
  244.6 2.6 copy.7
  247.2 10.9 %fusion = f32[1536,256]{0,1:T(8,128)S(1)} fusion(f32[1536,1536]{1,0:T(8,128)} %param.3, f32[192,8,2,128]{3,2,1,0:T(2,128)S(1)} %bitcast.32), kind=kOutput, calls=%fused_computation.4 | convolution fusion | flops 3624271872 | bytes 12582912 | tf_op jit(solution)/shard_map/dot_general | solution.py:86
  (41 shorter events, 23.9 us)
Async XLA Ops:
  7.2 149.2 %copy-start = (f32[1536,256]{1,0:T(8,128)S(1)}, f32[1536,256]{1,0:T(8,128)}, u32[]{:S(2)}) copy-start(f32[1536,256]{1,0:T(8,128)} %param.5) | copy-start | bytes 4718596
  7.2 112.8 %reduce-scatter.2.cloned.1.call-start = ((), (), s32[]{:S(2)}) async-start(), calls=%async_computation.1 | async-start | bytes 5898240 | tf_op jit(solution)/shard_map/reduce_scatter | solution.py:51
  39.8 5.1 %copy-start.1 = (f32[1536,1536]{1,0:T(8,128)}, f32[1536,1536]{1,0:T(8,128)S(1)}, u32[]{:S(2)}) copy-start(f32[1536,1536]{1,0:T(8,128)S(1)} %convolution_multiply_fusion) | copy-start | bytes 28311556
  44.9 8.3 %collective-permute-start = (f32[768,1536]{1,0:T(8,128)}, f32[768,1536]{1,0:T(8,128)}, u32[]{:S(2)}, u32[]{:S(2)}) collective-permute-start(f32[768,1536]{1,0:T(8,128)} %constant_dynamic-slice_fusion.4), channel_id=1, source_target_pairs={{0,1},{1,0},{2,3},{3,2},{4,5},{5,4},{6,7},{7,6},{8,9},{9,8},{10,11... | collective-permute-start | bytes 14155784 | tf_op jit(solution)/shard_map/ppermute | solution.py:11
  60.1 184.4 %all-gather.4.cloned.1.call-start = ((), (), s32[]{:S(2)}) async-start(), calls=%async_computation.2 | async-start | bytes 1769472 | tf_op jit(solution)/shard_map/all_gather | solution.py:80
  123.4 15.1 %collective-permute-start.1 = (f32[192,2,384]{2,1,0:T(2,128)S(1)}, f32[192,2,384]{2,1,0:T(2,128)S(1)}, u32[]{:S(2)}, u32[]{:S(2)}) collective-permute-start(f32[192,2,384]{2,1,0:T(2,128)S(1)} %bitcast.36), channel_id=1, source_target_pairs={{0,2},{1,3},{2,0},{3,1},{4,6},{5,7},{6,4},{7,5},{8,10},{9,11},{10,... | collective-permute-start | bytes 1769480 | tf_op jit(solution)/shard_map/ppermute | solution.py:11
  139.5 15.2 %collective-permute-start.2 = (f32[192,384]{1,0:T(8,128)S(1)}, f32[192,384]{1,0:T(8,128)S(1)}, u32[]{:S(2)}, u32[]{:S(2)}) collective-permute-start(f32[192,384]{1,0:T(8,128)S(1)} %bitcast.37), channel_id=1, source_target_pairs={{0,4},{1,5},{2,6},{3,7},{4,0},{5,1},{6,2},{7,3},{8,12},{9,13},{10,... | collective-permute-start | bytes 884744 | tf_op jit(solution)/shard_map/ppermute | solution.py:11
  154.7 1.6 collective-permute-start.3
  157.1 7.0 %collective-permute-start.4 = (f32[384,128]{1,0:T(8,128)S(1)}, f32[384,128]{1,0:T(8,128)S(1)}, u32[]{:S(2)}, u32[]{:S(2)}) collective-permute-start(f32[384,128]{1,0:T(8,128)S(1)} %fusion.10), channel_id=1, source_target_pairs={{0,2},{1,3},{2,0},{3,1},{4,6},{5,7},{6,4},{7,5},{8,10},{9,11},{10,... | collective-permute-start | bytes 589832 | tf_op jit(solution)/shard_map/ppermute | solution.py:11
  164.2 11.3 %collective-permute-start.5 = (f32[384,128]{1,0:T(8,128)S(1)}, f32[384,128]{1,0:T(8,128)S(1)}, u32[]{:S(2)}, u32[]{:S(2)}) collective-permute-start(f32[384,128]{1,0:T(8,128)S(1)} %add.90), channel_id=1, source_target_pairs={{0,4},{1,5},{2,6},{3,7},{4,0},{5,1},{6,2},{7,3},{8,12},{9,13},{10,... | collective-permute-start | bytes 589832 | tf_op jit(solution)/shard_map/ppermute | solution.py:11
  176.6 6.2 %collective-permute-start.6 = (f32[384,128]{1,0:T(8,128)S(1)}, f32[384,128]{1,0:T(8,128)S(1)}, u32[]{:S(2)}, u32[]{:S(2)}) collective-permute-start(f32[384,128]{1,0:T(8,128)S(1)} %fusion.9), channel_id=1, source_target_pairs={{0,8},{8,0},{16,24},{24,16},{1,9},{9,1},{17,25},{25,17},{2,10},{10... | collective-permute-start | bytes 589832 | tf_op jit(solution)/shard_map/ppermute | solution.py:11
  182.8 5.7 %collective-permute-start.7 = (f32[384,128]{1,0:T(8,128)S(1)}, f32[384,128]{1,0:T(8,128)S(1)}, u32[]{:S(2)}, u32[]{:S(2)}) collective-permute-start(f32[384,128]{1,0:T(8,128)S(1)} %add.92), channel_id=1, source_target_pairs={{0,16},{8,24},{16,0},{24,8},{1,17},{9,25},{17,1},{25,9},{2,18},{10... | collective-permute-start | bytes 589832 | tf_op jit(solution)/shard_map/ppermute | solution.py:11
  189.2 5.7 %collective-permute-start.8 = (f32[384,128]{1,0:T(8,128)S(1)}, f32[384,128]{1,0:T(8,128)S(1)}, u32[]{:S(2)}, u32[]{:S(2)}) collective-permute-start(f32[384,128]{1,0:T(8,128)S(1)} %fusion.8), channel_id=1, source_target_pairs={{0,2},{1,3},{2,0},{3,1},{4,6},{5,7},{6,4},{7,5},{8,10},{9,11},{10,... | collective-permute-start | bytes 589832 | tf_op jit(solution)/shard_map/ppermute | solution.py:11
  195.0 9.4 %collective-permute-start.9 = (f32[384,128]{1,0:T(8,128)S(1)}, f32[384,128]{1,0:T(8,128)S(1)}, u32[]{:S(2)}, u32[]{:S(2)}) collective-permute-start(f32[384,128]{1,0:T(8,128)S(1)} %add.94), channel_id=1, source_target_pairs={{0,4},{1,5},{2,6},{3,7},{4,0},{5,1},{6,2},{7,3},{8,12},{9,13},{10,... | collective-permute-start | bytes 589832 | tf_op jit(solution)/shard_map/ppermute | solution.py:11
  205.6 5.7 %collective-permute-start.10 = (f32[384,128]{1,0:T(8,128)S(1)}, f32[384,128]{1,0:T(8,128)S(1)}, u32[]{:S(2)}, u32[]{:S(2)}) collective-permute-start(f32[384,128]{1,0:T(8,128)S(1)} %fusion.7), channel_id=1, source_target_pairs={{0,8},{8,0},{16,24},{24,16},{1,9},{9,1},{17,25},{25,17},{2,10},{10... | collective-permute-start | bytes 589832 | tf_op jit(solution)/shard_map/ppermute | solution.py:11
  211.3 6.5 %collective-permute-start.11 = (f32[384,128]{1,0:T(8,128)S(1)}, f32[384,128]{1,0:T(8,128)S(1)}, u32[]{:S(2)}, u32[]{:S(2)}) collective-permute-start(f32[384,128]{1,0:T(8,128)S(1)} %add.96), channel_id=1, source_target_pairs={{0,16},{8,24},{16,0},{24,8},{1,17},{9,25},{17,1},{25,9},{2,18},{10... | collective-permute-start | bytes 589832 | tf_op jit(solution)/shard_map/ppermute | solution.py:11
  229.8 2.4 collective-permute-start.12
Sparse Core Ops, SparseCore 0:
  60.3 59.6 reduce-scatter.1
  218.7 24.5 all-gather.3

commit v4 on v3

--- a/solution.py
+++ b/solution.py
@@ -42,12 +42,13 @@
     core = col_index % 2
     chip = col_index // 2
     first = core == 0
-    partial_hankel = (
-        jnp.dot(adjoint.T, direct, precision=fast, preferred_element_type=jnp.float32) * scale
-    )
-    keep = lax.dynamic_slice_in_dim(partial_hankel, core * half_rows, half_rows, 0)
-    send = lax.dynamic_slice_in_dim(partial_hankel, (1 - core) * half_rows, half_rows, 0)
-    chip_sum = keep + exchange(send, "cols", 1)
+    def partial_rows(start):
+        columns = lax.dynamic_slice_in_dim(adjoint, start, half_rows, 1)
+        return jnp.dot(columns.T, direct, precision=fast, preferred_element_type=jnp.float32) * scale
+
+    received = exchange(partial_rows((1 - core) * half_rows), "cols", 1)
+    kept_rows = lax.optimization_barrier(partial_rows(core * half_rows))
+    chip_sum = kept_rows + received
     strip = lax.psum_scatter(chip_sum, "rows", scatter_dimension=0, tiled=True)
     bits = chip_count.bit_length() - 1
     strip = strip.reshape((part_rows,) + (2,) * bits + (chip_cols,))

time: 267 us -> 254 us (0.951)
  waiting for transfers between devices: 142 us -> 135 us
  local copies, waits for them, and re-layouts: 14.9 us -> 9.81 us
    ppermute x13, waiting for transfers between devices: 82.8 us -> 75.1 us  [exchange(): return lax.ppermute(x, axis, [(i, i ^ step) for i in range(count)])]
    dynamic_slice x1 -> x0, local copies, waits for them, and re-layouts: 2.69 us -> none  [shards(): lax.dynamic_slice_in_dim(partial_hankel, (1 - core) * half_rows, half_row...]
    unnamed x8 -> x6, local copies, waits for them, and re-layouts: 5.95 us -> 3.56 us
    dot_general x1 -> x2, matrix products: 32.6 us -> 34.5 us  [partial_rows(): jnp.dot(columns.T, direct, precision=fast, preferred_element_type=jnp.flo...]
  transfers between devices with their start and end apart: 15 -> 15, of which waited for: 14 -> 13; matrix products, arithmetic and copies ran while one was open for 5% -> 12% of each run, Pallas kernels for 0% -> 0%
where the time goes in v4:
time: 254 us
  waiting for transfers between devices  135 us (53%)
  matrix products  60 us (24%)
  starting transfers between devices  17.5 us (7%)
  between operations  14.3 us (6%)
  blocking collectives  11 us (4%)
  local copies, waits for them, and re-layouts  9.81 us (4%)
  other arithmetic  6.9 us (3%)
    ppermute x13, waiting for transfers between devices, exchange(): return lax.ppermute(x, axis, [(i, i ^ step) for i in range(count)])  75.1 us
    reduce_scatter x1, waiting for transfers between devices, shards(): strip = lax.psum_scatter(chip_sum, 'rows', scatter_dimension=0, tiled=True)  59.5 us
    dot_general x2, matrix products, partial_rows(): jnp.dot(columns.T, direct, precision=fast, preferred_element_type=jnp.flo...  34.5 us
    ppermute x13, starting transfers between devices, exchange(): return lax.ppermute(x, axis, [(i, i ^ step) for i in range(count)])  17.4 us
    all_gather x1, blocking collectives, shards(): gathered_a = lax.all_gather(coef_a, 'rows', axis=0, tiled=False)  11 us
    dot_general x1, matrix products, shards(): jnp.dot(adjoint, full_a, precision=fast, preferred_element_type=jnp.float32)  11 us
    dot_general x1, matrix products, shards(): jnp.dot(direct, full_d, precision=fast, preferred_element_type=jnp.float32)  10.9 us
    add x1, other arithmetic, shards(): chip_sum = kept_rows + received  5.51 us
  transfers between devices with their start and end apart: 15, of which 13 were waited for; matrix products, arithmetic and copies ran while one was open for 12% of the time, Pallas kernels for 0%

profile of v4, /device:TPU:0, one launch (start us, length us, event | category | flops | bytes accessed | tf_op | source)
XLA Modules:
  0.0 254.2 jit_solution(17233952485128074575)
XLA Ops:
  7.2 16.2 %fusion.7 = f32[768,1536]{1,0:T(8,128)} fusion(f32[1536,1536]{1,0:T(8,128)} %param.3, f32[1536,1536]{1,0:T(8,128)} %param.4, s32[]{:T(128)S(6)} %select_n.76), kind=kOutput, calls=%fused_computation.5 | convolution fusion | flops 10872815616 | bytes 18874372 | tf_op jit(solution)/shard_map/dot_general | solution.py:47
  23.9 18.3 %fusion.4 = f32[768,1536]{1,0:T(8,128)S(1)} fusion(f32[1536,1536]{1,0:T(8,128)} %param.3, f32[1536,1536]{1,0:T(8,128)} %param.4, s32[]{:T(128)S(6)} %select_n.75), kind=kOutput, calls=%fused_computation.4 | convolution fusion | flops 10872815616 | bytes 18874372 | tf_op jit(solution)/shard_map/dot_general | solution.py:47
  42.2 5.5 %add.79 = f32[768,1536]{1,0:T(8,128)} add(f32[768,1536]{1,0:T(8,128)S(1)} %fusion.4, f32[768,1536]{1,0:T(8,128)} %collective-permute-done) | non-fusion elementwise | flops 1179648 | bytes 14155776 | tf_op jit(solution)/shard_map/add | solution.py:51
  47.9 59.5 %reduce-scatter.2.cloned.1.call-done = f32[192,1536]{1,0:T(8,128)} async-done(((f32[768,1536]{1,0:T(8,128)}), f32[192,1536]{1,0:T(8,128)}) %reduce-scatter.2.cloned.1.call-update) | async-done | bytes 1179664 | tf_op jit(solution)/shard_map/reduce_scatter | solution.py:52
  107.4 2.0 reshape.19
  112.3 13.6 %collective-permute-done.1 = f32[192,2,384]{2,1,0:T(2,128)S(1)} collective-permute-done((f32[192,2,384]{2,1,0:T(2,128)S(1)}, f32[192,2,384]{2,1,0:T(2,128)S(1)}, u32[]{:S(2)}, u32[]{:S(2)}) %collective-permute-start.1) | collective-permute-done | bytes 589856 | tf_op jit(solution)/shard_map/ppermute | solution.py:11
  126.9 2.5 collective-permute-start.2
  129.3 12.7 %collective-permute-done.2 = f32[192,384]{1,0:T(8,128)S(1)} collective-permute-done((f32[192,384]{1,0:T(8,128)S(1)}, f32[192,384]{1,0:T(8,128)S(1)}, u32[]{:S(2)}, u32[]{:S(2)}) %collective-permute-start.2) | collective-permute-done | bytes 294944 | tf_op jit(solution)/shard_map/ppermute | solution.py:11
  145.1 6.5 %collective-permute-done.4 = f32[384,128]{1,0:T(8,128)S(1)} collective-permute-done((f32[384,128]{1,0:T(8,128)S(1)}, f32[384,128]{1,0:T(8,128)S(1)}, u32[]{:S(2)}, u32[]{:S(2)}) %collective-permute-start.4) | collective-permute-done | bytes 196640 | tf_op jit(solution)/shard_map/ppermute | solution.py:11
  151.6 2.2 collective-permute-start.5
  153.7 9.1 %collective-permute-done.5 = f32[384,128]{1,0:T(8,128)S(1)} collective-permute-done((f32[384,128]{1,0:T(8,128)S(1)}, f32[384,128]{1,0:T(8,128)S(1)}, u32[]{:S(2)}, u32[]{:S(2)}) %collective-permute-start.5) | collective-permute-done | bytes 196640 | tf_op jit(solution)/shard_map/ppermute | solution.py:11
  165.4 4.7 %collective-permute-done.6 = f32[384,128]{1,0:T(8,128)S(1)} collective-permute-done((f32[384,128]{1,0:T(8,128)S(1)}, f32[384,128]{1,0:T(8,128)S(1)}, u32[]{:S(2)}, u32[]{:S(2)}) %collective-permute-start.6) | collective-permute-done | bytes 196640 | tf_op jit(solution)/shard_map/ppermute | solution.py:11
  171.6 4.3 %collective-permute-done.7 = f32[384,128]{1,0:T(8,128)S(1)} collective-permute-done((f32[384,128]{1,0:T(8,128)S(1)}, f32[384,128]{1,0:T(8,128)S(1)}, u32[]{:S(2)}, u32[]{:S(2)}) %collective-permute-start.7) | collective-permute-done | bytes 196640 | tf_op jit(solution)/shard_map/ppermute | solution.py:11
  178.1 4.2 %collective-permute-done.8 = f32[384,128]{1,0:T(8,128)S(1)} collective-permute-done((f32[384,128]{1,0:T(8,128)S(1)}, f32[384,128]{1,0:T(8,128)S(1)}, u32[]{:S(2)}, u32[]{:S(2)}) %collective-permute-start.8) | collective-permute-done | bytes 196640 | tf_op jit(solution)/shard_map/ppermute | solution.py:11
  182.3 2.9 %collective-permute-start.9 = (f32[384,128]{1,0:T(8,128)S(1)}, f32[384,128]{1,0:T(8,128)S(1)}, u32[]{:S(2)}, u32[]{:S(2)}) collective-permute-start(f32[384,128]{1,0:T(8,128)S(1)} %add.94), channel_id=1, source_target_pairs={{0,4},{1,5},{2,6},{3,7},{4,0},{5,1},{6,2},{7,3},{8,12},{9,13},{10,... | collective-permute-start | bytes 589832 | tf_op jit(solution)/shard_map/ppermute | solution.py:11
  185.2 6.6 %collective-permute-done.9 = f32[384,128]{1,0:T(8,128)S(1)} collective-permute-done((f32[384,128]{1,0:T(8,128)S(1)}, f32[384,128]{1,0:T(8,128)S(1)}, u32[]{:S(2)}, u32[]{:S(2)}) %collective-permute-start.9) | collective-permute-done | bytes 196640 | tf_op jit(solution)/shard_map/ppermute | solution.py:11
  194.4 4.3 %collective-permute-done.10 = f32[384,128]{1,0:T(8,128)S(1)} collective-permute-done((f32[384,128]{1,0:T(8,128)S(1)}, f32[384,128]{1,0:T(8,128)S(1)}, u32[]{:S(2)}, u32[]{:S(2)}) %collective-permute-start.10) | collective-permute-done | bytes 196640 | tf_op jit(solution)/shard_map/ppermute | solution.py:11
  200.1 5.3 %collective-permute-done.11 = f32[384,128]{1,0:T(8,128)S(1)} collective-permute-done((f32[384,128]{1,0:T(8,128)S(1)}, f32[384,128]{1,0:T(8,128)S(1)}, u32[]{:S(2)}, u32[]{:S(2)}) %collective-permute-start.11) | collective-permute-done | bytes 196640 | tf_op jit(solution)/shard_map/ppermute | solution.py:11
  206.2 11.0 %all-gather.1 = f32[1536,128]{1,0:T(8,128)S(1)} all-gather(f32[384,128]{1,0:T(8,128)S(1)} %add.95), channel_id=3, replica_groups=mesh['rows'=4,'cols'=8] {'rows'}, dimensions={0}, use_global_device_ids=true | all-gather | bytes 983040 | tf_op jit(solution)/shard_map/all_gather | solution.py:74
  217.3 2.3 collective-permute-done.12
  219.6 11.0 %fusion.11 = f32[1536,256]{0,1:T(8,128)S(1)} fusion(f32[1536,1536]{1,0:T(8,128)} %param.4, f32[1536,128]{1,0:T(8,128)S(1)} %get-tuple-element.7, f32[1536,128]{1,0:T(8,128)S(1)} %get-tuple-element.6), kind=kOutput, calls=%fused_computation.9 | convolution fusion | flops 3624665088 | bytes 12582912 | tf_op jit(solution)/shard_map/dot_general | solution.py:88
  230.6 1.6 copy.10
  232.2 2.6 %copy.7 = f32[4,2,384,128]{3,1,2,0:T(2,128)S(1)} copy(f32[4,2,384,128]{3,2,1,0:T(8,128)} %bitcast.35) | data formatting | bytes 3145728 | tf_op jit(solution)/shard_map/reshape | solution.py:83
  234.9 10.9 %fusion.10 = f32[1536,256]{0,1:T(8,128)S(1)} fusion(f32[1536,1536]{1,0:T(8,128)} %param.3, f32[192,8,2,128]{3,2,1,0:T(2,128)S(1)} %bitcast.32), kind=kOutput, calls=%fused_computation.8 | convolution fusion | flops 3624271872 | bytes 12582912 | tf_op jit(solution)/shard_map/dot_general | solution.py:87
  (39 shorter events, 20.2 us)
Async XLA Ops:
  7.2 136.6 %copy-start = (f32[1536,256]{1,0:T(8,128)S(1)}, f32[1536,256]{1,0:T(8,128)}, u32[]{:S(2)}) copy-start(f32[1536,256]{1,0:T(8,128)} %param.5) | copy-start | bytes 4718596
  7.2 100.2 %reduce-scatter.2.cloned.1.call-start = ((), (), s32[]{:S(2)}) async-start(), calls=%async_computation.1 | async-start | bytes 5898240 | tf_op jit(solution)/shard_map/reduce_scatter | solution.py:52
  23.5 18.7 %collective-permute-start = (f32[768,1536]{1,0:T(8,128)}, f32[768,1536]{1,0:T(8,128)}, u32[]{:S(2)}, u32[]{:S(2)}) collective-permute-start(f32[768,1536]{1,0:T(8,128)} %fusion.7), channel_id=1, source_target_pairs={{0,1},{1,0},{2,3},{3,2},{4,5},{5,4},{6,7},{7,6},{8,9},{9,8},{10,11... | collective-permute-start | bytes 14155784 | tf_op jit(solution)/shard_map/ppermute | solution.py:11
  47.8 184.5 %all-gather.4.cloned.1.call-start = ((), (), s32[]{:S(2)}) async-start(), calls=%async_computation.2 | async-start | bytes 1769472 | tf_op jit(solution)/shard_map/all_gather | solution.py:81
  110.8 15.1 %collective-permute-start.1 = (f32[192,2,384]{2,1,0:T(2,128)S(1)}, f32[192,2,384]{2,1,0:T(2,128)S(1)}, u32[]{:S(2)}, u32[]{:S(2)}) collective-permute-start(f32[192,2,384]{2,1,0:T(2,128)S(1)} %bitcast.36), channel_id=1, source_target_pairs={{0,2},{1,3},{2,0},{3,1},{4,6},{5,7},{6,4},{7,5},{8,10},{9,11},{10,... | collective-permute-start | bytes 1769480 | tf_op jit(solution)/shard_map/ppermute | solution.py:11
  126.9 15.2 %collective-permute-start.2 = (f32[192,384]{1,0:T(8,128)S(1)}, f32[192,384]{1,0:T(8,128)S(1)}, u32[]{:S(2)}, u32[]{:S(2)}) collective-permute-start(f32[192,384]{1,0:T(8,128)S(1)} %bitcast.37), channel_id=1, source_target_pairs={{0,4},{1,5},{2,6},{3,7},{4,0},{5,1},{6,2},{7,3},{8,12},{9,13},{10,... | collective-permute-start | bytes 884744 | tf_op jit(solution)/shard_map/ppermute | solution.py:11
  142.1 1.6 collective-permute-start.3
  144.5 7.0 %collective-permute-start.4 = (f32[384,128]{1,0:T(8,128)S(1)}, f32[384,128]{1,0:T(8,128)S(1)}, u32[]{:S(2)}, u32[]{:S(2)}) collective-permute-start(f32[384,128]{1,0:T(8,128)S(1)} %fusion.20), channel_id=1, source_target_pairs={{0,2},{1,3},{2,0},{3,1},{4,6},{5,7},{6,4},{7,5},{8,10},{9,11},{10,... | collective-permute-start | bytes 589832 | tf_op jit(solution)/shard_map/ppermute | solution.py:11
  151.6 11.3 %collective-permute-start.5 = (f32[384,128]{1,0:T(8,128)S(1)}, f32[384,128]{1,0:T(8,128)S(1)}, u32[]{:S(2)}, u32[]{:S(2)}) collective-permute-start(f32[384,128]{1,0:T(8,128)S(1)} %add.90), channel_id=1, source_target_pairs={{0,4},{1,5},{2,6},{3,7},{4,0},{5,1},{6,2},{7,3},{8,12},{9,13},{10,... | collective-permute-start | bytes 589832 | tf_op jit(solution)/shard_map/ppermute | solution.py:11
  164.0 6.2 %collective-permute-start.6 = (f32[384,128]{1,0:T(8,128)S(1)}, f32[384,128]{1,0:T(8,128)S(1)}, u32[]{:S(2)}, u32[]{:S(2)}) collective-permute-start(f32[384,128]{1,0:T(8,128)S(1)} %fusion.19), channel_id=1, source_target_pairs={{0,8},{8,0},{16,24},{24,16},{1,9},{9,1},{17,25},{25,17},{2,10},{10... | collective-permute-start | bytes 589832 | tf_op jit(solution)/shard_map/ppermute | solution.py:11
  170.2 5.7 %collective-permute-start.7 = (f32[384,128]{1,0:T(8,128)S(1)}, f32[384,128]{1,0:T(8,128)S(1)}, u32[]{:S(2)}, u32[]{:S(2)}) collective-permute-start(f32[384,128]{1,0:T(8,128)S(1)} %add.92), channel_id=1, source_target_pairs={{0,16},{8,24},{16,0},{24,8},{1,17},{9,25},{17,1},{25,9},{2,18},{10... | collective-permute-start | bytes 589832 | tf_op jit(solution)/shard_map/ppermute | solution.py:11
  176.6 5.7 %collective-permute-start.8 = (f32[384,128]{1,0:T(8,128)S(1)}, f32[384,128]{1,0:T(8,128)S(1)}, u32[]{:S(2)}, u32[]{:S(2)}) collective-permute-start(f32[384,128]{1,0:T(8,128)S(1)} %fusion.18), channel_id=1, source_target_pairs={{0,2},{1,3},{2,0},{3,1},{4,6},{5,7},{6,4},{7,5},{8,10},{9,11},{10,... | collective-permute-start | bytes 589832 | tf_op jit(solution)/shard_map/ppermute | solution.py:11
  182.3 9.5 %collective-permute-start.9 = (f32[384,128]{1,0:T(8,128)S(1)}, f32[384,128]{1,0:T(8,128)S(1)}, u32[]{:S(2)}, u32[]{:S(2)}) collective-permute-start(f32[384,128]{1,0:T(8,128)S(1)} %add.94), channel_id=1, source_target_pairs={{0,4},{1,5},{2,6},{3,7},{4,0},{5,1},{6,2},{7,3},{8,12},{9,13},{10,... | collective-permute-start | bytes 589832 | tf_op jit(solution)/shard_map/ppermute | solution.py:11
  193.0 5.7 %collective-permute-start.10 = (f32[384,128]{1,0:T(8,128)S(1)}, f32[384,128]{1,0:T(8,128)S(1)}, u32[]{:S(2)}, u32[]{:S(2)}) collective-permute-start(f32[384,128]{1,0:T(8,128)S(1)} %fusion.17), channel_id=1, source_target_pairs={{0,8},{8,0},{16,24},{24,16},{1,9},{9,1},{17,25},{25,17},{2,10},{10... | collective-permute-start | bytes 589832 | tf_op jit(solution)/shard_map/ppermute | solution.py:11
  198.7 6.7 %collective-permute-start.11 = (f32[384,128]{1,0:T(8,128)S(1)}, f32[384,128]{1,0:T(8,128)S(1)}, u32[]{:S(2)}, u32[]{:S(2)}) collective-permute-start(f32[384,128]{1,0:T(8,128)S(1)} %add.96), channel_id=1, source_target_pairs={{0,16},{8,24},{16,0},{24,8},{1,17},{9,25},{17,1},{25,9},{2,18},{10... | collective-permute-start | bytes 589832 | tf_op jit(solution)/shard_map/ppermute | solution.py:11
  217.2 2.4 collective-permute-start.12
Sparse Core Ops, SparseCore 0:
  47.9 59.4 reduce-scatter.1
  206.3 24.2 all-gather.3

commit v5 on v4

--- a/solution.py
+++ b/solution.py
@@ -71,7 +71,12 @@
             jnp.dot(chip_tile.T, coef_a, precision=high, preferred_element_type=jnp.float32),
             "rows", 1, row_count,
         )
-    gathered_a = lax.all_gather(coef_a, "rows", axis=0, tiled=False)
+    gathered_a = coef_a[None]
+    step = 1
+    while step < row_count:
+        low = (lax.axis_index("rows") & step) == 0
+        gathered_a = in_order(low, gathered_a, exchange(gathered_a, "rows", step), 0)
+        step *= 2
     half_a = (
         gathered_a.reshape(row_count, 2, part_rows, probe_half)
         .transpose(1, 0, 2, 3)

time: 254 us -> 256 us (level)
  blocking collectives: 11 us -> 0 us
  waiting for transfers between devices: 135 us -> 145 us
    all_gather x1 -> x0, blocking collectives: 11 us -> none  [shards(): gathered_a = lax.all_gather(coef_a, 'rows', axis=0, tiled=False)]
    ppermute x13 -> x15, waiting for transfers between devices: 75.1 us -> 81.7 us  [exchange(): return lax.ppermute(x, axis, [(i, i ^ step) for i in range(count)])]
    all_gather x1, waiting for transfers between devices: 0.01 us -> 3.84 us  [shards(): gathered_d = lax.all_gather(coef_d, 'cols', axis=0, tiled=False)]
    ppermute x13 -> x15, starting transfers between devices: 17.4 us -> 19.7 us  [exchange(): return lax.ppermute(x, axis, [(i, i ^ step) for i in range(count)])]
  transfers between devices with their start and end apart: 15 -> 17, of which waited for: 13 -> 16; matrix products, arithmetic and copies ran while one was open for 12% -> 12% of each run, Pallas kernels for 0% -> 0%
where the time goes in v5:
time: 256 us
  waiting for transfers between devices  145 us (57%)
  matrix products  60 us (23%)
  starting transfers between devices  19.8 us (8%)
  between operations  14.3 us (6%)
  local copies, waits for them, and re-layouts  9.81 us (4%)
  other arithmetic  7.08 us (3%)
    ppermute x15, waiting for transfers between devices, exchange(): return lax.ppermute(x, axis, [(i, i ^ step) for i in range(count)])  81.7 us
    reduce_scatter x1, waiting for transfers between devices, shards(): strip = lax.psum_scatter(chip_sum, 'rows', scatter_dimension=0, tiled=True)  59.5 us
    dot_general x2, matrix products, partial_rows(): jnp.dot(columns.T, direct, precision=fast, preferred_element_type=jnp.flo...  34.6 us
    ppermute x15, starting transfers between devices, exchange(): return lax.ppermute(x, axis, [(i, i ^ step) for i in range(count)])  19.7 us
    dot_general x1, matrix products, shards(): jnp.dot(adjoint, full_a, precision=fast, preferred_element_type=jnp.float32)  10.9 us
    dot_general x1, matrix products, shards(): jnp.dot(direct, full_d, precision=fast, preferred_element_type=jnp.float32)  10.9 us
    add x1, other arithmetic, shards(): chip_sum = kept_rows + received  5.53 us
  transfers between devices with their start and end apart: 17, of which 16 were waited for; matrix products, arithmetic and copies ran while one was open for 12% of the time, Pallas kernels for 0%

profile of v5, /device:TPU:0, one launch (start us, length us, event | category | flops | bytes accessed | tf_op | source)
XLA Modules:
  0.0 256.1 jit_solution(16545081328059845668)
XLA Ops:
  7.2 16.3 %fusion.7 = f32[768,1536]{1,0:T(8,128)} fusion(f32[1536,1536]{1,0:T(8,128)} %param.3, f32[1536,1536]{1,0:T(8,128)} %param.4, s32[]{:T(128)S(6)} %select_n.100), kind=kOutput, calls=%fused_computation.5 | convolution fusion | flops 10872815616 | bytes 18874372 | tf_op jit(solution)/shard_map/dot_general | solution.py:47
  24.0 18.3 %fusion.4 = f32[768,1536]{1,0:T(8,128)S(1)} fusion(f32[1536,1536]{1,0:T(8,128)} %param.3, f32[1536,1536]{1,0:T(8,128)} %param.4, s32[]{:T(128)S(6)} %select_n.99), kind=kOutput, calls=%fused_computation.4 | convolution fusion | flops 10872815616 | bytes 18874372 | tf_op jit(solution)/shard_map/dot_general | solution.py:47
  42.3 5.5 %add.79 = f32[768,1536]{1,0:T(8,128)} add(f32[768,1536]{1,0:T(8,128)S(1)} %fusion.4, f32[768,1536]{1,0:T(8,128)} %collective-permute-done) | non-fusion elementwise | flops 1179648 | bytes 14155776 | tf_op jit(solution)/shard_map/add | solution.py:51
  47.9 59.5 %reduce-scatter.2.cloned.1.call-done = f32[192,1536]{1,0:T(8,128)} async-done(((f32[768,1536]{1,0:T(8,128)}), f32[192,1536]{1,0:T(8,128)}) %reduce-scatter.2.cloned.1.call-update) | async-done | bytes 1179664 | tf_op jit(solution)/shard_map/reduce_scatter | solution.py:52
  107.5 2.0 reshape.19
  112.4 13.6 %collective-permute-done.1 = f32[192,2,384]{2,1,0:T(2,128)S(1)} collective-permute-done((f32[192,2,384]{2,1,0:T(2,128)S(1)}, f32[192,2,384]{2,1,0:T(2,128)S(1)}, u32[]{:S(2)}, u32[]{:S(2)}) %collective-permute-start.1) | collective-permute-done | bytes 589856 | tf_op jit(solution)/shard_map/ppermute | solution.py:11
  126.9 2.5 collective-permute-start.2
  129.4 12.7 %collective-permute-done.2 = f32[192,384]{1,0:T(8,128)S(1)} collective-permute-done((f32[192,384]{1,0:T(8,128)S(1)}, f32[192,384]{1,0:T(8,128)S(1)}, u32[]{:S(2)}, u32[]{:S(2)}) %collective-permute-start.2) | collective-permute-done | bytes 294944 | tf_op jit(solution)/shard_map/ppermute | solution.py:11
  145.2 6.4 %collective-permute-done.4 = f32[384,128]{1,0:T(8,128)S(1)} collective-permute-done((f32[384,128]{1,0:T(8,128)S(1)}, f32[384,128]{1,0:T(8,128)S(1)}, u32[]{:S(2)}, u32[]{:S(2)}) %collective-permute-start.4) | collective-permute-done | bytes 196640 | tf_op jit(solution)/shard_map/ppermute | solution.py:11
  151.6 2.2 collective-permute-start.5
  153.8 9.1 %collective-permute-done.5 = f32[384,128]{1,0:T(8,128)S(1)} collective-permute-done((f32[384,128]{1,0:T(8,128)S(1)}, f32[384,128]{1,0:T(8,128)S(1)}, u32[]{:S(2)}, u32[]{:S(2)}) %collective-permute-start.5) | collective-permute-done | bytes 196640 | tf_op jit(solution)/shard_map/ppermute | solution.py:11
  165.5 4.7 %collective-permute-done.6 = f32[384,128]{1,0:T(8,128)S(1)} collective-permute-done((f32[384,128]{1,0:T(8,128)S(1)}, f32[384,128]{1,0:T(8,128)S(1)}, u32[]{:S(2)}, u32[]{:S(2)}) %collective-permute-start.6) | collective-permute-done | bytes 196640 | tf_op jit(solution)/shard_map/ppermute | solution.py:11
  171.7 4.3 %collective-permute-done.7 = f32[384,128]{1,0:T(8,128)S(1)} collective-permute-done((f32[384,128]{1,0:T(8,128)S(1)}, f32[384,128]{1,0:T(8,128)S(1)}, u32[]{:S(2)}, u32[]{:S(2)}) %collective-permute-start.7) | collective-permute-done | bytes 196640 | tf_op jit(solution)/shard_map/ppermute | solution.py:11
  178.1 4.2 %collective-permute-done.8 = f32[384,128]{1,0:T(8,128)S(1)} collective-permute-done((f32[384,128]{1,0:T(8,128)S(1)}, f32[384,128]{1,0:T(8,128)S(1)}, u32[]{:S(2)}, u32[]{:S(2)}) %collective-permute-start.8) | collective-permute-done | bytes 196640 | tf_op jit(solution)/shard_map/ppermute | solution.py:11
  182.4 2.9 %collective-permute-start.9 = (f32[384,128]{1,0:T(8,128)S(1)}, f32[384,128]{1,0:T(8,128)S(1)}, u32[]{:S(2)}, u32[]{:S(2)}) collective-permute-start(f32[384,128]{1,0:T(8,128)S(1)} %add.94), channel_id=1, source_target_pairs={{0,4},{1,5},{2,6},{3,7},{4,0},{5,1},{6,2},{7,3},{8,12},{9,13},{10,... | collective-permute-start | bytes 589832 | tf_op jit(solution)/shard_map/ppermute | solution.py:11
  185.3 6.6 %collective-permute-done.9 = f32[384,128]{1,0:T(8,128)S(1)} collective-permute-done((f32[384,128]{1,0:T(8,128)S(1)}, f32[384,128]{1,0:T(8,128)S(1)}, u32[]{:S(2)}, u32[]{:S(2)}) %collective-permute-start.9) | collective-permute-done | bytes 196640 | tf_op jit(solution)/shard_map/ppermute | solution.py:11
  195.2 3.6 %collective-permute-done.10 = f32[384,128]{1,0:T(8,128)S(1)} collective-permute-done((f32[384,128]{1,0:T(8,128)S(1)}, f32[384,128]{1,0:T(8,128)S(1)}, u32[]{:S(2)}, u32[]{:S(2)}) %collective-permute-start.10) | collective-permute-done | bytes 196640 | tf_op jit(solution)/shard_map/ppermute | solution.py:11
  200.9 5.6 %collective-permute-done.11 = f32[384,128]{1,0:T(8,128)S(1)} collective-permute-done((f32[384,128]{1,0:T(8,128)S(1)}, f32[384,128]{1,0:T(8,128)S(1)}, u32[]{:S(2)}, u32[]{:S(2)}) %collective-permute-start.11) | collective-permute-done | bytes 196640 | tf_op jit(solution)/shard_map/ppermute | solution.py:11
  208.7 6.4 %collective-permute-done.13 = f32[2,384,128]{2,1,0:T(8,128)S(1)} collective-permute-done((f32[2,384,128]{2,1,0:T(8,128)S(1)}, f32[2,384,128]{2,1,0:T(8,128)S(1)}, u32[]{:S(2)}, u32[]{:S(2)}) %collective-permute-start.13) | collective-permute-done | bytes 393248 | tf_op jit(solution)/shard_map/ppermute | solution.py:11
  215.4 2.3 collective-permute-done.14
  217.8 10.9 %fusion.11 = f32[1536,256]{0,1:T(8,128)S(1)} fusion(f32[1536,1536]{1,0:T(8,128)} %param.4, f32[1536,128]{1,0:T(8,128)S(1)} %get-tuple-element.7, f32[1536,128]{1,0:T(8,128)S(1)} %get-tuple-element.6), kind=kOutput, calls=%fused_computation.9 | convolution fusion | flops 3624665088 | bytes 12582912 | tf_op jit(solution)/shard_map/dot_general | solution.py:93
  230.3 3.8 %all-gather.3.cloned.1.call-done = f32[3072,128]{1,0:T(8,128)} async-done(((f32[384,128]{1,0:T(8,128)}), f32[3072,128]{1,0:T(8,128)}) %all-gather.3.cloned.1.call-update) | async-done | bytes 1572880 | tf_op jit(solution)/shard_map/all_gather | solution.py:86
  234.1 2.6 %copy.7 = f32[4,2,384,128]{3,1,2,0:T(2,128)S(1)} copy(f32[4,2,384,128]{3,2,1,0:T(8,128)} %bitcast.36) | data formatting | bytes 3145728 | tf_op jit(solution)/shard_map/reshape | solution.py:88
  236.8 10.9 %fusion.10 = f32[1536,256]{0,1:T(8,128)S(1)} fusion(f32[1536,1536]{1,0:T(8,128)} %param.3, f32[192,8,2,128]{3,2,1,0:T(2,128)S(1)} %bitcast.33), kind=kOutput, calls=%fused_computation.8 | convolution fusion | flops 3624271872 | bytes 12582912 | tf_op jit(solution)/shard_map/dot_general | solution.py:92
  (46 shorter events, 24.8 us)
Async XLA Ops:
  7.2 136.7 %copy-start = (f32[1536,256]{1,0:T(8,128)S(1)}, f32[1536,256]{1,0:T(8,128)}, u32[]{:S(2)}) copy-start(f32[1536,256]{1,0:T(8,128)} %param.5) | copy-start | bytes 4718596
  7.2 100.3 %reduce-scatter.2.cloned.1.call-start = ((), (), s32[]{:S(2)}) async-start(), calls=%async_computation.1 | async-start | bytes 5898240 | tf_op jit(solution)/shard_map/reduce_scatter | solution.py:52
  23.6 18.7 %collective-permute-start = (f32[768,1536]{1,0:T(8,128)}, f32[768,1536]{1,0:T(8,128)}, u32[]{:S(2)}, u32[]{:S(2)}) collective-permute-start(f32[768,1536]{1,0:T(8,128)} %fusion.7), channel_id=1, source_target_pairs={{0,1},{1,0},{2,3},{3,2},{4,5},{5,4},{6,7},{7,6},{8,9},{9,8},{10,11... | collective-permute-start | bytes 14155784 | tf_op jit(solution)/shard_map/ppermute | solution.py:11
  47.8 186.3 %all-gather.3.cloned.1.call-start = ((), (), s32[]{:S(2)}) async-start(), calls=%async_computation.2 | async-start | bytes 1769472 | tf_op jit(solution)/shard_map/all_gather | solution.py:86
  110.9 15.1 %collective-permute-start.1 = (f32[192,2,384]{2,1,0:T(2,128)S(1)}, f32[192,2,384]{2,1,0:T(2,128)S(1)}, u32[]{:S(2)}, u32[]{:S(2)}) collective-permute-start(f32[192,2,384]{2,1,0:T(2,128)S(1)} %bitcast.37), channel_id=1, source_target_pairs={{0,2},{1,3},{2,0},{3,1},{4,6},{5,7},{6,4},{7,5},{8,10},{9,11},{10,... | collective-permute-start | bytes 1769480 | tf_op jit(solution)/shard_map/ppermute | solution.py:11
  126.9 15.2 %collective-permute-start.2 = (f32[192,384]{1,0:T(8,128)S(1)}, f32[192,384]{1,0:T(8,128)S(1)}, u32[]{:S(2)}, u32[]{:S(2)}) collective-permute-start(f32[192,384]{1,0:T(8,128)S(1)} %bitcast.38), channel_id=1, source_target_pairs={{0,4},{1,5},{2,6},{3,7},{4,0},{5,1},{6,2},{7,3},{8,12},{9,13},{10,... | collective-permute-start | bytes 884744 | tf_op jit(solution)/shard_map/ppermute | solution.py:11
  142.1 1.6 collective-permute-start.3
  144.6 7.0 %collective-permute-start.4 = (f32[384,128]{1,0:T(8,128)S(1)}, f32[384,128]{1,0:T(8,128)S(1)}, u32[]{:S(2)}, u32[]{:S(2)}) collective-permute-start(f32[384,128]{1,0:T(8,128)S(1)} %fusion.20), channel_id=1, source_target_pairs={{0,2},{1,3},{2,0},{3,1},{4,6},{5,7},{6,4},{7,5},{8,10},{9,11},{10,... | collective-permute-start | bytes 589832 | tf_op jit(solution)/shard_map/ppermute | solution.py:11
  151.6 11.3 %collective-permute-start.5 = (f32[384,128]{1,0:T(8,128)S(1)}, f32[384,128]{1,0:T(8,128)S(1)}, u32[]{:S(2)}, u32[]{:S(2)}) collective-permute-start(f32[384,128]{1,0:T(8,128)S(1)} %add.90), channel_id=1, source_target_pairs={{0,4},{1,5},{2,6},{3,7},{4,0},{5,1},{6,2},{7,3},{8,12},{9,13},{10,... | collective-permute-start | bytes 589832 | tf_op jit(solution)/shard_map/ppermute | solution.py:11
  164.1 6.1 %collective-permute-start.6 = (f32[384,128]{1,0:T(8,128)S(1)}, f32[384,128]{1,0:T(8,128)S(1)}, u32[]{:S(2)}, u32[]{:S(2)}) collective-permute-start(f32[384,128]{1,0:T(8,128)S(1)} %fusion.19), channel_id=1, source_target_pairs={{0,8},{8,0},{16,24},{24,16},{1,9},{9,1},{17,25},{25,17},{2,10},{10... | collective-permute-start | bytes 589832 | tf_op jit(solution)/shard_map/ppermute | solution.py:11
  170.2 5.7 %collective-permute-start.7 = (f32[384,128]{1,0:T(8,128)S(1)}, f32[384,128]{1,0:T(8,128)S(1)}, u32[]{:S(2)}, u32[]{:S(2)}) collective-permute-start(f32[384,128]{1,0:T(8,128)S(1)} %add.92), channel_id=1, source_target_pairs={{0,16},{8,24},{16,0},{24,8},{1,17},{9,25},{17,1},{25,9},{2,18},{10... | collective-permute-start | bytes 589832 | tf_op jit(solution)/shard_map/ppermute | solution.py:11
  176.6 5.7 %collective-permute-start.8 = (f32[384,128]{1,0:T(8,128)S(1)}, f32[384,128]{1,0:T(8,128)S(1)}, u32[]{:S(2)}, u32[]{:S(2)}) collective-permute-start(f32[384,128]{1,0:T(8,128)S(1)} %fusion.18), channel_id=1, source_target_pairs={{0,2},{1,3},{2,0},{3,1},{4,6},{5,7},{6,4},{7,5},{8,10},{9,11},{10,... | collective-permute-start | bytes 589832 | tf_op jit(solution)/shard_map/ppermute | solution.py:11
  182.4 9.5 %collective-permute-start.9 = (f32[384,128]{1,0:T(8,128)S(1)}, f32[384,128]{1,0:T(8,128)S(1)}, u32[]{:S(2)}, u32[]{:S(2)}) collective-permute-start(f32[384,128]{1,0:T(8,128)S(1)} %add.94), channel_id=1, source_target_pairs={{0,4},{1,5},{2,6},{3,7},{4,0},{5,1},{6,2},{7,3},{8,12},{9,13},{10,... | collective-permute-start | bytes 589832 | tf_op jit(solution)/shard_map/ppermute | solution.py:11
  193.0 5.7 %collective-permute-start.10 = (f32[384,128]{1,0:T(8,128)S(1)}, f32[384,128]{1,0:T(8,128)S(1)}, u32[]{:S(2)}, u32[]{:S(2)}) collective-permute-start(f32[384,128]{1,0:T(8,128)S(1)} %fusion.17), channel_id=1, source_target_pairs={{0,8},{8,0},{16,24},{24,16},{1,9},{9,1},{17,25},{25,17},{2,10},{10... | collective-permute-start | bytes 589832 | tf_op jit(solution)/shard_map/ppermute | solution.py:11
  194.5 6.4 %collective-permute-start.12 = (f32[1,384,128]{2,1,0:T(8,128)S(1)}, f32[1,384,128]{2,1,0:T(8,128)S(1)}, u32[]{:S(2)}, u32[]{:S(2)}) collective-permute-start(f32[1,384,128]{2,1,0:T(8,128)S(1)} %add_bitcast_fusion), channel_id=1, source_target_pairs={{0,8},{8,0},{16,24},{24,16},{1,9},{9,1},{17,25},{25,17},{2,10},{10... | collective-permute-start | bytes 589832 | tf_op jit(solution)/shard_map/ppermute | solution.py:11
  198.8 7.7 %collective-permute-start.11 = (f32[384,128]{1,0:T(8,128)S(1)}, f32[384,128]{1,0:T(8,128)S(1)}, u32[]{:S(2)}, u32[]{:S(2)}) collective-permute-start(f32[384,128]{1,0:T(8,128)S(1)} %add.96), channel_id=1, source_target_pairs={{0,16},{8,24},{16,0},{24,8},{1,17},{9,25},{17,1},{25,9},{2,18},{10... | collective-permute-start | bytes 589832 | tf_op jit(solution)/shard_map/ppermute | solution.py:11
  207.3 7.8 %collective-permute-start.13 = (f32[2,384,128]{2,1,0:T(8,128)S(1)}, f32[2,384,128]{2,1,0:T(8,128)S(1)}, u32[]{:S(2)}, u32[]{:S(2)}) collective-permute-start(f32[2,384,128]{2,1,0:T(8,128)S(1)} %pad_maximum_fusion.2), channel_id=1, source_target_pairs={{0,16},{8,24},{16,0},{24,8},{1,17},{9,25},{17,1},{25,9},{2,18},{10... | collective-permute-start | bytes 1179656 | tf_op jit(solution)/shard_map/ppermute | solution.py:11
  215.3 2.4 collective-permute-start.14
Sparse Core Ops, SparseCore 0:
  48.0 59.4 reduce-scatter.1
  207.4 26.7 all-gather.2

commit v6 on v4

--- a/solution.py
+++ b/solution.py
@@ -60,17 +60,24 @@
     tile = strip
     chip_tile = in_order(first, tile, exchange(tile, "cols", 1), 0)
     own_probes = lax.dynamic_slice_in_dim(probes, core * probe_half, probe_half, 1)
-    coef_d = lax.dynamic_slice_in_dim(own_probes, chip * chip_cols, chip_cols, 0)
-    coef_a = jnp.zeros((2 * part_rows, probe_half), jnp.float32)
-    for rnd in range(2):
-        coef_a = doubling_sum(
-            jnp.dot(chip_tile, coef_d, precision=high, preferred_element_type=jnp.float32),
-            "cols", 2, col_count,
-        )
-        coef_d = doubling_sum(
-            jnp.dot(chip_tile.T, coef_a, precision=high, preferred_element_type=jnp.float32),
-            "rows", 1, row_count,
-        )
+    probes_d = lax.dynamic_slice_in_dim(own_probes, chip * chip_cols, chip_cols, 0)
+    chains_a, chains_d = [], []
+    quarter = probe_half // 2
+    for chain in range(2):
+        coef_d = probes_d[:, chain * quarter:(chain + 1) * quarter]
+        for rnd in range(2):
+            coef_a = doubling_sum(
+                jnp.dot(chip_tile, coef_d, precision=high, preferred_element_type=jnp.float32),
+                "cols", 2, col_count,
+            )
+            coef_d = doubling_sum(
+                jnp.dot(chip_tile.T, coef_a, precision=high, preferred_element_type=jnp.float32),
+                "rows", 1, row_count,
+            )
+        chains_a.append(coef_a)
+        chains_d.append(coef_d)
+    coef_a = jnp.concatenate(chains_a, axis=1)
+    coef_d = jnp.concatenate(chains_d, axis=1)
     gathered_a = lax.all_gather(coef_a, "rows", axis=0, tiled=False)
     half_a = (
         gathered_a.reshape(row_count, 2, part_rows, probe_half)

time: 254 us -> 248 us (0.976)
  waiting for transfers between devices: 135 us -> 110 us
  starting transfers between devices: 17.5 us -> 30.6 us
    ppermute x13 -> x21, waiting for transfers between devices: 75.1 us -> 50.1 us  [exchange(): return lax.ppermute(x, axis, [(i, i ^ step) for i in range(count)])]
    ppermute x13 -> x21, starting transfers between devices: 17.4 us -> 30.6 us  [exchange(): return lax.ppermute(x, axis, [(i, i ^ step) for i in range(count)])]
  transfers between devices with their start and end apart: 15 -> 23, of which waited for: 13 -> 17; matrix products, arithmetic and copies ran while one was open for 12% -> 14% of each run, Pallas kernels for 0% -> 0%
where the time goes in v6:
time: 248 us; the launch traced here: 247 us
  waiting for transfers between devices  110 us (44%)
  matrix products  61.3 us (25%)
  starting transfers between devices  30.6 us (12%)
  between operations  14.4 us (6%)
  local copies, waits for them, and re-layouts  12.3 us (5%)
  blocking collectives  12.2 us (5%)
  other arithmetic  6.94 us (3%)
    reduce_scatter x1, waiting for transfers between devices, shards(): strip = lax.psum_scatter(chip_sum, 'rows', scatter_dimension=0, tiled=True)  59.5 us
    ppermute x21, waiting for transfers between devices, exchange(): return lax.ppermute(x, axis, [(i, i ^ step) for i in range(count)])  50.1 us
    dot_general x2, matrix products, partial_rows(): jnp.dot(columns.T, direct, precision=fast, preferred_element_type=jnp.flo...  34.6 us
    ppermute x21, starting transfers between devices, exchange(): return lax.ppermute(x, axis, [(i, i ^ step) for i in range(count)])  30.6 us
    all_gather x1, blocking collectives, shards(): gathered_a = lax.all_gather(coef_a, 'rows', axis=0, tiled=False)  12.2 us
    dot_general x1, matrix products, shards(): jnp.dot(adjoint, full_a, precision=fast, preferred_element_type=jnp.float32)  10.9 us
    dot_general x1, matrix products, shards(): jnp.dot(direct, full_d, precision=fast, preferred_element_type=jnp.float32)  10.6 us
    add x1, other arithmetic, shards(): chip_sum = kept_rows + received  5.51 us
  transfers between devices with their start and end apart: 23, of which 17 were waited for; matrix products, arithmetic and copies ran while one was open for 14% of the time, Pallas kernels for 0%

profile of v6, /device:TPU:0, one launch (start us, length us, event | category | flops | bytes accessed | tf_op | source)
XLA Modules:
  0.0 247.4 jit_solution(15338016406146823342)
XLA Ops:
  7.2 16.4 %fusion.7 = f32[768,1536]{1,0:T(8,128)} fusion(f32[1536,1536]{1,0:T(8,128)} %param.3, f32[1536,1536]{1,0:T(8,128)} %param.4, s32[]{:T(128)S(6)} %select_n.76), kind=kOutput, calls=%fused_computation.5 | convolution fusion | flops 10872815616 | bytes 18874372 | tf_op jit(solution)/shard_map/dot_general | solution.py:47
  24.1 18.3 %fusion.4 = f32[768,1536]{1,0:T(8,128)S(1)} fusion(f32[1536,1536]{1,0:T(8,128)} %param.3, f32[1536,1536]{1,0:T(8,128)} %param.4, s32[]{:T(128)S(6)} %select_n.75), kind=kOutput, calls=%fused_computation.4 | convolution fusion | flops 10872815616 | bytes 18874372 | tf_op jit(solution)/shard_map/dot_general | solution.py:47
  42.3 5.5 %add.103 = f32[768,1536]{1,0:T(8,128)} add(f32[768,1536]{1,0:T(8,128)S(1)} %fusion.4, f32[768,1536]{1,0:T(8,128)} %collective-permute-done) | non-fusion elementwise | flops 1179648 | bytes 14155776 | tf_op jit(solution)/shard_map/add | solution.py:51
  48.0 59.5 %reduce-scatter.2.cloned.1.call-done = f32[192,1536]{1,0:T(8,128)} async-done(((f32[768,1536]{1,0:T(8,128)}), f32[192,1536]{1,0:T(8,128)}) %reduce-scatter.2.cloned.1.call-update) | async-done | bytes 1179664 | tf_op jit(solution)/shard_map/reduce_scatter | solution.py:52
  107.5 2.0 reshape.19
  112.4 13.6 %collective-permute-done.1 = f32[192,2,384]{2,1,0:T(2,128)S(1)} collective-permute-done((f32[192,2,384]{2,1,0:T(2,128)S(1)}, f32[192,2,384]{2,1,0:T(2,128)S(1)}, u32[]{:S(2)}, u32[]{:S(2)}) %collective-permute-start.1) | collective-permute-done | bytes 589856 | tf_op jit(solution)/shard_map/ppermute | solution.py:11
  127.0 2.5 %collective-permute-start.2 = (f32[192,384]{1,0:T(8,128)S(1)}, f32[192,384]{1,0:T(8,128)S(1)}, u32[]{:S(2)}, u32[]{:S(2)}) collective-permute-start(f32[192,384]{1,0:T(8,128)S(1)} %bitcast.38), channel_id=1, source_target_pairs={{0,4},{1,5},{2,6},{3,7},{4,0},{5,1},{6,2},{7,3},{8,12},{9,13},{10,... | collective-permute-start | bytes 884744 | tf_op jit(solution)/shard_map/ppermute | solution.py:11
  129.4 12.7 %collective-permute-done.2 = f32[192,384]{1,0:T(8,128)S(1)} collective-permute-done((f32[192,384]{1,0:T(8,128)S(1)}, f32[192,384]{1,0:T(8,128)S(1)}, u32[]{:S(2)}, u32[]{:S(2)}) %collective-permute-start.2) | collective-permute-done | bytes 294944 | tf_op jit(solution)/shard_map/ppermute | solution.py:11
  147.7 2.7 %collective-permute-done.4 = f32[384,64]{0,1:T(8,128)S(1)} collective-permute-done((f32[384,64]{0,1:T(8,128)S(1)}, f32[384,64]{0,1:T(8,128)S(1)}, u32[]{:S(2)}, u32[]{:S(2)}) %collective-permute-start.4) | collective-permute-done | bytes 98336 | tf_op jit(solution)/shard_map/ppermute | solution.py:11
  151.9 2.8 %collective-permute-start.13 = (f32[384,64]{0,1:T(8,128)S(1)}, f32[384,64]{0,1:T(8,128)S(1)}, u32[]{:S(2)}, u32[]{:S(2)}) collective-permute-start(f32[384,64]{0,1:T(8,128)S(1)} %add.122), channel_id=1, source_target_pairs={{0,4},{1,5},{2,6},{3,7},{4,0},{5,1},{6,2},{7,3},{8,12},{9,13},{10,... | collective-permute-start | bytes 294920 | tf_op jit(solution)/shard_map/ppermute | solution.py:11
  154.7 5.3 %collective-permute-done.5 = f32[384,64]{0,1:T(8,128)S(1)} collective-permute-done((f32[384,64]{0,1:T(8,128)S(1)}, f32[384,64]{0,1:T(8,128)S(1)}, u32[]{:S(2)}, u32[]{:S(2)}) %collective-permute-start.5) | collective-permute-done | bytes 98336 | tf_op jit(solution)/shard_map/ppermute | solution.py:11
  163.2 2.0 collective-permute-done.6
  167.9 2.0 collective-permute-done.7
  173.5 1.8 collective-permute-done.8
  175.3 3.6 %collective-permute-start.9 = (f32[384,64]{0,1:T(8,128)S(1)}, f32[384,64]{0,1:T(8,128)S(1)}, u32[]{:S(2)}, u32[]{:S(2)}) collective-permute-start(f32[384,64]{0,1:T(8,128)S(1)} %add.118), channel_id=1, source_target_pairs={{0,4},{1,5},{2,6},{3,7},{4,0},{5,1},{6,2},{7,3},{8,12},{9,13},{10,... | collective-permute-start | bytes 294920 | tf_op jit(solution)/shard_map/ppermute | solution.py:11
  179.0 2.7 %collective-permute-start.17 = (f32[384,64]{0,1:T(8,128)S(1)}, f32[384,64]{0,1:T(8,128)S(1)}, u32[]{:S(2)}, u32[]{:S(2)}) collective-permute-start(f32[384,64]{0,1:T(8,128)S(1)} %add.126), channel_id=1, source_target_pairs={{0,4},{1,5},{2,6},{3,7},{4,0},{5,1},{6,2},{7,3},{8,12},{9,13},{10,... | collective-permute-start | bytes 294920 | tf_op jit(solution)/shard_map/ppermute | solution.py:11
  186.9 1.9 collective-permute-start.11
  191.6 3.5 %collective-permute-done.19 = f32[384,64]{0,1:T(8,128)S(1)} collective-permute-done((f32[384,64]{0,1:T(8,128)S(1)}, f32[384,64]{0,1:T(8,128)S(1)}, u32[]{:S(2)}, u32[]{:S(2)}) %collective-permute-start.19) | collective-permute-done | bytes 98336 | tf_op jit(solution)/shard_map/ppermute | solution.py:11
  195.9 12.2 %all-gather.1 = f32[1536,128]{0,1:T(8,128)S(1)} all-gather(f32[384,128]{0,1:T(8,128)S(1)} %pad_maximum_fusion.2), channel_id=3, replica_groups=mesh['rows'=4,'cols'=8] {'rows'}, dimensions={0}, use_global_device_ids=true | all-gather | bytes 983040 | tf_op jit(solution)/shard_map/all_gather | solution.py:81
  208.5 2.3 collective-permute-done.20
  210.9 10.9 %fusion.11 = f32[1536,256]{0,1:T(8,128)S(1)} fusion(f32[1536,1536]{1,0:T(8,128)} %param.4, f32[1536,128]{1,0:T(8,128)S(1)} %get-tuple-element.7, f32[1536,128]{1,0:T(8,128)S(1)} %get-tuple-element.6), kind=kOutput, calls=%fused_computation.9 | convolution fusion | flops 3624665088 | bytes 12582912 | tf_op jit(solution)/shard_map/dot_general | solution.py:95
  223.5 2.6 %reshape.20 = f32[4,2,384,128]{2,1,0,3:T(2,128)S(1)} reshape(f32[3072,128]{0,1:T(8,128)} %all-gather.4.cloned.1.call-done) | data formatting | bytes 3145728 | tf_op jit(solution)/shard_map/reshape | solution.py:90
  226.2 2.2 copy.7
  228.3 10.6 %fusion.10 = f32[1536,256]{0,1:T(8,128)S(1)} fusion(f32[1536,1536]{1,0:T(8,128)} %param.3, f32[192,8,2,128]{3,2,1,0:T(2,128)} %bitcast.34), kind=kOutput, calls=%fused_computation.8 | convolution fusion | flops 3624271872 | bytes 12582912 | tf_op jit(solution)/shard_map/dot_general | solution.py:94
  (69 shorter events, 33.3 us)
Async XLA Ops:
  7.2 136.7 %copy-start = (f32[1536,256]{1,0:T(8,128)S(1)}, f32[1536,256]{1,0:T(8,128)}, u32[]{:S(2)}) copy-start(f32[1536,256]{1,0:T(8,128)} %param.5) | copy-start | bytes 4718596
  7.2 100.3 %reduce-scatter.2.cloned.1.call-start = ((), (), s32[]{:S(2)}) async-start(), calls=%async_computation.1 | async-start | bytes 5898240 | tf_op jit(solution)/shard_map/reduce_scatter | solution.py:52
  23.6 18.7 %collective-permute-start = (f32[768,1536]{1,0:T(8,128)}, f32[768,1536]{1,0:T(8,128)}, u32[]{:S(2)}, u32[]{:S(2)}) collective-permute-start(f32[768,1536]{1,0:T(8,128)} %fusion.7), channel_id=1, source_target_pairs={{0,1},{1,0},{2,3},{3,2},{4,5},{5,4},{6,7},{7,6},{8,9},{9,8},{10,11... | collective-permute-start | bytes 14155784 | tf_op jit(solution)/shard_map/ppermute | solution.py:11
  47.9 175.7 %all-gather.4.cloned.1.call-start = ((), (), s32[]{:S(2)}) async-start(), calls=%async_computation.2 | async-start | bytes 1769472 | tf_op jit(solution)/shard_map/all_gather | solution.py:88
  110.9 15.1 %collective-permute-start.1 = (f32[192,2,384]{2,1,0:T(2,128)S(1)}, f32[192,2,384]{2,1,0:T(2,128)S(1)}, u32[]{:S(2)}, u32[]{:S(2)}) collective-permute-start(f32[192,2,384]{2,1,0:T(2,128)S(1)} %bitcast.37), channel_id=1, source_target_pairs={{0,2},{1,3},{2,0},{3,1},{4,6},{5,7},{6,4},{7,5},{8,10},{9,11},{10,... | collective-permute-start | bytes 1769480 | tf_op jit(solution)/shard_map/ppermute | solution.py:11
  127.0 15.2 %collective-permute-start.2 = (f32[192,384]{1,0:T(8,128)S(1)}, f32[192,384]{1,0:T(8,128)S(1)}, u32[]{:S(2)}, u32[]{:S(2)}) collective-permute-start(f32[192,384]{1,0:T(8,128)S(1)} %bitcast.38), channel_id=1, source_target_pairs={{0,4},{1,5},{2,6},{3,7},{4,0},{5,1},{6,2},{7,3},{8,12},{9,13},{10,... | collective-permute-start | bytes 884744 | tf_op jit(solution)/shard_map/ppermute | solution.py:11
  142.2 1.6 collective-permute-start.3
  144.7 5.7 %collective-permute-start.4 = (f32[384,64]{0,1:T(8,128)S(1)}, f32[384,64]{0,1:T(8,128)S(1)}, u32[]{:S(2)}, u32[]{:S(2)}) collective-permute-start(f32[384,64]{0,1:T(8,128)S(1)} %fusion.19), channel_id=1, source_target_pairs={{0,2},{1,3},{2,0},{3,1},{4,6},{5,7},{6,4},{7,5},{8,10},{9,11},{10,... | collective-permute-start | bytes 294920 | tf_op jit(solution)/shard_map/ppermute | solution.py:11
  146.1 5.8 %collective-permute-start.12 = (f32[384,64]{0,1:T(8,128)S(1)}, f32[384,64]{0,1:T(8,128)S(1)}, u32[]{:S(2)}, u32[]{:S(2)}) collective-permute-start(f32[384,64]{0,1:T(8,128)S(1)} %fusion.17), channel_id=1, source_target_pairs={{0,2},{1,3},{2,0},{3,1},{4,6},{5,7},{6,4},{7,5},{8,10},{9,11},{10,... | collective-permute-start | bytes 294920 | tf_op jit(solution)/shard_map/ppermute | solution.py:11
  150.4 9.6 %collective-permute-start.5 = (f32[384,64]{0,1:T(8,128)S(1)}, f32[384,64]{0,1:T(8,128)S(1)}, u32[]{:S(2)}, u32[]{:S(2)}) collective-permute-start(f32[384,64]{0,1:T(8,128)S(1)} %add.114), channel_id=1, source_target_pairs={{0,4},{1,5},{2,6},{3,7},{4,0},{5,1},{6,2},{7,3},{8,12},{9,13},{10,... | collective-permute-start | bytes 294920 | tf_op jit(solution)/shard_map/ppermute | solution.py:11
  151.9 10.0 %collective-permute-start.13 = (f32[384,64]{0,1:T(8,128)S(1)}, f32[384,64]{0,1:T(8,128)S(1)}, u32[]{:S(2)}, u32[]{:S(2)}) collective-permute-start(f32[384,64]{0,1:T(8,128)S(1)} %add.122), channel_id=1, source_target_pairs={{0,4},{1,5},{2,6},{3,7},{4,0},{5,1},{6,2},{7,3},{8,12},{9,13},{10,... | collective-permute-start | bytes 294920 | tf_op jit(solution)/shard_map/ppermute | solution.py:11
  160.5 4.7 %collective-permute-start.6 = (f32[384,64]{0,1:T(8,128)S(1)}, f32[384,64]{0,1:T(8,128)S(1)}, u32[]{:S(2)}, u32[]{:S(2)}) collective-permute-start(f32[384,64]{0,1:T(8,128)S(1)} %fusion.27), channel_id=1, source_target_pairs={{0,8},{8,0},{16,24},{24,16},{1,9},{9,1},{17,25},{25,17},{2,10},{10... | collective-permute-start | bytes 294920 | tf_op jit(solution)/shard_map/ppermute | solution.py:11
  162.4 4.7 %collective-permute-start.14 = (f32[384,64]{0,1:T(8,128)S(1)}, f32[384,64]{0,1:T(8,128)S(1)}, u32[]{:S(2)}, u32[]{:S(2)}) collective-permute-start(f32[384,64]{0,1:T(8,128)S(1)} %fusion.23), channel_id=1, source_target_pairs={{0,8},{8,0},{16,24},{24,16},{1,9},{9,1},{17,25},{25,17},{2,10},{10... | collective-permute-start | bytes 294920 | tf_op jit(solution)/shard_map/ppermute | solution.py:11
  165.2 4.7 %collective-permute-start.7 = (f32[384,64]{0,1:T(8,128)S(1)}, f32[384,64]{0,1:T(8,128)S(1)}, u32[]{:S(2)}, u32[]{:S(2)}) collective-permute-start(f32[384,64]{0,1:T(8,128)S(1)} %add.116), channel_id=1, source_target_pairs={{0,16},{8,24},{16,0},{24,8},{1,17},{9,25},{17,1},{25,9},{2,18},{10... | collective-permute-start | bytes 294920 | tf_op jit(solution)/shard_map/ppermute | solution.py:11
  167.1 4.8 %collective-permute-start.15 = (f32[384,64]{0,1:T(8,128)S(1)}, f32[384,64]{0,1:T(8,128)S(1)}, u32[]{:S(2)}, u32[]{:S(2)}) collective-permute-start(f32[384,64]{0,1:T(8,128)S(1)} %add.124), channel_id=1, source_target_pairs={{0,16},{8,24},{16,0},{24,8},{1,17},{9,25},{17,1},{25,9},{2,18},{10... | collective-permute-start | bytes 294920 | tf_op jit(solution)/shard_map/ppermute | solution.py:11
  170.6 4.7 %collective-permute-start.8 = (f32[384,64]{0,1:T(8,128)S(1)}, f32[384,64]{0,1:T(8,128)S(1)}, u32[]{:S(2)}, u32[]{:S(2)}) collective-permute-start(f32[384,64]{0,1:T(8,128)S(1)} %fusion.25), channel_id=1, source_target_pairs={{0,2},{1,3},{2,0},{3,1},{4,6},{5,7},{6,4},{7,5},{8,10},{9,11},{10,... | collective-permute-start | bytes 294920 | tf_op jit(solution)/shard_map/ppermute | solution.py:11
  172.6 6.3 %collective-permute-start.16 = (f32[384,64]{0,1:T(8,128)S(1)}, f32[384,64]{0,1:T(8,128)S(1)}, u32[]{:S(2)}, u32[]{:S(2)}) collective-permute-start(f32[384,64]{0,1:T(8,128)S(1)} %fusion.21), channel_id=1, source_target_pairs={{0,2},{1,3},{2,0},{3,1},{4,6},{5,7},{6,4},{7,5},{8,10},{9,11},{10,... | collective-permute-start | bytes 294920 | tf_op jit(solution)/shard_map/ppermute | solution.py:11
  175.3 6.4 %collective-permute-start.9 = (f32[384,64]{0,1:T(8,128)S(1)}, f32[384,64]{0,1:T(8,128)S(1)}, u32[]{:S(2)}, u32[]{:S(2)}) collective-permute-start(f32[384,64]{0,1:T(8,128)S(1)} %add.118), channel_id=1, source_target_pairs={{0,4},{1,5},{2,6},{3,7},{4,0},{5,1},{6,2},{7,3},{8,12},{9,13},{10,... | collective-permute-start | bytes 294920 | tf_op jit(solution)/shard_map/ppermute | solution.py:11
  179.0 5.6 %collective-permute-start.17 = (f32[384,64]{0,1:T(8,128)S(1)}, f32[384,64]{0,1:T(8,128)S(1)}, u32[]{:S(2)}, u32[]{:S(2)}) collective-permute-start(f32[384,64]{0,1:T(8,128)S(1)} %add.126), channel_id=1, source_target_pairs={{0,4},{1,5},{2,6},{3,7},{4,0},{5,1},{6,2},{7,3},{8,12},{9,13},{10,... | collective-permute-start | bytes 294920 | tf_op jit(solution)/shard_map/ppermute | solution.py:11
  182.2 4.7 %collective-permute-start.10 = (f32[384,64]{0,1:T(8,128)S(1)}, f32[384,64]{0,1:T(8,128)S(1)}, u32[]{:S(2)}, u32[]{:S(2)}) collective-permute-start(f32[384,64]{0,1:T(8,128)S(1)} %fusion.33), channel_id=1, source_target_pairs={{0,8},{8,0},{16,24},{24,16},{1,9},{9,1},{17,25},{25,17},{2,10},{10... | collective-permute-start | bytes 294920 | tf_op jit(solution)/shard_map/ppermute | solution.py:11
  185.1 4.7 %collective-permute-start.18 = (f32[384,64]{0,1:T(8,128)S(1)}, f32[384,64]{0,1:T(8,128)S(1)}, u32[]{:S(2)}, u32[]{:S(2)}) collective-permute-start(f32[384,64]{0,1:T(8,128)S(1)} %fusion.32), channel_id=1, source_target_pairs={{0,8},{8,0},{16,24},{24,16},{1,9},{9,1},{17,25},{25,17},{2,10},{10... | collective-permute-start | bytes 294920 | tf_op jit(solution)/shard_map/ppermute | solution.py:11
  186.9 4.7 %collective-permute-start.11 = (f32[384,64]{0,1:T(8,128)S(1)}, f32[384,64]{0,1:T(8,128)S(1)}, u32[]{:S(2)}, u32[]{:S(2)}) collective-permute-start(f32[384,64]{0,1:T(8,128)S(1)} %add.120), channel_id=1, source_target_pairs={{0,16},{8,24},{16,0},{24,8},{1,17},{9,25},{17,1},{25,9},{2,18},{10... | collective-permute-start | bytes 294920 | tf_op jit(solution)/shard_map/ppermute | solution.py:11
  189.8 5.4 %collective-permute-start.19 = (f32[384,64]{0,1:T(8,128)S(1)}, f32[384,64]{0,1:T(8,128)S(1)}, u32[]{:S(2)}, u32[]{:S(2)}) collective-permute-start(f32[384,64]{0,1:T(8,128)S(1)} %add.128), channel_id=1, source_target_pairs={{0,16},{8,24},{16,0},{24,8},{1,17},{9,25},{17,1},{25,9},{2,18},{10... | collective-permute-start | bytes 294920 | tf_op jit(solution)/shard_map/ppermute | solution.py:11
  208.4 2.4 collective-permute-start.20
Sparse Core Ops, SparseCore 0:
  48.0 59.4 reduce-scatter.1
  196.0 25.5 all-gather.3

commit v7 on v6

--- a/solution.py
+++ b/solution.py
@@ -74,11 +74,16 @@
                 jnp.dot(chip_tile.T, coef_a, precision=high, preferred_element_type=jnp.float32),
                 "rows", 1, row_count,
             )
-        chains_a.append(coef_a)
+        gathered = coef_a[None]
+        step = 1
+        while step < row_count:
+            low = (lax.axis_index("rows") & step) == 0
+            gathered = in_order(low, gathered, exchange(gathered, "rows", step), 0)
+            step *= 2
+        chains_a.append(gathered)
         chains_d.append(coef_d)
-    coef_a = jnp.concatenate(chains_a, axis=1)
+    gathered_a = jnp.concatenate(chains_a, axis=2)
     coef_d = jnp.concatenate(chains_d, axis=1)
-    gathered_a = lax.all_gather(coef_a, "rows", axis=0, tiled=False)
     half_a = (
         gathered_a.reshape(row_count, 2, part_rows, probe_half)
         .transpose(1, 0, 2, 3)

time: 248 us -> 248 us (level)
  blocking collectives: 12.2 us -> 0 us
  waiting for transfers between devices: 110 us -> 119 us
    all_gather x1 -> x0, blocking collectives: 12.2 us -> none  [shards(): gathered_a = lax.all_gather(coef_a, 'rows', axis=0, tiled=False)]
    all_gather x1, waiting for transfers between devices: 0.01 us -> 5 us  [shards(): gathered_d = lax.all_gather(coef_d, 'cols', axis=0, tiled=False)]
    ppermute x21 -> x25, waiting for transfers between devices: 50.1 us -> 54.9 us  [exchange(): return lax.ppermute(x, axis, [(i, i ^ step) for i in range(count)])]
    ppermute x21 -> x25, starting transfers between devices: 30.6 us -> 32 us  [exchange(): return lax.ppermute(x, axis, [(i, i ^ step) for i in range(count)])]
    unnamed x6 -> x8, local copies, waits for them, and re-layouts: 3.56 us -> 4.98 us
  transfers between devices with their start and end apart: 23 -> 27, of which waited for: 17 -> 19; matrix products, arithmetic and copies ran while one was open for 14% -> 15% of each run, Pallas kernels for 0% -> 0%
where the time goes in v7:
time: 248 us
  waiting for transfers between devices  119 us (48%)
  matrix products  62.1 us (25%)
  starting transfers between devices  32.1 us (13%)
  between operations  14.4 us (6%)
  local copies, waits for them, and re-layouts  12.5 us (5%)
  other arithmetic  7.1 us (3%)
    reduce_scatter x1, waiting for transfers between devices, shards(): strip = lax.psum_scatter(chip_sum, 'rows', scatter_dimension=0, tiled=True)  59.5 us
    ppermute x25, waiting for transfers between devices, exchange(): return lax.ppermute(x, axis, [(i, i ^ step) for i in range(count)])  54.9 us
    dot_general x2, matrix products, partial_rows(): jnp.dot(columns.T, direct, precision=fast, preferred_element_type=jnp.flo...  34.6 us
    ppermute x25, starting transfers between devices, exchange(): return lax.ppermute(x, axis, [(i, i ^ step) for i in range(count)])  32 us
    dot_general x1, matrix products, shards(): jnp.dot(direct, full_d, precision=fast, preferred_element_type=jnp.float32)  11.7 us
    dot_general x1, matrix products, shards(): jnp.dot(adjoint, full_a, precision=fast, preferred_element_type=jnp.float32)  10.7 us
    add x1, other arithmetic, shards(): chip_sum = kept_rows + received  5.5 us
    all_gather x1, waiting for transfers between devices, shards(): gathered_d = lax.all_gather(coef_d, 'cols', axis=0, tiled=False)  5 us
  transfers between devices with their start and end apart: 27, of which 19 were waited for; matrix products, arithmetic and copies ran while one was open for 15% of the time, Pallas kernels for 0%

profile of v7, /device:TPU:0, one launch (start us, length us, event | category | flops | bytes accessed | tf_op | source)
XLA Modules:
  0.0 247.7 jit_solution(8080612102551711098)
XLA Ops:
  7.2 16.4 %fusion.7 = f32[768,1536]{1,0:T(8,128)} fusion(f32[1536,1536]{1,0:T(8,128)} %param.3, f32[1536,1536]{1,0:T(8,128)} %param.4, s32[]{:T(128)S(6)} %select_n.116), kind=kOutput, calls=%fused_computation.5 | convolution fusion | flops 10872815616 | bytes 18874372 | tf_op jit(solution)/shard_map/dot_general | solution.py:47
  24.1 18.3 %fusion.4 = f32[768,1536]{1,0:T(8,128)S(1)} fusion(f32[1536,1536]{1,0:T(8,128)} %param.3, f32[1536,1536]{1,0:T(8,128)} %param.4, s32[]{:T(128)S(6)} %select_n.115), kind=kOutput, calls=%fused_computation.4 | convolution fusion | flops 10872815616 | bytes 18874372 | tf_op jit(solution)/shard_map/dot_general | solution.py:47
  42.3 5.5 %add.103 = f32[768,1536]{1,0:T(8,128)} add(f32[768,1536]{1,0:T(8,128)S(1)} %fusion.4, f32[768,1536]{1,0:T(8,128)} %collective-permute-done) | non-fusion elementwise | flops 1179648 | bytes 14155776 | tf_op jit(solution)/shard_map/add | solution.py:51
  48.0 59.5 %reduce-scatter.2.cloned.1.call-done = f32[192,1536]{1,0:T(8,128)} async-done(((f32[768,1536]{1,0:T(8,128)}), f32[192,1536]{1,0:T(8,128)}) %reduce-scatter.2.cloned.1.call-update) | async-done | bytes 1179664 | tf_op jit(solution)/shard_map/reduce_scatter | solution.py:52
  107.5 2.0 reshape.19
  112.4 13.6 %collective-permute-done.1 = f32[192,2,384]{2,1,0:T(2,128)S(1)} collective-permute-done((f32[192,2,384]{2,1,0:T(2,128)S(1)}, f32[192,2,384]{2,1,0:T(2,128)S(1)}, u32[]{:S(2)}, u32[]{:S(2)}) %collective-permute-start.1) | collective-permute-done | bytes 589856 | tf_op jit(solution)/shard_map/ppermute | solution.py:11
  127.0 2.5 %collective-permute-start.2 = (f32[192,384]{1,0:T(8,128)S(1)}, f32[192,384]{1,0:T(8,128)S(1)}, u32[]{:S(2)}, u32[]{:S(2)}) collective-permute-start(f32[192,384]{1,0:T(8,128)S(1)} %bitcast.40), channel_id=1, source_target_pairs={{0,4},{1,5},{2,6},{3,7},{4,0},{5,1},{6,2},{7,3},{8,12},{9,13},{10,... | collective-permute-start | bytes 884744 | tf_op jit(solution)/shard_map/ppermute | solution.py:11
  129.4 12.7 %collective-permute-done.2 = f32[192,384]{1,0:T(8,128)S(1)} collective-permute-done((f32[192,384]{1,0:T(8,128)S(1)}, f32[192,384]{1,0:T(8,128)S(1)}, u32[]{:S(2)}, u32[]{:S(2)}) %collective-permute-start.2) | collective-permute-done | bytes 294944 | tf_op jit(solution)/shard_map/ppermute | solution.py:11
  147.7 2.7 %collective-permute-done.4 = f32[384,64]{0,1:T(8,128)S(1)} collective-permute-done((f32[384,64]{0,1:T(8,128)S(1)}, f32[384,64]{0,1:T(8,128)S(1)}, u32[]{:S(2)}, u32[]{:S(2)}) %collective-permute-start.4) | collective-permute-done | bytes 98336 | tf_op jit(solution)/shard_map/ppermute | solution.py:11
  151.9 2.8 %collective-permute-start.13 = (f32[384,64]{0,1:T(8,128)S(1)}, f32[384,64]{0,1:T(8,128)S(1)}, u32[]{:S(2)}, u32[]{:S(2)}) collective-permute-start(f32[384,64]{0,1:T(8,128)S(1)} %add.122), channel_id=1, source_target_pairs={{0,4},{1,5},{2,6},{3,7},{4,0},{5,1},{6,2},{7,3},{8,12},{9,13},{10,... | collective-permute-start | bytes 294920 | tf_op jit(solution)/shard_map/ppermute | solution.py:11
  154.7 5.3 %collective-permute-done.5 = f32[384,64]{0,1:T(8,128)S(1)} collective-permute-done((f32[384,64]{0,1:T(8,128)S(1)}, f32[384,64]{0,1:T(8,128)S(1)}, u32[]{:S(2)}, u32[]{:S(2)}) %collective-permute-start.5) | collective-permute-done | bytes 98336 | tf_op jit(solution)/shard_map/ppermute | solution.py:11
  163.2 2.0 collective-permute-done.6
  167.9 2.0 collective-permute-done.7
  175.3 3.6 %collective-permute-start.9 = (f32[384,64]{0,1:T(8,128)S(1)}, f32[384,64]{0,1:T(8,128)S(1)}, u32[]{:S(2)}, u32[]{:S(2)}) collective-permute-start(f32[384,64]{0,1:T(8,128)S(1)} %add.118), channel_id=1, source_target_pairs={{0,4},{1,5},{2,6},{3,7},{4,0},{5,1},{6,2},{7,3},{8,12},{9,13},{10,... | collective-permute-start | bytes 294920 | tf_op jit(solution)/shard_map/ppermute | solution.py:11
  178.9 2.6 %collective-permute-start.17 = (f32[384,64]{0,1:T(8,128)S(1)}, f32[384,64]{0,1:T(8,128)S(1)}, u32[]{:S(2)}, u32[]{:S(2)}) collective-permute-start(f32[384,64]{0,1:T(8,128)S(1)} %add.126), channel_id=1, source_target_pairs={{0,4},{1,5},{2,6},{3,7},{4,0},{5,1},{6,2},{7,3},{8,12},{9,13},{10,... | collective-permute-start | bytes 294920 | tf_op jit(solution)/shard_map/ppermute | solution.py:11
  181.6 2.0 collective-permute-start.20
  192.1 2.5 collective-permute-done.11
  198.0 4.3 %collective-permute-done.23 = f32[2,384,64]{1,2,0:T(8,128)S(1)} collective-permute-done((f32[2,384,64]{1,2,0:T(8,128)S(1)}, f32[2,384,64]{1,2,0:T(8,128)S(1)}, u32[]{:S(2)}, u32[]{:S(2)}) %collective-permute-start.23) | collective-permute-done | bytes 196640 | tf_op jit(solution)/shard_map/ppermute | solution.py:11
  202.8 2.3 collective-permute-done.24
  205.2 10.7 %fusion.11 = f32[1536,256]{0,1:T(8,128)S(1)} fusion(f32[1536,1536]{1,0:T(8,128)} %param.4, f32[1536,128]{1,0:T(8,128)S(1)} %get-tuple-element.7, f32[1536,128]{1,0:T(8,128)S(1)} %get-tuple-element.6), kind=kOutput, calls=%fused_computation.9 | convolution fusion | flops 3624665088 | bytes 12582912 | tf_op jit(solution)/shard_map/dot_general | solution.py:100
  217.4 5.0 %all-gather.3.cloned.1.call-done = f32[3072,128]{0,1:T(8,128)} async-done(((f32[384,128]{0,1:T(8,128)}), f32[3072,128]{0,1:T(8,128)}) %all-gather.3.cloned.1.call-update) | async-done | bytes 1572880 | tf_op jit(solution)/shard_map/all_gather | solution.py:93
  222.4 2.6 %reshape.20 = f32[4,2,384,128]{2,1,0,3:T(2,128)S(1)} reshape(f32[3072,128]{0,1:T(8,128)} %all-gather.3.cloned.1.call-done) | data formatting | bytes 3145728 | tf_op jit(solution)/shard_map/reshape | solution.py:95
  226.1 11.7 %fusion.10 = f32[1536,256]{0,1:T(8,128)} fusion(f32[1536,1536]{1,0:T(8,128)} %param.3, f32[192,8,2,128]{3,2,1,0:T(2,128)S(1)} %bitcast.36), kind=kOutput, calls=%fused_computation.8 | convolution fusion | flops 3624271872 | bytes 12582912 | tf_op jit(solution)/shard_map/dot_general | solution.py:99
  237.8 3.0 %copy.10 = f32[1536,256]{1,0:T(8,128)} copy(f32[1536,256]{0,1:T(8,128)} %fusion.10) | data formatting | bytes 3145728
  (84 shorter events, 37.7 us)
Async XLA Ops:
  7.2 100.3 %reduce-scatter.2.cloned.1.call-start = ((), (), s32[]{:S(2)}) async-start(), calls=%async_computation.1 | async-start | bytes 5898240 | tf_op jit(solution)/shard_map/reduce_scatter | solution.py:52
  23.6 18.7 %collective-permute-start = (f32[768,1536]{1,0:T(8,128)}, f32[768,1536]{1,0:T(8,128)}, u32[]{:S(2)}, u32[]{:S(2)}) collective-permute-start(f32[768,1536]{1,0:T(8,128)} %fusion.7), channel_id=1, source_target_pairs={{0,1},{1,0},{2,3},{3,2},{4,5},{5,4},{6,7},{7,6},{8,9},{9,8},{10,11... | collective-permute-start | bytes 14155784 | tf_op jit(solution)/shard_map/ppermute | solution.py:11
  47.9 174.6 %all-gather.3.cloned.1.call-start = ((), (), s32[]{:S(2)}) async-start(), calls=%async_computation.2 | async-start | bytes 1769472 | tf_op jit(solution)/shard_map/all_gather | solution.py:93
  110.9 15.1 %collective-permute-start.1 = (f32[192,2,384]{2,1,0:T(2,128)S(1)}, f32[192,2,384]{2,1,0:T(2,128)S(1)}, u32[]{:S(2)}, u32[]{:S(2)}) collective-permute-start(f32[192,2,384]{2,1,0:T(2,128)S(1)} %bitcast.39), channel_id=1, source_target_pairs={{0,2},{1,3},{2,0},{3,1},{4,6},{5,7},{6,4},{7,5},{8,10},{9,11},{10,... | collective-permute-start | bytes 1769480 | tf_op jit(solution)/shard_map/ppermute | solution.py:11
  127.0 15.2 %collective-permute-start.2 = (f32[192,384]{1,0:T(8,128)S(1)}, f32[192,384]{1,0:T(8,128)S(1)}, u32[]{:S(2)}, u32[]{:S(2)}) collective-permute-start(f32[192,384]{1,0:T(8,128)S(1)} %bitcast.40), channel_id=1, source_target_pairs={{0,4},{1,5},{2,6},{3,7},{4,0},{5,1},{6,2},{7,3},{8,12},{9,13},{10,... | collective-permute-start | bytes 884744 | tf_op jit(solution)/shard_map/ppermute | solution.py:11
  144.7 5.7 %collective-permute-start.4 = (f32[384,64]{0,1:T(8,128)S(1)}, f32[384,64]{0,1:T(8,128)S(1)}, u32[]{:S(2)}, u32[]{:S(2)}) collective-permute-start(f32[384,64]{0,1:T(8,128)S(1)} %fusion.19), channel_id=1, source_target_pairs={{0,2},{1,3},{2,0},{3,1},{4,6},{5,7},{6,4},{7,5},{8,10},{9,11},{10,... | collective-permute-start | bytes 294920 | tf_op jit(solution)/shard_map/ppermute | solution.py:11
  146.1 5.8 %collective-permute-start.12 = (f32[384,64]{0,1:T(8,128)S(1)}, f32[384,64]{0,1:T(8,128)S(1)}, u32[]{:S(2)}, u32[]{:S(2)}) collective-permute-start(f32[384,64]{0,1:T(8,128)S(1)} %fusion.17), channel_id=1, source_target_pairs={{0,2},{1,3},{2,0},{3,1},{4,6},{5,7},{6,4},{7,5},{8,10},{9,11},{10,... | collective-permute-start | bytes 294920 | tf_op jit(solution)/shard_map/ppermute | solution.py:11
  150.4 9.6 %collective-permute-start.5 = (f32[384,64]{0,1:T(8,128)S(1)}, f32[384,64]{0,1:T(8,128)S(1)}, u32[]{:S(2)}, u32[]{:S(2)}) collective-permute-start(f32[384,64]{0,1:T(8,128)S(1)} %add.114), channel_id=1, source_target_pairs={{0,4},{1,5},{2,6},{3,7},{4,0},{5,1},{6,2},{7,3},{8,12},{9,13},{10,... | collective-permute-start | bytes 294920 | tf_op jit(solution)/shard_map/ppermute | solution.py:11
  151.9 10.1 %collective-permute-start.13 = (f32[384,64]{0,1:T(8,128)S(1)}, f32[384,64]{0,1:T(8,128)S(1)}, u32[]{:S(2)}, u32[]{:S(2)}) collective-permute-start(f32[384,64]{0,1:T(8,128)S(1)} %add.122), channel_id=1, source_target_pairs={{0,4},{1,5},{2,6},{3,7},{4,0},{5,1},{6,2},{7,3},{8,12},{9,13},{10,... | collective-permute-start | bytes 294920 | tf_op jit(solution)/shard_map/ppermute | solution.py:11
  160.5 4.7 %collective-permute-start.6 = (f32[384,64]{0,1:T(8,128)S(1)}, f32[384,64]{0,1:T(8,128)S(1)}, u32[]{:S(2)}, u32[]{:S(2)}) collective-permute-start(f32[384,64]{0,1:T(8,128)S(1)} %fusion.27), channel_id=1, source_target_pairs={{0,8},{8,0},{16,24},{24,16},{1,9},{9,1},{17,25},{25,17},{2,10},{10... | collective-permute-start | bytes 294920 | tf_op jit(solution)/shard_map/ppermute | solution.py:11
  162.5 4.7 %collective-permute-start.14 = (f32[384,64]{0,1:T(8,128)S(1)}, f32[384,64]{0,1:T(8,128)S(1)}, u32[]{:S(2)}, u32[]{:S(2)}) collective-permute-start(f32[384,64]{0,1:T(8,128)S(1)} %fusion.23), channel_id=1, source_target_pairs={{0,8},{8,0},{16,24},{24,16},{1,9},{9,1},{17,25},{25,17},{2,10},{10... | collective-permute-start | bytes 294920 | tf_op jit(solution)/shard_map/ppermute | solution.py:11
  165.2 4.7 %collective-permute-start.7 = (f32[384,64]{0,1:T(8,128)S(1)}, f32[384,64]{0,1:T(8,128)S(1)}, u32[]{:S(2)}, u32[]{:S(2)}) collective-permute-start(f32[384,64]{0,1:T(8,128)S(1)} %add.116), channel_id=1, source_target_pairs={{0,16},{8,24},{16,0},{24,8},{1,17},{9,25},{17,1},{25,9},{2,18},{10... | collective-permute-start | bytes 294920 | tf_op jit(solution)/shard_map/ppermute | solution.py:11
  167.2 4.7 %collective-permute-start.15 = (f32[384,64]{0,1:T(8,128)S(1)}, f32[384,64]{0,1:T(8,128)S(1)}, u32[]{:S(2)}, u32[]{:S(2)}) collective-permute-start(f32[384,64]{0,1:T(8,128)S(1)} %add.124), channel_id=1, source_target_pairs={{0,16},{8,24},{16,0},{24,8},{1,17},{9,25},{17,1},{25,9},{2,18},{10... | collective-permute-start | bytes 294920 | tf_op jit(solution)/shard_map/ppermute | solution.py:11
  172.6 6.3 %collective-permute-start.16 = (f32[384,64]{0,1:T(8,128)S(1)}, f32[384,64]{0,1:T(8,128)S(1)}, u32[]{:S(2)}, u32[]{:S(2)}) collective-permute-start(f32[384,64]{0,1:T(8,128)S(1)} %fusion.21), channel_id=1, source_target_pairs={{0,2},{1,3},{2,0},{3,1},{4,6},{5,7},{6,4},{7,5},{8,10},{9,11},{10,... | collective-permute-start | bytes 294920 | tf_op jit(solution)/shard_map/ppermute | solution.py:11
  175.3 6.3 %collective-permute-start.9 = (f32[384,64]{0,1:T(8,128)S(1)}, f32[384,64]{0,1:T(8,128)S(1)}, u32[]{:S(2)}, u32[]{:S(2)}) collective-permute-start(f32[384,64]{0,1:T(8,128)S(1)} %add.118), channel_id=1, source_target_pairs={{0,4},{1,5},{2,6},{3,7},{4,0},{5,1},{6,2},{7,3},{8,12},{9,13},{10,... | collective-permute-start | bytes 294920 | tf_op jit(solution)/shard_map/ppermute | solution.py:11
  178.9 5.6 %collective-permute-start.17 = (f32[384,64]{0,1:T(8,128)S(1)}, f32[384,64]{0,1:T(8,128)S(1)}, u32[]{:S(2)}, u32[]{:S(2)}) collective-permute-start(f32[384,64]{0,1:T(8,128)S(1)} %add.126), channel_id=1, source_target_pairs={{0,4},{1,5},{2,6},{3,7},{4,0},{5,1},{6,2},{7,3},{8,12},{9,13},{10,... | collective-permute-start | bytes 294920 | tf_op jit(solution)/shard_map/ppermute | solution.py:11
  181.6 9.9 %collective-permute-start.20 = (f32[1,384,64]{1,2,0:T(8,128)S(1)}, f32[1,384,64]{1,2,0:T(8,128)S(1)}, u32[]{:S(2)}, u32[]{:S(2)}) collective-permute-start(f32[1,384,64]{1,2,0:T(8,128)S(1)} %add_bitcast_fusion.1), channel_id=1, source_target_pairs={{0,8},{8,0},{16,24},{24,16},{1,9},{9,1},{17,25},{25,17},{2,10},{10... | collective-permute-start | bytes 294920 | tf_op jit(solution)/shard_map/ppermute | solution.py:11
  184.2 4.7 %collective-permute-start.10 = (f32[384,64]{0,1:T(8,128)S(1)}, f32[384,64]{0,1:T(8,128)S(1)}, u32[]{:S(2)}, u32[]{:S(2)}) collective-permute-start(f32[384,64]{0,1:T(8,128)S(1)} %fusion.31), channel_id=1, source_target_pairs={{0,8},{8,0},{16,24},{24,16},{1,9},{9,1},{17,25},{25,17},{2,10},{10... | collective-permute-start | bytes 294920 | tf_op jit(solution)/shard_map/ppermute | solution.py:11
  185.0 4.9 %collective-permute-start.18 = (f32[384,64]{0,1:T(8,128)S(1)}, f32[384,64]{0,1:T(8,128)S(1)}, u32[]{:S(2)}, u32[]{:S(2)}) collective-permute-start(f32[384,64]{0,1:T(8,128)S(1)} %fusion.29), channel_id=1, source_target_pairs={{0,8},{8,0},{16,24},{24,16},{1,9},{9,1},{17,25},{25,17},{2,10},{10... | collective-permute-start | bytes 294920 | tf_op jit(solution)/shard_map/ppermute | solution.py:11
  186.8 9.6 %collective-permute-start.22 = (f32[1,384,64]{1,2,0:T(8,128)S(1)}, f32[1,384,64]{1,2,0:T(8,128)S(1)}, u32[]{:S(2)}, u32[]{:S(2)}) collective-permute-start(f32[1,384,64]{1,2,0:T(8,128)S(1)} %add_bitcast_fusion), channel_id=1, source_target_pairs={{0,8},{8,0},{16,24},{24,16},{1,9},{9,1},{17,25},{25,17},{2,10},{10... | collective-permute-start | bytes 294920 | tf_op jit(solution)/shard_map/ppermute | solution.py:11
  188.9 5.7 %collective-permute-start.11 = (f32[384,64]{0,1:T(8,128)S(1)}, f32[384,64]{0,1:T(8,128)S(1)}, u32[]{:S(2)}, u32[]{:S(2)}) collective-permute-start(f32[384,64]{0,1:T(8,128)S(1)} %add.120), channel_id=1, source_target_pairs={{0,16},{8,24},{16,0},{24,8},{1,17},{9,25},{17,1},{25,9},{2,18},{10... | collective-permute-start | bytes 294920 | tf_op jit(solution)/shard_map/ppermute | solution.py:11
  189.9 5.8 %collective-permute-start.19 = (f32[384,64]{0,1:T(8,128)S(1)}, f32[384,64]{0,1:T(8,128)S(1)}, u32[]{:S(2)}, u32[]{:S(2)}) collective-permute-start(f32[384,64]{0,1:T(8,128)S(1)} %add.128), channel_id=1, source_target_pairs={{0,16},{8,24},{16,0},{24,8},{1,17},{9,25},{17,1},{25,9},{2,18},{10... | collective-permute-start | bytes 294920 | tf_op jit(solution)/shard_map/ppermute | solution.py:11
  191.5 6.4 %collective-permute-start.21 = (f32[2,384,64]{1,2,0:T(8,128)S(1)}, f32[2,384,64]{1,2,0:T(8,128)S(1)}, u32[]{:S(2)}, u32[]{:S(2)}) collective-permute-start(f32[2,384,64]{1,2,0:T(8,128)S(1)} %pad_maximum_fusion.2), channel_id=1, source_target_pairs={{0,16},{8,24},{16,0},{24,8},{1,17},{9,25},{17,1},{25,9},{2,18},{10... | collective-permute-start | bytes 589832 | tf_op jit(solution)/shard_map/ppermute | solution.py:11
  196.5 5.7 %collective-permute-start.23 = (f32[2,384,64]{1,2,0:T(8,128)S(1)}, f32[2,384,64]{1,2,0:T(8,128)S(1)}, u32[]{:S(2)}, u32[]{:S(2)}) collective-permute-start(f32[2,384,64]{1,2,0:T(8,128)S(1)} %pad_maximum_fusion.3), channel_id=1, source_target_pairs={{0,16},{8,24},{16,0},{24,8},{1,17},{9,25},{17,1},{25,9},{2,18},{10... | collective-permute-start | bytes 589832 | tf_op jit(solution)/shard_map/ppermute | solution.py:11
  (5 other events, 160.1 us)
Sparse Core Ops, SparseCore 0:
  48.0 59.4 reduce-scatter.1
  196.6 25.8 all-gather.2

commit v8 on v6

--- a/solution.py
+++ b/solution.py
@@ -49,7 +49,24 @@
     received = exchange(partial_rows((1 - core) * half_rows), "cols", 1)
     kept_rows = lax.optimization_barrier(partial_rows(core * half_rows))
     chip_sum = kept_rows + received
-    strip = lax.psum_scatter(chip_sum, "rows", scatter_dimension=0, tiled=True)
+    row_bits = row_count.bit_length() - 1
+    row_index = lax.axis_index("rows")
+    chunk_cols = snap_count // row_bits
+    chunks = []
+    for rot in range(row_bits):
+        part = chip_sum[:, rot * chunk_cols:(rot + 1) * chunk_cols]
+        part = part.reshape((2,) * row_bits + (part_rows, chunk_cols))
+        left = list(range(row_bits - 1, -1, -1))
+        for k in range(row_bits):
+            bit = (rot + k) % row_bits
+            axis = left.index(bit)
+            mine = (row_index >> bit) % 2
+            kept = lax.dynamic_index_in_dim(part, mine, axis=axis, keepdims=False)
+            sent = lax.dynamic_index_in_dim(part, 1 - mine, axis=axis, keepdims=False)
+            part = kept + exchange(sent, "rows", 1 << bit)
+            left.pop(axis)
+        chunks.append(part)
+    strip = jnp.concatenate(chunks, axis=1)
     bits = chip_count.bit_length() - 1
     strip = strip.reshape((part_rows,) + (2,) * bits + (chip_cols,))
     for bit in range(bits):
@@ -85,7 +102,11 @@
         .reshape(snap_count, probe_half)
     )
     full_a = in_order(first, half_a, exchange(half_a, "cols", 1), 1)
-    gathered_d = lax.all_gather(coef_d, "cols", axis=0, tiled=False)
+    col_bits = col_count.bit_length() - 1
+    gathered_d = coef_d.reshape((1,) * col_bits + coef_d.shape)
+    for bit in range(col_bits - 1, -1, -1):
+        low = (col_index >> bit) % 2 == 0
+        gathered_d = in_order(low, gathered_d, exchange(gathered_d, "cols", 1 << bit), col_bits - 1 - bit)
     full_d = (
         gathered_d.reshape(chip_count, 2, chip_cols, probe_half)
         .transpose(0, 2, 1, 3)

time: 248 us -> 242 us (0.976)
  waiting for transfers between devices: 110 us -> 90.7 us
  between operations: 14.4 us -> 0.99 us
  starting transfers between devices: 30.6 us -> 42.4 us
  other arithmetic: 6.94 us -> 17.7 us
  local copies, waits for them, and re-layouts: 12.3 us -> 18 us
    reduce_scatter x1 -> x0, waiting for transfers between devices: 59.5 us -> none  [shards(): strip = lax.psum_scatter(chip_sum, 'rows', scatter_dimension=0, tiled=True)]
    ppermute x21 -> x28, waiting for transfers between devices: 50.1 us -> 90.7 us  [exchange(): return lax.ppermute(x, axis, [(i, i ^ step) for i in range(count)])]
    ppermute x21 -> x28, starting transfers between devices: 30.6 us -> 42.4 us  [exchange(): return lax.ppermute(x, axis, [(i, i ^ step) for i in range(count)])]
    add x0 -> x4, other arithmetic: none -> 5.46 us  [shards(): part = kept + exchange(sent, 'rows', 1 << bit)]
    select_n x2 -> x5, other arithmetic: 0.15 us -> 4.65 us  [in_order(): jnp.where(first, mine, theirs)]
    squeeze x0 -> x4, local copies, waits for them, and re-layouts: none -> 3.34 us  [shards(): sent = lax.dynamic_index_in_dim(part, 1 - mine, axis=axis, keepdims=False)]
    unnamed x6 -> x16, local copies, waits for them, and re-layouts: 3.56 us -> 6.74 us
    reshape x2 -> x1, local copies, waits for them, and re-layouts: 4.81 us -> 2.08 us  [shards(): gathered_d.reshape(chip_count, 2, chip_cols, probe_half)]
  transfers between devices with their start and end apart: 23 -> 28, of which waited for: 17 -> 19; matrix products, arithmetic and copies ran while one was open for 14% -> 19% of each run, Pallas kernels for 0% -> 0%
where the time goes in v8:
time: 242 us; the launch traced here: 241 us
  waiting for transfers between devices  90.7 us (37%)
  matrix products  59.2 us (24%)
  starting transfers between devices  42.4 us (18%)
  local copies, waits for them, and re-layouts  18 us (7%)
  other arithmetic  17.7 us (7%)
  blocking collectives  12.1 us (5%)
    ppermute x28, waiting for transfers between devices, exchange(): return lax.ppermute(x, axis, [(i, i ^ step) for i in range(count)])  90.7 us
    ppermute x28, starting transfers between devices, exchange(): return lax.ppermute(x, axis, [(i, i ^ step) for i in range(count)])  42.4 us
    dot_general x2, matrix products, partial_rows(): jnp.dot(columns.T, direct, precision=fast, preferred_element_type=jnp.flo...  32.5 us
    all_gather x1, blocking collectives, shards(): gathered_a = lax.all_gather(coef_a, 'rows', axis=0, tiled=False)  12.1 us
    dot_general x1, matrix products, shards(): jnp.dot(adjoint, full_a, precision=fast, preferred_element_type=jnp.float32)  10.9 us
    dot_general x1, matrix products, shards(): jnp.dot(direct, full_d, precision=fast, preferred_element_type=jnp.float32)  10.6 us
    unnamed x16, local copies, waits for them, and re-layouts  6.74 us
    add x4, other arithmetic, shards(): part = kept + exchange(sent, 'rows', 1 << bit)  5.46 us
  transfers between devices with their start and end apart: 28, of which 19 were waited for; matrix products, arithmetic and copies ran while one was open for 19% of the time, Pallas kernels for 0%

profile of v8, /device:TPU:0, one launch (start us, length us, event | category | flops | bytes accessed | tf_op | source)
XLA Modules:
  0.0 241.1 jit_solution(2005820401392788193)
XLA Ops:
  0.7 16.4 %fusion.7 = f32[768,1536]{1,0:T(8,128)} fusion(f32[1536,1536]{1,0:T(8,128)} %param.3, f32[1536,1536]{1,0:T(8,128)} %param.4, s32[]{:T(128)S(6)} %select_n.161), kind=kOutput, calls=%fused_computation.5 | convolution fusion | flops 10872815616 | bytes 18874372 | tf_op jit(solution)/shard_map/dot_general | solution.py:47
  17.5 16.2 %fusion.4 = f32[768,1536]{1,0:T(8,128)} fusion(f32[1536,1536]{1,0:T(8,128)} %param.3, f32[1536,1536]{1,0:T(8,128)} %param.4, s32[]{:T(128)S(6)} %select_n.160), kind=kOutput, calls=%fused_computation.4 | convolution fusion | flops 10872815616 | bytes 18874372 | tf_op jit(solution)/shard_map/dot_general | solution.py:47
  33.7 4.8 %add.154 = f32[768,1536]{1,0:T(8,128)S(1)} add(f32[768,1536]{1,0:T(8,128)} %fusion.4, f32[768,1536]{1,0:T(8,128)} %collective-permute-done) | non-fusion elementwise | flops 1179648 | bytes 14155776 | tf_op jit(solution)/shard_map/add | solution.py:51
  41.7 2.6 %collective-permute-start.1 = (f32[2,192,768]{2,1,0:T(8,128)S(1)}, f32[2,192,768]{2,1,0:T(8,128)}, u32[]{:S(2)}, u32[]{:S(2)}) collective-permute-start(f32[2,192,768]{2,1,0:T(8,128)S(1)} %dynamic-slice_bitcast_fusion.1), channel_id=1, source_target_pairs={{0,8},{8,0},{16,24},{24,16},{1,9},{9,1},{17,25},{25,17},{2,10},{10... | collective-permute-start | bytes 3538952 | tf_op jit(solution)/shard_map/ppermute | solution.py:11
  44.2 2.4 dynamic-slice_bitcast_fusion
  48.1 22.9 %collective-permute-done.1 = f32[2,192,768]{2,1,0:T(8,128)} collective-permute-done((f32[2,192,768]{2,1,0:T(8,128)S(1)}, f32[2,192,768]{2,1,0:T(8,128)}, u32[]{:S(2)}, u32[]{:S(2)}) %collective-permute-start.1) | collective-permute-done | bytes 1179680 | tf_op jit(solution)/shard_map/ppermute | solution.py:11
  79.4 8.7 %collective-permute-done.2 = f32[192,768]{1,0:T(8,128)} collective-permute-done((f32[192,768]{1,0:T(8,128)S(1)}, f32[192,768]{1,0:T(8,128)}, u32[]{:S(2)}, u32[]{:S(2)}) %collective-permute-start.2) | collective-permute-done | bytes 589856 | tf_op jit(solution)/shard_map/ppermute | solution.py:11
  89.2 4.0 %collective-permute-done.4 = f32[192,768]{1,0:T(8,128)} collective-permute-done((f32[192,768]{1,0:T(8,128)}, f32[192,768]{1,0:T(8,128)}, u32[]{:S(2)}, u32[]{:S(2)}) %collective-permute-start.4) | collective-permute-done | bytes 589856 | tf_op jit(solution)/shard_map/ppermute | solution.py:11
  95.5 2.2 reshape.30
  100.7 12.1 %collective-permute-done.5 = f32[192,2,384]{2,1,0:T(2,128)S(1)} collective-permute-done((f32[192,2,384]{2,1,0:T(2,128)S(1)}, f32[192,2,384]{2,1,0:T(2,128)S(1)}, u32[]{:S(2)}, u32[]{:S(2)}) %collective-permute-start.5) | collective-permute-done | bytes 589856 | tf_op jit(solution)/shard_map/ppermute | solution.py:11
  113.8 2.7 %collective-permute-start.6 = (f32[192,384]{1,0:T(8,128)S(1)}, f32[192,384]{1,0:T(8,128)S(1)}, u32[]{:S(2)}, u32[]{:S(2)}) collective-permute-start(f32[192,384]{1,0:T(8,128)S(1)} %bitcast.66), channel_id=1, source_target_pairs={{0,4},{1,5},{2,6},{3,7},{4,0},{5,1},{6,2},{7,3},{8,12},{9,13},{10,... | collective-permute-start | bytes 884744 | tf_op jit(solution)/shard_map/ppermute | solution.py:11
  116.5 11.1 %collective-permute-done.6 = f32[192,384]{1,0:T(8,128)S(1)} collective-permute-done((f32[192,384]{1,0:T(8,128)S(1)}, f32[192,384]{1,0:T(8,128)S(1)}, u32[]{:S(2)}, u32[]{:S(2)}) %collective-permute-start.6) | collective-permute-done | bytes 294944 | tf_op jit(solution)/shard_map/ppermute | solution.py:11
  133.1 2.7 %collective-permute-done.8 = f32[384,64]{0,1:T(8,128)S(1)} collective-permute-done((f32[384,64]{0,1:T(8,128)S(1)}, f32[384,64]{0,1:T(8,128)S(1)}, u32[]{:S(2)}, u32[]{:S(2)}) %collective-permute-start.8) | collective-permute-done | bytes 98336 | tf_op jit(solution)/shard_map/ppermute | solution.py:11
  137.5 2.8 %collective-permute-start.17 = (f32[384,64]{0,1:T(8,128)S(1)}, f32[384,64]{0,1:T(8,128)S(1)}, u32[]{:S(2)}, u32[]{:S(2)}) collective-permute-start(f32[384,64]{0,1:T(8,128)S(1)} %add.183), channel_id=1, source_target_pairs={{0,4},{1,5},{2,6},{3,7},{4,0},{5,1},{6,2},{7,3},{8,12},{9,13},{10,... | collective-permute-start | bytes 294920 | tf_op jit(solution)/shard_map/ppermute | solution.py:11
  140.4 5.3 %collective-permute-done.9 = f32[384,64]{0,1:T(8,128)S(1)} collective-permute-done((f32[384,64]{0,1:T(8,128)S(1)}, f32[384,64]{0,1:T(8,128)S(1)}, u32[]{:S(2)}, u32[]{:S(2)}) %collective-permute-start.9) | collective-permute-done | bytes 98336 | tf_op jit(solution)/shard_map/ppermute | solution.py:11
  148.8 2.2 collective-permute-done.10
  161.1 3.5 %collective-permute-start.13 = (f32[384,64]{0,1:T(8,128)S(1)}, f32[384,64]{0,1:T(8,128)S(1)}, u32[]{:S(2)}, u32[]{:S(2)}) collective-permute-start(f32[384,64]{0,1:T(8,128)S(1)} %add.179), channel_id=1, source_target_pairs={{0,4},{1,5},{2,6},{3,7},{4,0},{5,1},{6,2},{7,3},{8,12},{9,13},{10,... | collective-permute-start | bytes 294920 | tf_op jit(solution)/shard_map/ppermute | solution.py:11
  164.7 2.7 %collective-permute-start.21 = (f32[384,64]{0,1:T(8,128)S(1)}, f32[384,64]{0,1:T(8,128)S(1)}, u32[]{:S(2)}, u32[]{:S(2)}) collective-permute-start(f32[384,64]{0,1:T(8,128)S(1)} %add.187), channel_id=1, source_target_pairs={{0,4},{1,5},{2,6},{3,7},{4,0},{5,1},{6,2},{7,3},{8,12},{9,13},{10,... | collective-permute-start | bytes 294920 | tf_op jit(solution)/shard_map/ppermute | solution.py:11
  177.3 3.7 %collective-permute-done.23 = f32[384,64]{0,1:T(8,128)S(1)} collective-permute-done((f32[384,64]{0,1:T(8,128)S(1)}, f32[384,64]{0,1:T(8,128)S(1)}, u32[]{:S(2)}, u32[]{:S(2)}) %collective-permute-start.23) | collective-permute-done | bytes 98336 | tf_op jit(solution)/shard_map/ppermute | solution.py:11
  183.0 12.1 %all-gather = f32[1536,128]{0,1:T(8,128)S(1)} all-gather(f32[384,128]{0,1:T(8,128)S(1)} %pad_maximum_fusion.5), channel_id=2, replica_groups=mesh['rows'=4,'cols'=8] {'rows'}, dimensions={0}, use_global_device_ids=true | all-gather | bytes 983040 | tf_op jit(solution)/shard_map/all_gather | solution.py:98
  196.5 2.3 collective-permute-start.25
  198.9 9.9 %collective-permute-done.25 = f32[2,1,1,384,128]{3,4,2,1,0:T(8,128)} collective-permute-done((f32[2,1,1,384,128]{3,4,2,1,0:T(8,128)S(1)}, f32[2,1,1,384,128]{3,4,2,1,0:T(8,128)}, u32[]{:S(2)}, u32[]{:S(2)}) %collective-permute-start.25) | collective-permute-done | bytes 393248 | tf_op jit(solution)/shard_map/ppermute | solution.py:11
  212.7 10.9 %fusion.11 = f32[1536,256]{0,1:T(8,128)S(1)} fusion(f32[1536,1536]{1,0:T(8,128)} %param.4, f32[1536,128]{1,0:T(8,128)S(1)} %get-tuple-element.9, f32[1536,128]{1,0:T(8,128)S(1)} %get-tuple-element.8), kind=kOutput, calls=%fused_computation.9 | convolution fusion | flops 3624665088 | bytes 12582912 | tf_op jit(solution)/shard_map/dot_general | solution.py:116
  228.8 10.6 %fusion.10 = f32[1536,256]{0,1:T(8,128)S(1)} fusion(f32[1536,1536]{1,0:T(8,128)} %param.3, f32[192,8,2,128]{3,2,1,0:T(2,128)} %bitcast.62), kind=kOutput, calls=%fused_computation.8 | convolution fusion | flops 3624271872 | bytes 12582912 | tf_op jit(solution)/shard_map/dot_general | solution.py:115
  (102 shorter events, 65.5 us)
Async XLA Ops:
  17.0 16.6 %collective-permute-start = (f32[768,1536]{1,0:T(8,128)}, f32[768,1536]{1,0:T(8,128)}, u32[]{:S(2)}, u32[]{:S(2)}) collective-permute-start(f32[768,1536]{1,0:T(8,128)} %fusion.7), channel_id=1, source_target_pairs={{0,1},{1,0},{2,3},{3,2},{4,5},{5,4},{6,7},{7,6},{8,9},{9,8},{10,11... | collective-permute-start | bytes 14155784 | tf_op jit(solution)/shard_map/ppermute | solution.py:11
  41.7 29.3 %collective-permute-start.1 = (f32[2,192,768]{2,1,0:T(8,128)S(1)}, f32[2,192,768]{2,1,0:T(8,128)}, u32[]{:S(2)}, u32[]{:S(2)}) collective-permute-start(f32[2,192,768]{2,1,0:T(8,128)S(1)} %dynamic-slice_bitcast_fusion.1), channel_id=1, source_target_pairs={{0,8},{8,0},{16,24},{24,16},{1,9},{9,1},{17,25},{25,17},{2,10},{10... | collective-permute-start | bytes 3538952 | tf_op jit(solution)/shard_map/ppermute | solution.py:11
  46.6 28.4 %collective-permute-start.3 = (f32[2,192,768]{2,1,0:T(8,128)}, f32[2,192,768]{2,1,0:T(8,128)}, u32[]{:S(2)}, u32[]{:S(2)}) collective-permute-start(f32[2,192,768]{2,1,0:T(8,128)} %dynamic-slice_bitcast_fusion), channel_id=1, source_target_pairs={{0,16},{8,24},{16,0},{24,8},{1,17},{9,25},{17,1},{25,9},{2,18},{10... | collective-permute-start | bytes 3538952 | tf_op jit(solution)/shard_map/ppermute | solution.py:11
  72.8 15.3 %collective-permute-start.2 = (f32[192,768]{1,0:T(8,128)S(1)}, f32[192,768]{1,0:T(8,128)}, u32[]{:S(2)}, u32[]{:S(2)}) collective-permute-start(f32[192,768]{1,0:T(8,128)S(1)} %dynamic-slice_bitcast_fusion.3), channel_id=1, source_target_pairs={{0,16},{8,24},{16,0},{24,8},{1,17},{9,25},{17,1},{25,9},{2,18},{10... | collective-permute-start | bytes 1769480 | tf_op jit(solution)/shard_map/ppermute | solution.py:11
  78.3 14.9 %collective-permute-start.4 = (f32[192,768]{1,0:T(8,128)}, f32[192,768]{1,0:T(8,128)}, u32[]{:S(2)}, u32[]{:S(2)}) collective-permute-start(f32[192,768]{1,0:T(8,128)} %dynamic-slice_bitcast_fusion.2), channel_id=1, source_target_pairs={{0,8},{8,0},{16,24},{24,16},{1,9},{9,1},{17,25},{25,17},{2,10},{10... | collective-permute-start | bytes 1769480 | tf_op jit(solution)/shard_map/ppermute | solution.py:11
  99.1 13.8 %collective-permute-start.5 = (f32[192,2,384]{2,1,0:T(2,128)S(1)}, f32[192,2,384]{2,1,0:T(2,128)S(1)}, u32[]{:S(2)}, u32[]{:S(2)}) collective-permute-start(f32[192,2,384]{2,1,0:T(2,128)S(1)} %bitcast.65), channel_id=1, source_target_pairs={{0,2},{1,3},{2,0},{3,1},{4,6},{5,7},{6,4},{7,5},{8,10},{9,11},{10,... | collective-permute-start | bytes 1769480 | tf_op jit(solution)/shard_map/ppermute | solution.py:11
  113.8 13.8 %collective-permute-start.6 = (f32[192,384]{1,0:T(8,128)S(1)}, f32[192,384]{1,0:T(8,128)S(1)}, u32[]{:S(2)}, u32[]{:S(2)}) collective-permute-start(f32[192,384]{1,0:T(8,128)S(1)} %bitcast.66), channel_id=1, source_target_pairs={{0,4},{1,5},{2,6},{3,7},{4,0},{5,1},{6,2},{7,3},{8,12},{9,13},{10,... | collective-permute-start | bytes 884744 | tf_op jit(solution)/shard_map/ppermute | solution.py:11
  130.2 5.7 %collective-permute-start.8 = (f32[384,64]{0,1:T(8,128)S(1)}, f32[384,64]{0,1:T(8,128)S(1)}, u32[]{:S(2)}, u32[]{:S(2)}) collective-permute-start(f32[384,64]{0,1:T(8,128)S(1)} %fusion.19), channel_id=1, source_target_pairs={{0,2},{1,3},{2,0},{3,1},{4,6},{5,7},{6,4},{7,5},{8,10},{9,11},{10,... | collective-permute-start | bytes 294920 | tf_op jit(solution)/shard_map/ppermute | solution.py:11
  131.7 5.8 %collective-permute-start.16 = (f32[384,64]{0,1:T(8,128)S(1)}, f32[384,64]{0,1:T(8,128)S(1)}, u32[]{:S(2)}, u32[]{:S(2)}) collective-permute-start(f32[384,64]{0,1:T(8,128)S(1)} %fusion.17), channel_id=1, source_target_pairs={{0,2},{1,3},{2,0},{3,1},{4,6},{5,7},{6,4},{7,5},{8,10},{9,11},{10,... | collective-permute-start | bytes 294920 | tf_op jit(solution)/shard_map/ppermute | solution.py:11
  135.9 9.8 %collective-permute-start.9 = (f32[384,64]{0,1:T(8,128)S(1)}, f32[384,64]{0,1:T(8,128)S(1)}, u32[]{:S(2)}, u32[]{:S(2)}) collective-permute-start(f32[384,64]{0,1:T(8,128)S(1)} %add.175), channel_id=1, source_target_pairs={{0,4},{1,5},{2,6},{3,7},{4,0},{5,1},{6,2},{7,3},{8,12},{9,13},{10,... | collective-permute-start | bytes 294920 | tf_op jit(solution)/shard_map/ppermute | solution.py:11
  137.5 9.9 %collective-permute-start.17 = (f32[384,64]{0,1:T(8,128)S(1)}, f32[384,64]{0,1:T(8,128)S(1)}, u32[]{:S(2)}, u32[]{:S(2)}) collective-permute-start(f32[384,64]{0,1:T(8,128)S(1)} %add.183), channel_id=1, source_target_pairs={{0,4},{1,5},{2,6},{3,7},{4,0},{5,1},{6,2},{7,3},{8,12},{9,13},{10,... | collective-permute-start | bytes 294920 | tf_op jit(solution)/shard_map/ppermute | solution.py:11
  146.1 4.8 %collective-permute-start.10 = (f32[384,64]{0,1:T(8,128)S(1)}, f32[384,64]{0,1:T(8,128)S(1)}, u32[]{:S(2)}, u32[]{:S(2)}) collective-permute-start(f32[384,64]{0,1:T(8,128)S(1)} %fusion.27), channel_id=1, source_target_pairs={{0,8},{8,0},{16,24},{24,16},{1,9},{9,1},{17,25},{25,17},{2,10},{10... | collective-permute-start | bytes 294920 | tf_op jit(solution)/shard_map/ppermute | solution.py:11
  147.9 4.7 %collective-permute-start.18 = (f32[384,64]{0,1:T(8,128)S(1)}, f32[384,64]{0,1:T(8,128)S(1)}, u32[]{:S(2)}, u32[]{:S(2)}) collective-permute-start(f32[384,64]{0,1:T(8,128)S(1)} %fusion.23), channel_id=1, source_target_pairs={{0,8},{8,0},{16,24},{24,16},{1,9},{9,1},{17,25},{25,17},{2,10},{10... | collective-permute-start | bytes 294920 | tf_op jit(solution)/shard_map/ppermute | solution.py:11
  152.6 4.9 %collective-permute-start.19 = (f32[384,64]{0,1:T(8,128)S(1)}, f32[384,64]{0,1:T(8,128)S(1)}, u32[]{:S(2)}, u32[]{:S(2)}) collective-permute-start(f32[384,64]{0,1:T(8,128)S(1)} %add.185), channel_id=1, source_target_pairs={{0,16},{8,24},{16,0},{24,8},{1,17},{9,25},{17,1},{25,9},{2,18},{10... | collective-permute-start | bytes 294920 | tf_op jit(solution)/shard_map/ppermute | solution.py:11
  158.3 6.3 %collective-permute-start.20 = (f32[384,64]{0,1:T(8,128)S(1)}, f32[384,64]{0,1:T(8,128)S(1)}, u32[]{:S(2)}, u32[]{:S(2)}) collective-permute-start(f32[384,64]{0,1:T(8,128)S(1)} %fusion.21), channel_id=1, source_target_pairs={{0,2},{1,3},{2,0},{3,1},{4,6},{5,7},{6,4},{7,5},{8,10},{9,11},{10,... | collective-permute-start | bytes 294920 | tf_op jit(solution)/shard_map/ppermute | solution.py:11
  161.1 6.3 %collective-permute-start.13 = (f32[384,64]{0,1:T(8,128)S(1)}, f32[384,64]{0,1:T(8,128)S(1)}, u32[]{:S(2)}, u32[]{:S(2)}) collective-permute-start(f32[384,64]{0,1:T(8,128)S(1)} %add.179), channel_id=1, source_target_pairs={{0,4},{1,5},{2,6},{3,7},{4,0},{5,1},{6,2},{7,3},{8,12},{9,13},{10,... | collective-permute-start | bytes 294920 | tf_op jit(solution)/shard_map/ppermute | solution.py:11
  164.7 5.6 %collective-permute-start.21 = (f32[384,64]{0,1:T(8,128)S(1)}, f32[384,64]{0,1:T(8,128)S(1)}, u32[]{:S(2)}, u32[]{:S(2)}) collective-permute-start(f32[384,64]{0,1:T(8,128)S(1)} %add.187), channel_id=1, source_target_pairs={{0,4},{1,5},{2,6},{3,7},{4,0},{5,1},{6,2},{7,3},{8,12},{9,13},{10,... | collective-permute-start | bytes 294920 | tf_op jit(solution)/shard_map/ppermute | solution.py:11
  167.9 4.7 %collective-permute-start.14 = (f32[384,64]{0,1:T(8,128)S(1)}, f32[384,64]{0,1:T(8,128)S(1)}, u32[]{:S(2)}, u32[]{:S(2)}) collective-permute-start(f32[384,64]{0,1:T(8,128)S(1)} %fusion.33), channel_id=1, source_target_pairs={{0,8},{8,0},{16,24},{24,16},{1,9},{9,1},{17,25},{25,17},{2,10},{10... | collective-permute-start | bytes 294920 | tf_op jit(solution)/shard_map/ppermute | solution.py:11
  172.6 4.7 %collective-permute-start.15 = (f32[384,64]{0,1:T(8,128)S(1)}, f32[384,64]{0,1:T(8,128)S(1)}, u32[]{:S(2)}, u32[]{:S(2)}) collective-permute-start(f32[384,64]{0,1:T(8,128)S(1)} %add.181), channel_id=1, source_target_pairs={{0,16},{8,24},{16,0},{24,8},{1,17},{9,25},{17,1},{25,9},{2,18},{10... | collective-permute-start | bytes 294920 | tf_op jit(solution)/shard_map/ppermute | solution.py:11
  175.5 5.5 %collective-permute-start.23 = (f32[384,64]{0,1:T(8,128)S(1)}, f32[384,64]{0,1:T(8,128)S(1)}, u32[]{:S(2)}, u32[]{:S(2)}) collective-permute-start(f32[384,64]{0,1:T(8,128)S(1)} %add.189), channel_id=1, source_target_pairs={{0,16},{8,24},{16,0},{24,8},{1,17},{9,25},{17,1},{25,9},{2,18},{10... | collective-permute-start | bytes 294920 | tf_op jit(solution)/shard_map/ppermute | solution.py:11
  181.0 14.5 %collective-permute-start.24 = (f32[1,1,1,384,128]{3,4,2,1,0:T(8,128)S(1)}, f32[1,1,1,384,128]{3,4,2,1,0:T(8,128)}, u32[]{:S(2)}, u32[]{:S(2)}) collective-permute-start(f32[1,1,1,384,128]{3,4,2,1,0:T(8,128)S(1)} %maximum_bitcast_fusion), channel_id=1, source_target_pairs={{0,4},{1,5},{2,6},{3,7},{4,0},{5,1},{6,2},{7,3},{8,12},{9,13},{10,... | collective-permute-start | bytes 589832 | tf_op jit(solution)/shard_map/ppermute | solution.py:11
  195.4 16.1 %collective-permute-start.27 = (f32[1536,128]{1,0:T(8,128)S(1)}, f32[1536,128]{1,0:T(8,128)}, u32[]{:S(2)}, u32[]{:S(2)}) collective-permute-start(f32[1536,128]{1,0:T(8,128)S(1)} %bitcast.64), channel_id=1, source_target_pairs={{0,1},{1,0},{2,3},{3,2},{4,5},{5,4},{6,7},{7,6},{8,9},{9,8},{10,11... | collective-permute-start | bytes 2359304 | tf_op jit(solution)/shard_map/ppermute | solution.py:11
  196.5 12.2 %collective-permute-start.25 = (f32[2,1,1,384,128]{3,4,2,1,0:T(8,128)S(1)}, f32[2,1,1,384,128]{3,4,2,1,0:T(8,128)}, u32[]{:S(2)}, u32[]{:S(2)}) collective-permute-start(f32[2,1,1,384,128]{3,4,2,1,0:T(8,128)S(1)} %pad_maximum_fusion.4), channel_id=1, source_target_pairs={{0,2},{1,3},{2,0},{3,1},{4,6},{5,7},{6,4},{7,5},{8,10},{9,11},{10,... | collective-permute-start | bytes 1179656 | tf_op jit(solution)/shard_map/ppermute | solution.py:11
  211.5 13.8 %collective-permute-start.26 = (f32[2,2,1,384,128]{3,4,2,1,0:T(8,128)}, f32[2,2,1,384,128]{3,4,2,1,0:T(8,128)}, u32[]{:S(2)}, u32[]{:S(2)}) collective-permute-start(f32[2,2,1,384,128]{3,4,2,1,0:T(8,128)} %pad_maximum_fusion.2), channel_id=1, source_target_pairs={{0,1},{1,0},{2,3},{3,2},{4,5},{5,4},{6,7},{7,6},{8,9},{9,8},{10,11... | collective-permute-start | bytes 2359304 | tf_op jit(solution)/shard_map/ppermute | solution.py:11
  (10 other events, 188.3 us)

commit v9 on v8

--- a/solution.py
+++ b/solution.py
@@ -91,11 +91,16 @@
                 jnp.dot(chip_tile.T, coef_a, precision=high, preferred_element_type=jnp.float32),
                 "rows", 1, row_count,
             )
-        chains_a.append(coef_a)
+        gathered = coef_a[None]
+        step = 1
+        while step < row_count:
+            low = (row_index & step) == 0
+            gathered = in_order(low, gathered, exchange(gathered, "rows", step), 0)
+            step *= 2
+        chains_a.append(gathered)
         chains_d.append(coef_d)
-    coef_a = jnp.concatenate(chains_a, axis=1)
+    gathered_a = jnp.concatenate(chains_a, axis=2)
     coef_d = jnp.concatenate(chains_d, axis=1)
-    gathered_a = lax.all_gather(coef_a, "rows", axis=0, tiled=False)
     half_a = (
         gathered_a.reshape(row_count, 2, part_rows, probe_half)
         .transpose(1, 0, 2, 3)

time: 242 us -> 234 us (0.967)
  blocking collectives: 12.1 us -> 0 us
  waiting for transfers between devices: 90.7 us -> 93.4 us
    all_gather x1 -> x0, blocking collectives: 12.1 us -> none  [shards(): gathered_a = lax.all_gather(coef_a, 'rows', axis=0, tiled=False)]
    ppermute x28 -> x32, waiting for transfers between devices: 90.7 us -> 93.4 us  [exchange(): return lax.ppermute(x, axis, [(i, i ^ step) for i in range(count)])]
    ppermute x28 -> x32, starting transfers between devices: 42.4 us -> 44.1 us  [exchange(): return lax.ppermute(x, axis, [(i, i ^ step) for i in range(count)])]
  transfers between devices with their start and end apart: 28 -> 32, of which waited for: 19 -> 19; matrix products, arithmetic and copies ran while one was open for 19% -> 19% of each run, Pallas kernels for 0% -> 0%
where the time goes in v9:
time: 234 us
  waiting for transfers between devices  93.4 us (40%)
  matrix products  59.2 us (25%)
  starting transfers between devices  44.1 us (19%)
  local copies, waits for them, and re-layouts  18 us (8%)
  other arithmetic  17.9 us (8%)
    ppermute x32, waiting for transfers between devices, exchange(): return lax.ppermute(x, axis, [(i, i ^ step) for i in range(count)])  93.4 us
    ppermute x32, starting transfers between devices, exchange(): return lax.ppermute(x, axis, [(i, i ^ step) for i in range(count)])  44.1 us
    dot_general x2, matrix products, partial_rows(): jnp.dot(columns.T, direct, precision=fast, preferred_element_type=jnp.flo...  32.6 us
    dot_general x1, matrix products, shards(): jnp.dot(adjoint, full_a, precision=fast, preferred_element_type=jnp.float32)  10.9 us
    dot_general x1, matrix products, shards(): jnp.dot(direct, full_d, precision=fast, preferred_element_type=jnp.float32)  10.6 us
    unnamed x16, local copies, waits for them, and re-layouts  6.75 us
    add x4, other arithmetic, shards(): part = kept + exchange(sent, 'rows', 1 << bit)  5.46 us
    add x1, other arithmetic, shards(): chip_sum = kept_rows + received  4.76 us
  transfers between devices with their start and end apart: 32, of which 19 were waited for; matrix products, arithmetic and copies ran while one was open for 19% of the time, Pallas kernels for 0%

profile of v9, /device:TPU:0, one launch (start us, length us, event | category | flops | bytes accessed | tf_op | source)
XLA Modules:
  0.0 233.6 jit_solution(3922486315871197464)
XLA Ops:
  0.7 16.3 %fusion.7 = f32[768,1536]{1,0:T(8,128)} fusion(f32[1536,1536]{1,0:T(8,128)} %param.3, f32[1536,1536]{1,0:T(8,128)} %param.4, s32[]{:T(128)S(6)} %select_n.201), kind=kOutput, calls=%fused_computation.5 | convolution fusion | flops 10872815616 | bytes 18874372 | tf_op jit(solution)/shard_map/dot_general | solution.py:47
  17.4 16.2 %fusion.4 = f32[768,1536]{1,0:T(8,128)} fusion(f32[1536,1536]{1,0:T(8,128)} %param.3, f32[1536,1536]{1,0:T(8,128)} %param.4, s32[]{:T(128)S(6)} %select_n.200), kind=kOutput, calls=%fused_computation.4 | convolution fusion | flops 10872815616 | bytes 18874372 | tf_op jit(solution)/shard_map/dot_general | solution.py:47
  33.7 4.8 %add.154 = f32[768,1536]{1,0:T(8,128)S(1)} add(f32[768,1536]{1,0:T(8,128)} %fusion.4, f32[768,1536]{1,0:T(8,128)} %collective-permute-done) | non-fusion elementwise | flops 1179648 | bytes 14155776 | tf_op jit(solution)/shard_map/add | solution.py:51
  41.7 2.6 %collective-permute-start.1 = (f32[2,192,768]{2,1,0:T(8,128)S(1)}, f32[2,192,768]{2,1,0:T(8,128)}, u32[]{:S(2)}, u32[]{:S(2)}) collective-permute-start(f32[2,192,768]{2,1,0:T(8,128)S(1)} %dynamic-slice_bitcast_fusion.1), channel_id=1, source_target_pairs={{0,8},{8,0},{16,24},{24,16},{1,9},{9,1},{17,25},{25,17},{2,10},{10... | collective-permute-start | bytes 3538952 | tf_op jit(solution)/shard_map/ppermute | solution.py:11
  44.2 2.4 %dynamic-slice_bitcast_fusion = f32[2,192,768]{2,1,0:T(8,128)} fusion(f32[2,2,192,768]{3,2,1,0:T(8,128)} %bitcast.59, s32[]{:T(128)S(6)} %select_n.207), kind=kLoop, calls=%fused_computation.19 | loop fusion | bytes 2359300 | tf_op jit(solution)/shard_map/jit(dynamic_index_in_dim)/squeeze | solution.py:65
  48.1 22.9 %collective-permute-done.1 = f32[2,192,768]{2,1,0:T(8,128)} collective-permute-done((f32[2,192,768]{2,1,0:T(8,128)S(1)}, f32[2,192,768]{2,1,0:T(8,128)}, u32[]{:S(2)}, u32[]{:S(2)}) %collective-permute-start.1) | collective-permute-done | bytes 1179680 | tf_op jit(solution)/shard_map/ppermute | solution.py:11
  79.4 8.7 %collective-permute-done.2 = f32[192,768]{1,0:T(8,128)} collective-permute-done((f32[192,768]{1,0:T(8,128)S(1)}, f32[192,768]{1,0:T(8,128)}, u32[]{:S(2)}, u32[]{:S(2)}) %collective-permute-start.2) | collective-permute-done | bytes 589856 | tf_op jit(solution)/shard_map/ppermute | solution.py:11
  89.3 4.0 %collective-permute-done.4 = f32[192,768]{1,0:T(8,128)} collective-permute-done((f32[192,768]{1,0:T(8,128)}, f32[192,768]{1,0:T(8,128)}, u32[]{:S(2)}, u32[]{:S(2)}) %collective-permute-start.4) | collective-permute-done | bytes 589856 | tf_op jit(solution)/shard_map/ppermute | solution.py:11
  95.6 2.2 reshape.30
  100.8 12.1 %collective-permute-done.5 = f32[192,2,384]{2,1,0:T(2,128)S(1)} collective-permute-done((f32[192,2,384]{2,1,0:T(2,128)S(1)}, f32[192,2,384]{2,1,0:T(2,128)S(1)}, u32[]{:S(2)}, u32[]{:S(2)}) %collective-permute-start.5) | collective-permute-done | bytes 589856 | tf_op jit(solution)/shard_map/ppermute | solution.py:11
  113.8 2.7 %collective-permute-start.6 = (f32[192,384]{1,0:T(8,128)S(1)}, f32[192,384]{1,0:T(8,128)S(1)}, u32[]{:S(2)}, u32[]{:S(2)}) collective-permute-start(f32[192,384]{1,0:T(8,128)S(1)} %bitcast.68), channel_id=1, source_target_pairs={{0,4},{1,5},{2,6},{3,7},{4,0},{5,1},{6,2},{7,3},{8,12},{9,13},{10,... | collective-permute-start | bytes 884744 | tf_op jit(solution)/shard_map/ppermute | solution.py:11
  116.5 11.1 %collective-permute-done.6 = f32[192,384]{1,0:T(8,128)S(1)} collective-permute-done((f32[192,384]{1,0:T(8,128)S(1)}, f32[192,384]{1,0:T(8,128)S(1)}, u32[]{:S(2)}, u32[]{:S(2)}) %collective-permute-start.6) | collective-permute-done | bytes 294944 | tf_op jit(solution)/shard_map/ppermute | solution.py:11
  133.2 2.7 %collective-permute-done.8 = f32[384,64]{0,1:T(8,128)S(1)} collective-permute-done((f32[384,64]{0,1:T(8,128)S(1)}, f32[384,64]{0,1:T(8,128)S(1)}, u32[]{:S(2)}, u32[]{:S(2)}) %collective-permute-start.8) | collective-permute-done | bytes 98336 | tf_op jit(solution)/shard_map/ppermute | solution.py:11
  137.6 2.8 %collective-permute-start.17 = (f32[384,64]{0,1:T(8,128)S(1)}, f32[384,64]{0,1:T(8,128)S(1)}, u32[]{:S(2)}, u32[]{:S(2)}) collective-permute-start(f32[384,64]{0,1:T(8,128)S(1)} %add.183), channel_id=1, source_target_pairs={{0,4},{1,5},{2,6},{3,7},{4,0},{5,1},{6,2},{7,3},{8,12},{9,13},{10,... | collective-permute-start | bytes 294920 | tf_op jit(solution)/shard_map/ppermute | solution.py:11
  140.4 5.3 %collective-permute-done.9 = f32[384,64]{0,1:T(8,128)S(1)} collective-permute-done((f32[384,64]{0,1:T(8,128)S(1)}, f32[384,64]{0,1:T(8,128)S(1)}, u32[]{:S(2)}, u32[]{:S(2)}) %collective-permute-start.9) | collective-permute-done | bytes 98336 | tf_op jit(solution)/shard_map/ppermute | solution.py:11
  148.8 2.2 collective-permute-done.10
  161.1 3.5 %collective-permute-start.13 = (f32[384,64]{0,1:T(8,128)S(1)}, f32[384,64]{0,1:T(8,128)S(1)}, u32[]{:S(2)}, u32[]{:S(2)}) collective-permute-start(f32[384,64]{0,1:T(8,128)S(1)} %add.179), channel_id=1, source_target_pairs={{0,4},{1,5},{2,6},{3,7},{4,0},{5,1},{6,2},{7,3},{8,12},{9,13},{10,... | collective-permute-start | bytes 294920 | tf_op jit(solution)/shard_map/ppermute | solution.py:11
  164.7 2.7 %collective-permute-start.21 = (f32[384,64]{0,1:T(8,128)S(1)}, f32[384,64]{0,1:T(8,128)S(1)}, u32[]{:S(2)}, u32[]{:S(2)}) collective-permute-start(f32[384,64]{0,1:T(8,128)S(1)} %add.187), channel_id=1, source_target_pairs={{0,4},{1,5},{2,6},{3,7},{4,0},{5,1},{6,2},{7,3},{8,12},{9,13},{10,... | collective-permute-start | bytes 294920 | tf_op jit(solution)/shard_map/ppermute | solution.py:11
  183.4 2.2 collective-permute-start.24
  186.2 6.2 %collective-permute-done.24 = f32[1,1,1,384,128]{3,4,2,1,0:T(8,128)} collective-permute-done((f32[1,1,1,384,128]{3,4,2,1,0:T(8,128)S(1)}, f32[1,1,1,384,128]{3,4,2,1,0:T(8,128)}, u32[]{:S(2)}, u32[]{:S(2)}) %collective-permute-start.24) | collective-permute-done | bytes 196640 | tf_op jit(solution)/shard_map/ppermute | solution.py:11
  193.5 7.8 %collective-permute-done.25 = f32[2,1,1,384,128]{3,4,2,1,0:T(8,128)} collective-permute-done((f32[2,1,1,384,128]{3,4,2,1,0:T(8,128)S(1)}, f32[2,1,1,384,128]{3,4,2,1,0:T(8,128)}, u32[]{:S(2)}, u32[]{:S(2)}) %collective-permute-start.25) | collective-permute-done | bytes 393248 | tf_op jit(solution)/shard_map/ppermute | solution.py:11
  205.3 10.9 %fusion.11 = f32[1536,256]{0,1:T(8,128)S(1)} fusion(f32[1536,1536]{1,0:T(8,128)} %param.4, f32[1536,128]{1,0:T(8,128)S(1)} %get-tuple-element.9, f32[1536,128]{1,0:T(8,128)S(1)} %get-tuple-element.8), kind=kOutput, calls=%fused_computation.9 | convolution fusion | flops 3624665088 | bytes 12582912 | tf_op jit(solution)/shard_map/dot_general | solution.py:121
  219.3 2.1 copy.7
  221.4 10.6 %fusion.10 = f32[1536,256]{0,1:T(8,128)S(1)} fusion(f32[1536,1536]{1,0:T(8,128)} %param.3, f32[192,8,2,128]{3,2,1,0:T(2,128)} %bitcast.64), kind=kOutput, calls=%fused_computation.8 | convolution fusion | flops 3624271872 | bytes 12582912 | tf_op jit(solution)/shard_map/dot_general | solution.py:120
  (115 shorter events, 67.7 us)
Async XLA Ops:
  17.0 16.7 %collective-permute-start = (f32[768,1536]{1,0:T(8,128)}, f32[768,1536]{1,0:T(8,128)}, u32[]{:S(2)}, u32[]{:S(2)}) collective-permute-start(f32[768,1536]{1,0:T(8,128)} %fusion.7), channel_id=1, source_target_pairs={{0,1},{1,0},{2,3},{3,2},{4,5},{5,4},{6,7},{7,6},{8,9},{9,8},{10,11... | collective-permute-start | bytes 14155784 | tf_op jit(solution)/shard_map/ppermute | solution.py:11
  41.7 29.3 %collective-permute-start.1 = (f32[2,192,768]{2,1,0:T(8,128)S(1)}, f32[2,192,768]{2,1,0:T(8,128)}, u32[]{:S(2)}, u32[]{:S(2)}) collective-permute-start(f32[2,192,768]{2,1,0:T(8,128)S(1)} %dynamic-slice_bitcast_fusion.1), channel_id=1, source_target_pairs={{0,8},{8,0},{16,24},{24,16},{1,9},{9,1},{17,25},{25,17},{2,10},{10... | collective-permute-start | bytes 3538952 | tf_op jit(solution)/shard_map/ppermute | solution.py:11
  46.6 28.4 %collective-permute-start.3 = (f32[2,192,768]{2,1,0:T(8,128)}, f32[2,192,768]{2,1,0:T(8,128)}, u32[]{:S(2)}, u32[]{:S(2)}) collective-permute-start(f32[2,192,768]{2,1,0:T(8,128)} %dynamic-slice_bitcast_fusion), channel_id=1, source_target_pairs={{0,16},{8,24},{16,0},{24,8},{1,17},{9,25},{17,1},{25,9},{2,18},{10... | collective-permute-start | bytes 3538952 | tf_op jit(solution)/shard_map/ppermute | solution.py:11
  72.8 15.3 %collective-permute-start.2 = (f32[192,768]{1,0:T(8,128)S(1)}, f32[192,768]{1,0:T(8,128)}, u32[]{:S(2)}, u32[]{:S(2)}) collective-permute-start(f32[192,768]{1,0:T(8,128)S(1)} %dynamic-slice_bitcast_fusion.3), channel_id=1, source_target_pairs={{0,16},{8,24},{16,0},{24,8},{1,17},{9,25},{17,1},{25,9},{2,18},{10... | collective-permute-start | bytes 1769480 | tf_op jit(solution)/shard_map/ppermute | solution.py:11
  78.3 14.9 %collective-permute-start.4 = (f32[192,768]{1,0:T(8,128)}, f32[192,768]{1,0:T(8,128)}, u32[]{:S(2)}, u32[]{:S(2)}) collective-permute-start(f32[192,768]{1,0:T(8,128)} %dynamic-slice_bitcast_fusion.2), channel_id=1, source_target_pairs={{0,8},{8,0},{16,24},{24,16},{1,9},{9,1},{17,25},{25,17},{2,10},{10... | collective-permute-start | bytes 1769480 | tf_op jit(solution)/shard_map/ppermute | solution.py:11
  99.1 13.8 %collective-permute-start.5 = (f32[192,2,384]{2,1,0:T(2,128)S(1)}, f32[192,2,384]{2,1,0:T(2,128)S(1)}, u32[]{:S(2)}, u32[]{:S(2)}) collective-permute-start(f32[192,2,384]{2,1,0:T(2,128)S(1)} %bitcast.67), channel_id=1, source_target_pairs={{0,2},{1,3},{2,0},{3,1},{4,6},{5,7},{6,4},{7,5},{8,10},{9,11},{10,... | collective-permute-start | bytes 1769480 | tf_op jit(solution)/shard_map/ppermute | solution.py:11
  113.8 13.8 %collective-permute-start.6 = (f32[192,384]{1,0:T(8,128)S(1)}, f32[192,384]{1,0:T(8,128)S(1)}, u32[]{:S(2)}, u32[]{:S(2)}) collective-permute-start(f32[192,384]{1,0:T(8,128)S(1)} %bitcast.68), channel_id=1, source_target_pairs={{0,4},{1,5},{2,6},{3,7},{4,0},{5,1},{6,2},{7,3},{8,12},{9,13},{10,... | collective-permute-start | bytes 884744 | tf_op jit(solution)/shard_map/ppermute | solution.py:11
  130.2 5.7 %collective-permute-start.8 = (f32[384,64]{0,1:T(8,128)S(1)}, f32[384,64]{0,1:T(8,128)S(1)}, u32[]{:S(2)}, u32[]{:S(2)}) collective-permute-start(f32[384,64]{0,1:T(8,128)S(1)} %fusion.19), channel_id=1, source_target_pairs={{0,2},{1,3},{2,0},{3,1},{4,6},{5,7},{6,4},{7,5},{8,10},{9,11},{10,... | collective-permute-start | bytes 294920 | tf_op jit(solution)/shard_map/ppermute | solution.py:11
  131.7 5.8 %collective-permute-start.16 = (f32[384,64]{0,1:T(8,128)S(1)}, f32[384,64]{0,1:T(8,128)S(1)}, u32[]{:S(2)}, u32[]{:S(2)}) collective-permute-start(f32[384,64]{0,1:T(8,128)S(1)} %fusion.17), channel_id=1, source_target_pairs={{0,2},{1,3},{2,0},{3,1},{4,6},{5,7},{6,4},{7,5},{8,10},{9,11},{10,... | collective-permute-start | bytes 294920 | tf_op jit(solution)/shard_map/ppermute | solution.py:11
  135.9 9.8 %collective-permute-start.9 = (f32[384,64]{0,1:T(8,128)S(1)}, f32[384,64]{0,1:T(8,128)S(1)}, u32[]{:S(2)}, u32[]{:S(2)}) collective-permute-start(f32[384,64]{0,1:T(8,128)S(1)} %add.175), channel_id=1, source_target_pairs={{0,4},{1,5},{2,6},{3,7},{4,0},{5,1},{6,2},{7,3},{8,12},{9,13},{10,... | collective-permute-start | bytes 294920 | tf_op jit(solution)/shard_map/ppermute | solution.py:11
  137.6 9.9 %collective-permute-start.17 = (f32[384,64]{0,1:T(8,128)S(1)}, f32[384,64]{0,1:T(8,128)S(1)}, u32[]{:S(2)}, u32[]{:S(2)}) collective-permute-start(f32[384,64]{0,1:T(8,128)S(1)} %add.183), channel_id=1, source_target_pairs={{0,4},{1,5},{2,6},{3,7},{4,0},{5,1},{6,2},{7,3},{8,12},{9,13},{10,... | collective-permute-start | bytes 294920 | tf_op jit(solution)/shard_map/ppermute | solution.py:11
  158.3 6.3 %collective-permute-start.20 = (f32[384,64]{0,1:T(8,128)S(1)}, f32[384,64]{0,1:T(8,128)S(1)}, u32[]{:S(2)}, u32[]{:S(2)}) collective-permute-start(f32[384,64]{0,1:T(8,128)S(1)} %fusion.21), channel_id=1, source_target_pairs={{0,2},{1,3},{2,0},{3,1},{4,6},{5,7},{6,4},{7,5},{8,10},{9,11},{10,... | collective-permute-start | bytes 294920 | tf_op jit(solution)/shard_map/ppermute | solution.py:11
  161.1 6.3 %collective-permute-start.13 = (f32[384,64]{0,1:T(8,128)S(1)}, f32[384,64]{0,1:T(8,128)S(1)}, u32[]{:S(2)}, u32[]{:S(2)}) collective-permute-start(f32[384,64]{0,1:T(8,128)S(1)} %add.179), channel_id=1, source_target_pairs={{0,4},{1,5},{2,6},{3,7},{4,0},{5,1},{6,2},{7,3},{8,12},{9,13},{10,... | collective-permute-start | bytes 294920 | tf_op jit(solution)/shard_map/ppermute | solution.py:11
  164.7 5.6 %collective-permute-start.21 = (f32[384,64]{0,1:T(8,128)S(1)}, f32[384,64]{0,1:T(8,128)S(1)}, u32[]{:S(2)}, u32[]{:S(2)}) collective-permute-start(f32[384,64]{0,1:T(8,128)S(1)} %add.187), channel_id=1, source_target_pairs={{0,4},{1,5},{2,6},{3,7},{4,0},{5,1},{6,2},{7,3},{8,12},{9,13},{10,... | collective-permute-start | bytes 294920 | tf_op jit(solution)/shard_map/ppermute | solution.py:11
  167.5 7.4 %collective-permute-start.27 = (f32[1,384,64]{1,2,0:T(8,128)S(1)}, f32[1,384,64]{1,2,0:T(8,128)S(1)}, u32[]{:S(2)}, u32[]{:S(2)}) collective-permute-start(f32[1,384,64]{1,2,0:T(8,128)S(1)} %add_bitcast_fusion.1), channel_id=1, source_target_pairs={{0,8},{8,0},{16,24},{24,16},{1,9},{9,1},{17,25},{25,17},{2,10},{10... | collective-permute-start | bytes 294920 | tf_op jit(solution)/shard_map/ppermute | solution.py:11
  170.3 9.5 %collective-permute-start.29 = (f32[1,384,64]{1,2,0:T(8,128)S(1)}, f32[1,384,64]{1,2,0:T(8,128)S(1)}, u32[]{:S(2)}, u32[]{:S(2)}) collective-permute-start(f32[1,384,64]{1,2,0:T(8,128)S(1)} %add_bitcast_fusion), channel_id=1, source_target_pairs={{0,8},{8,0},{16,24},{24,16},{1,9},{9,1},{17,25},{25,17},{2,10},{10... | collective-permute-start | bytes 294920 | tf_op jit(solution)/shard_map/ppermute | solution.py:11
  174.9 10.8 %collective-permute-start.28 = (f32[2,384,64]{1,2,0:T(8,128)S(1)}, f32[2,384,64]{1,2,0:T(8,128)S(1)}, u32[]{:S(2)}, u32[]{:S(2)}) collective-permute-start(f32[2,384,64]{1,2,0:T(8,128)S(1)} %pad_maximum_fusion.5), channel_id=1, source_target_pairs={{0,16},{8,24},{16,0},{24,8},{1,17},{9,25},{17,1},{25,9},{2,18},{10... | collective-permute-start | bytes 589832 | tf_op jit(solution)/shard_map/ppermute | solution.py:11
  176.9 5.4 %collective-permute-start.15 = (f32[384,64]{0,1:T(8,128)S(1)}, f32[384,64]{0,1:T(8,128)S(1)}, u32[]{:S(2)}, u32[]{:S(2)}) collective-permute-start(f32[384,64]{0,1:T(8,128)S(1)} %add.181), channel_id=1, source_target_pairs={{0,16},{8,24},{16,0},{24,8},{1,17},{9,25},{17,1},{25,9},{2,18},{10... | collective-permute-start | bytes 294920 | tf_op jit(solution)/shard_map/ppermute | solution.py:11
  178.2 5.1 %collective-permute-start.23 = (f32[384,64]{0,1:T(8,128)S(1)}, f32[384,64]{0,1:T(8,128)S(1)}, u32[]{:S(2)}, u32[]{:S(2)}) collective-permute-start(f32[384,64]{0,1:T(8,128)S(1)} %add.189), channel_id=1, source_target_pairs={{0,16},{8,24},{16,0},{24,8},{1,17},{9,25},{17,1},{25,9},{2,18},{10... | collective-permute-start | bytes 294920 | tf_op jit(solution)/shard_map/ppermute | solution.py:11
  179.9 5.8 %collective-permute-start.30 = (f32[2,384,64]{1,2,0:T(8,128)S(1)}, f32[2,384,64]{1,2,0:T(8,128)S(1)}, u32[]{:S(2)}, u32[]{:S(2)}) collective-permute-start(f32[2,384,64]{1,2,0:T(8,128)S(1)} %pad_maximum_fusion.6), channel_id=1, source_target_pairs={{0,16},{8,24},{16,0},{24,8},{1,17},{9,25},{17,1},{25,9},{2,18},{10... | collective-permute-start | bytes 589832 | tf_op jit(solution)/shard_map/ppermute | solution.py:11
  183.4 9.0 %collective-permute-start.24 = (f32[1,1,1,384,128]{3,4,2,1,0:T(8,128)S(1)}, f32[1,1,1,384,128]{3,4,2,1,0:T(8,128)}, u32[]{:S(2)}, u32[]{:S(2)}) collective-permute-start(f32[1,1,1,384,128]{3,4,2,1,0:T(8,128)S(1)} %maximum_bitcast_fusion), channel_id=1, source_target_pairs={{0,4},{1,5},{2,6},{3,7},{4,0},{5,1},{6,2},{7,3},{8,12},{9,13},{10,... | collective-permute-start | bytes 589832 | tf_op jit(solution)/shard_map/ppermute | solution.py:11
  186.1 17.9 %collective-permute-start.31 = (f32[1536,128]{1,0:T(8,128)S(1)}, f32[1536,128]{1,0:T(8,128)}, u32[]{:S(2)}, u32[]{:S(2)}) collective-permute-start(f32[1536,128]{1,0:T(8,128)S(1)} %bitcast.66), channel_id=1, source_target_pairs={{0,1},{1,0},{2,3},{3,2},{4,5},{5,4},{6,7},{7,6},{8,9},{9,8},{10,11... | collective-permute-start | bytes 2359304 | tf_op jit(solution)/shard_map/ppermute | solution.py:11
  193.3 7.9 %collective-permute-start.25 = (f32[2,1,1,384,128]{3,4,2,1,0:T(8,128)S(1)}, f32[2,1,1,384,128]{3,4,2,1,0:T(8,128)}, u32[]{:S(2)}, u32[]{:S(2)}) collective-permute-start(f32[2,1,1,384,128]{3,4,2,1,0:T(8,128)S(1)} %pad_maximum_fusion.4), channel_id=1, source_target_pairs={{0,2},{1,3},{2,0},{3,1},{4,6},{5,7},{6,4},{7,5},{8,10},{9,11},{10,... | collective-permute-start | bytes 1179656 | tf_op jit(solution)/shard_map/ppermute | solution.py:11
  204.0 13.8 %collective-permute-start.26 = (f32[2,2,1,384,128]{3,4,2,1,0:T(8,128)}, f32[2,2,1,384,128]{3,4,2,1,0:T(8,128)}, u32[]{:S(2)}, u32[]{:S(2)}) collective-permute-start(f32[2,2,1,384,128]{3,4,2,1,0:T(8,128)} %pad_maximum_fusion.2), channel_id=1, source_target_pairs={{0,1},{1,0},{2,3},{3,2},{4,5},{5,4},{6,7},{7,6},{8,9},{9,8},{10,11... | collective-permute-start | bytes 2359304 | tf_op jit(solution)/shard_map/ppermute | solution.py:11
  (14 other events, 207.5 us)

commit v10 on v9

--- a/solution.py
+++ b/solution.py
@@ -26,7 +26,6 @@
 
 
 def shards(direct, adjoint, probes):
-    high = lax.Precision.HIGHEST
     fast = lax.Precision.HIGH
     row_count = lax.axis_size("rows")
     col_count = lax.axis_size("cols")
@@ -84,11 +83,11 @@
         coef_d = probes_d[:, chain * quarter:(chain + 1) * quarter]
         for rnd in range(2):
             coef_a = doubling_sum(
-                jnp.dot(chip_tile, coef_d, precision=high, preferred_element_type=jnp.float32),
+                jnp.dot(chip_tile, coef_d, precision=fast, preferred_element_type=jnp.float32),
                 "cols", 2, col_count,
             )
             coef_d = doubling_sum(
-                jnp.dot(chip_tile.T, coef_a, precision=high, preferred_element_type=jnp.float32),
+                jnp.dot(chip_tile.T, coef_a, precision=fast, preferred_element_type=jnp.float32),
                 "rows", 1, row_count,
             )
         gathered = coef_a[None]

time: 234 us -> 235 us (level)
  no operation moved by 1% of the time
where the time goes in v10:
time: 235 us; the launch traced here: 234 us
  waiting for transfers between devices  95 us (40%)
  matrix products  57.2 us (24%)
  starting transfers between devices  44.9 us (19%)
  local copies, waits for them, and re-layouts  18 us (8%)
  other arithmetic  17.9 us (8%)
    ppermute x32, waiting for transfers between devices, exchange(): return lax.ppermute(x, axis, [(i, i ^ step) for i in range(count)])  95 us
    ppermute x32, starting transfers between devices, exchange(): return lax.ppermute(x, axis, [(i, i ^ step) for i in range(count)])  44.9 us
    dot_general x2, matrix products, partial_rows(): jnp.dot(columns.T, direct, precision=fast, preferred_element_type=jnp.flo...  32.6 us
    dot_general x1, matrix products, shards(): jnp.dot(adjoint, full_a, precision=fast, preferred_element_type=jnp.float32)  10.9 us
    dot_general x1, matrix products, shards(): jnp.dot(direct, full_d, precision=fast, preferred_element_type=jnp.float32)  10.6 us
    unnamed x16, local copies, waits for them, and re-layouts  6.75 us
    add x4, other arithmetic, shards(): part = kept + exchange(sent, 'rows', 1 << bit)  5.46 us
    add x1, other arithmetic, shards(): chip_sum = kept_rows + received  4.76 us
  transfers between devices with their start and end apart: 32, of which 19 were waited for; matrix products, arithmetic and copies ran while one was open for 19% of the time, Pallas kernels for 0%

profile of v10, /device:TPU:0, one launch (start us, length us, event | category | flops | bytes accessed | tf_op | source)
XLA Modules:
  0.0 234.0 jit_solution(928514816801685561)
XLA Ops:
  0.7 16.3 %fusion.7 = f32[768,1536]{1,0:T(8,128)} fusion(f32[1536,1536]{1,0:T(8,128)} %param.3, f32[1536,1536]{1,0:T(8,128)} %param.4, s32[]{:T(128)S(6)} %select_n.201), kind=kOutput, calls=%fused_computation.5 | convolution fusion | flops 10872815616 | bytes 18874372 | tf_op jit(solution)/shard_map/dot_general | solution.py:46
  17.4 16.2 %fusion.4 = f32[768,1536]{1,0:T(8,128)} fusion(f32[1536,1536]{1,0:T(8,128)} %param.3, f32[1536,1536]{1,0:T(8,128)} %param.4, s32[]{:T(128)S(6)} %select_n.200), kind=kOutput, calls=%fused_computation.4 | convolution fusion | flops 10872815616 | bytes 18874372 | tf_op jit(solution)/shard_map/dot_general | solution.py:46
  33.7 4.8 %add.154 = f32[768,1536]{1,0:T(8,128)S(1)} add(f32[768,1536]{1,0:T(8,128)} %fusion.4, f32[768,1536]{1,0:T(8,128)} %collective-permute-done) | non-fusion elementwise | flops 1179648 | bytes 14155776 | tf_op jit(solution)/shard_map/add | solution.py:50
  41.7 2.6 %collective-permute-start.1 = (f32[2,192,768]{2,1,0:T(8,128)S(1)}, f32[2,192,768]{2,1,0:T(8,128)}, u32[]{:S(2)}, u32[]{:S(2)}) collective-permute-start(f32[2,192,768]{2,1,0:T(8,128)S(1)} %dynamic-slice_bitcast_fusion.1), channel_id=1, source_target_pairs={{0,8},{8,0},{16,24},{24,16},{1,9},{9,1},{17,25},{25,17},{2,10},{10... | collective-permute-start | bytes 3538952 | tf_op jit(solution)/shard_map/ppermute | solution.py:11
  44.2 2.4 %dynamic-slice_bitcast_fusion = f32[2,192,768]{2,1,0:T(8,128)} fusion(f32[2,2,192,768]{3,2,1,0:T(8,128)} %bitcast.59, s32[]{:T(128)S(6)} %select_n.207), kind=kLoop, calls=%fused_computation.19 | loop fusion | bytes 2359300 | tf_op jit(solution)/shard_map/jit(dynamic_index_in_dim)/squeeze | solution.py:64
  48.1 22.9 %collective-permute-done.1 = f32[2,192,768]{2,1,0:T(8,128)} collective-permute-done((f32[2,192,768]{2,1,0:T(8,128)S(1)}, f32[2,192,768]{2,1,0:T(8,128)}, u32[]{:S(2)}, u32[]{:S(2)}) %collective-permute-start.1) | collective-permute-done | bytes 1179680 | tf_op jit(solution)/shard_map/ppermute | solution.py:11
  79.4 8.7 %collective-permute-done.2 = f32[192,768]{1,0:T(8,128)} collective-permute-done((f32[192,768]{1,0:T(8,128)S(1)}, f32[192,768]{1,0:T(8,128)}, u32[]{:S(2)}, u32[]{:S(2)}) %collective-permute-start.2) | collective-permute-done | bytes 589856 | tf_op jit(solution)/shard_map/ppermute | solution.py:11
  89.3 4.0 %collective-permute-done.4 = f32[192,768]{1,0:T(8,128)} collective-permute-done((f32[192,768]{1,0:T(8,128)}, f32[192,768]{1,0:T(8,128)}, u32[]{:S(2)}, u32[]{:S(2)}) %collective-permute-start.4) | collective-permute-done | bytes 589856 | tf_op jit(solution)/shard_map/ppermute | solution.py:11
  95.6 2.2 reshape.30
  100.8 12.1 %collective-permute-done.5 = f32[192,2,384]{2,1,0:T(2,128)S(1)} collective-permute-done((f32[192,2,384]{2,1,0:T(2,128)S(1)}, f32[192,2,384]{2,1,0:T(2,128)S(1)}, u32[]{:S(2)}, u32[]{:S(2)}) %collective-permute-start.5) | collective-permute-done | bytes 589856 | tf_op jit(solution)/shard_map/ppermute | solution.py:11
  113.8 2.7 %collective-permute-start.6 = (f32[192,384]{1,0:T(8,128)S(1)}, f32[192,384]{1,0:T(8,128)S(1)}, u32[]{:S(2)}, u32[]{:S(2)}) collective-permute-start(f32[192,384]{1,0:T(8,128)S(1)} %bitcast.68), channel_id=1, source_target_pairs={{0,4},{1,5},{2,6},{3,7},{4,0},{5,1},{6,2},{7,3},{8,12},{9,13},{10,... | collective-permute-start | bytes 884744 | tf_op jit(solution)/shard_map/ppermute | solution.py:11
  116.5 11.1 %collective-permute-done.6 = f32[192,384]{1,0:T(8,128)S(1)} collective-permute-done((f32[192,384]{1,0:T(8,128)S(1)}, f32[192,384]{1,0:T(8,128)S(1)}, u32[]{:S(2)}, u32[]{:S(2)}) %collective-permute-start.6) | collective-permute-done | bytes 294944 | tf_op jit(solution)/shard_map/ppermute | solution.py:11
  132.5 3.0 %collective-permute-done.8 = f32[384,64]{0,1:T(8,128)S(1)} collective-permute-done((f32[384,64]{0,1:T(8,128)S(1)}, f32[384,64]{0,1:T(8,128)S(1)}, u32[]{:S(2)}, u32[]{:S(2)}) %collective-permute-start.8) | collective-permute-done | bytes 98336 | tf_op jit(solution)/shard_map/ppermute | solution.py:11
  137.2 2.2 collective-permute-start.17
  139.4 6.0 %collective-permute-done.9 = f32[384,64]{0,1:T(8,128)S(1)} collective-permute-done((f32[384,64]{0,1:T(8,128)S(1)}, f32[384,64]{0,1:T(8,128)S(1)}, u32[]{:S(2)}, u32[]{:S(2)}) %collective-permute-start.9) | collective-permute-done | bytes 98336 | tf_op jit(solution)/shard_map/ppermute | solution.py:11
  148.1 2.4 %collective-permute-done.10 = f32[384,64]{0,1:T(8,128)S(1)} collective-permute-done((f32[384,64]{0,1:T(8,128)S(1)}, f32[384,64]{0,1:T(8,128)S(1)}, u32[]{:S(2)}, u32[]{:S(2)}) %collective-permute-start.10) | collective-permute-done | bytes 98336 | tf_op jit(solution)/shard_map/ppermute | solution.py:11
  160.3 3.1 %collective-permute-start.13 = (f32[384,64]{0,1:T(8,128)S(1)}, f32[384,64]{0,1:T(8,128)S(1)}, u32[]{:S(2)}, u32[]{:S(2)}) collective-permute-start(f32[384,64]{0,1:T(8,128)S(1)} %add.179), channel_id=1, source_target_pairs={{0,4},{1,5},{2,6},{3,7},{4,0},{5,1},{6,2},{7,3},{8,12},{9,13},{10,... | collective-permute-start | bytes 294920 | tf_op jit(solution)/shard_map/ppermute | solution.py:11
  165.1 2.9 %collective-permute-done.13 = f32[384,64]{0,1:T(8,128)S(1)} collective-permute-done((f32[384,64]{0,1:T(8,128)S(1)}, f32[384,64]{0,1:T(8,128)S(1)}, u32[]{:S(2)}, u32[]{:S(2)}) %collective-permute-start.13) | collective-permute-done | bytes 98336 | tf_op jit(solution)/shard_map/ppermute | solution.py:11
  181.5 2.9 %collective-permute-start.24 = (f32[1,1,1,384,128]{3,4,2,1,0:T(8,128)S(1)}, f32[1,1,1,384,128]{3,4,2,1,0:T(8,128)}, u32[]{:S(2)}, u32[]{:S(2)}) collective-permute-start(f32[1,1,1,384,128]{3,4,2,1,0:T(8,128)S(1)} %maximum_bitcast_fusion), channel_id=1, source_target_pairs={{0,4},{1,5},{2,6},{3,7},{4,0},{5,1},{6,2},{7,3},{8,12},{9,13},{10,... | collective-permute-start | bytes 589832 | tf_op jit(solution)/shard_map/ppermute | solution.py:11
  185.0 5.4 %collective-permute-done.24 = f32[1,1,1,384,128]{3,4,2,1,0:T(8,128)} collective-permute-done((f32[1,1,1,384,128]{3,4,2,1,0:T(8,128)S(1)}, f32[1,1,1,384,128]{3,4,2,1,0:T(8,128)}, u32[]{:S(2)}, u32[]{:S(2)}) %collective-permute-start.24) | collective-permute-done | bytes 196640 | tf_op jit(solution)/shard_map/ppermute | solution.py:11
  191.4 3.6 %collective-permute-start.25 = (f32[2,1,1,384,128]{3,4,2,1,0:T(8,128)S(1)}, f32[2,1,1,384,128]{3,4,2,1,0:T(8,128)}, u32[]{:S(2)}, u32[]{:S(2)}) collective-permute-start(f32[2,1,1,384,128]{3,4,2,1,0:T(8,128)S(1)} %pad_maximum_fusion.4), channel_id=1, source_target_pairs={{0,2},{1,3},{2,0},{3,1},{4,6},{5,7},{6,4},{7,5},{8,10},{9,11},{10,... | collective-permute-start | bytes 1179656 | tf_op jit(solution)/shard_map/ppermute | solution.py:11
  195.0 6.7 %collective-permute-done.25 = f32[2,1,1,384,128]{3,4,2,1,0:T(8,128)} collective-permute-done((f32[2,1,1,384,128]{3,4,2,1,0:T(8,128)S(1)}, f32[2,1,1,384,128]{3,4,2,1,0:T(8,128)}, u32[]{:S(2)}, u32[]{:S(2)}) %collective-permute-start.25) | collective-permute-done | bytes 393248 | tf_op jit(solution)/shard_map/ppermute | solution.py:11
  205.6 10.9 %fusion.11 = f32[1536,256]{0,1:T(8,128)S(1)} fusion(f32[1536,1536]{1,0:T(8,128)} %param.4, f32[1536,128]{1,0:T(8,128)S(1)} %get-tuple-element.9, f32[1536,128]{1,0:T(8,128)S(1)} %get-tuple-element.8), kind=kOutput, calls=%fused_computation.9 | convolution fusion | flops 3624665088 | bytes 12582912 | tf_op jit(solution)/shard_map/dot_general | solution.py:120
  221.7 10.6 %fusion.10 = f32[1536,256]{0,1:T(8,128)S(1)} fusion(f32[1536,1536]{1,0:T(8,128)} %param.3, f32[192,8,2,128]{3,2,1,0:T(2,128)} %bitcast.64), kind=kOutput, calls=%fused_computation.8 | convolution fusion | flops 3624271872 | bytes 12582912 | tf_op jit(solution)/shard_map/dot_general | solution.py:119
  (115 shorter events, 67.5 us)
Async XLA Ops:
  17.0 16.7 %collective-permute-start = (f32[768,1536]{1,0:T(8,128)}, f32[768,1536]{1,0:T(8,128)}, u32[]{:S(2)}, u32[]{:S(2)}) collective-permute-start(f32[768,1536]{1,0:T(8,128)} %fusion.7), channel_id=1, source_target_pairs={{0,1},{1,0},{2,3},{3,2},{4,5},{5,4},{6,7},{7,6},{8,9},{9,8},{10,11... | collective-permute-start | bytes 14155784 | tf_op jit(solution)/shard_map/ppermute | solution.py:11
  41.7 29.3 %collective-permute-start.1 = (f32[2,192,768]{2,1,0:T(8,128)S(1)}, f32[2,192,768]{2,1,0:T(8,128)}, u32[]{:S(2)}, u32[]{:S(2)}) collective-permute-start(f32[2,192,768]{2,1,0:T(8,128)S(1)} %dynamic-slice_bitcast_fusion.1), channel_id=1, source_target_pairs={{0,8},{8,0},{16,24},{24,16},{1,9},{9,1},{17,25},{25,17},{2,10},{10... | collective-permute-start | bytes 3538952 | tf_op jit(solution)/shard_map/ppermute | solution.py:11
  46.6 28.4 %collective-permute-start.3 = (f32[2,192,768]{2,1,0:T(8,128)}, f32[2,192,768]{2,1,0:T(8,128)}, u32[]{:S(2)}, u32[]{:S(2)}) collective-permute-start(f32[2,192,768]{2,1,0:T(8,128)} %dynamic-slice_bitcast_fusion), channel_id=1, source_target_pairs={{0,16},{8,24},{16,0},{24,8},{1,17},{9,25},{17,1},{25,9},{2,18},{10... | collective-permute-start | bytes 3538952 | tf_op jit(solution)/shard_map/ppermute | solution.py:11
  72.8 15.3 %collective-permute-start.2 = (f32[192,768]{1,0:T(8,128)S(1)}, f32[192,768]{1,0:T(8,128)}, u32[]{:S(2)}, u32[]{:S(2)}) collective-permute-start(f32[192,768]{1,0:T(8,128)S(1)} %dynamic-slice_bitcast_fusion.3), channel_id=1, source_target_pairs={{0,16},{8,24},{16,0},{24,8},{1,17},{9,25},{17,1},{25,9},{2,18},{10... | collective-permute-start | bytes 1769480 | tf_op jit(solution)/shard_map/ppermute | solution.py:11
  78.3 14.9 %collective-permute-start.4 = (f32[192,768]{1,0:T(8,128)}, f32[192,768]{1,0:T(8,128)}, u32[]{:S(2)}, u32[]{:S(2)}) collective-permute-start(f32[192,768]{1,0:T(8,128)} %dynamic-slice_bitcast_fusion.2), channel_id=1, source_target_pairs={{0,8},{8,0},{16,24},{24,16},{1,9},{9,1},{17,25},{25,17},{2,10},{10... | collective-permute-start | bytes 1769480 | tf_op jit(solution)/shard_map/ppermute | solution.py:11
  99.1 13.8 %collective-permute-start.5 = (f32[192,2,384]{2,1,0:T(2,128)S(1)}, f32[192,2,384]{2,1,0:T(2,128)S(1)}, u32[]{:S(2)}, u32[]{:S(2)}) collective-permute-start(f32[192,2,384]{2,1,0:T(2,128)S(1)} %bitcast.67), channel_id=1, source_target_pairs={{0,2},{1,3},{2,0},{3,1},{4,6},{5,7},{6,4},{7,5},{8,10},{9,11},{10,... | collective-permute-start | bytes 1769480 | tf_op jit(solution)/shard_map/ppermute | solution.py:11
  113.8 13.8 %collective-permute-start.6 = (f32[192,384]{1,0:T(8,128)S(1)}, f32[192,384]{1,0:T(8,128)S(1)}, u32[]{:S(2)}, u32[]{:S(2)}) collective-permute-start(f32[192,384]{1,0:T(8,128)S(1)} %bitcast.68), channel_id=1, source_target_pairs={{0,4},{1,5},{2,6},{3,7},{4,0},{5,1},{6,2},{7,3},{8,12},{9,13},{10,... | collective-permute-start | bytes 884744 | tf_op jit(solution)/shard_map/ppermute | solution.py:11
  129.9 5.7 %collective-permute-start.8 = (f32[384,64]{0,1:T(8,128)S(1)}, f32[384,64]{0,1:T(8,128)S(1)}, u32[]{:S(2)}, u32[]{:S(2)}) collective-permute-start(f32[384,64]{0,1:T(8,128)S(1)} %fusion.19), channel_id=1, source_target_pairs={{0,2},{1,3},{2,0},{3,1},{4,6},{5,7},{6,4},{7,5},{8,10},{9,11},{10,... | collective-permute-start | bytes 294920 | tf_op jit(solution)/shard_map/ppermute | solution.py:11
  131.1 6.1 %collective-permute-start.16 = (f32[384,64]{0,1:T(8,128)S(1)}, f32[384,64]{0,1:T(8,128)S(1)}, u32[]{:S(2)}, u32[]{:S(2)}) collective-permute-start(f32[384,64]{0,1:T(8,128)S(1)} %fusion.17), channel_id=1, source_target_pairs={{0,2},{1,3},{2,0},{3,1},{4,6},{5,7},{6,4},{7,5},{8,10},{9,11},{10,... | collective-permute-start | bytes 294920 | tf_op jit(solution)/shard_map/ppermute | solution.py:11
  135.6 9.8 %collective-permute-start.9 = (f32[384,64]{0,1:T(8,128)S(1)}, f32[384,64]{0,1:T(8,128)S(1)}, u32[]{:S(2)}, u32[]{:S(2)}) collective-permute-start(f32[384,64]{0,1:T(8,128)S(1)} %add.175), channel_id=1, source_target_pairs={{0,4},{1,5},{2,6},{3,7},{4,0},{5,1},{6,2},{7,3},{8,12},{9,13},{10,... | collective-permute-start | bytes 294920 | tf_op jit(solution)/shard_map/ppermute | solution.py:11
  137.2 9.7 %collective-permute-start.17 = (f32[384,64]{0,1:T(8,128)S(1)}, f32[384,64]{0,1:T(8,128)S(1)}, u32[]{:S(2)}, u32[]{:S(2)}) collective-permute-start(f32[384,64]{0,1:T(8,128)S(1)} %add.183), channel_id=1, source_target_pairs={{0,4},{1,5},{2,6},{3,7},{4,0},{5,1},{6,2},{7,3},{8,12},{9,13},{10,... | collective-permute-start | bytes 294920 | tf_op jit(solution)/shard_map/ppermute | solution.py:11
  145.6 4.9 %collective-permute-start.10 = (f32[384,64]{0,1:T(8,128)S(1)}, f32[384,64]{0,1:T(8,128)S(1)}, u32[]{:S(2)}, u32[]{:S(2)}) collective-permute-start(f32[384,64]{0,1:T(8,128)S(1)} %fusion.27), channel_id=1, source_target_pairs={{0,8},{8,0},{16,24},{24,16},{1,9},{9,1},{17,25},{25,17},{2,10},{10... | collective-permute-start | bytes 294920 | tf_op jit(solution)/shard_map/ppermute | solution.py:11
  147.2 4.9 %collective-permute-start.18 = (f32[384,64]{0,1:T(8,128)S(1)}, f32[384,64]{0,1:T(8,128)S(1)}, u32[]{:S(2)}, u32[]{:S(2)}) collective-permute-start(f32[384,64]{0,1:T(8,128)S(1)} %fusion.23), channel_id=1, source_target_pairs={{0,8},{8,0},{16,24},{24,16},{1,9},{9,1},{17,25},{25,17},{2,10},{10... | collective-permute-start | bytes 294920 | tf_op jit(solution)/shard_map/ppermute | solution.py:11
  157.2 6.2 %collective-permute-start.20 = (f32[384,64]{0,1:T(8,128)S(1)}, f32[384,64]{0,1:T(8,128)S(1)}, u32[]{:S(2)}, u32[]{:S(2)}) collective-permute-start(f32[384,64]{0,1:T(8,128)S(1)} %fusion.21), channel_id=1, source_target_pairs={{0,2},{1,3},{2,0},{3,1},{4,6},{5,7},{6,4},{7,5},{8,10},{9,11},{10,... | collective-permute-start | bytes 294920 | tf_op jit(solution)/shard_map/ppermute | solution.py:11
  160.3 7.8 %collective-permute-start.13 = (f32[384,64]{0,1:T(8,128)S(1)}, f32[384,64]{0,1:T(8,128)S(1)}, u32[]{:S(2)}, u32[]{:S(2)}) collective-permute-start(f32[384,64]{0,1:T(8,128)S(1)} %add.179), channel_id=1, source_target_pairs={{0,4},{1,5},{2,6},{3,7},{4,0},{5,1},{6,2},{7,3},{8,12},{9,13},{10,... | collective-permute-start | bytes 294920 | tf_op jit(solution)/shard_map/ppermute | solution.py:11
  163.4 6.0 %collective-permute-start.21 = (f32[384,64]{0,1:T(8,128)S(1)}, f32[384,64]{0,1:T(8,128)S(1)}, u32[]{:S(2)}, u32[]{:S(2)}) collective-permute-start(f32[384,64]{0,1:T(8,128)S(1)} %add.187), channel_id=1, source_target_pairs={{0,4},{1,5},{2,6},{3,7},{4,0},{5,1},{6,2},{7,3},{8,12},{9,13},{10,... | collective-permute-start | bytes 294920 | tf_op jit(solution)/shard_map/ppermute | solution.py:11
  168.1 5.1 %collective-permute-start.27 = (f32[1,384,64]{1,2,0:T(8,128)S(1)}, f32[1,384,64]{1,2,0:T(8,128)S(1)}, u32[]{:S(2)}, u32[]{:S(2)}) collective-permute-start(f32[1,384,64]{1,2,0:T(8,128)S(1)} %add_bitcast_fusion.1), channel_id=1, source_target_pairs={{0,8},{8,0},{16,24},{24,16},{1,9},{9,1},{17,25},{25,17},{2,10},{10... | collective-permute-start | bytes 294920 | tf_op jit(solution)/shard_map/ppermute | solution.py:11
  169.4 8.8 %collective-permute-start.29 = (f32[1,384,64]{1,2,0:T(8,128)S(1)}, f32[1,384,64]{1,2,0:T(8,128)S(1)}, u32[]{:S(2)}, u32[]{:S(2)}) collective-permute-start(f32[1,384,64]{1,2,0:T(8,128)S(1)} %add_bitcast_fusion), channel_id=1, source_target_pairs={{0,8},{8,0},{16,24},{24,16},{1,9},{9,1},{17,25},{25,17},{2,10},{10... | collective-permute-start | bytes 294920 | tf_op jit(solution)/shard_map/ppermute | solution.py:11
  173.2 11.3 %collective-permute-start.28 = (f32[2,384,64]{1,2,0:T(8,128)S(1)}, f32[2,384,64]{1,2,0:T(8,128)S(1)}, u32[]{:S(2)}, u32[]{:S(2)}) collective-permute-start(f32[2,384,64]{1,2,0:T(8,128)S(1)} %pad_maximum_fusion.5), channel_id=1, source_target_pairs={{0,16},{8,24},{16,0},{24,8},{1,17},{9,25},{17,1},{25,9},{2,18},{10... | collective-permute-start | bytes 589832 | tf_op jit(solution)/shard_map/ppermute | solution.py:11
  178.2 6.3 %collective-permute-start.30 = (f32[2,384,64]{1,2,0:T(8,128)S(1)}, f32[2,384,64]{1,2,0:T(8,128)S(1)}, u32[]{:S(2)}, u32[]{:S(2)}) collective-permute-start(f32[2,384,64]{1,2,0:T(8,128)S(1)} %pad_maximum_fusion.6), channel_id=1, source_target_pairs={{0,16},{8,24},{16,0},{24,8},{1,17},{9,25},{17,1},{25,9},{2,18},{10... | collective-permute-start | bytes 589832 | tf_op jit(solution)/shard_map/ppermute | solution.py:11
  181.5 8.8 %collective-permute-start.24 = (f32[1,1,1,384,128]{3,4,2,1,0:T(8,128)S(1)}, f32[1,1,1,384,128]{3,4,2,1,0:T(8,128)}, u32[]{:S(2)}, u32[]{:S(2)}) collective-permute-start(f32[1,1,1,384,128]{3,4,2,1,0:T(8,128)S(1)} %maximum_bitcast_fusion), channel_id=1, source_target_pairs={{0,4},{1,5},{2,6},{3,7},{4,0},{5,1},{6,2},{7,3},{8,12},{9,13},{10,... | collective-permute-start | bytes 589832 | tf_op jit(solution)/shard_map/ppermute | solution.py:11
  184.9 19.5 %collective-permute-start.31 = (f32[1536,128]{1,0:T(8,128)S(1)}, f32[1536,128]{1,0:T(8,128)}, u32[]{:S(2)}, u32[]{:S(2)}) collective-permute-start(f32[1536,128]{1,0:T(8,128)S(1)} %bitcast.66), channel_id=1, source_target_pairs={{0,1},{1,0},{2,3},{3,2},{4,5},{5,4},{6,7},{7,6},{8,9},{9,8},{10,11... | collective-permute-start | bytes 2359304 | tf_op jit(solution)/shard_map/ppermute | solution.py:11
  191.4 10.3 %collective-permute-start.25 = (f32[2,1,1,384,128]{3,4,2,1,0:T(8,128)S(1)}, f32[2,1,1,384,128]{3,4,2,1,0:T(8,128)}, u32[]{:S(2)}, u32[]{:S(2)}) collective-permute-start(f32[2,1,1,384,128]{3,4,2,1,0:T(8,128)S(1)} %pad_maximum_fusion.4), channel_id=1, source_target_pairs={{0,2},{1,3},{2,0},{3,1},{4,6},{5,7},{6,4},{7,5},{8,10},{9,11},{10,... | collective-permute-start | bytes 1179656 | tf_op jit(solution)/shard_map/ppermute | solution.py:11
  204.4 13.8 %collective-permute-start.26 = (f32[2,2,1,384,128]{3,4,2,1,0:T(8,128)}, f32[2,2,1,384,128]{3,4,2,1,0:T(8,128)}, u32[]{:S(2)}, u32[]{:S(2)}) collective-permute-start(f32[2,2,1,384,128]{3,4,2,1,0:T(8,128)} %pad_maximum_fusion.2), channel_id=1, source_target_pairs={{0,1},{1,0},{2,3},{3,2},{4,5},{5,4},{6,7},{7,6},{8,9},{9,8},{10,11... | collective-permute-start | bytes 2359304 | tf_op jit(solution)/shard_map/ppermute | solution.py:11
  (14 other events, 207.0 us)

commit v11 on v9

--- a/solution.py
+++ b/solution.py
@@ -79,6 +79,7 @@
     own_probes = lax.dynamic_slice_in_dim(probes, core * probe_half, probe_half, 1)
     probes_d = lax.dynamic_slice_in_dim(own_probes, chip * chip_cols, chip_cols, 0)
     chains_a, chains_d = [], []
+    col_bits = col_count.bit_length() - 1
     quarter = probe_half // 2
     for chain in range(2):
         coef_d = probes_d[:, chain * quarter:(chain + 1) * quarter]
@@ -98,20 +99,19 @@
             gathered = in_order(low, gathered, exchange(gathered, "rows", step), 0)
             step *= 2
         chains_a.append(gathered)
-        chains_d.append(coef_d)
+        gathered = coef_d.reshape((1,) * col_bits + coef_d.shape)
+        for bit in range(col_bits - 1, -1, -1):
+            low = (col_index >> bit) % 2 == 0
+            gathered = in_order(low, gathered, exchange(gathered, "cols", 1 << bit), col_bits - 1 - bit)
+        chains_d.append(gathered)
     gathered_a = jnp.concatenate(chains_a, axis=2)
-    coef_d = jnp.concatenate(chains_d, axis=1)
+    gathered_d = jnp.concatenate(chains_d, axis=-1)
     half_a = (
         gathered_a.reshape(row_count, 2, part_rows, probe_half)
         .transpose(1, 0, 2, 3)
         .reshape(snap_count, probe_half)
     )
     full_a = in_order(first, half_a, exchange(half_a, "cols", 1), 1)
-    col_bits = col_count.bit_length() - 1
-    gathered_d = coef_d.reshape((1,) * col_bits + coef_d.shape)
-    for bit in range(col_bits - 1, -1, -1):
-        low = (col_index >> bit) % 2 == 0
-        gathered_d = in_order(low, gathered_d, exchange(gathered_d, "cols", 1 << bit), col_bits - 1 - bit)
     full_d = (
         gathered_d.reshape(chip_count, 2, chip_cols, probe_half)
         .transpose(0, 2, 1, 3)

time: 234 us -> 230 us (0.983)
  waiting for transfers between devices: 93.4 us -> 82.9 us
  starting transfers between devices: 44.1 us -> 50.7 us
    ppermute x32 -> x35, waiting for transfers between devices: 93.4 us -> 82.9 us  [exchange(): return lax.ppermute(x, axis, [(i, i ^ step) for i in range(count)])]
    ppermute x32 -> x35, starting transfers between devices: 44.1 us -> 50.7 us  [exchange(): return lax.ppermute(x, axis, [(i, i ^ step) for i in range(count)])]
    select_n x9 -> x12, other arithmetic: 4.75 us -> 3.82 us  [in_order(): jnp.where(first, mine, theirs)]
    unnamed x16 -> x22, local copies, waits for them, and re-layouts: 6.75 us -> 6.08 us
  transfers between devices with their start and end apart: 32 -> 35, of which waited for: 19 -> 20; matrix products, arithmetic and copies ran while one was open for 19% -> 21% of each run, Pallas kernels for 0% -> 0%
where the time goes in v11:
time: 230 us
  waiting for transfers between devices  82.9 us (36%)
  matrix products  59 us (26%)
  starting transfers between devices  50.7 us (22%)
  local copies, waits for them, and re-layouts  18.2 us (8%)
  other arithmetic  17.6 us (8%)
    ppermute x35, waiting for transfers between devices, exchange(): return lax.ppermute(x, axis, [(i, i ^ step) for i in range(count)])  82.9 us
    ppermute x35, starting transfers between devices, exchange(): return lax.ppermute(x, axis, [(i, i ^ step) for i in range(count)])  50.7 us
    dot_general x2, matrix products, partial_rows(): jnp.dot(columns.T, direct, precision=fast, preferred_element_type=jnp.flo...  32.6 us
    dot_general x1, matrix products, shards(): jnp.dot(adjoint, full_a, precision=fast, preferred_element_type=jnp.float32)  10.7 us
    dot_general x1, matrix products, shards(): jnp.dot(direct, full_d, precision=fast, preferred_element_type=jnp.float32)  10.6 us
    unnamed x22, local copies, waits for them, and re-layouts  6.08 us
    add x4, other arithmetic, shards(): part = kept + exchange(sent, 'rows', 1 << bit)  5.46 us
    add x1, other arithmetic, shards(): chip_sum = kept_rows + received  4.76 us
  transfers between devices with their start and end apart: 35, of which 20 were waited for; matrix products, arithmetic and copies ran while one was open for 21% of the time, Pallas kernels for 0%

profile of v11, /device:TPU:0, one launch (start us, length us, event | category | flops | bytes accessed | tf_op | source)
XLA Modules:
  0.0 229.5 jit_solution(5147436986500270197)
XLA Ops:
  0.7 16.3 %fusion.7 = f32[768,1536]{1,0:T(8,128)} fusion(f32[1536,1536]{1,0:T(8,128)} %param.3, f32[1536,1536]{1,0:T(8,128)} %param.4, s32[]{:T(128)S(6)} %select_n.231), kind=kOutput, calls=%fused_computation.5 | convolution fusion | flops 10872815616 | bytes 18874372 | tf_op jit(solution)/shard_map/dot_general | solution.py:47
  17.4 16.2 %fusion.4 = f32[768,1536]{1,0:T(8,128)} fusion(f32[1536,1536]{1,0:T(8,128)} %param.3, f32[1536,1536]{1,0:T(8,128)} %param.4, s32[]{:T(128)S(6)} %select_n.230), kind=kOutput, calls=%fused_computation.4 | convolution fusion | flops 10872815616 | bytes 18874372 | tf_op jit(solution)/shard_map/dot_general | solution.py:47
  33.7 4.8 %add.157 = f32[768,1536]{1,0:T(8,128)S(1)} add(f32[768,1536]{1,0:T(8,128)} %fusion.4, f32[768,1536]{1,0:T(8,128)} %collective-permute-done) | non-fusion elementwise | flops 1179648 | bytes 14155776 | tf_op jit(solution)/shard_map/add | solution.py:51
  41.7 2.6 %collective-permute-start.1 = (f32[2,192,768]{2,1,0:T(8,128)S(1)}, f32[2,192,768]{2,1,0:T(8,128)}, u32[]{:S(2)}, u32[]{:S(2)}) collective-permute-start(f32[2,192,768]{2,1,0:T(8,128)S(1)} %dynamic-slice_bitcast_fusion.1), channel_id=1, source_target_pairs={{0,8},{8,0},{16,24},{24,16},{1,9},{9,1},{17,25},{25,17},{2,10},{10... | collective-permute-start | bytes 3538952 | tf_op jit(solution)/shard_map/ppermute | solution.py:11
  44.3 2.4 %dynamic-slice_bitcast_fusion = f32[2,192,768]{2,1,0:T(8,128)} fusion(f32[2,2,192,768]{3,2,1,0:T(8,128)} %bitcast.57, s32[]{:T(128)S(6)} %select_n.237), kind=kLoop, calls=%fused_computation.19 | loop fusion | bytes 2359300 | tf_op jit(solution)/shard_map/jit(dynamic_index_in_dim)/squeeze | solution.py:65
  48.2 22.9 %collective-permute-done.1 = f32[2,192,768]{2,1,0:T(8,128)} collective-permute-done((f32[2,192,768]{2,1,0:T(8,128)S(1)}, f32[2,192,768]{2,1,0:T(8,128)}, u32[]{:S(2)}, u32[]{:S(2)}) %collective-permute-start.1) | collective-permute-done | bytes 1179680 | tf_op jit(solution)/shard_map/ppermute | solution.py:11
  79.5 8.7 %collective-permute-done.2 = f32[192,768]{1,0:T(8,128)} collective-permute-done((f32[192,768]{1,0:T(8,128)S(1)}, f32[192,768]{1,0:T(8,128)}, u32[]{:S(2)}, u32[]{:S(2)}) %collective-permute-start.2) | collective-permute-done | bytes 589856 | tf_op jit(solution)/shard_map/ppermute | solution.py:11
  89.3 4.0 %collective-permute-done.4 = f32[192,768]{1,0:T(8,128)} collective-permute-done((f32[192,768]{1,0:T(8,128)}, f32[192,768]{1,0:T(8,128)}, u32[]{:S(2)}, u32[]{:S(2)}) %collective-permute-start.4) | collective-permute-done | bytes 589856 | tf_op jit(solution)/shard_map/ppermute | solution.py:11
  95.6 2.2 reshape.33
  100.8 12.1 %collective-permute-done.5 = f32[192,2,384]{2,1,0:T(2,128)S(1)} collective-permute-done((f32[192,2,384]{2,1,0:T(2,128)S(1)}, f32[192,2,384]{2,1,0:T(2,128)S(1)}, u32[]{:S(2)}, u32[]{:S(2)}) %collective-permute-start.5) | collective-permute-done | bytes 589856 | tf_op jit(solution)/shard_map/ppermute | solution.py:11
  113.9 2.7 %collective-permute-start.6 = (f32[192,384]{1,0:T(8,128)S(1)}, f32[192,384]{1,0:T(8,128)S(1)}, u32[]{:S(2)}, u32[]{:S(2)}) collective-permute-start(f32[192,384]{1,0:T(8,128)S(1)} %bitcast.65), channel_id=1, source_target_pairs={{0,4},{1,5},{2,6},{3,7},{4,0},{5,1},{6,2},{7,3},{8,12},{9,13},{10,... | collective-permute-start | bytes 884744 | tf_op jit(solution)/shard_map/ppermute | solution.py:11
  116.5 11.1 %collective-permute-done.6 = f32[192,384]{1,0:T(8,128)S(1)} collective-permute-done((f32[192,384]{1,0:T(8,128)S(1)}, f32[192,384]{1,0:T(8,128)S(1)}, u32[]{:S(2)}, u32[]{:S(2)}) %collective-permute-start.6) | collective-permute-done | bytes 294944 | tf_op jit(solution)/shard_map/ppermute | solution.py:11
  133.2 2.7 %collective-permute-done.8 = f32[384,64]{0,1:T(8,128)S(1)} collective-permute-done((f32[384,64]{0,1:T(8,128)S(1)}, f32[384,64]{0,1:T(8,128)S(1)}, u32[]{:S(2)}, u32[]{:S(2)}) %collective-permute-start.8) | collective-permute-done | bytes 98336 | tf_op jit(solution)/shard_map/ppermute | solution.py:11
  137.6 2.8 %collective-permute-start.20 = (f32[384,64]{0,1:T(8,128)S(1)}, f32[384,64]{0,1:T(8,128)S(1)}, u32[]{:S(2)}, u32[]{:S(2)}) collective-permute-start(f32[384,64]{0,1:T(8,128)S(1)} %add.186), channel_id=1, source_target_pairs={{0,4},{1,5},{2,6},{3,7},{4,0},{5,1},{6,2},{7,3},{8,12},{9,13},{10,... | collective-permute-start | bytes 294920 | tf_op jit(solution)/shard_map/ppermute | solution.py:11
  140.4 5.3 %collective-permute-done.9 = f32[384,64]{0,1:T(8,128)S(1)} collective-permute-done((f32[384,64]{0,1:T(8,128)S(1)}, f32[384,64]{0,1:T(8,128)S(1)}, u32[]{:S(2)}, u32[]{:S(2)}) %collective-permute-start.9) | collective-permute-done | bytes 98336 | tf_op jit(solution)/shard_map/ppermute | solution.py:11
  148.8 2.2 collective-permute-done.10
  161.2 3.5 %collective-permute-start.13 = (f32[384,64]{0,1:T(8,128)S(1)}, f32[384,64]{0,1:T(8,128)S(1)}, u32[]{:S(2)}, u32[]{:S(2)}) collective-permute-start(f32[384,64]{0,1:T(8,128)S(1)} %add.182), channel_id=1, source_target_pairs={{0,4},{1,5},{2,6},{3,7},{4,0},{5,1},{6,2},{7,3},{8,12},{9,13},{10,... | collective-permute-start | bytes 294920 | tf_op jit(solution)/shard_map/ppermute | solution.py:11
  164.7 2.7 %collective-permute-start.24 = (f32[384,64]{0,1:T(8,128)S(1)}, f32[384,64]{0,1:T(8,128)S(1)}, u32[]{:S(2)}, u32[]{:S(2)}) collective-permute-start(f32[384,64]{0,1:T(8,128)S(1)} %add.190), channel_id=1, source_target_pairs={{0,4},{1,5},{2,6},{3,7},{4,0},{5,1},{6,2},{7,3},{8,12},{9,13},{10,... | collective-permute-start | bytes 294920 | tf_op jit(solution)/shard_map/ppermute | solution.py:11
  181.7 2.7 %collective-permute-start.16 = (f32[1,1,1,384,64]{3,4,2,1,0:T(8,128)S(1)}, f32[1,1,1,384,64]{3,4,2,1,0:T(8,128)S(1)}, u32[]{:S(2)}, u32[]{:S(2)}) collective-permute-start(f32[1,1,1,384,64]{3,4,2,1,0:T(8,128)S(1)} %add_bitcast_fusion.1), channel_id=1, source_target_pairs={{0,4},{1,5},{2,6},{3,7},{4,0},{5,1},{6,2},{7,3},{8,12},{9,13},{10,... | collective-permute-start | bytes 294920 | tf_op jit(solution)/shard_map/ppermute | solution.py:11
  184.9 2.7 %collective-permute-start.27 = (f32[1,1,1,384,64]{3,4,2,1,0:T(8,128)S(1)}, f32[1,1,1,384,64]{3,4,2,1,0:T(8,128)S(1)}, u32[]{:S(2)}, u32[]{:S(2)}) collective-permute-start(f32[1,1,1,384,64]{3,4,2,1,0:T(8,128)S(1)} %add_bitcast_fusion), channel_id=1, source_target_pairs={{0,4},{1,5},{2,6},{3,7},{4,0},{5,1},{6,2},{7,3},{8,12},{9,13},{10,... | collective-permute-start | bytes 294920 | tf_op jit(solution)/shard_map/ppermute | solution.py:11
  187.6 2.6 %collective-permute-start.17 = (f32[2,1,1,384,64]{3,4,2,1,0:T(8,128)S(1)}, f32[2,1,1,384,64]{3,4,2,1,0:T(8,128)S(1)}, u32[]{:S(2)}, u32[]{:S(2)}) collective-permute-start(f32[2,1,1,384,64]{3,4,2,1,0:T(8,128)S(1)} %pad_maximum_fusion.4), channel_id=1, source_target_pairs={{0,2},{1,3},{2,0},{3,1},{4,6},{5,7},{6,4},{7,5},{8,10},{9,11},{10,... | collective-permute-start | bytes 589832 | tf_op jit(solution)/shard_map/ppermute | solution.py:11
  201.4 2.1 copy.7
  203.5 10.6 %fusion.10 = f32[1536,256]{0,1:T(8,128)S(1)} fusion(f32[1536,1536]{1,0:T(8,128)} %param.3, f32[192,8,2,128]{3,2,1,0:T(2,128)} %bitcast.62), kind=kOutput, calls=%fused_computation.8 | convolution fusion | flops 3624271872 | bytes 12582912 | tf_op jit(solution)/shard_map/dot_general | solution.py:120
  217.2 10.7 %fusion.11 = f32[1536,256]{0,1:T(8,128)S(1)} fusion(f32[1536,1536]{1,0:T(8,128)} %param.4, f32[1536,128]{1,0:T(8,128)S(1)} %get-tuple-element.9, f32[1536,128]{1,0:T(8,128)S(1)} %get-tuple-element.8), kind=kOutput, calls=%fused_computation.9 | convolution fusion | flops 3624665088 | bytes 12582912 | tf_op jit(solution)/shard_map/dot_general | solution.py:121
  (131 shorter events, 71.9 us)
Async XLA Ops:
  17.0 16.7 %collective-permute-start = (f32[768,1536]{1,0:T(8,128)}, f32[768,1536]{1,0:T(8,128)}, u32[]{:S(2)}, u32[]{:S(2)}) collective-permute-start(f32[768,1536]{1,0:T(8,128)} %fusion.7), channel_id=1, source_target_pairs={{0,1},{1,0},{2,3},{3,2},{4,5},{5,4},{6,7},{7,6},{8,9},{9,8},{10,11... | collective-permute-start | bytes 14155784 | tf_op jit(solution)/shard_map/ppermute | solution.py:11
  41.7 29.3 %collective-permute-start.1 = (f32[2,192,768]{2,1,0:T(8,128)S(1)}, f32[2,192,768]{2,1,0:T(8,128)}, u32[]{:S(2)}, u32[]{:S(2)}) collective-permute-start(f32[2,192,768]{2,1,0:T(8,128)S(1)} %dynamic-slice_bitcast_fusion.1), channel_id=1, source_target_pairs={{0,8},{8,0},{16,24},{24,16},{1,9},{9,1},{17,25},{25,17},{2,10},{10... | collective-permute-start | bytes 3538952 | tf_op jit(solution)/shard_map/ppermute | solution.py:11
  46.6 28.4 %collective-permute-start.3 = (f32[2,192,768]{2,1,0:T(8,128)}, f32[2,192,768]{2,1,0:T(8,128)}, u32[]{:S(2)}, u32[]{:S(2)}) collective-permute-start(f32[2,192,768]{2,1,0:T(8,128)} %dynamic-slice_bitcast_fusion), channel_id=1, source_target_pairs={{0,16},{8,24},{16,0},{24,8},{1,17},{9,25},{17,1},{25,9},{2,18},{10... | collective-permute-start | bytes 3538952 | tf_op jit(solution)/shard_map/ppermute | solution.py:11
  72.8 15.3 %collective-permute-start.2 = (f32[192,768]{1,0:T(8,128)S(1)}, f32[192,768]{1,0:T(8,128)}, u32[]{:S(2)}, u32[]{:S(2)}) collective-permute-start(f32[192,768]{1,0:T(8,128)S(1)} %dynamic-slice_bitcast_fusion.3), channel_id=1, source_target_pairs={{0,16},{8,24},{16,0},{24,8},{1,17},{9,25},{17,1},{25,9},{2,18},{10... | collective-permute-start | bytes 1769480 | tf_op jit(solution)/shard_map/ppermute | solution.py:11
  78.3 14.9 %collective-permute-start.4 = (f32[192,768]{1,0:T(8,128)}, f32[192,768]{1,0:T(8,128)}, u32[]{:S(2)}, u32[]{:S(2)}) collective-permute-start(f32[192,768]{1,0:T(8,128)} %dynamic-slice_bitcast_fusion.2), channel_id=1, source_target_pairs={{0,8},{8,0},{16,24},{24,16},{1,9},{9,1},{17,25},{25,17},{2,10},{10... | collective-permute-start | bytes 1769480 | tf_op jit(solution)/shard_map/ppermute | solution.py:11
  99.2 13.8 %collective-permute-start.5 = (f32[192,2,384]{2,1,0:T(2,128)S(1)}, f32[192,2,384]{2,1,0:T(2,128)S(1)}, u32[]{:S(2)}, u32[]{:S(2)}) collective-permute-start(f32[192,2,384]{2,1,0:T(2,128)S(1)} %bitcast.64), channel_id=1, source_target_pairs={{0,2},{1,3},{2,0},{3,1},{4,6},{5,7},{6,4},{7,5},{8,10},{9,11},{10,... | collective-permute-start | bytes 1769480 | tf_op jit(solution)/shard_map/ppermute | solution.py:11
  113.9 13.8 %collective-permute-start.6 = (f32[192,384]{1,0:T(8,128)S(1)}, f32[192,384]{1,0:T(8,128)S(1)}, u32[]{:S(2)}, u32[]{:S(2)}) collective-permute-start(f32[192,384]{1,0:T(8,128)S(1)} %bitcast.65), channel_id=1, source_target_pairs={{0,4},{1,5},{2,6},{3,7},{4,0},{5,1},{6,2},{7,3},{8,12},{9,13},{10,... | collective-permute-start | bytes 884744 | tf_op jit(solution)/shard_map/ppermute | solution.py:11
  130.2 5.7 %collective-permute-start.8 = (f32[384,64]{0,1:T(8,128)S(1)}, f32[384,64]{0,1:T(8,128)S(1)}, u32[]{:S(2)}, u32[]{:S(2)}) collective-permute-start(f32[384,64]{0,1:T(8,128)S(1)} %fusion.19), channel_id=1, source_target_pairs={{0,2},{1,3},{2,0},{3,1},{4,6},{5,7},{6,4},{7,5},{8,10},{9,11},{10,... | collective-permute-start | bytes 294920 | tf_op jit(solution)/shard_map/ppermute | solution.py:11
  131.8 5.8 %collective-permute-start.19 = (f32[384,64]{0,1:T(8,128)S(1)}, f32[384,64]{0,1:T(8,128)S(1)}, u32[]{:S(2)}, u32[]{:S(2)}) collective-permute-start(f32[384,64]{0,1:T(8,128)S(1)} %fusion.17), channel_id=1, source_target_pairs={{0,2},{1,3},{2,0},{3,1},{4,6},{5,7},{6,4},{7,5},{8,10},{9,11},{10,... | collective-permute-start | bytes 294920 | tf_op jit(solution)/shard_map/ppermute | solution.py:11
  135.9 9.8 %collective-permute-start.9 = (f32[384,64]{0,1:T(8,128)S(1)}, f32[384,64]{0,1:T(8,128)S(1)}, u32[]{:S(2)}, u32[]{:S(2)}) collective-permute-start(f32[384,64]{0,1:T(8,128)S(1)} %add.178), channel_id=1, source_target_pairs={{0,4},{1,5},{2,6},{3,7},{4,0},{5,1},{6,2},{7,3},{8,12},{9,13},{10,... | collective-permute-start | bytes 294920 | tf_op jit(solution)/shard_map/ppermute | solution.py:11
  137.6 9.9 %collective-permute-start.20 = (f32[384,64]{0,1:T(8,128)S(1)}, f32[384,64]{0,1:T(8,128)S(1)}, u32[]{:S(2)}, u32[]{:S(2)}) collective-permute-start(f32[384,64]{0,1:T(8,128)S(1)} %add.186), channel_id=1, source_target_pairs={{0,4},{1,5},{2,6},{3,7},{4,0},{5,1},{6,2},{7,3},{8,12},{9,13},{10,... | collective-permute-start | bytes 294920 | tf_op jit(solution)/shard_map/ppermute | solution.py:11
  158.4 6.3 %collective-permute-start.23 = (f32[384,64]{0,1:T(8,128)S(1)}, f32[384,64]{0,1:T(8,128)S(1)}, u32[]{:S(2)}, u32[]{:S(2)}) collective-permute-start(f32[384,64]{0,1:T(8,128)S(1)} %fusion.21), channel_id=1, source_target_pairs={{0,2},{1,3},{2,0},{3,1},{4,6},{5,7},{6,4},{7,5},{8,10},{9,11},{10,... | collective-permute-start | bytes 294920 | tf_op jit(solution)/shard_map/ppermute | solution.py:11
  161.2 6.3 %collective-permute-start.13 = (f32[384,64]{0,1:T(8,128)S(1)}, f32[384,64]{0,1:T(8,128)S(1)}, u32[]{:S(2)}, u32[]{:S(2)}) collective-permute-start(f32[384,64]{0,1:T(8,128)S(1)} %add.182), channel_id=1, source_target_pairs={{0,4},{1,5},{2,6},{3,7},{4,0},{5,1},{6,2},{7,3},{8,12},{9,13},{10,... | collective-permute-start | bytes 294920 | tf_op jit(solution)/shard_map/ppermute | solution.py:11
  167.5 7.4 %collective-permute-start.30 = (f32[1,384,64]{1,2,0:T(8,128)S(1)}, f32[1,384,64]{1,2,0:T(8,128)S(1)}, u32[]{:S(2)}, u32[]{:S(2)}) collective-permute-start(f32[1,384,64]{1,2,0:T(8,128)S(1)} %add_bitcast_fusion.3), channel_id=1, source_target_pairs={{0,8},{8,0},{16,24},{24,16},{1,9},{9,1},{17,25},{25,17},{2,10},{10... | collective-permute-start | bytes 294920 | tf_op jit(solution)/shard_map/ppermute | solution.py:11
  170.3 7.4 %collective-permute-start.32 = (f32[1,384,64]{1,2,0:T(8,128)S(1)}, f32[1,384,64]{1,2,0:T(8,128)S(1)}, u32[]{:S(2)}, u32[]{:S(2)}) collective-permute-start(f32[1,384,64]{1,2,0:T(8,128)S(1)} %add_bitcast_fusion.2), channel_id=1, source_target_pairs={{0,8},{8,0},{16,24},{24,16},{1,9},{9,1},{17,25},{25,17},{2,10},{10... | collective-permute-start | bytes 294920 | tf_op jit(solution)/shard_map/ppermute | solution.py:11
  173.5 5.6 %collective-permute-start.25 = (f32[384,64]{0,1:T(8,128)S(1)}, f32[384,64]{0,1:T(8,128)S(1)}, u32[]{:S(2)}, u32[]{:S(2)}) collective-permute-start(f32[384,64]{0,1:T(8,128)S(1)} %fusion.29), channel_id=1, source_target_pairs={{0,8},{8,0},{16,24},{24,16},{1,9},{9,1},{17,25},{25,17},{2,10},{10... | collective-permute-start | bytes 294920 | tf_op jit(solution)/shard_map/ppermute | solution.py:11
  174.9 17.7 %collective-permute-start.31 = (f32[2,384,64]{1,2,0:T(8,128)S(1)}, f32[2,384,64]{1,2,0:T(8,128)S(1)}, u32[]{:S(2)}, u32[]{:S(2)}) collective-permute-start(f32[2,384,64]{1,2,0:T(8,128)S(1)} %pad_maximum_fusion.6), channel_id=1, source_target_pairs={{0,16},{8,24},{16,0},{24,8},{1,17},{9,25},{17,1},{25,9},{2,18},{10... | collective-permute-start | bytes 589832 | tf_op jit(solution)/shard_map/ppermute | solution.py:11
  177.8 19.4 %collective-permute-start.33 = (f32[2,384,64]{1,2,0:T(8,128)S(1)}, f32[2,384,64]{1,2,0:T(8,128)S(1)}, u32[]{:S(2)}, u32[]{:S(2)}) collective-permute-start(f32[2,384,64]{1,2,0:T(8,128)S(1)} %pad_maximum_fusion.7), channel_id=1, source_target_pairs={{0,16},{8,24},{16,0},{24,8},{1,17},{9,25},{17,1},{25,9},{2,18},{10... | collective-permute-start | bytes 589832 | tf_op jit(solution)/shard_map/ppermute | solution.py:11
  179.1 5.7 %collective-permute-start.26 = (f32[384,64]{0,1:T(8,128)S(1)}, f32[384,64]{0,1:T(8,128)S(1)}, u32[]{:S(2)}, u32[]{:S(2)}) collective-permute-start(f32[384,64]{0,1:T(8,128)S(1)} %add.192), channel_id=1, source_target_pairs={{0,16},{8,24},{16,0},{24,8},{1,17},{9,25},{17,1},{25,9},{2,18},{10... | collective-permute-start | bytes 294920 | tf_op jit(solution)/shard_map/ppermute | solution.py:11
  181.7 5.8 %collective-permute-start.16 = (f32[1,1,1,384,64]{3,4,2,1,0:T(8,128)S(1)}, f32[1,1,1,384,64]{3,4,2,1,0:T(8,128)S(1)}, u32[]{:S(2)}, u32[]{:S(2)}) collective-permute-start(f32[1,1,1,384,64]{3,4,2,1,0:T(8,128)S(1)} %add_bitcast_fusion.1), channel_id=1, source_target_pairs={{0,4},{1,5},{2,6},{3,7},{4,0},{5,1},{6,2},{7,3},{8,12},{9,13},{10,... | collective-permute-start | bytes 294920 | tf_op jit(solution)/shard_map/ppermute | solution.py:11
  184.9 5.7 %collective-permute-start.27 = (f32[1,1,1,384,64]{3,4,2,1,0:T(8,128)S(1)}, f32[1,1,1,384,64]{3,4,2,1,0:T(8,128)S(1)}, u32[]{:S(2)}, u32[]{:S(2)}) collective-permute-start(f32[1,1,1,384,64]{3,4,2,1,0:T(8,128)S(1)} %add_bitcast_fusion), channel_id=1, source_target_pairs={{0,4},{1,5},{2,6},{3,7},{4,0},{5,1},{6,2},{7,3},{8,12},{9,13},{10,... | collective-permute-start | bytes 294920 | tf_op jit(solution)/shard_map/ppermute | solution.py:11
  187.6 6.3 %collective-permute-start.17 = (f32[2,1,1,384,64]{3,4,2,1,0:T(8,128)S(1)}, f32[2,1,1,384,64]{3,4,2,1,0:T(8,128)S(1)}, u32[]{:S(2)}, u32[]{:S(2)}) collective-permute-start(f32[2,1,1,384,64]{3,4,2,1,0:T(8,128)S(1)} %pad_maximum_fusion.4), channel_id=1, source_target_pairs={{0,2},{1,3},{2,0},{3,1},{4,6},{5,7},{6,4},{7,5},{8,10},{9,11},{10,... | collective-permute-start | bytes 589832 | tf_op jit(solution)/shard_map/ppermute | solution.py:11
  190.6 5.7 %collective-permute-start.28 = (f32[2,1,1,384,64]{3,4,2,1,0:T(8,128)S(1)}, f32[2,1,1,384,64]{3,4,2,1,0:T(8,128)S(1)}, u32[]{:S(2)}, u32[]{:S(2)}) collective-permute-start(f32[2,1,1,384,64]{3,4,2,1,0:T(8,128)S(1)} %pad_maximum_fusion.5), channel_id=1, source_target_pairs={{0,2},{1,3},{2,0},{3,1},{4,6},{5,7},{6,4},{7,5},{8,10},{9,11},{10,... | collective-permute-start | bytes 589832 | tf_op jit(solution)/shard_map/ppermute | solution.py:11
  198.6 17.2 %collective-permute-start.34 = (f32[1536,128]{1,0:T(8,128)}, f32[1536,128]{1,0:T(8,128)}, u32[]{:S(2)}, u32[]{:S(2)}) collective-permute-start(f32[1536,128]{1,0:T(8,128)} %bitcast.19), channel_id=1, source_target_pairs={{0,1},{1,0},{2,3},{3,2},{4,5},{5,4},{6,7},{7,6},{8,9},{9,8},{10,11... | collective-permute-start | bytes 2359304 | tf_op jit(solution)/shard_map/ppermute | solution.py:11
  (20 other events, 226.8 us)

commit v12 on v11

--- a/solution.py
+++ b/solution.py
@@ -42,19 +42,20 @@
     core = col_index % 2
     chip = col_index // 2
     first = core == 0
-    def partial_rows(start):
-        columns = lax.dynamic_slice_in_dim(adjoint, start, half_rows, 1)
-        return jnp.dot(columns.T, direct, precision=fast, preferred_element_type=jnp.float32) * scale
-
-    received = exchange(partial_rows((1 - core) * half_rows), "cols", 1)
-    kept_rows = lax.optimization_barrier(partial_rows(core * half_rows))
-    chip_sum = kept_rows + received
     row_bits = row_count.bit_length() - 1
     row_index = lax.axis_index("rows")
     chunk_cols = snap_count // row_bits
+
+    def partial_rows(start, rot):
+        columns = lax.dynamic_slice_in_dim(adjoint, start, half_rows, 1)
+        snaps = direct[:, rot * chunk_cols:(rot + 1) * chunk_cols]
+        return jnp.dot(columns.T, snaps, precision=fast, preferred_element_type=jnp.float32) * scale
+
     chunks = []
     for rot in range(row_bits):
-        part = chip_sum[:, rot * chunk_cols:(rot + 1) * chunk_cols]
+        received = exchange(partial_rows((1 - core) * half_rows, rot), "cols", 1)
+        kept_rows = lax.optimization_barrier(partial_rows(core * half_rows, rot))
+        part = kept_rows + received
         part = part.reshape((2,) * row_bits + (part_rows, chunk_cols))
         left = list(range(row_bits - 1, -1, -1))
         for k in range(row_bits):

time: 230 us -> 235 us (1.022)
  matrix products: 59 us -> 67.9 us
  starting transfers between devices: 50.7 us -> 44.7 us
  waiting for transfers between devices: 82.9 us -> 86.3 us
    dot_general x2 -> x4, matrix products: 32.6 us -> 41.5 us  [partial_rows(): jnp.dot(columns.T, snaps, precision=fast, preferred_element_type=jnp.floa...]
    ppermute x35 -> x36, starting transfers between devices: 50.7 us -> 44.7 us  [exchange(): return lax.ppermute(x, axis, [(i, i ^ step) for i in range(count)])]
    ppermute x35 -> x36, waiting for transfers between devices: 82.9 us -> 86.3 us  [exchange(): return lax.ppermute(x, axis, [(i, i ^ step) for i in range(count)])]
    unnamed x22 -> x24, local copies, waits for them, and re-layouts: 6.08 us -> 7.39 us
    add x1 -> x2, other arithmetic: 4.76 us -> 5.37 us  [shards(): part = kept_rows + received]
  transfers between devices with their start and end apart: 35 -> 36, of which waited for: 20 -> 22; matrix products, arithmetic and copies ran while one was open for 21% -> 28% of each run, Pallas kernels for 0% -> 0%
where the time goes in v12:
time: 235 us
  waiting for transfers between devices  86.3 us (37%)
  matrix products  67.9 us (29%)
  starting transfers between devices  44.7 us (19%)
  other arithmetic  18.4 us (8%)
  local copies, waits for them, and re-layouts  16.3 us (7%)
    ppermute x36, waiting for transfers between devices, exchange(): return lax.ppermute(x, axis, [(i, i ^ step) for i in range(count)])  86.3 us
    ppermute x36, starting transfers between devices, exchange(): return lax.ppermute(x, axis, [(i, i ^ step) for i in range(count)])  44.7 us
    dot_general x4, matrix products, partial_rows(): jnp.dot(columns.T, snaps, precision=fast, preferred_element_type=jnp.floa...  41.5 us
    dot_general x1, matrix products, shards(): jnp.dot(adjoint, full_a, precision=fast, preferred_element_type=jnp.float32)  10.7 us
    dot_general x1, matrix products, shards(): jnp.dot(direct, full_d, precision=fast, preferred_element_type=jnp.float32)  10.6 us
    unnamed x24, local copies, waits for them, and re-layouts  7.39 us
    add x4, other arithmetic, shards(): part = kept + exchange(sent, 'rows', 1 << bit)  5.63 us
    add x2, other arithmetic, shards(): part = kept_rows + received  5.37 us
  transfers between devices with their start and end apart: 36, of which 22 were waited for; matrix products, arithmetic and copies ran while one was open for 28% of the time, Pallas kernels for 0%

profile of v12, /device:TPU:0, one launch (start us, length us, event | category | flops | bytes accessed | tf_op | source)
XLA Modules:
  0.0 234.8 jit_solution(9435024240245848811)
XLA Ops:
  0.7 10.8 %fusion.19 = f32[768,768]{1,0:T(8,128)} fusion(f32[1536,1536]{1,0:T(8,128)} %param.3, f32[1536,1536]{1,0:T(8,128)} %param.4, s32[]{:T(128)S(6)} %select_n.233), kind=kOutput, calls=%fused_computation.17 | convolution fusion | flops 5436407808 | bytes 11796484 | tf_op jit(solution)/shard_map/dot_general | solution.py:52
  11.9 9.3 %fusion.29 = f32[768,768]{1,0:T(8,128)} fusion(f32[1536,1536]{1,0:T(8,128)S(1)} %copy-done.4, f32[1536,1536]{1,0:T(8,128)} %param.4, s32[]{:T(128)S(6)} %select_n.233), kind=kOutput, calls=%fused_computation.19 | convolution fusion | flops 5436407808 | bytes 11796484 | tf_op jit(solution)/shard_map/dot_general | solution.py:52
  21.3 10.7 %fusion.14 = f32[768,768]{1,0:T(8,128)} fusion(f32[1536,1536]{1,0:T(8,128)} %param.3, f32[1536,1536]{1,0:T(8,128)} %param.4, s32[]{:T(128)S(6)} %select_n.232), kind=kOutput, calls=%fused_computation.16 | convolution fusion | flops 5436407808 | bytes 11796484 | tf_op jit(solution)/shard_map/dot_general | solution.py:52
  32.0 2.7 %add.162 = f32[768,768]{1,0:T(8,128)S(1)} add(f32[768,768]{1,0:T(8,128)} %fusion.14, f32[768,768]{1,0:T(8,128)} %collective-permute-done) | non-fusion elementwise | flops 589824 | bytes 7077888 | tf_op jit(solution)/shard_map/add | solution.py:58
  36.2 3.0 %collective-permute-start.1 = (f32[2,192,768]{2,1,0:T(8,128)S(1)}, f32[2,192,768]{2,1,0:T(8,128)}, u32[]{:S(2)}, u32[]{:S(2)}) collective-permute-start(f32[2,192,768]{2,1,0:T(8,128)S(1)} %dynamic-slice_bitcast_fusion.1), channel_id=1, source_target_pairs={{0,8},{8,0},{16,24},{24,16},{1,9},{9,1},{17,25},{25,17},{2,10},{10... | collective-permute-start | bytes 3538952 | tf_op jit(solution)/shard_map/ppermute | solution.py:11
  39.2 10.6 %fusion.24 = f32[768,768]{1,0:T(8,128)} fusion(f32[1536,1536]{1,0:T(8,128)} %param.3, f32[1536,1536]{1,0:T(8,128)} %param.4, s32[]{:T(128)S(6)} %select_n.232), kind=kOutput, calls=%fused_computation.18 | convolution fusion | flops 5436407808 | bytes 11796484 | tf_op jit(solution)/shard_map/dot_general | solution.py:52
  49.8 2.7 %add.171 = f32[768,768]{1,0:T(8,128)S(1)} add(f32[768,768]{1,0:T(8,128)} %fusion.24, f32[768,768]{1,0:T(8,128)} %collective-permute-done.3) | non-fusion elementwise | flops 589824 | bytes 7077888 | tf_op jit(solution)/shard_map/add | solution.py:58
  56.5 8.9 %collective-permute-done.1 = f32[2,192,768]{2,1,0:T(8,128)} collective-permute-done((f32[2,192,768]{2,1,0:T(8,128)S(1)}, f32[2,192,768]{2,1,0:T(8,128)}, u32[]{:S(2)}, u32[]{:S(2)}) %collective-permute-start.1) | collective-permute-done | bytes 1179680 | tf_op jit(solution)/shard_map/ppermute | solution.py:11
  69.1 15.1 %collective-permute-done.4 = f32[2,192,768]{2,1,0:T(8,128)} collective-permute-done((f32[2,192,768]{2,1,0:T(8,128)}, f32[2,192,768]{2,1,0:T(8,128)}, u32[]{:S(2)}, u32[]{:S(2)}) %collective-permute-start.4) | collective-permute-done | bytes 1179680 | tf_op jit(solution)/shard_map/ppermute | solution.py:11
  87.7 7.9 %collective-permute-done.2 = f32[192,768]{1,0:T(8,128)} collective-permute-done((f32[192,768]{1,0:T(8,128)S(1)}, f32[192,768]{1,0:T(8,128)}, u32[]{:S(2)}, u32[]{:S(2)}) %collective-permute-start.2) | collective-permute-done | bytes 589856 | tf_op jit(solution)/shard_map/ppermute | solution.py:11
  96.7 3.9 %collective-permute-done.5 = f32[192,768]{1,0:T(8,128)} collective-permute-done((f32[192,768]{1,0:T(8,128)}, f32[192,768]{1,0:T(8,128)}, u32[]{:S(2)}, u32[]{:S(2)}) %collective-permute-start.5) | collective-permute-done | bytes 589856 | tf_op jit(solution)/shard_map/ppermute | solution.py:11
  108.1 10.3 %collective-permute-done.6 = f32[192,2,384]{2,1,0:T(2,128)S(1)} collective-permute-done((f32[192,2,384]{2,1,0:T(2,128)S(1)}, f32[192,2,384]{2,1,0:T(2,128)S(1)}, u32[]{:S(2)}, u32[]{:S(2)}) %collective-permute-start.6) | collective-permute-done | bytes 589856 | tf_op jit(solution)/shard_map/ppermute | solution.py:11
  119.4 3.4 %collective-permute-start.7 = (f32[192,384]{1,0:T(8,128)S(1)}, f32[192,384]{1,0:T(8,128)S(1)}, u32[]{:S(2)}, u32[]{:S(2)}) collective-permute-start(f32[192,384]{1,0:T(8,128)S(1)} %bitcast.63), channel_id=1, source_target_pairs={{0,4},{1,5},{2,6},{3,7},{4,0},{5,1},{6,2},{7,3},{8,12},{9,13},{10,... | collective-permute-start | bytes 884744 | tf_op jit(solution)/shard_map/ppermute | solution.py:11
  122.7 8.6 %collective-permute-done.7 = f32[192,384]{1,0:T(8,128)S(1)} collective-permute-done((f32[192,384]{1,0:T(8,128)S(1)}, f32[192,384]{1,0:T(8,128)S(1)}, u32[]{:S(2)}, u32[]{:S(2)}) %collective-permute-start.7) | collective-permute-done | bytes 294944 | tf_op jit(solution)/shard_map/ppermute | solution.py:11
  136.9 2.7 %collective-permute-done.9 = f32[384,64]{0,1:T(8,128)S(1)} collective-permute-done((f32[384,64]{0,1:T(8,128)S(1)}, f32[384,64]{0,1:T(8,128)S(1)}, u32[]{:S(2)}, u32[]{:S(2)}) %collective-permute-start.9) | collective-permute-done | bytes 98336 | tf_op jit(solution)/shard_map/ppermute | solution.py:11
  141.2 2.8 %collective-permute-start.21 = (f32[384,64]{0,1:T(8,128)S(1)}, f32[384,64]{0,1:T(8,128)S(1)}, u32[]{:S(2)}, u32[]{:S(2)}) collective-permute-start(f32[384,64]{0,1:T(8,128)S(1)} %add.192), channel_id=1, source_target_pairs={{0,4},{1,5},{2,6},{3,7},{4,0},{5,1},{6,2},{7,3},{8,12},{9,13},{10,... | collective-permute-start | bytes 294920 | tf_op jit(solution)/shard_map/ppermute | solution.py:11
  144.1 5.3 %collective-permute-done.10 = f32[384,64]{0,1:T(8,128)S(1)} collective-permute-done((f32[384,64]{0,1:T(8,128)S(1)}, f32[384,64]{0,1:T(8,128)S(1)}, u32[]{:S(2)}, u32[]{:S(2)}) %collective-permute-start.10) | collective-permute-done | bytes 98336 | tf_op jit(solution)/shard_map/ppermute | solution.py:11
  164.9 3.6 %collective-permute-start.14 = (f32[384,64]{0,1:T(8,128)S(1)}, f32[384,64]{0,1:T(8,128)S(1)}, u32[]{:S(2)}, u32[]{:S(2)}) collective-permute-start(f32[384,64]{0,1:T(8,128)S(1)} %add.188), channel_id=1, source_target_pairs={{0,4},{1,5},{2,6},{3,7},{4,0},{5,1},{6,2},{7,3},{8,12},{9,13},{10,... | collective-permute-start | bytes 294920 | tf_op jit(solution)/shard_map/ppermute | solution.py:11
  168.5 2.6 %collective-permute-start.25 = (f32[384,64]{0,1:T(8,128)S(1)}, f32[384,64]{0,1:T(8,128)S(1)}, u32[]{:S(2)}, u32[]{:S(2)}) collective-permute-start(f32[384,64]{0,1:T(8,128)S(1)} %add.196), channel_id=1, source_target_pairs={{0,4},{1,5},{2,6},{3,7},{4,0},{5,1},{6,2},{7,3},{8,12},{9,13},{10,... | collective-permute-start | bytes 294920 | tf_op jit(solution)/shard_map/ppermute | solution.py:11
  183.6 2.3 collective-permute-done.16
  193.0 2.8 %collective-permute-done.28 = f32[1,1,1,384,64]{3,4,2,1,0:T(8,128)S(1)} collective-permute-done((f32[1,1,1,384,64]{3,4,2,1,0:T(8,128)S(1)}, f32[1,1,1,384,64]{3,4,2,1,0:T(8,128)S(1)}, u32[]{:S(2)}, u32[]{:S(2)}) %collective-permute-start.28) | collective-permute-done | bytes 98336 | tf_op jit(solution)/shard_map/ppermute | solution.py:11
  199.2 2.3 %collective-permute-done.29 = f32[2,1,1,384,64]{3,4,2,1,0:T(8,128)S(1)} collective-permute-done((f32[2,1,1,384,64]{3,4,2,1,0:T(8,128)S(1)}, f32[2,1,1,384,64]{3,4,2,1,0:T(8,128)S(1)}, u32[]{:S(2)}, u32[]{:S(2)}) %collective-permute-start.29) | collective-permute-done | bytes 196640 | tf_op jit(solution)/shard_map/ppermute | solution.py:11
  208.7 10.6 %fusion.12 = f32[1536,256]{0,1:T(8,128)S(1)} fusion(f32[1536,1536]{1,0:T(8,128)} %param.3, f32[192,8,2,128]{3,2,1,0:T(2,128)} %bitcast.60), kind=kOutput, calls=%fused_computation.14 | convolution fusion | flops 3624271872 | bytes 12582912 | tf_op jit(solution)/shard_map/dot_general | solution.py:121
  222.5 10.7 %fusion.13 = f32[1536,256]{0,1:T(8,128)S(1)} fusion(f32[1536,1536]{1,0:T(8,128)} %param.4, f32[1536,128]{1,0:T(8,128)S(1)} %get-tuple-element.7, f32[1536,128]{1,0:T(8,128)S(1)} %get-tuple-element.6), kind=kOutput, calls=%fused_computation.15 | convolution fusion | flops 3624665088 | bytes 12582912 | tf_op jit(solution)/shard_map/dot_general | solution.py:122
  (137 shorter events, 79.9 us)
Async XLA Ops:
  11.5 20.5 %collective-permute-start = (f32[768,768]{1,0:T(8,128)}, f32[768,768]{1,0:T(8,128)}, u32[]{:S(2)}, u32[]{:S(2)}) collective-permute-start(f32[768,768]{1,0:T(8,128)} %fusion.19), channel_id=1, source_target_pairs={{0,1},{1,0},{2,3},{3,2},{4,5},{5,4},{6,7},{7,6},{8,9},{9,8},{10,11... | collective-permute-start | bytes 7077896 | tf_op jit(solution)/shard_map/ppermute | solution.py:11
  21.3 28.5 %collective-permute-start.3 = (f32[768,768]{1,0:T(8,128)}, f32[768,768]{1,0:T(8,128)}, u32[]{:S(2)}, u32[]{:S(2)}) collective-permute-start(f32[768,768]{1,0:T(8,128)} %fusion.29), channel_id=1, source_target_pairs={{0,1},{1,0},{2,3},{3,2},{4,5},{5,4},{6,7},{7,6},{8,9},{9,8},{10,11... | collective-permute-start | bytes 7077896 | tf_op jit(solution)/shard_map/ppermute | solution.py:11
  36.2 29.3 %collective-permute-start.1 = (f32[2,192,768]{2,1,0:T(8,128)S(1)}, f32[2,192,768]{2,1,0:T(8,128)}, u32[]{:S(2)}, u32[]{:S(2)}) collective-permute-start(f32[2,192,768]{2,1,0:T(8,128)S(1)} %dynamic-slice_bitcast_fusion.1), channel_id=1, source_target_pairs={{0,8},{8,0},{16,24},{24,16},{1,9},{9,1},{17,25},{25,17},{2,10},{10... | collective-permute-start | bytes 3538952 | tf_op jit(solution)/shard_map/ppermute | solution.py:11
  55.0 29.2 %collective-permute-start.4 = (f32[2,192,768]{2,1,0:T(8,128)}, f32[2,192,768]{2,1,0:T(8,128)}, u32[]{:S(2)}, u32[]{:S(2)}) collective-permute-start(f32[2,192,768]{2,1,0:T(8,128)} %dynamic-slice_bitcast_fusion), channel_id=1, source_target_pairs={{0,16},{8,24},{16,0},{24,8},{1,17},{9,25},{17,1},{25,9},{2,18},{10... | collective-permute-start | bytes 3538952 | tf_op jit(solution)/shard_map/ppermute | solution.py:11
  67.3 28.3 %collective-permute-start.2 = (f32[192,768]{1,0:T(8,128)S(1)}, f32[192,768]{1,0:T(8,128)}, u32[]{:S(2)}, u32[]{:S(2)}) collective-permute-start(f32[192,768]{1,0:T(8,128)S(1)} %dynamic-slice_bitcast_fusion.3), channel_id=1, source_target_pairs={{0,16},{8,24},{16,0},{24,8},{1,17},{9,25},{17,1},{25,9},{2,18},{10... | collective-permute-start | bytes 1769480 | tf_op jit(solution)/shard_map/ppermute | solution.py:11
  87.5 13.1 %collective-permute-start.5 = (f32[192,768]{1,0:T(8,128)}, f32[192,768]{1,0:T(8,128)}, u32[]{:S(2)}, u32[]{:S(2)}) collective-permute-start(f32[192,768]{1,0:T(8,128)} %dynamic-slice_bitcast_fusion.2), channel_id=1, source_target_pairs={{0,8},{8,0},{16,24},{24,16},{1,9},{9,1},{17,25},{25,17},{2,10},{10... | collective-permute-start | bytes 1769480 | tf_op jit(solution)/shard_map/ppermute | solution.py:11
  106.5 12.0 %collective-permute-start.6 = (f32[192,2,384]{2,1,0:T(2,128)S(1)}, f32[192,2,384]{2,1,0:T(2,128)S(1)}, u32[]{:S(2)}, u32[]{:S(2)}) collective-permute-start(f32[192,2,384]{2,1,0:T(2,128)S(1)} %bitcast.62), channel_id=1, source_target_pairs={{0,2},{1,3},{2,0},{3,1},{4,6},{5,7},{6,4},{7,5},{8,10},{9,11},{10,... | collective-permute-start | bytes 1769480 | tf_op jit(solution)/shard_map/ppermute | solution.py:11
  119.4 11.9 %collective-permute-start.7 = (f32[192,384]{1,0:T(8,128)S(1)}, f32[192,384]{1,0:T(8,128)S(1)}, u32[]{:S(2)}, u32[]{:S(2)}) collective-permute-start(f32[192,384]{1,0:T(8,128)S(1)} %bitcast.63), channel_id=1, source_target_pairs={{0,4},{1,5},{2,6},{3,7},{4,0},{5,1},{6,2},{7,3},{8,12},{9,13},{10,... | collective-permute-start | bytes 884744 | tf_op jit(solution)/shard_map/ppermute | solution.py:11
  135.4 5.8 %collective-permute-start.20 = (f32[384,64]{0,1:T(8,128)S(1)}, f32[384,64]{0,1:T(8,128)S(1)}, u32[]{:S(2)}, u32[]{:S(2)}) collective-permute-start(f32[384,64]{0,1:T(8,128)S(1)} %fusion.39), channel_id=1, source_target_pairs={{0,2},{1,3},{2,0},{3,1},{4,6},{5,7},{6,4},{7,5},{8,10},{9,11},{10,... | collective-permute-start | bytes 294920 | tf_op jit(solution)/shard_map/ppermute | solution.py:11
  139.6 9.7 %collective-permute-start.10 = (f32[384,64]{0,1:T(8,128)S(1)}, f32[384,64]{0,1:T(8,128)S(1)}, u32[]{:S(2)}, u32[]{:S(2)}) collective-permute-start(f32[384,64]{0,1:T(8,128)S(1)} %add.184), channel_id=1, source_target_pairs={{0,4},{1,5},{2,6},{3,7},{4,0},{5,1},{6,2},{7,3},{8,12},{9,13},{10,... | collective-permute-start | bytes 294920 | tf_op jit(solution)/shard_map/ppermute | solution.py:11
  141.2 10.0 %collective-permute-start.21 = (f32[384,64]{0,1:T(8,128)S(1)}, f32[384,64]{0,1:T(8,128)S(1)}, u32[]{:S(2)}, u32[]{:S(2)}) collective-permute-start(f32[384,64]{0,1:T(8,128)S(1)} %add.192), channel_id=1, source_target_pairs={{0,4},{1,5},{2,6},{3,7},{4,0},{5,1},{6,2},{7,3},{8,12},{9,13},{10,... | collective-permute-start | bytes 294920 | tf_op jit(solution)/shard_map/ppermute | solution.py:11
  162.1 6.3 %collective-permute-start.24 = (f32[384,64]{0,1:T(8,128)S(1)}, f32[384,64]{0,1:T(8,128)S(1)}, u32[]{:S(2)}, u32[]{:S(2)}) collective-permute-start(f32[384,64]{0,1:T(8,128)S(1)} %fusion.43), channel_id=1, source_target_pairs={{0,2},{1,3},{2,0},{3,1},{4,6},{5,7},{6,4},{7,5},{8,10},{9,11},{10,... | collective-permute-start | bytes 294920 | tf_op jit(solution)/shard_map/ppermute | solution.py:11
  164.9 6.7 %collective-permute-start.14 = (f32[384,64]{0,1:T(8,128)S(1)}, f32[384,64]{0,1:T(8,128)S(1)}, u32[]{:S(2)}, u32[]{:S(2)}) collective-permute-start(f32[384,64]{0,1:T(8,128)S(1)} %add.188), channel_id=1, source_target_pairs={{0,4},{1,5},{2,6},{3,7},{4,0},{5,1},{6,2},{7,3},{8,12},{9,13},{10,... | collective-permute-start | bytes 294920 | tf_op jit(solution)/shard_map/ppermute | solution.py:11
  171.5 7.6 %collective-permute-start.31 = (f32[1,384,64]{1,2,0:T(8,128)S(1)}, f32[1,384,64]{1,2,0:T(8,128)S(1)}, u32[]{:S(2)}, u32[]{:S(2)}) collective-permute-start(f32[1,384,64]{1,2,0:T(8,128)S(1)} %add_bitcast_fusion.3), channel_id=1, source_target_pairs={{0,8},{8,0},{16,24},{24,16},{1,9},{9,1},{17,25},{25,17},{2,10},{10... | collective-permute-start | bytes 294920 | tf_op jit(solution)/shard_map/ppermute | solution.py:11
  174.1 7.3 %collective-permute-start.33 = (f32[1,384,64]{1,2,0:T(8,128)S(1)}, f32[1,384,64]{1,2,0:T(8,128)S(1)}, u32[]{:S(2)}, u32[]{:S(2)}) collective-permute-start(f32[1,384,64]{1,2,0:T(8,128)S(1)} %add_bitcast_fusion.2), channel_id=1, source_target_pairs={{0,8},{8,0},{16,24},{24,16},{1,9},{9,1},{17,25},{25,17},{2,10},{10... | collective-permute-start | bytes 294920 | tf_op jit(solution)/shard_map/ppermute | solution.py:11
  177.2 6.2 %collective-permute-start.26 = (f32[384,64]{0,1:T(8,128)S(1)}, f32[384,64]{0,1:T(8,128)S(1)}, u32[]{:S(2)}, u32[]{:S(2)}) collective-permute-start(f32[384,64]{0,1:T(8,128)S(1)} %fusion.51), channel_id=1, source_target_pairs={{0,8},{8,0},{16,24},{24,16},{1,9},{9,1},{17,25},{25,17},{2,10},{10... | collective-permute-start | bytes 294920 | tf_op jit(solution)/shard_map/ppermute | solution.py:11
  179.2 16.9 %collective-permute-start.32 = (f32[2,384,64]{1,2,0:T(8,128)S(1)}, f32[2,384,64]{1,2,0:T(8,128)S(1)}, u32[]{:S(2)}, u32[]{:S(2)}) collective-permute-start(f32[2,384,64]{1,2,0:T(8,128)S(1)} %pad_maximum_fusion.6), channel_id=1, source_target_pairs={{0,16},{8,24},{16,0},{24,8},{1,17},{9,25},{17,1},{25,9},{2,18},{10... | collective-permute-start | bytes 589832 | tf_op jit(solution)/shard_map/ppermute | solution.py:11
  181.4 21.0 %collective-permute-start.34 = (f32[2,384,64]{1,2,0:T(8,128)S(1)}, f32[2,384,64]{1,2,0:T(8,128)S(1)}, u32[]{:S(2)}, u32[]{:S(2)}) collective-permute-start(f32[2,384,64]{1,2,0:T(8,128)S(1)} %pad_maximum_fusion.7), channel_id=1, source_target_pairs={{0,16},{8,24},{16,0},{24,8},{1,17},{9,25},{17,1},{25,9},{2,18},{10... | collective-permute-start | bytes 589832 | tf_op jit(solution)/shard_map/ppermute | solution.py:11
  183.4 5.7 %collective-permute-start.27 = (f32[384,64]{0,1:T(8,128)S(1)}, f32[384,64]{0,1:T(8,128)S(1)}, u32[]{:S(2)}, u32[]{:S(2)}) collective-permute-start(f32[384,64]{0,1:T(8,128)S(1)} %add.198), channel_id=1, source_target_pairs={{0,16},{8,24},{16,0},{24,8},{1,17},{9,25},{17,1},{25,9},{2,18},{10... | collective-permute-start | bytes 294920 | tf_op jit(solution)/shard_map/ppermute | solution.py:11
  186.0 6.6 %collective-permute-start.17 = (f32[1,1,1,384,64]{3,4,2,1,0:T(8,128)S(1)}, f32[1,1,1,384,64]{3,4,2,1,0:T(8,128)S(1)}, u32[]{:S(2)}, u32[]{:S(2)}) collective-permute-start(f32[1,1,1,384,64]{3,4,2,1,0:T(8,128)S(1)} %add_bitcast_fusion.1), channel_id=1, source_target_pairs={{0,4},{1,5},{2,6},{3,7},{4,0},{5,1},{6,2},{7,3},{8,12},{9,13},{10,... | collective-permute-start | bytes 294920 | tf_op jit(solution)/shard_map/ppermute | solution.py:11
  189.1 6.6 %collective-permute-start.28 = (f32[1,1,1,384,64]{3,4,2,1,0:T(8,128)S(1)}, f32[1,1,1,384,64]{3,4,2,1,0:T(8,128)S(1)}, u32[]{:S(2)}, u32[]{:S(2)}) collective-permute-start(f32[1,1,1,384,64]{3,4,2,1,0:T(8,128)S(1)} %add_bitcast_fusion), channel_id=1, source_target_pairs={{0,4},{1,5},{2,6},{3,7},{4,0},{5,1},{6,2},{7,3},{8,12},{9,13},{10,... | collective-permute-start | bytes 294920 | tf_op jit(solution)/shard_map/ppermute | solution.py:11
  192.7 5.7 %collective-permute-start.18 = (f32[2,1,1,384,64]{3,4,2,1,0:T(8,128)S(1)}, f32[2,1,1,384,64]{3,4,2,1,0:T(8,128)S(1)}, u32[]{:S(2)}, u32[]{:S(2)}) collective-permute-start(f32[2,1,1,384,64]{3,4,2,1,0:T(8,128)S(1)} %pad_maximum_fusion.4), channel_id=1, source_target_pairs={{0,2},{1,3},{2,0},{3,1},{4,6},{5,7},{6,4},{7,5},{8,10},{9,11},{10,... | collective-permute-start | bytes 589832 | tf_op jit(solution)/shard_map/ppermute | solution.py:11
  195.8 5.7 %collective-permute-start.29 = (f32[2,1,1,384,64]{3,4,2,1,0:T(8,128)S(1)}, f32[2,1,1,384,64]{3,4,2,1,0:T(8,128)S(1)}, u32[]{:S(2)}, u32[]{:S(2)}) collective-permute-start(f32[2,1,1,384,64]{3,4,2,1,0:T(8,128)S(1)} %pad_maximum_fusion.5), channel_id=1, source_target_pairs={{0,2},{1,3},{2,0},{3,1},{4,6},{5,7},{6,4},{7,5},{8,10},{9,11},{10,... | collective-permute-start | bytes 589832 | tf_op jit(solution)/shard_map/ppermute | solution.py:11
  203.8 17.1 %collective-permute-start.35 = (f32[1536,128]{1,0:T(8,128)}, f32[1536,128]{1,0:T(8,128)}, u32[]{:S(2)}, u32[]{:S(2)}) collective-permute-start(f32[1536,128]{1,0:T(8,128)} %bitcast.19), channel_id=1, source_target_pairs={{0,1},{1,0},{2,3},{3,2},{4,5},{5,4},{6,7},{7,6},{8,9},{9,8},{10,11... | collective-permute-start | bytes 2359304 | tf_op jit(solution)/shard_map/ppermute | solution.py:11
  (22 other events, 236.5 us)

commit v13 on v11

--- a/solution.py
+++ b/solution.py
@@ -69,11 +69,23 @@
     strip = jnp.concatenate(chunks, axis=1)
     bits = chip_count.bit_length() - 1
     strip = strip.reshape((part_rows,) + (2,) * bits + (chip_cols,))
-    for bit in range(bits):
-        mine = (chip >> bit) % 2
-        kept = lax.dynamic_index_in_dim(strip, mine, axis=strip.ndim - 2, keepdims=False)
-        sent = lax.dynamic_index_in_dim(strip, 1 - mine, axis=strip.ndim - 2, keepdims=False)
-        strip = kept + exchange(sent, "cols", 2 << bit)
+    orders = (list(range(bits)), list(range(bits - 1, -1, -1)))
+    lefts = [list(range(bits - 1, -1, -1)) for _ in orders]
+    for k in range(bits):
+        halves = []
+        for order, left in zip(orders, lefts):
+            bit = order[k]
+            axis = 1 + left.index(bit)
+            mine = (chip >> bit) % 2
+            halves.append((
+                lax.dynamic_index_in_dim(strip, mine, axis=axis, keepdims=False),
+                lax.dynamic_index_in_dim(strip, 1 - mine, axis=axis, keepdims=False),
+            ))
+            left.remove(bit)
+        kept = jnp.where(first, halves[0][0], halves[1][0])
+        sent = jnp.where(first, halves[0][1], halves[1][1])
+        pairs = [(i, i ^ (2 << orders[i % 2][k])) for i in range(col_count)]
+        strip = kept + lax.ppermute(sent, "cols", pairs)
     tile = strip
     chip_tile = in_order(first, tile, exchange(tile, "cols", 1), 0)
     own_probes = lax.dynamic_slice_in_dim(probes, core * probe_half, probe_half, 1)

time: 230 us -> 228 us (level)
    ppermute x35 -> x33, waiting for transfers between devices: 82.9 us -> 59.2 us  [exchange(): return lax.ppermute(x, axis, [(i, i ^ step) for i in range(count)])]
    ppermute x0 -> x2, waiting for transfers between devices: none -> 21.6 us  [shards(): strip = kept + lax.ppermute(sent, 'cols', pairs)]
    ppermute x0 -> x2, starting transfers between devices: none -> 4.41 us  [shards(): strip = kept + lax.ppermute(sent, 'cols', pairs)]
    ppermute x35 -> x33, starting transfers between devices: 50.7 us -> 47 us  [exchange(): return lax.ppermute(x, axis, [(i, i ^ step) for i in range(count)])]
    unnamed x22 -> x20, local copies, waits for them, and re-layouts: 6.08 us -> 5.75 us
  transfers between devices with their start and end apart: 35 -> 35, of which waited for: 20 -> 21; matrix products, arithmetic and copies ran while one was open for 21% -> 21% of each run, Pallas kernels for 0% -> 0%
where the time goes in v13:
time: 228 us
  waiting for transfers between devices  80.9 us (35%)
  matrix products  59 us (26%)
  starting transfers between devices  51.4 us (23%)
  local copies, waits for them, and re-layouts  17.8 us (8%)
  other arithmetic  17.5 us (8%)
    ppermute x33, waiting for transfers between devices, exchange(): return lax.ppermute(x, axis, [(i, i ^ step) for i in range(count)])  59.2 us
    ppermute x33, starting transfers between devices, exchange(): return lax.ppermute(x, axis, [(i, i ^ step) for i in range(count)])  47 us
    dot_general x2, matrix products, partial_rows(): jnp.dot(columns.T, direct, precision=fast, preferred_element_type=jnp.flo...  32.6 us
    ppermute x2, waiting for transfers between devices, shards(): strip = kept + lax.ppermute(sent, 'cols', pairs)  21.6 us
    dot_general x1, matrix products, shards(): jnp.dot(adjoint, full_a, precision=fast, preferred_element_type=jnp.float32)  10.7 us
    dot_general x1, matrix products, shards(): jnp.dot(direct, full_d, precision=fast, preferred_element_type=jnp.float32)  10.6 us
    unnamed x20, local copies, waits for them, and re-layouts  5.75 us
    add x4, other arithmetic, shards(): part = kept + exchange(sent, 'rows', 1 << bit)  5.46 us
  transfers between devices with their start and end apart: 35, of which 21 were waited for; matrix products, arithmetic and copies ran while one was open for 21% of the time, Pallas kernels for 0%

profile of v13, /device:TPU:0, one launch (start us, length us, event | category | flops | bytes accessed | tf_op | source)
XLA Modules:
  0.0 227.5 jit_solution(7607645192438115431)
XLA Ops:
  0.7 16.3 %fusion.7 = f32[768,1536]{1,0:T(8,128)} fusion(f32[1536,1536]{1,0:T(8,128)} %param.3, f32[1536,1536]{1,0:T(8,128)} %param.4, s32[]{:T(128)S(6)} %select_n.270), kind=kOutput, calls=%fused_computation.5 | convolution fusion | flops 10872815616 | bytes 18874372 | tf_op jit(solution)/shard_map/dot_general | solution.py:47
  17.4 16.2 %fusion.4 = f32[768,1536]{1,0:T(8,128)} fusion(f32[1536,1536]{1,0:T(8,128)} %param.3, f32[1536,1536]{1,0:T(8,128)} %param.4, s32[]{:T(128)S(6)} %select_n.269), kind=kOutput, calls=%fused_computation.4 | convolution fusion | flops 10872815616 | bytes 18874372 | tf_op jit(solution)/shard_map/dot_general | solution.py:47
  33.7 4.8 %add.164 = f32[768,1536]{1,0:T(8,128)S(1)} add(f32[768,1536]{1,0:T(8,128)} %fusion.4, f32[768,1536]{1,0:T(8,128)} %collective-permute-done) | non-fusion elementwise | flops 1179648 | bytes 14155776 | tf_op jit(solution)/shard_map/add | solution.py:51
  41.7 2.6 %collective-permute-start.1 = (f32[2,192,768]{2,1,0:T(8,128)S(1)}, f32[2,192,768]{2,1,0:T(8,128)}, u32[]{:S(2)}, u32[]{:S(2)}) collective-permute-start(f32[2,192,768]{2,1,0:T(8,128)S(1)} %dynamic-slice_bitcast_fusion.1), channel_id=1, source_target_pairs={{0,8},{8,0},{16,24},{24,16},{1,9},{9,1},{17,25},{25,17},{2,10},{10... | collective-permute-start | bytes 3538952 | tf_op jit(solution)/shard_map/ppermute | solution.py:11
  44.3 2.4 %dynamic-slice_bitcast_fusion = f32[2,192,768]{2,1,0:T(8,128)} fusion(f32[2,2,192,768]{3,2,1,0:T(8,128)} %bitcast.61, s32[]{:T(128)S(6)} %select_n.276), kind=kLoop, calls=%fused_computation.19 | loop fusion | bytes 2359300 | tf_op jit(solution)/shard_map/jit(dynamic_index_in_dim)/squeeze | solution.py:65
  48.2 22.9 %collective-permute-done.1 = f32[2,192,768]{2,1,0:T(8,128)} collective-permute-done((f32[2,192,768]{2,1,0:T(8,128)S(1)}, f32[2,192,768]{2,1,0:T(8,128)}, u32[]{:S(2)}, u32[]{:S(2)}) %collective-permute-start.1) | collective-permute-done | bytes 1179680 | tf_op jit(solution)/shard_map/ppermute | solution.py:11
  79.5 8.7 %collective-permute-done.2 = f32[192,768]{1,0:T(8,128)} collective-permute-done((f32[192,768]{1,0:T(8,128)S(1)}, f32[192,768]{1,0:T(8,128)}, u32[]{:S(2)}, u32[]{:S(2)}) %collective-permute-start.2) | collective-permute-done | bytes 589856 | tf_op jit(solution)/shard_map/ppermute | solution.py:11
  89.3 4.0 %collective-permute-done.4 = f32[192,768]{1,0:T(8,128)} collective-permute-done((f32[192,768]{1,0:T(8,128)}, f32[192,768]{1,0:T(8,128)}, u32[]{:S(2)}, u32[]{:S(2)}) %collective-permute-start.4) | collective-permute-done | bytes 589856 | tf_op jit(solution)/shard_map/ppermute | solution.py:11
  95.6 2.2 reshape.37
  101.0 13.5 %collective-permute-done.5 = f32[192,2,384]{2,0,1:T(8,128)S(1)} collective-permute-done((f32[192,2,384]{2,0,1:T(8,128)S(1)}, f32[192,2,384]{2,0,1:T(8,128)S(1)}, u32[]{:S(2)}, u32[]{:S(2)}) %collective-permute-start.5) | collective-permute-done | bytes 589856 | tf_op jit(solution)/shard_map/ppermute | solution.py:88
  114.7 2.8 %collective-permute-start.6 = (f32[192,384]{1,0:T(8,128)S(1)}, f32[192,384]{1,0:T(8,128)S(1)}, u32[]{:S(2)}, u32[]{:S(2)}) collective-permute-start(f32[192,384]{1,0:T(8,128)S(1)} %select_bitcast_fusion), channel_id=1, source_target_pairs={{0,4},{1,3},{2,6},{3,1},{4,0},{5,7},{6,2},{7,5},{8,12},{9,11},{10,... | collective-permute-start | bytes 884744 | tf_op jit(solution)/shard_map/ppermute | solution.py:88
  117.4 8.1 %collective-permute-done.6 = f32[192,384]{1,0:T(8,128)S(1)} collective-permute-done((f32[192,384]{1,0:T(8,128)S(1)}, f32[192,384]{1,0:T(8,128)S(1)}, u32[]{:S(2)}, u32[]{:S(2)}) %collective-permute-start.6) | collective-permute-done | bytes 294944 | tf_op jit(solution)/shard_map/ppermute | solution.py:88
  131.1 2.7 %collective-permute-done.8 = f32[384,64]{0,1:T(8,128)S(1)} collective-permute-done((f32[384,64]{0,1:T(8,128)S(1)}, f32[384,64]{0,1:T(8,128)S(1)}, u32[]{:S(2)}, u32[]{:S(2)}) %collective-permute-start.8) | collective-permute-done | bytes 98336 | tf_op jit(solution)/shard_map/ppermute | solution.py:11
  135.6 2.8 %collective-permute-start.20 = (f32[384,64]{0,1:T(8,128)S(1)}, f32[384,64]{0,1:T(8,128)S(1)}, u32[]{:S(2)}, u32[]{:S(2)}) collective-permute-start(f32[384,64]{0,1:T(8,128)S(1)} %add.193), channel_id=1, source_target_pairs={{0,4},{1,5},{2,6},{3,7},{4,0},{5,1},{6,2},{7,3},{8,12},{9,13},{10,... | collective-permute-start | bytes 294920 | tf_op jit(solution)/shard_map/ppermute | solution.py:11
  138.4 5.1 %collective-permute-done.9 = f32[384,64]{0,1:T(8,128)S(1)} collective-permute-done((f32[384,64]{0,1:T(8,128)S(1)}, f32[384,64]{0,1:T(8,128)S(1)}, u32[]{:S(2)}, u32[]{:S(2)}) %collective-permute-start.9) | collective-permute-done | bytes 98336 | tf_op jit(solution)/shard_map/ppermute | solution.py:11
  146.7 2.4 %collective-permute-done.10 = f32[384,64]{0,1:T(8,128)S(1)} collective-permute-done((f32[384,64]{0,1:T(8,128)S(1)}, f32[384,64]{0,1:T(8,128)S(1)}, u32[]{:S(2)}, u32[]{:S(2)}) %collective-permute-start.10) | collective-permute-done | bytes 98336 | tf_op jit(solution)/shard_map/ppermute | solution.py:11
  159.2 3.6 %collective-permute-start.13 = (f32[384,64]{0,1:T(8,128)S(1)}, f32[384,64]{0,1:T(8,128)S(1)}, u32[]{:S(2)}, u32[]{:S(2)}) collective-permute-start(f32[384,64]{0,1:T(8,128)S(1)} %add.189), channel_id=1, source_target_pairs={{0,4},{1,5},{2,6},{3,7},{4,0},{5,1},{6,2},{7,3},{8,12},{9,13},{10,... | collective-permute-start | bytes 294920 | tf_op jit(solution)/shard_map/ppermute | solution.py:11
  162.8 2.6 %collective-permute-start.24 = (f32[384,64]{0,1:T(8,128)S(1)}, f32[384,64]{0,1:T(8,128)S(1)}, u32[]{:S(2)}, u32[]{:S(2)}) collective-permute-start(f32[384,64]{0,1:T(8,128)S(1)} %add.197), channel_id=1, source_target_pairs={{0,4},{1,5},{2,6},{3,7},{4,0},{5,1},{6,2},{7,3},{8,12},{9,13},{10,... | collective-permute-start | bytes 294920 | tf_op jit(solution)/shard_map/ppermute | solution.py:11
  179.6 2.7 %collective-permute-start.16 = (f32[1,1,1,384,64]{3,4,2,1,0:T(8,128)S(1)}, f32[1,1,1,384,64]{3,4,2,1,0:T(8,128)S(1)}, u32[]{:S(2)}, u32[]{:S(2)}) collective-permute-start(f32[1,1,1,384,64]{3,4,2,1,0:T(8,128)S(1)} %add_bitcast_fusion.1), channel_id=1, source_target_pairs={{0,4},{1,5},{2,6},{3,7},{4,0},{5,1},{6,2},{7,3},{8,12},{9,13},{10,... | collective-permute-start | bytes 294920 | tf_op jit(solution)/shard_map/ppermute | solution.py:11
  183.0 2.5 %collective-permute-start.27 = (f32[1,1,1,384,64]{3,4,2,1,0:T(8,128)S(1)}, f32[1,1,1,384,64]{3,4,2,1,0:T(8,128)S(1)}, u32[]{:S(2)}, u32[]{:S(2)}) collective-permute-start(f32[1,1,1,384,64]{3,4,2,1,0:T(8,128)S(1)} %add_bitcast_fusion), channel_id=1, source_target_pairs={{0,4},{1,5},{2,6},{3,7},{4,0},{5,1},{6,2},{7,3},{8,12},{9,13},{10,... | collective-permute-start | bytes 294920 | tf_op jit(solution)/shard_map/ppermute | solution.py:11
  185.6 2.6 %collective-permute-start.17 = (f32[2,1,1,384,64]{3,4,2,1,0:T(8,128)S(1)}, f32[2,1,1,384,64]{3,4,2,1,0:T(8,128)S(1)}, u32[]{:S(2)}, u32[]{:S(2)}) collective-permute-start(f32[2,1,1,384,64]{3,4,2,1,0:T(8,128)S(1)} %pad_maximum_fusion.4), channel_id=1, source_target_pairs={{0,2},{1,3},{2,0},{3,1},{4,6},{5,7},{6,4},{7,5},{8,10},{9,11},{10,... | collective-permute-start | bytes 589832 | tf_op jit(solution)/shard_map/ppermute | solution.py:11
  199.4 2.1 copy.19
  201.5 10.6 %fusion.10 = f32[1536,256]{0,1:T(8,128)S(1)} fusion(f32[1536,1536]{1,0:T(8,128)} %param.3, f32[192,8,2,128]{3,2,1,0:T(2,128)} %bitcast.66), kind=kOutput, calls=%fused_computation.8 | convolution fusion | flops 3624271872 | bytes 12582912 | tf_op jit(solution)/shard_map/dot_general | solution.py:132
  215.2 10.7 %fusion.11 = f32[1536,256]{0,1:T(8,128)S(1)} fusion(f32[1536,1536]{1,0:T(8,128)} %param.4, f32[1536,128]{1,0:T(8,128)S(1)} %get-tuple-element.11, f32[1536,128]{1,0:T(8,128)S(1)} %get-tuple-element.10), kind=kOutput, calls=%fused_computation.9 | convolution fusion | flops 3624665088 | bytes 12582912 | tf_op jit(solution)/shard_map/dot_general | solution.py:133
  (131 shorter events, 71.7 us)
Async XLA Ops:
  17.0 16.7 %collective-permute-start = (f32[768,1536]{1,0:T(8,128)}, f32[768,1536]{1,0:T(8,128)}, u32[]{:S(2)}, u32[]{:S(2)}) collective-permute-start(f32[768,1536]{1,0:T(8,128)} %fusion.7), channel_id=1, source_target_pairs={{0,1},{1,0},{2,3},{3,2},{4,5},{5,4},{6,7},{7,6},{8,9},{9,8},{10,11... | collective-permute-start | bytes 14155784 | tf_op jit(solution)/shard_map/ppermute | solution.py:11
  41.7 29.3 %collective-permute-start.1 = (f32[2,192,768]{2,1,0:T(8,128)S(1)}, f32[2,192,768]{2,1,0:T(8,128)}, u32[]{:S(2)}, u32[]{:S(2)}) collective-permute-start(f32[2,192,768]{2,1,0:T(8,128)S(1)} %dynamic-slice_bitcast_fusion.1), channel_id=1, source_target_pairs={{0,8},{8,0},{16,24},{24,16},{1,9},{9,1},{17,25},{25,17},{2,10},{10... | collective-permute-start | bytes 3538952 | tf_op jit(solution)/shard_map/ppermute | solution.py:11
  46.6 28.4 %collective-permute-start.3 = (f32[2,192,768]{2,1,0:T(8,128)}, f32[2,192,768]{2,1,0:T(8,128)}, u32[]{:S(2)}, u32[]{:S(2)}) collective-permute-start(f32[2,192,768]{2,1,0:T(8,128)} %dynamic-slice_bitcast_fusion), channel_id=1, source_target_pairs={{0,16},{8,24},{16,0},{24,8},{1,17},{9,25},{17,1},{25,9},{2,18},{10... | collective-permute-start | bytes 3538952 | tf_op jit(solution)/shard_map/ppermute | solution.py:11
  72.8 15.3 %collective-permute-start.2 = (f32[192,768]{1,0:T(8,128)S(1)}, f32[192,768]{1,0:T(8,128)}, u32[]{:S(2)}, u32[]{:S(2)}) collective-permute-start(f32[192,768]{1,0:T(8,128)S(1)} %dynamic-slice_bitcast_fusion.3), channel_id=1, source_target_pairs={{0,16},{8,24},{16,0},{24,8},{1,17},{9,25},{17,1},{25,9},{2,18},{10... | collective-permute-start | bytes 1769480 | tf_op jit(solution)/shard_map/ppermute | solution.py:11
  78.3 14.9 %collective-permute-start.4 = (f32[192,768]{1,0:T(8,128)}, f32[192,768]{1,0:T(8,128)}, u32[]{:S(2)}, u32[]{:S(2)}) collective-permute-start(f32[192,768]{1,0:T(8,128)} %dynamic-slice_bitcast_fusion.2), channel_id=1, source_target_pairs={{0,8},{8,0},{16,24},{24,16},{1,9},{9,1},{17,25},{25,17},{2,10},{10... | collective-permute-start | bytes 1769480 | tf_op jit(solution)/shard_map/ppermute | solution.py:11
  99.3 15.2 %collective-permute-start.5 = (f32[192,2,384]{2,0,1:T(8,128)S(1)}, f32[192,2,384]{2,0,1:T(8,128)S(1)}, u32[]{:S(2)}, u32[]{:S(2)}) collective-permute-start(f32[192,2,384]{2,0,1:T(8,128)S(1)} %bitcast_select_fusion), channel_id=1, source_target_pairs={{0,2},{1,5},{2,0},{3,7},{4,6},{5,1},{6,4},{7,3},{8,10},{9,13},{10,... | collective-permute-start | bytes 1769480 | tf_op jit(solution)/shard_map/ppermute | solution.py:88
  114.7 10.9 %collective-permute-start.6 = (f32[192,384]{1,0:T(8,128)S(1)}, f32[192,384]{1,0:T(8,128)S(1)}, u32[]{:S(2)}, u32[]{:S(2)}) collective-permute-start(f32[192,384]{1,0:T(8,128)S(1)} %select_bitcast_fusion), channel_id=1, source_target_pairs={{0,4},{1,3},{2,6},{3,1},{4,0},{5,7},{6,2},{7,5},{8,12},{9,11},{10,... | collective-permute-start | bytes 884744 | tf_op jit(solution)/shard_map/ppermute | solution.py:88
  128.1 5.6 %collective-permute-start.8 = (f32[384,64]{0,1:T(8,128)S(1)}, f32[384,64]{0,1:T(8,128)S(1)}, u32[]{:S(2)}, u32[]{:S(2)}) collective-permute-start(f32[384,64]{0,1:T(8,128)S(1)} %fusion.20), channel_id=1, source_target_pairs={{0,2},{1,3},{2,0},{3,1},{4,6},{5,7},{6,4},{7,5},{8,10},{9,11},{10,... | collective-permute-start | bytes 294920 | tf_op jit(solution)/shard_map/ppermute | solution.py:11
  129.8 5.8 %collective-permute-start.19 = (f32[384,64]{0,1:T(8,128)S(1)}, f32[384,64]{0,1:T(8,128)S(1)}, u32[]{:S(2)}, u32[]{:S(2)}) collective-permute-start(f32[384,64]{0,1:T(8,128)S(1)} %fusion.18), channel_id=1, source_target_pairs={{0,2},{1,3},{2,0},{3,1},{4,6},{5,7},{6,4},{7,5},{8,10},{9,11},{10,... | collective-permute-start | bytes 294920 | tf_op jit(solution)/shard_map/ppermute | solution.py:11
  133.8 9.7 %collective-permute-start.9 = (f32[384,64]{0,1:T(8,128)S(1)}, f32[384,64]{0,1:T(8,128)S(1)}, u32[]{:S(2)}, u32[]{:S(2)}) collective-permute-start(f32[384,64]{0,1:T(8,128)S(1)} %add.185), channel_id=1, source_target_pairs={{0,4},{1,5},{2,6},{3,7},{4,0},{5,1},{6,2},{7,3},{8,12},{9,13},{10,... | collective-permute-start | bytes 294920 | tf_op jit(solution)/shard_map/ppermute | solution.py:11
  135.6 9.7 %collective-permute-start.20 = (f32[384,64]{0,1:T(8,128)S(1)}, f32[384,64]{0,1:T(8,128)S(1)}, u32[]{:S(2)}, u32[]{:S(2)}) collective-permute-start(f32[384,64]{0,1:T(8,128)S(1)} %add.193), channel_id=1, source_target_pairs={{0,4},{1,5},{2,6},{3,7},{4,0},{5,1},{6,2},{7,3},{8,12},{9,13},{10,... | collective-permute-start | bytes 294920 | tf_op jit(solution)/shard_map/ppermute | solution.py:11
  156.5 6.3 %collective-permute-start.23 = (f32[384,64]{0,1:T(8,128)S(1)}, f32[384,64]{0,1:T(8,128)S(1)}, u32[]{:S(2)}, u32[]{:S(2)}) collective-permute-start(f32[384,64]{0,1:T(8,128)S(1)} %fusion.22), channel_id=1, source_target_pairs={{0,2},{1,3},{2,0},{3,1},{4,6},{5,7},{6,4},{7,5},{8,10},{9,11},{10,... | collective-permute-start | bytes 294920 | tf_op jit(solution)/shard_map/ppermute | solution.py:11
  159.2 6.7 %collective-permute-start.13 = (f32[384,64]{0,1:T(8,128)S(1)}, f32[384,64]{0,1:T(8,128)S(1)}, u32[]{:S(2)}, u32[]{:S(2)}) collective-permute-start(f32[384,64]{0,1:T(8,128)S(1)} %add.189), channel_id=1, source_target_pairs={{0,4},{1,5},{2,6},{3,7},{4,0},{5,1},{6,2},{7,3},{8,12},{9,13},{10,... | collective-permute-start | bytes 294920 | tf_op jit(solution)/shard_map/ppermute | solution.py:11
  162.8 5.6 %collective-permute-start.24 = (f32[384,64]{0,1:T(8,128)S(1)}, f32[384,64]{0,1:T(8,128)S(1)}, u32[]{:S(2)}, u32[]{:S(2)}) collective-permute-start(f32[384,64]{0,1:T(8,128)S(1)} %add.197), channel_id=1, source_target_pairs={{0,4},{1,5},{2,6},{3,7},{4,0},{5,1},{6,2},{7,3},{8,12},{9,13},{10,... | collective-permute-start | bytes 294920 | tf_op jit(solution)/shard_map/ppermute | solution.py:11
  165.9 6.9 %collective-permute-start.30 = (f32[1,384,64]{1,2,0:T(8,128)S(1)}, f32[1,384,64]{1,2,0:T(8,128)S(1)}, u32[]{:S(2)}, u32[]{:S(2)}) collective-permute-start(f32[1,384,64]{1,2,0:T(8,128)S(1)} %add_bitcast_fusion.3), channel_id=1, source_target_pairs={{0,8},{8,0},{16,24},{24,16},{1,9},{9,1},{17,25},{25,17},{2,10},{10... | collective-permute-start | bytes 294920 | tf_op jit(solution)/shard_map/ppermute | solution.py:11
  168.4 7.7 %collective-permute-start.32 = (f32[1,384,64]{1,2,0:T(8,128)S(1)}, f32[1,384,64]{1,2,0:T(8,128)S(1)}, u32[]{:S(2)}, u32[]{:S(2)}) collective-permute-start(f32[1,384,64]{1,2,0:T(8,128)S(1)} %add_bitcast_fusion.2), channel_id=1, source_target_pairs={{0,8},{8,0},{16,24},{24,16},{1,9},{9,1},{17,25},{25,17},{2,10},{10... | collective-permute-start | bytes 294920 | tf_op jit(solution)/shard_map/ppermute | solution.py:11
  172.8 17.7 %collective-permute-start.31 = (f32[2,384,64]{1,2,0:T(8,128)S(1)}, f32[2,384,64]{1,2,0:T(8,128)S(1)}, u32[]{:S(2)}, u32[]{:S(2)}) collective-permute-start(f32[2,384,64]{1,2,0:T(8,128)S(1)} %pad_maximum_fusion.6), channel_id=1, source_target_pairs={{0,16},{8,24},{16,0},{24,8},{1,17},{9,25},{17,1},{25,9},{2,18},{10... | collective-permute-start | bytes 589832 | tf_op jit(solution)/shard_map/ppermute | solution.py:11
  176.2 19.1 %collective-permute-start.33 = (f32[2,384,64]{1,2,0:T(8,128)S(1)}, f32[2,384,64]{1,2,0:T(8,128)S(1)}, u32[]{:S(2)}, u32[]{:S(2)}) collective-permute-start(f32[2,384,64]{1,2,0:T(8,128)S(1)} %pad_maximum_fusion.7), channel_id=1, source_target_pairs={{0,16},{8,24},{16,0},{24,8},{1,17},{9,25},{17,1},{25,9},{2,18},{10... | collective-permute-start | bytes 589832 | tf_op jit(solution)/shard_map/ppermute | solution.py:11
  177.0 5.9 %collective-permute-start.26 = (f32[384,64]{0,1:T(8,128)S(1)}, f32[384,64]{0,1:T(8,128)S(1)}, u32[]{:S(2)}, u32[]{:S(2)}) collective-permute-start(f32[384,64]{0,1:T(8,128)S(1)} %add.199), channel_id=1, source_target_pairs={{0,16},{8,24},{16,0},{24,8},{1,17},{9,25},{17,1},{25,9},{2,18},{10... | collective-permute-start | bytes 294920 | tf_op jit(solution)/shard_map/ppermute | solution.py:11
  179.6 5.9 %collective-permute-start.16 = (f32[1,1,1,384,64]{3,4,2,1,0:T(8,128)S(1)}, f32[1,1,1,384,64]{3,4,2,1,0:T(8,128)S(1)}, u32[]{:S(2)}, u32[]{:S(2)}) collective-permute-start(f32[1,1,1,384,64]{3,4,2,1,0:T(8,128)S(1)} %add_bitcast_fusion.1), channel_id=1, source_target_pairs={{0,4},{1,5},{2,6},{3,7},{4,0},{5,1},{6,2},{7,3},{8,12},{9,13},{10,... | collective-permute-start | bytes 294920 | tf_op jit(solution)/shard_map/ppermute | solution.py:11
  183.0 5.6 %collective-permute-start.27 = (f32[1,1,1,384,64]{3,4,2,1,0:T(8,128)S(1)}, f32[1,1,1,384,64]{3,4,2,1,0:T(8,128)S(1)}, u32[]{:S(2)}, u32[]{:S(2)}) collective-permute-start(f32[1,1,1,384,64]{3,4,2,1,0:T(8,128)S(1)} %add_bitcast_fusion), channel_id=1, source_target_pairs={{0,4},{1,5},{2,6},{3,7},{4,0},{5,1},{6,2},{7,3},{8,12},{9,13},{10,... | collective-permute-start | bytes 294920 | tf_op jit(solution)/shard_map/ppermute | solution.py:11
  185.6 6.2 %collective-permute-start.17 = (f32[2,1,1,384,64]{3,4,2,1,0:T(8,128)S(1)}, f32[2,1,1,384,64]{3,4,2,1,0:T(8,128)S(1)}, u32[]{:S(2)}, u32[]{:S(2)}) collective-permute-start(f32[2,1,1,384,64]{3,4,2,1,0:T(8,128)S(1)} %pad_maximum_fusion.4), channel_id=1, source_target_pairs={{0,2},{1,3},{2,0},{3,1},{4,6},{5,7},{6,4},{7,5},{8,10},{9,11},{10,... | collective-permute-start | bytes 589832 | tf_op jit(solution)/shard_map/ppermute | solution.py:11
  188.6 5.7 %collective-permute-start.28 = (f32[2,1,1,384,64]{3,4,2,1,0:T(8,128)S(1)}, f32[2,1,1,384,64]{3,4,2,1,0:T(8,128)S(1)}, u32[]{:S(2)}, u32[]{:S(2)}) collective-permute-start(f32[2,1,1,384,64]{3,4,2,1,0:T(8,128)S(1)} %pad_maximum_fusion.5), channel_id=1, source_target_pairs={{0,2},{1,3},{2,0},{3,1},{4,6},{5,7},{6,4},{7,5},{8,10},{9,11},{10,... | collective-permute-start | bytes 589832 | tf_op jit(solution)/shard_map/ppermute | solution.py:11
  196.6 17.1 %collective-permute-start.34 = (f32[1536,128]{1,0:T(8,128)}, f32[1536,128]{1,0:T(8,128)}, u32[]{:S(2)}, u32[]{:S(2)}) collective-permute-start(f32[1536,128]{1,0:T(8,128)} %bitcast.25), channel_id=1, source_target_pairs={{0,1},{1,0},{2,3},{3,2},{4,5},{5,4},{6,7},{7,6},{8,9},{9,8},{10,11... | collective-permute-start | bytes 2359304 | tf_op jit(solution)/shard_map/ppermute | solution.py:11
  (20 other events, 225.3 us)

commit v14 on v13

--- a/solution.py
+++ b/solution.py
@@ -48,23 +48,28 @@
 
     received = exchange(partial_rows((1 - core) * half_rows), "cols", 1)
     kept_rows = lax.optimization_barrier(partial_rows(core * half_rows))
-    chip_sum = kept_rows + received
     row_bits = row_count.bit_length() - 1
     row_index = lax.axis_index("rows")
     chunk_cols = snap_count // row_bits
     chunks = []
     for rot in range(row_bits):
-        part = chip_sum[:, rot * chunk_cols:(rot + 1) * chunk_cols]
-        part = part.reshape((2,) * row_bits + (part_rows, chunk_cols))
+        pieces = [
+            x[:, rot * chunk_cols:(rot + 1) * chunk_cols].reshape((2,) * row_bits + (part_rows, chunk_cols))
+            for x in (kept_rows, received)
+        ]
         left = list(range(row_bits - 1, -1, -1))
         for k in range(row_bits):
             bit = (rot + k) % row_bits
             axis = left.index(bit)
             mine = (row_index >> bit) % 2
-            kept = lax.dynamic_index_in_dim(part, mine, axis=axis, keepdims=False)
-            sent = lax.dynamic_index_in_dim(part, 1 - mine, axis=axis, keepdims=False)
-            part = kept + exchange(sent, "rows", 1 << bit)
+            kept, sent = [
+                sum(lax.dynamic_index_in_dim(x, side, axis=axis, keepdims=False) for x in pieces[1:])
+                + lax.dynamic_index_in_dim(pieces[0], side, axis=axis, keepdims=False)
+                for side in (mine, 1 - mine)
+            ]
+            pieces = [kept + exchange(sent, "rows", 1 << bit)]
             left.pop(axis)
+        part = pieces[0]
         chunks.append(part)
     strip = jnp.concatenate(chunks, axis=1)
     bits = chip_count.bit_length() - 1

time: 228 us -> 231 us (1.013)
  local copies, waits for them, and re-layouts: 17.8 us -> 22.5 us
    slice x1 -> x2, local copies, waits for them, and re-layouts: 1.7 us -> 8.98 us  [shards(): x[:, rot * chunk_cols:(rot + 1) * chunk_cols]]
    squeeze x4 -> x2, local copies, waits for them, and re-layouts: 3.34 us -> 0.9 us  [shards(): lax.dynamic_index_in_dim(pieces[0], side, axis=axis, keepdims=False)]
    add x5 -> x6, other arithmetic: 10.2 us -> 9.03 us  [the longest x4 6.1 us: shards(): pieces = [kept + exchange(sent, 'rows', 1 << bit)]]
    unnamed x20 -> x24, local copies, waits for them, and re-layouts: 5.75 us -> 5.63 us
  transfers between devices with their start and end apart: 35 -> 35, of which waited for: 21 -> 20; matrix products, arithmetic and copies ran while one was open for 21% -> 23% of each run, Pallas kernels for 0% -> 0%
where the time goes in v14:
time: 231 us
  waiting for transfers between devices  79.1 us (34%)
  matrix products  58.9 us (25%)
  starting transfers between devices  52.7 us (23%)
  local copies, waits for them, and re-layouts  22.5 us (10%)
  other arithmetic  16.2 us (7%)
    ppermute x33, waiting for transfers between devices, exchange(): return lax.ppermute(x, axis, [(i, i ^ step) for i in range(count)])  57.5 us
    ppermute x33, starting transfers between devices, exchange(): return lax.ppermute(x, axis, [(i, i ^ step) for i in range(count)])  48.3 us
    dot_general x2, matrix products, partial_rows(): jnp.dot(columns.T, direct, precision=fast, preferred_element_type=jnp.flo...  32.5 us
    ppermute x2, waiting for transfers between devices, shards(): strip = kept + lax.ppermute(sent, 'cols', pairs)  21.6 us
    dot_general x1, matrix products, shards(): jnp.dot(adjoint, full_a, precision=fast, preferred_element_type=jnp.float32)  10.7 us
    dot_general x1, matrix products, shards(): jnp.dot(direct, full_d, precision=fast, preferred_element_type=jnp.float32)  10.6 us
    slice x2, local copies, waits for them, and re-layouts, shards(): x[:, rot * chunk_cols:(rot + 1) * chunk_cols]  8.98 us
    add x4, other arithmetic, shards(): pieces = [kept + exchange(sent, 'rows', 1 << bit)]  6.1 us
  transfers between devices with their start and end apart: 35, of which 20 were waited for; matrix products, arithmetic and copies ran while one was open for 23% of the time, Pallas kernels for 0%

profile of v14, /device:TPU:0, one launch (start us, length us, event | category | flops | bytes accessed | tf_op | source)
XLA Modules:
  0.0 230.6 jit_solution(15995605502232558556)
XLA Ops:
  0.7 16.3 %fusion.4 = f32[768,1536]{1,0:T(8,128)} fusion(f32[1536,1536]{1,0:T(8,128)} %param.3, f32[1536,1536]{1,0:T(8,128)} %param.4, s32[]{:T(128)S(6)} %select_n.273), kind=kOutput, calls=%fused_computation.4 | convolution fusion | flops 10872815616 | bytes 18874372 | tf_op jit(solution)/shard_map/dot_general | solution.py:47
  17.4 16.2 %fusion.7 = f32[768,1536]{1,0:T(8,128)} fusion(f32[1536,1536]{1,0:T(8,128)} %param.3, f32[1536,1536]{1,0:T(8,128)} %param.4, s32[]{:T(128)S(6)} %select_n.276), kind=kOutput, calls=%fused_computation.5 | convolution fusion | flops 10872815616 | bytes 18874372 | tf_op jit(solution)/shard_map/dot_general | solution.py:47
  33.6 4.0 %fusion.40 = (f32[768,768]{1,0:T(8,128)S(1)}, f32[768,768]{1,0:T(8,128)}) fusion(f32[768,1536]{1,0:T(8,128)} %fusion.7), kind=kLoop, calls=%fused_computation.92 | loop fusion | bytes 9437184 | tf_op jit(solution)/shard_map/slice | solution.py:57
  37.6 4.9 %fusion.39 = (f32[768,768]{1,0:T(8,128)S(1)}, f32[768,768]{1,0:T(8,128)}) fusion(f32[768,1536]{1,0:T(8,128)} %collective-permute-done), kind=kLoop, calls=%fused_computation.91 | loop fusion | bytes 9437184 | tf_op jit(solution)/shard_map/slice | solution.py:57
  44.1 2.5 %collective-permute-start.1 = (f32[2,192,768]{2,1,0:T(8,128)S(1)}, f32[2,192,768]{2,1,0:T(8,128)}, u32[]{:S(2)}, u32[]{:S(2)}) collective-permute-start(f32[2,192,768]{2,1,0:T(8,128)S(1)} %add_bitcast_fusion.1), channel_id=1, source_target_pairs={{0,8},{8,0},{16,24},{24,16},{1,9},{9,1},{17,25},{25,17},{2,10},{10... | collective-permute-start | bytes 3538952 | tf_op jit(solution)/shard_map/ppermute | solution.py:11
  46.6 2.8 %add_bitcast_fusion = f32[2,192,768]{2,1,0:T(8,128)} fusion(f32[2,2,192,768]{3,2,1,0:T(8,128)} %bitcast.73, s32[]{:T(128)S(6)} %select_n.280, f32[2,2,192,768]{3,2,1,0:T(8,128)} %bitcast.75), kind=kLoop, calls=%fused_computation.21 | loop fusion | flops 294912 | bytes 3538948 | tf_op jit(solution)/shard_map/add | solution.py:66
  50.9 22.4 %collective-permute-done.1 = f32[2,192,768]{2,1,0:T(8,128)} collective-permute-done((f32[2,192,768]{2,1,0:T(8,128)S(1)}, f32[2,192,768]{2,1,0:T(8,128)}, u32[]{:S(2)}, u32[]{:S(2)}) %collective-permute-start.1) | collective-permute-done | bytes 1179680 | tf_op jit(solution)/shard_map/ppermute | solution.py:11
  73.3 2.3 %fusion.18 = f32[2,192,768]{2,1,0:T(8,128)S(1)} fusion(f32[2,192,768]{2,1,0:T(8,128)} %collective-permute-done.1, f32[2,2,192,768]{3,2,1,0:T(8,128)} %bitcast.78, s32[]{:T(128)S(6)} %select_n.275, f32[2,2,192,768]{3,2,1,0:T(8,128)} %bitcast.80), kind=kLoop, calls=%fused_computation.19 | loop fusion | flops 589824 | bytes 4718596 | tf_op jit(solution)/shard_map/add | solution.py:70
  82.4 8.6 %collective-permute-done.2 = f32[192,768]{1,0:T(8,128)} collective-permute-done((f32[192,768]{1,0:T(8,128)S(1)}, f32[192,768]{1,0:T(8,128)}, u32[]{:S(2)}, u32[]{:S(2)}) %collective-permute-start.2) | collective-permute-done | bytes 589856 | tf_op jit(solution)/shard_map/ppermute | solution.py:11
  92.1 3.9 %collective-permute-done.4 = f32[192,768]{1,0:T(8,128)} collective-permute-done((f32[192,768]{1,0:T(8,128)}, f32[192,768]{1,0:T(8,128)}, u32[]{:S(2)}, u32[]{:S(2)}) %collective-permute-start.4) | collective-permute-done | bytes 589856 | tf_op jit(solution)/shard_map/ppermute | solution.py:11
  98.4 2.2 reshape.49
  103.8 13.5 %collective-permute-done.5 = f32[192,2,384]{2,0,1:T(8,128)S(1)} collective-permute-done((f32[192,2,384]{2,0,1:T(8,128)S(1)}, f32[192,2,384]{2,0,1:T(8,128)S(1)}, u32[]{:S(2)}, u32[]{:S(2)}) %collective-permute-start.5) | collective-permute-done | bytes 589856 | tf_op jit(solution)/shard_map/ppermute | solution.py:93
  117.4 2.8 %collective-permute-start.6 = (f32[192,384]{1,0:T(8,128)S(1)}, f32[192,384]{1,0:T(8,128)S(1)}, u32[]{:S(2)}, u32[]{:S(2)}) collective-permute-start(f32[192,384]{1,0:T(8,128)S(1)} %select_bitcast_fusion), channel_id=1, source_target_pairs={{0,4},{1,3},{2,6},{3,1},{4,0},{5,7},{6,2},{7,5},{8,12},{9,11},{10,... | collective-permute-start | bytes 884744 | tf_op jit(solution)/shard_map/ppermute | solution.py:93
  120.2 8.1 %collective-permute-done.6 = f32[192,384]{1,0:T(8,128)S(1)} collective-permute-done((f32[192,384]{1,0:T(8,128)S(1)}, f32[192,384]{1,0:T(8,128)S(1)}, u32[]{:S(2)}, u32[]{:S(2)}) %collective-permute-start.6) | collective-permute-done | bytes 294944 | tf_op jit(solution)/shard_map/ppermute | solution.py:93
  133.9 2.7 %collective-permute-done.8 = f32[384,64]{0,1:T(8,128)S(1)} collective-permute-done((f32[384,64]{0,1:T(8,128)S(1)}, f32[384,64]{0,1:T(8,128)S(1)}, u32[]{:S(2)}, u32[]{:S(2)}) %collective-permute-start.8) | collective-permute-done | bytes 98336 | tf_op jit(solution)/shard_map/ppermute | solution.py:11
  138.4 2.8 %collective-permute-start.20 = (f32[384,64]{0,1:T(8,128)S(1)}, f32[384,64]{0,1:T(8,128)S(1)}, u32[]{:S(2)}, u32[]{:S(2)}) collective-permute-start(f32[384,64]{0,1:T(8,128)S(1)} %add.225), channel_id=1, source_target_pairs={{0,4},{1,5},{2,6},{3,7},{4,0},{5,1},{6,2},{7,3},{8,12},{9,13},{10,... | collective-permute-start | bytes 294920 | tf_op jit(solution)/shard_map/ppermute | solution.py:11
  141.2 5.1 %collective-permute-done.9 = f32[384,64]{0,1:T(8,128)S(1)} collective-permute-done((f32[384,64]{0,1:T(8,128)S(1)}, f32[384,64]{0,1:T(8,128)S(1)}, u32[]{:S(2)}, u32[]{:S(2)}) %collective-permute-start.9) | collective-permute-done | bytes 98336 | tf_op jit(solution)/shard_map/ppermute | solution.py:11
  149.5 2.4 %collective-permute-done.10 = f32[384,64]{0,1:T(8,128)S(1)} collective-permute-done((f32[384,64]{0,1:T(8,128)S(1)}, f32[384,64]{0,1:T(8,128)S(1)}, u32[]{:S(2)}, u32[]{:S(2)}) %collective-permute-start.10) | collective-permute-done | bytes 98336 | tf_op jit(solution)/shard_map/ppermute | solution.py:11
  162.0 3.4 %collective-permute-start.13 = (f32[384,64]{0,1:T(8,128)S(1)}, f32[384,64]{0,1:T(8,128)S(1)}, u32[]{:S(2)}, u32[]{:S(2)}) collective-permute-start(f32[384,64]{0,1:T(8,128)S(1)} %add.221), channel_id=1, source_target_pairs={{0,4},{1,5},{2,6},{3,7},{4,0},{5,1},{6,2},{7,3},{8,12},{9,13},{10,... | collective-permute-start | bytes 294920 | tf_op jit(solution)/shard_map/ppermute | solution.py:11
  165.4 2.7 %collective-permute-start.24 = (f32[384,64]{0,1:T(8,128)S(1)}, f32[384,64]{0,1:T(8,128)S(1)}, u32[]{:S(2)}, u32[]{:S(2)}) collective-permute-start(f32[384,64]{0,1:T(8,128)S(1)} %add.229), channel_id=1, source_target_pairs={{0,4},{1,5},{2,6},{3,7},{4,0},{5,1},{6,2},{7,3},{8,12},{9,13},{10,... | collective-permute-start | bytes 294920 | tf_op jit(solution)/shard_map/ppermute | solution.py:11
  182.7 2.7 %collective-permute-start.16 = (f32[1,1,1,384,64]{3,4,2,1,0:T(8,128)S(1)}, f32[1,1,1,384,64]{3,4,2,1,0:T(8,128)S(1)}, u32[]{:S(2)}, u32[]{:S(2)}) collective-permute-start(f32[1,1,1,384,64]{3,4,2,1,0:T(8,128)S(1)} %add_bitcast_fusion.3), channel_id=1, source_target_pairs={{0,4},{1,5},{2,6},{3,7},{4,0},{5,1},{6,2},{7,3},{8,12},{9,13},{10,... | collective-permute-start | bytes 294920 | tf_op jit(solution)/shard_map/ppermute | solution.py:11
  186.1 2.9 %collective-permute-start.27 = (f32[1,1,1,384,64]{3,4,2,1,0:T(8,128)S(1)}, f32[1,1,1,384,64]{3,4,2,1,0:T(8,128)S(1)}, u32[]{:S(2)}, u32[]{:S(2)}) collective-permute-start(f32[1,1,1,384,64]{3,4,2,1,0:T(8,128)S(1)} %add_bitcast_fusion.2), channel_id=1, source_target_pairs={{0,4},{1,5},{2,6},{3,7},{4,0},{5,1},{6,2},{7,3},{8,12},{9,13},{10,... | collective-permute-start | bytes 294920 | tf_op jit(solution)/shard_map/ppermute | solution.py:11
  204.6 10.6 %fusion.10 = f32[1536,256]{0,1:T(8,128)S(1)} fusion(f32[1536,1536]{1,0:T(8,128)} %param.3, f32[192,8,2,128]{3,2,1,0:T(2,128)} %bitcast.82), kind=kOutput, calls=%fused_computation.8 | convolution fusion | flops 3624271872 | bytes 12582912 | tf_op jit(solution)/shard_map/dot_general | solution.py:137
  218.3 10.7 %fusion.11 = f32[1536,256]{0,1:T(8,128)S(1)} fusion(f32[1536,1536]{1,0:T(8,128)} %param.4, f32[1536,128]{1,0:T(8,128)S(1)} %get-tuple-element.13, f32[1536,128]{1,0:T(8,128)S(1)} %get-tuple-element.12), kind=kOutput, calls=%fused_computation.9 | convolution fusion | flops 3624665088 | bytes 12582912 | tf_op jit(solution)/shard_map/dot_general | solution.py:138
  (135 shorter events, 72.9 us)
Async XLA Ops:
  17.0 20.7 %collective-permute-start = (f32[768,1536]{1,0:T(8,128)}, f32[768,1536]{1,0:T(8,128)}, u32[]{:S(2)}, u32[]{:S(2)}) collective-permute-start(f32[768,1536]{1,0:T(8,128)} %fusion.4), channel_id=1, source_target_pairs={{0,1},{1,0},{2,3},{3,2},{4,5},{5,4},{6,7},{7,6},{8,9},{9,8},{10,11... | collective-permute-start | bytes 14155784 | tf_op jit(solution)/shard_map/ppermute | solution.py:11
  44.1 29.2 %collective-permute-start.1 = (f32[2,192,768]{2,1,0:T(8,128)S(1)}, f32[2,192,768]{2,1,0:T(8,128)}, u32[]{:S(2)}, u32[]{:S(2)}) collective-permute-start(f32[2,192,768]{2,1,0:T(8,128)S(1)} %add_bitcast_fusion.1), channel_id=1, source_target_pairs={{0,8},{8,0},{16,24},{24,16},{1,9},{9,1},{17,25},{25,17},{2,10},{10... | collective-permute-start | bytes 3538952 | tf_op jit(solution)/shard_map/ppermute | solution.py:11
  49.3 28.4 %collective-permute-start.3 = (f32[2,192,768]{2,1,0:T(8,128)}, f32[2,192,768]{2,1,0:T(8,128)}, u32[]{:S(2)}, u32[]{:S(2)}) collective-permute-start(f32[2,192,768]{2,1,0:T(8,128)} %add_bitcast_fusion), channel_id=1, source_target_pairs={{0,16},{8,24},{16,0},{24,8},{1,17},{9,25},{17,1},{25,9},{2,18},{10... | collective-permute-start | bytes 3538952 | tf_op jit(solution)/shard_map/ppermute | solution.py:11
  75.7 15.3 %collective-permute-start.2 = (f32[192,768]{1,0:T(8,128)S(1)}, f32[192,768]{1,0:T(8,128)}, u32[]{:S(2)}, u32[]{:S(2)}) collective-permute-start(f32[192,768]{1,0:T(8,128)S(1)} %dynamic-slice_bitcast_fusion.1), channel_id=1, source_target_pairs={{0,16},{8,24},{16,0},{24,8},{1,17},{9,25},{17,1},{25,9},{2,18},{10... | collective-permute-start | bytes 1769480 | tf_op jit(solution)/shard_map/ppermute | solution.py:11
  81.1 14.9 %collective-permute-start.4 = (f32[192,768]{1,0:T(8,128)}, f32[192,768]{1,0:T(8,128)}, u32[]{:S(2)}, u32[]{:S(2)}) collective-permute-start(f32[192,768]{1,0:T(8,128)} %dynamic-slice_bitcast_fusion), channel_id=1, source_target_pairs={{0,8},{8,0},{16,24},{24,16},{1,9},{9,1},{17,25},{25,17},{2,10},{10... | collective-permute-start | bytes 1769480 | tf_op jit(solution)/shard_map/ppermute | solution.py:11
  102.1 15.2 %collective-permute-start.5 = (f32[192,2,384]{2,0,1:T(8,128)S(1)}, f32[192,2,384]{2,0,1:T(8,128)S(1)}, u32[]{:S(2)}, u32[]{:S(2)}) collective-permute-start(f32[192,2,384]{2,0,1:T(8,128)S(1)} %bitcast_select_fusion), channel_id=1, source_target_pairs={{0,2},{1,5},{2,0},{3,7},{4,6},{5,1},{6,4},{7,3},{8,10},{9,13},{10,... | collective-permute-start | bytes 1769480 | tf_op jit(solution)/shard_map/ppermute | solution.py:93
  117.4 10.9 %collective-permute-start.6 = (f32[192,384]{1,0:T(8,128)S(1)}, f32[192,384]{1,0:T(8,128)S(1)}, u32[]{:S(2)}, u32[]{:S(2)}) collective-permute-start(f32[192,384]{1,0:T(8,128)S(1)} %select_bitcast_fusion), channel_id=1, source_target_pairs={{0,4},{1,3},{2,6},{3,1},{4,0},{5,7},{6,2},{7,5},{8,12},{9,11},{10,... | collective-permute-start | bytes 884744 | tf_op jit(solution)/shard_map/ppermute | solution.py:93
  130.9 5.7 %collective-permute-start.8 = (f32[384,64]{0,1:T(8,128)S(1)}, f32[384,64]{0,1:T(8,128)S(1)}, u32[]{:S(2)}, u32[]{:S(2)}) collective-permute-start(f32[384,64]{0,1:T(8,128)S(1)} %fusion.22), channel_id=1, source_target_pairs={{0,2},{1,3},{2,0},{3,1},{4,6},{5,7},{6,4},{7,5},{8,10},{9,11},{10,... | collective-permute-start | bytes 294920 | tf_op jit(solution)/shard_map/ppermute | solution.py:11
  132.6 5.8 %collective-permute-start.19 = (f32[384,64]{0,1:T(8,128)S(1)}, f32[384,64]{0,1:T(8,128)S(1)}, u32[]{:S(2)}, u32[]{:S(2)}) collective-permute-start(f32[384,64]{0,1:T(8,128)S(1)} %fusion.20), channel_id=1, source_target_pairs={{0,2},{1,3},{2,0},{3,1},{4,6},{5,7},{6,4},{7,5},{8,10},{9,11},{10,... | collective-permute-start | bytes 294920 | tf_op jit(solution)/shard_map/ppermute | solution.py:11
  136.6 9.7 %collective-permute-start.9 = (f32[384,64]{0,1:T(8,128)S(1)}, f32[384,64]{0,1:T(8,128)S(1)}, u32[]{:S(2)}, u32[]{:S(2)}) collective-permute-start(f32[384,64]{0,1:T(8,128)S(1)} %add.217), channel_id=1, source_target_pairs={{0,4},{1,5},{2,6},{3,7},{4,0},{5,1},{6,2},{7,3},{8,12},{9,13},{10,... | collective-permute-start | bytes 294920 | tf_op jit(solution)/shard_map/ppermute | solution.py:11
  138.4 9.8 %collective-permute-start.20 = (f32[384,64]{0,1:T(8,128)S(1)}, f32[384,64]{0,1:T(8,128)S(1)}, u32[]{:S(2)}, u32[]{:S(2)}) collective-permute-start(f32[384,64]{0,1:T(8,128)S(1)} %add.225), channel_id=1, source_target_pairs={{0,4},{1,5},{2,6},{3,7},{4,0},{5,1},{6,2},{7,3},{8,12},{9,13},{10,... | collective-permute-start | bytes 294920 | tf_op jit(solution)/shard_map/ppermute | solution.py:11
  159.0 6.3 %collective-permute-start.23 = (f32[384,64]{0,1:T(8,128)S(1)}, f32[384,64]{0,1:T(8,128)S(1)}, u32[]{:S(2)}, u32[]{:S(2)}) collective-permute-start(f32[384,64]{0,1:T(8,128)S(1)} %fusion.24), channel_id=1, source_target_pairs={{0,2},{1,3},{2,0},{3,1},{4,6},{5,7},{6,4},{7,5},{8,10},{9,11},{10,... | collective-permute-start | bytes 294920 | tf_op jit(solution)/shard_map/ppermute | solution.py:11
  162.0 6.2 %collective-permute-start.13 = (f32[384,64]{0,1:T(8,128)S(1)}, f32[384,64]{0,1:T(8,128)S(1)}, u32[]{:S(2)}, u32[]{:S(2)}) collective-permute-start(f32[384,64]{0,1:T(8,128)S(1)} %add.221), channel_id=1, source_target_pairs={{0,4},{1,5},{2,6},{3,7},{4,0},{5,1},{6,2},{7,3},{8,12},{9,13},{10,... | collective-permute-start | bytes 294920 | tf_op jit(solution)/shard_map/ppermute | solution.py:11
  165.4 5.6 %collective-permute-start.24 = (f32[384,64]{0,1:T(8,128)S(1)}, f32[384,64]{0,1:T(8,128)S(1)}, u32[]{:S(2)}, u32[]{:S(2)}) collective-permute-start(f32[384,64]{0,1:T(8,128)S(1)} %add.229), channel_id=1, source_target_pairs={{0,4},{1,5},{2,6},{3,7},{4,0},{5,1},{6,2},{7,3},{8,12},{9,13},{10,... | collective-permute-start | bytes 294920 | tf_op jit(solution)/shard_map/ppermute | solution.py:11
  168.2 7.5 %collective-permute-start.30 = (f32[1,384,64]{1,2,0:T(8,128)S(1)}, f32[1,384,64]{1,2,0:T(8,128)S(1)}, u32[]{:S(2)}, u32[]{:S(2)}) collective-permute-start(f32[1,384,64]{1,2,0:T(8,128)S(1)} %add_bitcast_fusion.5), channel_id=1, source_target_pairs={{0,8},{8,0},{16,24},{24,16},{1,9},{9,1},{17,25},{25,17},{2,10},{10... | collective-permute-start | bytes 294920 | tf_op jit(solution)/shard_map/ppermute | solution.py:11
  171.0 8.2 %collective-permute-start.32 = (f32[1,384,64]{1,2,0:T(8,128)S(1)}, f32[1,384,64]{1,2,0:T(8,128)S(1)}, u32[]{:S(2)}, u32[]{:S(2)}) collective-permute-start(f32[1,384,64]{1,2,0:T(8,128)S(1)} %add_bitcast_fusion.4), channel_id=1, source_target_pairs={{0,8},{8,0},{16,24},{24,16},{1,9},{9,1},{17,25},{25,17},{2,10},{10... | collective-permute-start | bytes 294920 | tf_op jit(solution)/shard_map/ppermute | solution.py:11
  174.2 5.8 %collective-permute-start.25 = (f32[384,64]{0,1:T(8,128)S(1)}, f32[384,64]{0,1:T(8,128)S(1)}, u32[]{:S(2)}, u32[]{:S(2)}) collective-permute-start(f32[384,64]{0,1:T(8,128)S(1)} %fusion.32), channel_id=1, source_target_pairs={{0,8},{8,0},{16,24},{24,16},{1,9},{9,1},{17,25},{25,17},{2,10},{10... | collective-permute-start | bytes 294920 | tf_op jit(solution)/shard_map/ppermute | solution.py:11
  175.8 18.0 %collective-permute-start.31 = (f32[2,384,64]{1,2,0:T(8,128)S(1)}, f32[2,384,64]{1,2,0:T(8,128)S(1)}, u32[]{:S(2)}, u32[]{:S(2)}) collective-permute-start(f32[2,384,64]{1,2,0:T(8,128)S(1)} %pad_maximum_fusion.6), channel_id=1, source_target_pairs={{0,16},{8,24},{16,0},{24,8},{1,17},{9,25},{17,1},{25,9},{2,18},{10... | collective-permute-start | bytes 589832 | tf_op jit(solution)/shard_map/ppermute | solution.py:11
  179.3 19.0 %collective-permute-start.33 = (f32[2,384,64]{1,2,0:T(8,128)S(1)}, f32[2,384,64]{1,2,0:T(8,128)S(1)}, u32[]{:S(2)}, u32[]{:S(2)}) collective-permute-start(f32[2,384,64]{1,2,0:T(8,128)S(1)} %pad_maximum_fusion.7), channel_id=1, source_target_pairs={{0,16},{8,24},{16,0},{24,8},{1,17},{9,25},{17,1},{25,9},{2,18},{10... | collective-permute-start | bytes 589832 | tf_op jit(solution)/shard_map/ppermute | solution.py:11
  180.0 6.1 %collective-permute-start.26 = (f32[384,64]{0,1:T(8,128)S(1)}, f32[384,64]{0,1:T(8,128)S(1)}, u32[]{:S(2)}, u32[]{:S(2)}) collective-permute-start(f32[384,64]{0,1:T(8,128)S(1)} %add.231), channel_id=1, source_target_pairs={{0,16},{8,24},{16,0},{24,8},{1,17},{9,25},{17,1},{25,9},{2,18},{10... | collective-permute-start | bytes 294920 | tf_op jit(solution)/shard_map/ppermute | solution.py:11
  182.7 6.2 %collective-permute-start.16 = (f32[1,1,1,384,64]{3,4,2,1,0:T(8,128)S(1)}, f32[1,1,1,384,64]{3,4,2,1,0:T(8,128)S(1)}, u32[]{:S(2)}, u32[]{:S(2)}) collective-permute-start(f32[1,1,1,384,64]{3,4,2,1,0:T(8,128)S(1)} %add_bitcast_fusion.3), channel_id=1, source_target_pairs={{0,4},{1,5},{2,6},{3,7},{4,0},{5,1},{6,2},{7,3},{8,12},{9,13},{10,... | collective-permute-start | bytes 294920 | tf_op jit(solution)/shard_map/ppermute | solution.py:11
  189.0 5.7 %collective-permute-start.17 = (f32[2,1,1,384,64]{3,4,2,1,0:T(8,128)S(1)}, f32[2,1,1,384,64]{3,4,2,1,0:T(8,128)S(1)}, u32[]{:S(2)}, u32[]{:S(2)}) collective-permute-start(f32[2,1,1,384,64]{3,4,2,1,0:T(8,128)S(1)} %pad_maximum_fusion.4), channel_id=1, source_target_pairs={{0,2},{1,3},{2,0},{3,1},{4,6},{5,7},{6,4},{7,5},{8,10},{9,11},{10,... | collective-permute-start | bytes 589832 | tf_op jit(solution)/shard_map/ppermute | solution.py:11
  191.7 5.7 %collective-permute-start.28 = (f32[2,1,1,384,64]{3,4,2,1,0:T(8,128)S(1)}, f32[2,1,1,384,64]{3,4,2,1,0:T(8,128)S(1)}, u32[]{:S(2)}, u32[]{:S(2)}) collective-permute-start(f32[2,1,1,384,64]{3,4,2,1,0:T(8,128)S(1)} %pad_maximum_fusion.5), channel_id=1, source_target_pairs={{0,2},{1,3},{2,0},{3,1},{4,6},{5,7},{6,4},{7,5},{8,10},{9,11},{10,... | collective-permute-start | bytes 589832 | tf_op jit(solution)/shard_map/ppermute | solution.py:11
  199.7 17.1 %collective-permute-start.34 = (f32[1536,128]{1,0:T(8,128)}, f32[1536,128]{1,0:T(8,128)}, u32[]{:S(2)}, u32[]{:S(2)}) collective-permute-start(f32[1536,128]{1,0:T(8,128)} %bitcast.27), channel_id=1, source_target_pairs={{0,1},{1,0},{2,3},{3,2},{4,5},{5,4},{6,7},{7,6},{8,9},{9,8},{10,11... | collective-permute-start | bytes 2359304 | tf_op jit(solution)/shard_map/ppermute | solution.py:11
  (22 other events, 214.9 us)

commit v15 on v13

--- a/solution.py
+++ b/solution.py
@@ -96,10 +96,10 @@
     for chain in range(2):
         coef_d = probes_d[:, chain * quarter:(chain + 1) * quarter]
         for rnd in range(2):
-            coef_a = doubling_sum(
-                jnp.dot(chip_tile, coef_d, precision=high, preferred_element_type=jnp.float32),
-                "cols", 2, col_count,
-            )
+            coef_a = jnp.dot(chip_tile, coef_d, precision=high, preferred_element_type=jnp.float32)
+            for k in range(bits):
+                pairs = [(i, i ^ (2 << orders[i % 2][k])) for i in range(col_count)]
+                coef_a = coef_a + lax.ppermute(coef_a, "cols", pairs)
             coef_d = doubling_sum(
                 jnp.dot(chip_tile.T, coef_a, precision=high, preferred_element_type=jnp.float32),
                 "rows", 1, row_count,

time: 228 us -> 226 us (level)
  starting transfers between devices: 51.4 us -> 39.2 us
  waiting for transfers between devices: 80.9 us -> 91 us
    ppermute x33 -> x25, starting transfers between devices: 47 us -> 23.2 us  [exchange(): return lax.ppermute(x, axis, [(i, i ^ step) for i in range(count)])]
    ppermute x0 -> x8, waiting for transfers between devices: none -> 13.2 us  [shards(): coef_a = coef_a + lax.ppermute(coef_a, 'cols', pairs)]
    ppermute x0 -> x8, starting transfers between devices: none -> 11.5 us  [shards(): coef_a = coef_a + lax.ppermute(coef_a, 'cols', pairs)]
    ppermute x33 -> x25, waiting for transfers between devices: 59.2 us -> 56.2 us  [exchange(): return lax.ppermute(x, axis, [(i, i ^ step) for i in range(count)])]
  transfers between devices with their start and end apart: 35 -> 35, of which waited for: 21 -> 23; matrix products, arithmetic and copies ran while one was open for 21% -> 21% of each run, Pallas kernels for 0% -> 0%
where the time goes in v15:
time: 226 us
  waiting for transfers between devices  91 us (40%)
  matrix products  59 us (26%)
  starting transfers between devices  39.2 us (17%)
  local copies, waits for them, and re-layouts  17.8 us (8%)
  other arithmetic  17.5 us (8%)
    ppermute x25, waiting for transfers between devices, exchange(): return lax.ppermute(x, axis, [(i, i ^ step) for i in range(count)])  56.2 us
    dot_general x2, matrix products, partial_rows(): jnp.dot(columns.T, direct, precision=fast, preferred_element_type=jnp.flo...  32.6 us
    ppermute x25, starting transfers between devices, exchange(): return lax.ppermute(x, axis, [(i, i ^ step) for i in range(count)])  23.2 us
    ppermute x2, waiting for transfers between devices, shards(): strip = kept + lax.ppermute(sent, 'cols', pairs)  21.6 us
    ppermute x8, waiting for transfers between devices, shards(): coef_a = coef_a + lax.ppermute(coef_a, 'cols', pairs)  13.2 us
    ppermute x8, starting transfers between devices, shards(): coef_a = coef_a + lax.ppermute(coef_a, 'cols', pairs)  11.5 us
    dot_general x1, matrix products, shards(): jnp.dot(adjoint, full_a, precision=fast, preferred_element_type=jnp.float32)  10.7 us
    dot_general x1, matrix products, shards(): jnp.dot(direct, full_d, precision=fast, preferred_element_type=jnp.float32)  10.6 us
  transfers between devices with their start and end apart: 35, of which 23 were waited for; matrix products, arithmetic and copies ran while one was open for 21% of the time, Pallas kernels for 0%

profile of v15, /device:TPU:0, one launch (start us, length us, event | category | flops | bytes accessed | tf_op | source)
XLA Modules:
  0.0 225.6 jit_solution(7740956423967992085)
XLA Ops:
  0.7 16.3 %fusion.7 = f32[768,1536]{1,0:T(8,128)} fusion(f32[1536,1536]{1,0:T(8,128)} %param.3, f32[1536,1536]{1,0:T(8,128)} %param.4, s32[]{:T(128)S(6)} %select_n.270), kind=kOutput, calls=%fused_computation.5 | convolution fusion | flops 10872815616 | bytes 18874372 | tf_op jit(solution)/shard_map/dot_general | solution.py:47
  17.4 16.2 %fusion.4 = f32[768,1536]{1,0:T(8,128)} fusion(f32[1536,1536]{1,0:T(8,128)} %param.3, f32[1536,1536]{1,0:T(8,128)} %param.4, s32[]{:T(128)S(6)} %select_n.269), kind=kOutput, calls=%fused_computation.4 | convolution fusion | flops 10872815616 | bytes 18874372 | tf_op jit(solution)/shard_map/dot_general | solution.py:47
  33.7 4.8 %add.164 = f32[768,1536]{1,0:T(8,128)S(1)} add(f32[768,1536]{1,0:T(8,128)} %fusion.4, f32[768,1536]{1,0:T(8,128)} %collective-permute-done) | non-fusion elementwise | flops 1179648 | bytes 14155776 | tf_op jit(solution)/shard_map/add | solution.py:51
  41.7 2.6 %collective-permute-start.1 = (f32[2,192,768]{2,1,0:T(8,128)S(1)}, f32[2,192,768]{2,1,0:T(8,128)}, u32[]{:S(2)}, u32[]{:S(2)}) collective-permute-start(f32[2,192,768]{2,1,0:T(8,128)S(1)} %dynamic-slice_bitcast_fusion.1), channel_id=1, source_target_pairs={{0,8},{8,0},{16,24},{24,16},{1,9},{9,1},{17,25},{25,17},{2,10},{10... | collective-permute-start | bytes 3538952 | tf_op jit(solution)/shard_map/ppermute | solution.py:11
  44.3 2.4 %dynamic-slice_bitcast_fusion = f32[2,192,768]{2,1,0:T(8,128)} fusion(f32[2,2,192,768]{3,2,1,0:T(8,128)} %bitcast.61, s32[]{:T(128)S(6)} %select_n.276), kind=kLoop, calls=%fused_computation.19 | loop fusion | bytes 2359300 | tf_op jit(solution)/shard_map/jit(dynamic_index_in_dim)/squeeze | solution.py:65
  48.2 22.9 %collective-permute-done.1 = f32[2,192,768]{2,1,0:T(8,128)} collective-permute-done((f32[2,192,768]{2,1,0:T(8,128)S(1)}, f32[2,192,768]{2,1,0:T(8,128)}, u32[]{:S(2)}, u32[]{:S(2)}) %collective-permute-start.1) | collective-permute-done | bytes 1179680 | tf_op jit(solution)/shard_map/ppermute | solution.py:11
  79.5 8.7 %collective-permute-done.2 = f32[192,768]{1,0:T(8,128)} collective-permute-done((f32[192,768]{1,0:T(8,128)S(1)}, f32[192,768]{1,0:T(8,128)}, u32[]{:S(2)}, u32[]{:S(2)}) %collective-permute-start.2) | collective-permute-done | bytes 589856 | tf_op jit(solution)/shard_map/ppermute | solution.py:11
  89.3 4.0 %collective-permute-done.4 = f32[192,768]{1,0:T(8,128)} collective-permute-done((f32[192,768]{1,0:T(8,128)}, f32[192,768]{1,0:T(8,128)}, u32[]{:S(2)}, u32[]{:S(2)}) %collective-permute-start.4) | collective-permute-done | bytes 589856 | tf_op jit(solution)/shard_map/ppermute | solution.py:11
  95.6 2.2 reshape.37
  101.0 13.5 %collective-permute-done.5 = f32[192,2,384]{2,0,1:T(8,128)S(1)} collective-permute-done((f32[192,2,384]{2,0,1:T(8,128)S(1)}, f32[192,2,384]{2,0,1:T(8,128)S(1)}, u32[]{:S(2)}, u32[]{:S(2)}) %collective-permute-start.5) | collective-permute-done | bytes 589856 | tf_op jit(solution)/shard_map/ppermute | solution.py:88
  114.7 2.8 %collective-permute-start.6 = (f32[192,384]{1,0:T(8,128)S(1)}, f32[192,384]{1,0:T(8,128)S(1)}, u32[]{:S(2)}, u32[]{:S(2)}) collective-permute-start(f32[192,384]{1,0:T(8,128)S(1)} %select_bitcast_fusion), channel_id=1, source_target_pairs={{0,4},{1,3},{2,6},{3,1},{4,0},{5,7},{6,2},{7,5},{8,12},{9,11},{10,... | collective-permute-start | bytes 884744 | tf_op jit(solution)/shard_map/ppermute | solution.py:88
  117.4 8.1 %collective-permute-done.6 = f32[192,384]{1,0:T(8,128)S(1)} collective-permute-done((f32[192,384]{1,0:T(8,128)S(1)}, f32[192,384]{1,0:T(8,128)S(1)}, u32[]{:S(2)}, u32[]{:S(2)}) %collective-permute-start.6) | collective-permute-done | bytes 294944 | tf_op jit(solution)/shard_map/ppermute | solution.py:88
  131.1 3.1 %collective-permute-done.8 = f32[384,64]{0,1:T(8,128)S(1)} collective-permute-done((f32[384,64]{0,1:T(8,128)S(1)}, f32[384,64]{0,1:T(8,128)S(1)}, u32[]{:S(2)}, u32[]{:S(2)}) %collective-permute-start.8) | collective-permute-done | bytes 98336 | tf_op jit(solution)/shard_map/ppermute | solution.py:102
  136.1 2.9 %collective-permute-start.20 = (f32[384,64]{0,1:T(8,128)S(1)}, f32[384,64]{0,1:T(8,128)S(1)}, u32[]{:S(2)}, u32[]{:S(2)}) collective-permute-start(f32[384,64]{0,1:T(8,128)S(1)} %add.193), channel_id=1, source_target_pairs={{0,4},{1,3},{2,6},{3,1},{4,0},{5,7},{6,2},{7,5},{8,12},{9,11},{10,... | collective-permute-start | bytes 294920 | tf_op jit(solution)/shard_map/ppermute | solution.py:102
  144.0 2.0 collective-permute-done.10
  155.0 2.8 %collective-permute-done.12 = f32[384,64]{0,1:T(8,128)S(1)} collective-permute-done((f32[384,64]{0,1:T(8,128)S(1)}, f32[384,64]{0,1:T(8,128)S(1)}, u32[]{:S(2)}, u32[]{:S(2)}) %collective-permute-start.12) | collective-permute-done | bytes 98336 | tf_op jit(solution)/shard_map/ppermute | solution.py:102
  161.0 3.4 %collective-permute-done.13 = f32[384,64]{0,1:T(8,128)S(1)} collective-permute-done((f32[384,64]{0,1:T(8,128)S(1)}, f32[384,64]{0,1:T(8,128)S(1)}, u32[]{:S(2)}, u32[]{:S(2)}) %collective-permute-start.13) | collective-permute-done | bytes 98336 | tf_op jit(solution)/shard_map/ppermute | solution.py:102
  178.0 2.6 %collective-permute-done.26 = f32[384,64]{0,1:T(8,128)S(1)} collective-permute-done((f32[384,64]{0,1:T(8,128)S(1)}, f32[384,64]{0,1:T(8,128)S(1)}, u32[]{:S(2)}, u32[]{:S(2)}) %collective-permute-start.26) | collective-permute-done | bytes 98336 | tf_op jit(solution)/shard_map/ppermute | solution.py:11
  181.2 2.6 %collective-permute-done.16 = f32[1,1,1,384,64]{3,4,2,1,0:T(8,128)S(1)} collective-permute-done((f32[1,1,1,384,64]{3,4,2,1,0:T(8,128)S(1)}, f32[1,1,1,384,64]{3,4,2,1,0:T(8,128)S(1)}, u32[]{:S(2)}, u32[]{:S(2)}) %collective-permute-start.16) | collective-permute-done | bytes 98336 | tf_op jit(solution)/shard_map/ppermute | solution.py:11
  184.0 2.5 %collective-permute-done.27 = f32[1,1,1,384,64]{3,4,2,1,0:T(8,128)S(1)} collective-permute-done((f32[1,1,1,384,64]{3,4,2,1,0:T(8,128)S(1)}, f32[1,1,1,384,64]{3,4,2,1,0:T(8,128)S(1)}, u32[]{:S(2)}, u32[]{:S(2)}) %collective-permute-start.27) | collective-permute-done | bytes 98336 | tf_op jit(solution)/shard_map/ppermute | solution.py:11
  186.7 2.9 %collective-permute-done.17 = f32[2,1,1,384,64]{3,4,2,1,0:T(8,128)S(1)} collective-permute-done((f32[2,1,1,384,64]{3,4,2,1,0:T(8,128)S(1)}, f32[2,1,1,384,64]{3,4,2,1,0:T(8,128)S(1)}, u32[]{:S(2)}, u32[]{:S(2)}) %collective-permute-start.17) | collective-permute-done | bytes 196640 | tf_op jit(solution)/shard_map/ppermute | solution.py:11
  197.4 2.1 copy.19
  199.5 10.6 %fusion.10 = f32[1536,256]{0,1:T(8,128)S(1)} fusion(f32[1536,1536]{1,0:T(8,128)} %param.3, f32[192,8,2,128]{3,2,1,0:T(2,128)} %bitcast.66), kind=kOutput, calls=%fused_computation.8 | convolution fusion | flops 3624271872 | bytes 12582912 | tf_op jit(solution)/shard_map/dot_general | solution.py:132
  213.2 10.7 %fusion.11 = f32[1536,256]{0,1:T(8,128)S(1)} fusion(f32[1536,1536]{1,0:T(8,128)} %param.4, f32[1536,128]{1,0:T(8,128)S(1)} %get-tuple-element.11, f32[1536,128]{1,0:T(8,128)S(1)} %get-tuple-element.10), kind=kOutput, calls=%fused_computation.9 | convolution fusion | flops 3624665088 | bytes 12582912 | tf_op jit(solution)/shard_map/dot_general | solution.py:133
  (131 shorter events, 71.8 us)
Async XLA Ops:
  17.0 16.7 %collective-permute-start = (f32[768,1536]{1,0:T(8,128)}, f32[768,1536]{1,0:T(8,128)}, u32[]{:S(2)}, u32[]{:S(2)}) collective-permute-start(f32[768,1536]{1,0:T(8,128)} %fusion.7), channel_id=1, source_target_pairs={{0,1},{1,0},{2,3},{3,2},{4,5},{5,4},{6,7},{7,6},{8,9},{9,8},{10,11... | collective-permute-start | bytes 14155784 | tf_op jit(solution)/shard_map/ppermute | solution.py:11
  41.7 29.3 %collective-permute-start.1 = (f32[2,192,768]{2,1,0:T(8,128)S(1)}, f32[2,192,768]{2,1,0:T(8,128)}, u32[]{:S(2)}, u32[]{:S(2)}) collective-permute-start(f32[2,192,768]{2,1,0:T(8,128)S(1)} %dynamic-slice_bitcast_fusion.1), channel_id=1, source_target_pairs={{0,8},{8,0},{16,24},{24,16},{1,9},{9,1},{17,25},{25,17},{2,10},{10... | collective-permute-start | bytes 3538952 | tf_op jit(solution)/shard_map/ppermute | solution.py:11
  46.6 28.4 %collective-permute-start.3 = (f32[2,192,768]{2,1,0:T(8,128)}, f32[2,192,768]{2,1,0:T(8,128)}, u32[]{:S(2)}, u32[]{:S(2)}) collective-permute-start(f32[2,192,768]{2,1,0:T(8,128)} %dynamic-slice_bitcast_fusion), channel_id=1, source_target_pairs={{0,16},{8,24},{16,0},{24,8},{1,17},{9,25},{17,1},{25,9},{2,18},{10... | collective-permute-start | bytes 3538952 | tf_op jit(solution)/shard_map/ppermute | solution.py:11
  72.8 15.3 %collective-permute-start.2 = (f32[192,768]{1,0:T(8,128)S(1)}, f32[192,768]{1,0:T(8,128)}, u32[]{:S(2)}, u32[]{:S(2)}) collective-permute-start(f32[192,768]{1,0:T(8,128)S(1)} %dynamic-slice_bitcast_fusion.3), channel_id=1, source_target_pairs={{0,16},{8,24},{16,0},{24,8},{1,17},{9,25},{17,1},{25,9},{2,18},{10... | collective-permute-start | bytes 1769480 | tf_op jit(solution)/shard_map/ppermute | solution.py:11
  78.3 14.9 %collective-permute-start.4 = (f32[192,768]{1,0:T(8,128)}, f32[192,768]{1,0:T(8,128)}, u32[]{:S(2)}, u32[]{:S(2)}) collective-permute-start(f32[192,768]{1,0:T(8,128)} %dynamic-slice_bitcast_fusion.2), channel_id=1, source_target_pairs={{0,8},{8,0},{16,24},{24,16},{1,9},{9,1},{17,25},{25,17},{2,10},{10... | collective-permute-start | bytes 1769480 | tf_op jit(solution)/shard_map/ppermute | solution.py:11
  99.3 15.2 %collective-permute-start.5 = (f32[192,2,384]{2,0,1:T(8,128)S(1)}, f32[192,2,384]{2,0,1:T(8,128)S(1)}, u32[]{:S(2)}, u32[]{:S(2)}) collective-permute-start(f32[192,2,384]{2,0,1:T(8,128)S(1)} %bitcast_select_fusion), channel_id=1, source_target_pairs={{0,2},{1,5},{2,0},{3,7},{4,6},{5,1},{6,4},{7,3},{8,10},{9,13},{10,... | collective-permute-start | bytes 1769480 | tf_op jit(solution)/shard_map/ppermute | solution.py:88
  114.7 10.9 %collective-permute-start.6 = (f32[192,384]{1,0:T(8,128)S(1)}, f32[192,384]{1,0:T(8,128)S(1)}, u32[]{:S(2)}, u32[]{:S(2)}) collective-permute-start(f32[192,384]{1,0:T(8,128)S(1)} %select_bitcast_fusion), channel_id=1, source_target_pairs={{0,4},{1,3},{2,6},{3,1},{4,0},{5,7},{6,2},{7,5},{8,12},{9,11},{10,... | collective-permute-start | bytes 884744 | tf_op jit(solution)/shard_map/ppermute | solution.py:88
  128.1 6.1 %collective-permute-start.8 = (f32[384,64]{0,1:T(8,128)S(1)}, f32[384,64]{0,1:T(8,128)S(1)}, u32[]{:S(2)}, u32[]{:S(2)}) collective-permute-start(f32[384,64]{0,1:T(8,128)S(1)} %fusion.20), channel_id=1, source_target_pairs={{0,2},{1,5},{2,0},{3,7},{4,6},{5,1},{6,4},{7,3},{8,10},{9,13},{10,... | collective-permute-start | bytes 294920 | tf_op jit(solution)/shard_map/ppermute | solution.py:102
  129.8 6.3 %collective-permute-start.19 = (f32[384,64]{0,1:T(8,128)S(1)}, f32[384,64]{0,1:T(8,128)S(1)}, u32[]{:S(2)}, u32[]{:S(2)}) collective-permute-start(f32[384,64]{0,1:T(8,128)S(1)} %fusion.18), channel_id=1, source_target_pairs={{0,2},{1,5},{2,0},{3,7},{4,6},{5,1},{6,4},{7,3},{8,10},{9,13},{10,... | collective-permute-start | bytes 294920 | tf_op jit(solution)/shard_map/ppermute | solution.py:102
  134.3 5.8 %collective-permute-start.9 = (f32[384,64]{0,1:T(8,128)S(1)}, f32[384,64]{0,1:T(8,128)S(1)}, u32[]{:S(2)}, u32[]{:S(2)}) collective-permute-start(f32[384,64]{0,1:T(8,128)S(1)} %add.185), channel_id=1, source_target_pairs={{0,4},{1,3},{2,6},{3,1},{4,0},{5,7},{6,2},{7,5},{8,12},{9,11},{10,... | collective-permute-start | bytes 294920 | tf_op jit(solution)/shard_map/ppermute | solution.py:102
  136.1 6.2 %collective-permute-start.20 = (f32[384,64]{0,1:T(8,128)S(1)}, f32[384,64]{0,1:T(8,128)S(1)}, u32[]{:S(2)}, u32[]{:S(2)}) collective-permute-start(f32[384,64]{0,1:T(8,128)S(1)} %add.193), channel_id=1, source_target_pairs={{0,4},{1,3},{2,6},{3,1},{4,0},{5,7},{6,2},{7,5},{8,12},{9,11},{10,... | collective-permute-start | bytes 294920 | tf_op jit(solution)/shard_map/ppermute | solution.py:102
  151.6 6.1 %collective-permute-start.12 = (f32[384,64]{0,1:T(8,128)S(1)}, f32[384,64]{0,1:T(8,128)S(1)}, u32[]{:S(2)}, u32[]{:S(2)}) collective-permute-start(f32[384,64]{0,1:T(8,128)S(1)} %fusion.26), channel_id=1, source_target_pairs={{0,2},{1,5},{2,0},{3,7},{4,6},{5,1},{6,4},{7,3},{8,10},{9,13},{10,... | collective-permute-start | bytes 294920 | tf_op jit(solution)/shard_map/ppermute | solution.py:102
  153.6 6.0 %collective-permute-start.23 = (f32[384,64]{0,1:T(8,128)S(1)}, f32[384,64]{0,1:T(8,128)S(1)}, u32[]{:S(2)}, u32[]{:S(2)}) collective-permute-start(f32[384,64]{0,1:T(8,128)S(1)} %fusion.22), channel_id=1, source_target_pairs={{0,2},{1,5},{2,0},{3,7},{4,6},{5,1},{6,4},{7,3},{8,10},{9,13},{10,... | collective-permute-start | bytes 294920 | tf_op jit(solution)/shard_map/ppermute | solution.py:102
  157.8 6.6 %collective-permute-start.13 = (f32[384,64]{0,1:T(8,128)S(1)}, f32[384,64]{0,1:T(8,128)S(1)}, u32[]{:S(2)}, u32[]{:S(2)}) collective-permute-start(f32[384,64]{0,1:T(8,128)S(1)} %add.189), channel_id=1, source_target_pairs={{0,4},{1,3},{2,6},{3,1},{4,0},{5,7},{6,2},{7,5},{8,12},{9,11},{10,... | collective-permute-start | bytes 294920 | tf_op jit(solution)/shard_map/ppermute | solution.py:102
  159.6 6.9 %collective-permute-start.24 = (f32[384,64]{0,1:T(8,128)S(1)}, f32[384,64]{0,1:T(8,128)S(1)}, u32[]{:S(2)}, u32[]{:S(2)}) collective-permute-start(f32[384,64]{0,1:T(8,128)S(1)} %add.197), channel_id=1, source_target_pairs={{0,4},{1,3},{2,6},{3,1},{4,0},{5,7},{6,2},{7,5},{8,12},{9,11},{10,... | collective-permute-start | bytes 294920 | tf_op jit(solution)/shard_map/ppermute | solution.py:102
  164.4 6.3 %collective-permute-start.30 = (f32[1,384,64]{1,2,0:T(8,128)S(1)}, f32[1,384,64]{1,2,0:T(8,128)S(1)}, u32[]{:S(2)}, u32[]{:S(2)}) collective-permute-start(f32[1,384,64]{1,2,0:T(8,128)S(1)} %add_bitcast_fusion.3), channel_id=1, source_target_pairs={{0,8},{8,0},{16,24},{24,16},{1,9},{9,1},{17,25},{25,17},{2,10},{10... | collective-permute-start | bytes 294920 | tf_op jit(solution)/shard_map/ppermute | solution.py:11
  166.5 7.3 %collective-permute-start.32 = (f32[1,384,64]{1,2,0:T(8,128)S(1)}, f32[1,384,64]{1,2,0:T(8,128)S(1)}, u32[]{:S(2)}, u32[]{:S(2)}) collective-permute-start(f32[1,384,64]{1,2,0:T(8,128)S(1)} %add_bitcast_fusion.2), channel_id=1, source_target_pairs={{0,8},{8,0},{16,24},{24,16},{1,9},{9,1},{17,25},{25,17},{2,10},{10... | collective-permute-start | bytes 294920 | tf_op jit(solution)/shard_map/ppermute | solution.py:11
  170.7 16.0 %collective-permute-start.31 = (f32[2,384,64]{1,2,0:T(8,128)S(1)}, f32[2,384,64]{1,2,0:T(8,128)S(1)}, u32[]{:S(2)}, u32[]{:S(2)}) collective-permute-start(f32[2,384,64]{1,2,0:T(8,128)S(1)} %pad_maximum_fusion.6), channel_id=1, source_target_pairs={{0,16},{8,24},{16,0},{24,8},{1,17},{9,25},{17,1},{25,9},{2,18},{10... | collective-permute-start | bytes 589832 | tf_op jit(solution)/shard_map/ppermute | solution.py:11
  173.9 19.4 %collective-permute-start.33 = (f32[2,384,64]{1,2,0:T(8,128)S(1)}, f32[2,384,64]{1,2,0:T(8,128)S(1)}, u32[]{:S(2)}, u32[]{:S(2)}) collective-permute-start(f32[2,384,64]{1,2,0:T(8,128)S(1)} %pad_maximum_fusion.7), channel_id=1, source_target_pairs={{0,16},{8,24},{16,0},{24,8},{1,17},{9,25},{17,1},{25,9},{2,18},{10... | collective-permute-start | bytes 589832 | tf_op jit(solution)/shard_map/ppermute | solution.py:11
  177.5 6.3 %collective-permute-start.16 = (f32[1,1,1,384,64]{3,4,2,1,0:T(8,128)S(1)}, f32[1,1,1,384,64]{3,4,2,1,0:T(8,128)S(1)}, u32[]{:S(2)}, u32[]{:S(2)}) collective-permute-start(f32[1,1,1,384,64]{3,4,2,1,0:T(8,128)S(1)} %add_bitcast_fusion.1), channel_id=1, source_target_pairs={{0,4},{1,5},{2,6},{3,7},{4,0},{5,1},{6,2},{7,3},{8,12},{9,13},{10,... | collective-permute-start | bytes 294920 | tf_op jit(solution)/shard_map/ppermute | solution.py:11
  180.7 5.9 %collective-permute-start.27 = (f32[1,1,1,384,64]{3,4,2,1,0:T(8,128)S(1)}, f32[1,1,1,384,64]{3,4,2,1,0:T(8,128)S(1)}, u32[]{:S(2)}, u32[]{:S(2)}) collective-permute-start(f32[1,1,1,384,64]{3,4,2,1,0:T(8,128)S(1)} %add_bitcast_fusion), channel_id=1, source_target_pairs={{0,4},{1,5},{2,6},{3,7},{4,0},{5,1},{6,2},{7,3},{8,12},{9,13},{10,... | collective-permute-start | bytes 294920 | tf_op jit(solution)/shard_map/ppermute | solution.py:11
  183.9 5.7 %collective-permute-start.17 = (f32[2,1,1,384,64]{3,4,2,1,0:T(8,128)S(1)}, f32[2,1,1,384,64]{3,4,2,1,0:T(8,128)S(1)}, u32[]{:S(2)}, u32[]{:S(2)}) collective-permute-start(f32[2,1,1,384,64]{3,4,2,1,0:T(8,128)S(1)} %pad_maximum_fusion.4), channel_id=1, source_target_pairs={{0,2},{1,3},{2,0},{3,1},{4,6},{5,7},{6,4},{7,5},{8,10},{9,11},{10,... | collective-permute-start | bytes 589832 | tf_op jit(solution)/shard_map/ppermute | solution.py:11
  186.6 5.7 %collective-permute-start.28 = (f32[2,1,1,384,64]{3,4,2,1,0:T(8,128)S(1)}, f32[2,1,1,384,64]{3,4,2,1,0:T(8,128)S(1)}, u32[]{:S(2)}, u32[]{:S(2)}) collective-permute-start(f32[2,1,1,384,64]{3,4,2,1,0:T(8,128)S(1)} %pad_maximum_fusion.5), channel_id=1, source_target_pairs={{0,2},{1,3},{2,0},{3,1},{4,6},{5,7},{6,4},{7,5},{8,10},{9,11},{10,... | collective-permute-start | bytes 589832 | tf_op jit(solution)/shard_map/ppermute | solution.py:11
  194.6 17.1 %collective-permute-start.34 = (f32[1536,128]{1,0:T(8,128)}, f32[1536,128]{1,0:T(8,128)}, u32[]{:S(2)}, u32[]{:S(2)}) collective-permute-start(f32[1536,128]{1,0:T(8,128)} %bitcast.25), channel_id=1, source_target_pairs={{0,1},{1,0},{2,3},{3,2},{4,5},{5,4},{6,7},{7,6},{8,9},{9,8},{10,11... | collective-permute-start | bytes 2359304 | tf_op jit(solution)/shard_map/ppermute | solution.py:11
  (20 other events, 227.1 us)

commit v16 on v15

--- a/solution.py
+++ b/solution.py
@@ -100,10 +100,14 @@
             for k in range(bits):
                 pairs = [(i, i ^ (2 << orders[i % 2][k])) for i in range(col_count)]
                 coef_a = coef_a + lax.ppermute(coef_a, "cols", pairs)
-            coef_d = doubling_sum(
-                jnp.dot(chip_tile.T, coef_a, precision=high, preferred_element_type=jnp.float32),
-                "rows", 1, row_count,
-            )
+            coef_d = jnp.dot(chip_tile.T, coef_a, precision=high, preferred_element_type=jnp.float32)
+            for k in range(row_bits):
+                pairs = []
+                for i in range(row_count * col_count):
+                    r, c = divmod(i, col_count)
+                    bit = row_bits - 1 - k if c % 2 else k
+                    pairs.append((i, (r ^ (1 << bit)) * col_count + c))
+                coef_d = coef_d + lax.ppermute(coef_d, ("rows", "cols"), pairs)
         gathered = coef_a[None]
         step = 1
         while step < row_count:

time: 226 us -> 227 us (level)
  starting transfers between devices: 39.2 us -> 42.4 us
    ppermute x0 -> x8, starting transfers between devices: none -> 10.4 us  [shards(): coef_d = coef_d + lax.ppermute(coef_d, ('rows', 'cols'), pairs)]
    ppermute x25 -> x17, starting transfers between devices: 23.2 us -> 13.6 us  [exchange(): return lax.ppermute(x, axis, [(i, i ^ step) for i in range(count)])]
    ppermute x25 -> x17, waiting for transfers between devices: 56.2 us -> 48.2 us  [exchange(): return lax.ppermute(x, axis, [(i, i ^ step) for i in range(count)])]
    ppermute x0 -> x8, waiting for transfers between devices: none -> 7.29 us  [shards(): coef_d = coef_d + lax.ppermute(coef_d, ('rows', 'cols'), pairs)]
    ppermute x8, starting transfers between devices: 11.5 us -> 14 us  [shards(): coef_a = coef_a + lax.ppermute(coef_a, 'cols', pairs)]
  transfers between devices with their start and end apart: 35 -> 35, of which waited for: 23 -> 24; matrix products, arithmetic and copies ran while one was open for 21% -> 21% of each run, Pallas kernels for 0% -> 0%
where the time goes in v16:
time: 227 us
  waiting for transfers between devices  88.8 us (39%)
  matrix products  59 us (26%)
  starting transfers between devices  42.4 us (19%)
  local copies, waits for them, and re-layouts  17.8 us (8%)
  other arithmetic  17.5 us (8%)
    ppermute x17, waiting for transfers between devices, exchange(): return lax.ppermute(x, axis, [(i, i ^ step) for i in range(count)])  48.2 us
    dot_general x2, matrix products, partial_rows(): jnp.dot(columns.T, direct, precision=fast, preferred_element_type=jnp.flo...  32.6 us
    ppermute x2, waiting for transfers between devices, shards(): strip = kept + lax.ppermute(sent, 'cols', pairs)  21.6 us
    ppermute x8, starting transfers between devices, shards(): coef_a = coef_a + lax.ppermute(coef_a, 'cols', pairs)  14 us
    ppermute x17, starting transfers between devices, exchange(): return lax.ppermute(x, axis, [(i, i ^ step) for i in range(count)])  13.6 us
    ppermute x8, waiting for transfers between devices, shards(): coef_a = coef_a + lax.ppermute(coef_a, 'cols', pairs)  11.6 us
    dot_general x1, matrix products, shards(): jnp.dot(adjoint, full_a, precision=fast, preferred_element_type=jnp.float32)  10.7 us
    dot_general x1, matrix products, shards(): jnp.dot(direct, full_d, precision=fast, preferred_element_type=jnp.float32)  10.6 us
  transfers between devices with their start and end apart: 35, of which 24 were waited for; matrix products, arithmetic and copies ran while one was open for 21% of the time, Pallas kernels for 0%

profile of v16, /device:TPU:0, one launch (start us, length us, event | category | flops | bytes accessed | tf_op | source)
XLA Modules:
  0.0 226.5 jit_solution(17085582477596249356)
XLA Ops:
  0.7 16.3 %fusion.7 = f32[768,1536]{1,0:T(8,128)} fusion(f32[1536,1536]{1,0:T(8,128)} %param.3, f32[1536,1536]{1,0:T(8,128)} %param.4, s32[]{:T(128)S(6)} %select_n.270), kind=kOutput, calls=%fused_computation.5 | convolution fusion | flops 10872815616 | bytes 18874372 | tf_op jit(solution)/shard_map/dot_general | solution.py:47
  17.4 16.2 %fusion.4 = f32[768,1536]{1,0:T(8,128)} fusion(f32[1536,1536]{1,0:T(8,128)} %param.3, f32[1536,1536]{1,0:T(8,128)} %param.4, s32[]{:T(128)S(6)} %select_n.269), kind=kOutput, calls=%fused_computation.4 | convolution fusion | flops 10872815616 | bytes 18874372 | tf_op jit(solution)/shard_map/dot_general | solution.py:47
  33.7 4.8 %add.164 = f32[768,1536]{1,0:T(8,128)S(1)} add(f32[768,1536]{1,0:T(8,128)} %fusion.4, f32[768,1536]{1,0:T(8,128)} %collective-permute-done) | non-fusion elementwise | flops 1179648 | bytes 14155776 | tf_op jit(solution)/shard_map/add | solution.py:51
  41.7 2.6 %collective-permute-start.1 = (f32[2,192,768]{2,1,0:T(8,128)S(1)}, f32[2,192,768]{2,1,0:T(8,128)}, u32[]{:S(2)}, u32[]{:S(2)}) collective-permute-start(f32[2,192,768]{2,1,0:T(8,128)S(1)} %dynamic-slice_bitcast_fusion.1), channel_id=1, source_target_pairs={{0,8},{8,0},{16,24},{24,16},{1,9},{9,1},{17,25},{25,17},{2,10},{10... | collective-permute-start | bytes 3538952 | tf_op jit(solution)/shard_map/ppermute | solution.py:11
  44.3 2.4 %dynamic-slice_bitcast_fusion = f32[2,192,768]{2,1,0:T(8,128)} fusion(f32[2,2,192,768]{3,2,1,0:T(8,128)} %bitcast.61, s32[]{:T(128)S(6)} %select_n.276), kind=kLoop, calls=%fused_computation.19 | loop fusion | bytes 2359300 | tf_op jit(solution)/shard_map/jit(dynamic_index_in_dim)/squeeze | solution.py:65
  48.2 22.9 %collective-permute-done.1 = f32[2,192,768]{2,1,0:T(8,128)} collective-permute-done((f32[2,192,768]{2,1,0:T(8,128)S(1)}, f32[2,192,768]{2,1,0:T(8,128)}, u32[]{:S(2)}, u32[]{:S(2)}) %collective-permute-start.1) | collective-permute-done | bytes 1179680 | tf_op jit(solution)/shard_map/ppermute | solution.py:11
  79.5 8.7 %collective-permute-done.2 = f32[192,768]{1,0:T(8,128)} collective-permute-done((f32[192,768]{1,0:T(8,128)S(1)}, f32[192,768]{1,0:T(8,128)}, u32[]{:S(2)}, u32[]{:S(2)}) %collective-permute-start.2) | collective-permute-done | bytes 589856 | tf_op jit(solution)/shard_map/ppermute | solution.py:11
  89.3 4.0 %collective-permute-done.4 = f32[192,768]{1,0:T(8,128)} collective-permute-done((f32[192,768]{1,0:T(8,128)}, f32[192,768]{1,0:T(8,128)}, u32[]{:S(2)}, u32[]{:S(2)}) %collective-permute-start.4) | collective-permute-done | bytes 589856 | tf_op jit(solution)/shard_map/ppermute | solution.py:11
  95.6 2.2 reshape.37
  101.0 13.5 %collective-permute-done.5 = f32[192,2,384]{2,0,1:T(8,128)S(1)} collective-permute-done((f32[192,2,384]{2,0,1:T(8,128)S(1)}, f32[192,2,384]{2,0,1:T(8,128)S(1)}, u32[]{:S(2)}, u32[]{:S(2)}) %collective-permute-start.5) | collective-permute-done | bytes 589856 | tf_op jit(solution)/shard_map/ppermute | solution.py:88
  114.7 2.8 %collective-permute-start.6 = (f32[192,384]{1,0:T(8,128)S(1)}, f32[192,384]{1,0:T(8,128)S(1)}, u32[]{:S(2)}, u32[]{:S(2)}) collective-permute-start(f32[192,384]{1,0:T(8,128)S(1)} %select_bitcast_fusion), channel_id=1, source_target_pairs={{0,4},{1,3},{2,6},{3,1},{4,0},{5,7},{6,2},{7,5},{8,12},{9,11},{10,... | collective-permute-start | bytes 884744 | tf_op jit(solution)/shard_map/ppermute | solution.py:88
  117.4 8.1 %collective-permute-done.6 = f32[192,384]{1,0:T(8,128)S(1)} collective-permute-done((f32[192,384]{1,0:T(8,128)S(1)}, f32[192,384]{1,0:T(8,128)S(1)}, u32[]{:S(2)}, u32[]{:S(2)}) %collective-permute-start.6) | collective-permute-done | bytes 294944 | tf_op jit(solution)/shard_map/ppermute | solution.py:88
  131.1 3.1 %collective-permute-done.8 = f32[384,64]{0,1:T(8,128)S(1)} collective-permute-done((f32[384,64]{0,1:T(8,128)S(1)}, f32[384,64]{0,1:T(8,128)S(1)}, u32[]{:S(2)}, u32[]{:S(2)}) %collective-permute-start.8) | collective-permute-done | bytes 98336 | tf_op jit(solution)/shard_map/ppermute | solution.py:102
  136.1 2.9 %collective-permute-start.20 = (f32[384,64]{0,1:T(8,128)S(1)}, f32[384,64]{0,1:T(8,128)S(1)}, u32[]{:S(2)}, u32[]{:S(2)}) collective-permute-start(f32[384,64]{0,1:T(8,128)S(1)} %add.193), channel_id=1, source_target_pairs={{0,4},{1,3},{2,6},{3,1},{4,0},{5,7},{6,2},{7,5},{8,12},{9,11},{10,... | collective-permute-start | bytes 294920 | tf_op jit(solution)/shard_map/ppermute | solution.py:102
  150.6 3.0 %collective-permute-start.12 = (f32[384,64]{0,1:T(8,128)S(1)}, f32[384,64]{0,1:T(8,128)S(1)}, u32[]{:S(2)}, u32[]{:S(2)}) collective-permute-start(f32[384,64]{0,1:T(8,128)S(1)} %fusion.26), channel_id=1, source_target_pairs={{0,2},{1,5},{2,0},{3,7},{4,6},{5,1},{6,4},{7,3},{8,10},{9,13},{10,... | collective-permute-start | bytes 294920 | tf_op jit(solution)/shard_map/ppermute | solution.py:102
  163.5 2.7 %collective-permute-done.24 = f32[384,64]{0,1:T(8,128)S(1)} collective-permute-done((f32[384,64]{0,1:T(8,128)S(1)}, f32[384,64]{0,1:T(8,128)S(1)}, u32[]{:S(2)}, u32[]{:S(2)}) %collective-permute-start.24) | collective-permute-done | bytes 98336 | tf_op jit(solution)/shard_map/ppermute | solution.py:102
  169.9 2.2 collective-permute-start.31
  178.3 2.7 %collective-permute-done.26 = f32[384,64]{0,1:T(8,128)S(1)} collective-permute-done((f32[384,64]{0,1:T(8,128)S(1)}, f32[384,64]{0,1:T(8,128)S(1)}, u32[]{:S(2)}, u32[]{:S(2)}) %collective-permute-start.26) | collective-permute-done | bytes 98336 | tf_op jit(solution)/shard_map/ppermute | solution.py:110
  181.4 2.6 %collective-permute-done.16 = f32[1,1,1,384,64]{3,4,2,1,0:T(8,128)S(1)} collective-permute-done((f32[1,1,1,384,64]{3,4,2,1,0:T(8,128)S(1)}, f32[1,1,1,384,64]{3,4,2,1,0:T(8,128)S(1)}, u32[]{:S(2)}, u32[]{:S(2)}) %collective-permute-start.16) | collective-permute-done | bytes 98336 | tf_op jit(solution)/shard_map/ppermute | solution.py:11
  184.1 3.4 %collective-permute-done.27 = f32[1,1,1,384,64]{3,4,2,1,0:T(8,128)S(1)} collective-permute-done((f32[1,1,1,384,64]{3,4,2,1,0:T(8,128)S(1)}, f32[1,1,1,384,64]{3,4,2,1,0:T(8,128)S(1)}, u32[]{:S(2)}, u32[]{:S(2)}) %collective-permute-start.27) | collective-permute-done | bytes 98336 | tf_op jit(solution)/shard_map/ppermute | solution.py:11
  187.7 2.1 collective-permute-done.17
  190.6 2.7 %collective-permute-done.28 = f32[2,1,1,384,64]{3,4,2,1,0:T(8,128)S(1)} collective-permute-done((f32[2,1,1,384,64]{3,4,2,1,0:T(8,128)S(1)}, f32[2,1,1,384,64]{3,4,2,1,0:T(8,128)S(1)}, u32[]{:S(2)}, u32[]{:S(2)}) %collective-permute-start.28) | collective-permute-done | bytes 196640 | tf_op jit(solution)/shard_map/ppermute | solution.py:11
  200.5 10.6 %fusion.10 = f32[1536,256]{0,1:T(8,128)S(1)} fusion(f32[1536,1536]{1,0:T(8,128)} %param.3, f32[192,8,2,128]{3,2,1,0:T(2,128)} %bitcast.66), kind=kOutput, calls=%fused_computation.8 | convolution fusion | flops 3624271872 | bytes 12582912 | tf_op jit(solution)/shard_map/dot_general | solution.py:136
  214.2 10.7 %fusion.11 = f32[1536,256]{0,1:T(8,128)S(1)} fusion(f32[1536,1536]{1,0:T(8,128)} %param.4, f32[1536,128]{1,0:T(8,128)S(1)} %get-tuple-element.11, f32[1536,128]{1,0:T(8,128)S(1)} %get-tuple-element.10), kind=kOutput, calls=%fused_computation.9 | convolution fusion | flops 3624665088 | bytes 12582912 | tf_op jit(solution)/shard_map/dot_general | solution.py:137
  (131 shorter events, 72.4 us)
Async XLA Ops:
  17.0 16.7 %collective-permute-start = (f32[768,1536]{1,0:T(8,128)}, f32[768,1536]{1,0:T(8,128)}, u32[]{:S(2)}, u32[]{:S(2)}) collective-permute-start(f32[768,1536]{1,0:T(8,128)} %fusion.7), channel_id=1, source_target_pairs={{0,1},{1,0},{2,3},{3,2},{4,5},{5,4},{6,7},{7,6},{8,9},{9,8},{10,11... | collective-permute-start | bytes 14155784 | tf_op jit(solution)/shard_map/ppermute | solution.py:11
  41.7 29.3 %collective-permute-start.1 = (f32[2,192,768]{2,1,0:T(8,128)S(1)}, f32[2,192,768]{2,1,0:T(8,128)}, u32[]{:S(2)}, u32[]{:S(2)}) collective-permute-start(f32[2,192,768]{2,1,0:T(8,128)S(1)} %dynamic-slice_bitcast_fusion.1), channel_id=1, source_target_pairs={{0,8},{8,0},{16,24},{24,16},{1,9},{9,1},{17,25},{25,17},{2,10},{10... | collective-permute-start | bytes 3538952 | tf_op jit(solution)/shard_map/ppermute | solution.py:11
  46.6 28.4 %collective-permute-start.3 = (f32[2,192,768]{2,1,0:T(8,128)}, f32[2,192,768]{2,1,0:T(8,128)}, u32[]{:S(2)}, u32[]{:S(2)}) collective-permute-start(f32[2,192,768]{2,1,0:T(8,128)} %dynamic-slice_bitcast_fusion), channel_id=1, source_target_pairs={{0,16},{8,24},{16,0},{24,8},{1,17},{9,25},{17,1},{25,9},{2,18},{10... | collective-permute-start | bytes 3538952 | tf_op jit(solution)/shard_map/ppermute | solution.py:11
  72.8 15.3 %collective-permute-start.2 = (f32[192,768]{1,0:T(8,128)S(1)}, f32[192,768]{1,0:T(8,128)}, u32[]{:S(2)}, u32[]{:S(2)}) collective-permute-start(f32[192,768]{1,0:T(8,128)S(1)} %dynamic-slice_bitcast_fusion.3), channel_id=1, source_target_pairs={{0,16},{8,24},{16,0},{24,8},{1,17},{9,25},{17,1},{25,9},{2,18},{10... | collective-permute-start | bytes 1769480 | tf_op jit(solution)/shard_map/ppermute | solution.py:11
  78.3 14.9 %collective-permute-start.4 = (f32[192,768]{1,0:T(8,128)}, f32[192,768]{1,0:T(8,128)}, u32[]{:S(2)}, u32[]{:S(2)}) collective-permute-start(f32[192,768]{1,0:T(8,128)} %dynamic-slice_bitcast_fusion.2), channel_id=1, source_target_pairs={{0,8},{8,0},{16,24},{24,16},{1,9},{9,1},{17,25},{25,17},{2,10},{10... | collective-permute-start | bytes 1769480 | tf_op jit(solution)/shard_map/ppermute | solution.py:11
  99.3 15.2 %collective-permute-start.5 = (f32[192,2,384]{2,0,1:T(8,128)S(1)}, f32[192,2,384]{2,0,1:T(8,128)S(1)}, u32[]{:S(2)}, u32[]{:S(2)}) collective-permute-start(f32[192,2,384]{2,0,1:T(8,128)S(1)} %bitcast_select_fusion), channel_id=1, source_target_pairs={{0,2},{1,5},{2,0},{3,7},{4,6},{5,1},{6,4},{7,3},{8,10},{9,13},{10,... | collective-permute-start | bytes 1769480 | tf_op jit(solution)/shard_map/ppermute | solution.py:88
  114.7 10.9 %collective-permute-start.6 = (f32[192,384]{1,0:T(8,128)S(1)}, f32[192,384]{1,0:T(8,128)S(1)}, u32[]{:S(2)}, u32[]{:S(2)}) collective-permute-start(f32[192,384]{1,0:T(8,128)S(1)} %select_bitcast_fusion), channel_id=1, source_target_pairs={{0,4},{1,3},{2,6},{3,1},{4,0},{5,7},{6,2},{7,5},{8,12},{9,11},{10,... | collective-permute-start | bytes 884744 | tf_op jit(solution)/shard_map/ppermute | solution.py:88
  128.1 6.1 %collective-permute-start.8 = (f32[384,64]{0,1:T(8,128)S(1)}, f32[384,64]{0,1:T(8,128)S(1)}, u32[]{:S(2)}, u32[]{:S(2)}) collective-permute-start(f32[384,64]{0,1:T(8,128)S(1)} %fusion.20), channel_id=1, source_target_pairs={{0,2},{1,5},{2,0},{3,7},{4,6},{5,1},{6,4},{7,3},{8,10},{9,13},{10,... | collective-permute-start | bytes 294920 | tf_op jit(solution)/shard_map/ppermute | solution.py:102
  129.8 6.3 %collective-permute-start.19 = (f32[384,64]{0,1:T(8,128)S(1)}, f32[384,64]{0,1:T(8,128)S(1)}, u32[]{:S(2)}, u32[]{:S(2)}) collective-permute-start(f32[384,64]{0,1:T(8,128)S(1)} %fusion.18), channel_id=1, source_target_pairs={{0,2},{1,5},{2,0},{3,7},{4,6},{5,1},{6,4},{7,3},{8,10},{9,13},{10,... | collective-permute-start | bytes 294920 | tf_op jit(solution)/shard_map/ppermute | solution.py:102
  134.3 5.8 %collective-permute-start.9 = (f32[384,64]{0,1:T(8,128)S(1)}, f32[384,64]{0,1:T(8,128)S(1)}, u32[]{:S(2)}, u32[]{:S(2)}) collective-permute-start(f32[384,64]{0,1:T(8,128)S(1)} %add.185), channel_id=1, source_target_pairs={{0,4},{1,3},{2,6},{3,1},{4,0},{5,7},{6,2},{7,5},{8,12},{9,11},{10,... | collective-permute-start | bytes 294920 | tf_op jit(solution)/shard_map/ppermute | solution.py:102
  136.1 6.2 %collective-permute-start.20 = (f32[384,64]{0,1:T(8,128)S(1)}, f32[384,64]{0,1:T(8,128)S(1)}, u32[]{:S(2)}, u32[]{:S(2)}) collective-permute-start(f32[384,64]{0,1:T(8,128)S(1)} %add.193), channel_id=1, source_target_pairs={{0,4},{1,3},{2,6},{3,1},{4,0},{5,7},{6,2},{7,5},{8,12},{9,11},{10,... | collective-permute-start | bytes 294920 | tf_op jit(solution)/shard_map/ppermute | solution.py:102
  147.9 5.7 %collective-permute-start.22 = (f32[384,64]{0,1:T(8,128)S(1)}, f32[384,64]{0,1:T(8,128)S(1)}, u32[]{:S(2)}, u32[]{:S(2)}) collective-permute-start(f32[384,64]{0,1:T(8,128)S(1)} %add.195), channel_id=1, source_target_pairs={{0,16},{1,9},{2,18},{3,11},{4,20},{5,13},{6,22},{7,15},{8,24},{9,1... | collective-permute-start | bytes 294920 | tf_op jit(solution)/shard_map/ppermute | solution.py:110
  150.6 6.5 %collective-permute-start.12 = (f32[384,64]{0,1:T(8,128)S(1)}, f32[384,64]{0,1:T(8,128)S(1)}, u32[]{:S(2)}, u32[]{:S(2)}) collective-permute-start(f32[384,64]{0,1:T(8,128)S(1)} %fusion.26), channel_id=1, source_target_pairs={{0,2},{1,5},{2,0},{3,7},{4,6},{5,1},{6,4},{7,3},{8,10},{9,13},{10,... | collective-permute-start | bytes 294920 | tf_op jit(solution)/shard_map/ppermute | solution.py:102
  159.6 6.6 %collective-permute-start.24 = (f32[384,64]{0,1:T(8,128)S(1)}, f32[384,64]{0,1:T(8,128)S(1)}, u32[]{:S(2)}, u32[]{:S(2)}) collective-permute-start(f32[384,64]{0,1:T(8,128)S(1)} %add.197), channel_id=1, source_target_pairs={{0,4},{1,3},{2,6},{3,1},{4,0},{5,7},{6,2},{7,5},{8,12},{9,11},{10,... | collective-permute-start | bytes 294920 | tf_op jit(solution)/shard_map/ppermute | solution.py:102
  162.8 7.1 %collective-permute-start.30 = (f32[1,384,64]{1,2,0:T(8,128)S(1)}, f32[1,384,64]{1,2,0:T(8,128)S(1)}, u32[]{:S(2)}, u32[]{:S(2)}) collective-permute-start(f32[1,384,64]{1,2,0:T(8,128)S(1)} %add_bitcast_fusion.3), channel_id=1, source_target_pairs={{0,8},{8,0},{16,24},{24,16},{1,9},{9,1},{17,25},{25,17},{2,10},{10... | collective-permute-start | bytes 294920 | tf_op jit(solution)/shard_map/ppermute | solution.py:11
  166.2 7.9 %collective-permute-start.32 = (f32[1,384,64]{1,2,0:T(8,128)S(1)}, f32[1,384,64]{1,2,0:T(8,128)S(1)}, u32[]{:S(2)}, u32[]{:S(2)}) collective-permute-start(f32[1,384,64]{1,2,0:T(8,128)S(1)} %add_bitcast_fusion.2), channel_id=1, source_target_pairs={{0,8},{8,0},{16,24},{24,16},{1,9},{9,1},{17,25},{25,17},{2,10},{10... | collective-permute-start | bytes 294920 | tf_op jit(solution)/shard_map/ppermute | solution.py:11
  169.9 17.8 %collective-permute-start.31 = (f32[2,384,64]{1,2,0:T(8,128)S(1)}, f32[2,384,64]{1,2,0:T(8,128)S(1)}, u32[]{:S(2)}, u32[]{:S(2)}) collective-permute-start(f32[2,384,64]{1,2,0:T(8,128)S(1)} %pad_maximum_fusion.6), channel_id=1, source_target_pairs={{0,16},{8,24},{16,0},{24,8},{1,17},{9,25},{17,1},{25,9},{2,18},{10... | collective-permute-start | bytes 589832 | tf_op jit(solution)/shard_map/ppermute | solution.py:11
  174.2 20.0 %collective-permute-start.33 = (f32[2,384,64]{1,2,0:T(8,128)S(1)}, f32[2,384,64]{1,2,0:T(8,128)S(1)}, u32[]{:S(2)}, u32[]{:S(2)}) collective-permute-start(f32[2,384,64]{1,2,0:T(8,128)S(1)} %pad_maximum_fusion.7), channel_id=1, source_target_pairs={{0,16},{8,24},{16,0},{24,8},{1,17},{9,25},{17,1},{25,9},{2,18},{10... | collective-permute-start | bytes 589832 | tf_op jit(solution)/shard_map/ppermute | solution.py:11
  174.9 6.1 %collective-permute-start.26 = (f32[384,64]{0,1:T(8,128)S(1)}, f32[384,64]{0,1:T(8,128)S(1)}, u32[]{:S(2)}, u32[]{:S(2)}) collective-permute-start(f32[384,64]{0,1:T(8,128)S(1)} %add.199), channel_id=1, source_target_pairs={{0,16},{1,9},{2,18},{3,11},{4,20},{5,13},{6,22},{7,15},{8,24},{9,1... | collective-permute-start | bytes 294920 | tf_op jit(solution)/shard_map/ppermute | solution.py:110
  177.4 6.6 %collective-permute-start.16 = (f32[1,1,1,384,64]{3,4,2,1,0:T(8,128)S(1)}, f32[1,1,1,384,64]{3,4,2,1,0:T(8,128)S(1)}, u32[]{:S(2)}, u32[]{:S(2)}) collective-permute-start(f32[1,1,1,384,64]{3,4,2,1,0:T(8,128)S(1)} %add_bitcast_fusion.1), channel_id=1, source_target_pairs={{0,4},{1,5},{2,6},{3,7},{4,0},{5,1},{6,2},{7,3},{8,12},{9,13},{10,... | collective-permute-start | bytes 294920 | tf_op jit(solution)/shard_map/ppermute | solution.py:11
  181.0 6.5 %collective-permute-start.27 = (f32[1,1,1,384,64]{3,4,2,1,0:T(8,128)S(1)}, f32[1,1,1,384,64]{3,4,2,1,0:T(8,128)S(1)}, u32[]{:S(2)}, u32[]{:S(2)}) collective-permute-start(f32[1,1,1,384,64]{3,4,2,1,0:T(8,128)S(1)} %add_bitcast_fusion), channel_id=1, source_target_pairs={{0,4},{1,5},{2,6},{3,7},{4,0},{5,1},{6,2},{7,3},{8,12},{9,13},{10,... | collective-permute-start | bytes 294920 | tf_op jit(solution)/shard_map/ppermute | solution.py:11
  184.0 5.7 %collective-permute-start.17 = (f32[2,1,1,384,64]{3,4,2,1,0:T(8,128)S(1)}, f32[2,1,1,384,64]{3,4,2,1,0:T(8,128)S(1)}, u32[]{:S(2)}, u32[]{:S(2)}) collective-permute-start(f32[2,1,1,384,64]{3,4,2,1,0:T(8,128)S(1)} %pad_maximum_fusion.4), channel_id=1, source_target_pairs={{0,2},{1,3},{2,0},{3,1},{4,6},{5,7},{6,4},{7,5},{8,10},{9,11},{10,... | collective-permute-start | bytes 589832 | tf_op jit(solution)/shard_map/ppermute | solution.py:11
  187.6 5.7 %collective-permute-start.28 = (f32[2,1,1,384,64]{3,4,2,1,0:T(8,128)S(1)}, f32[2,1,1,384,64]{3,4,2,1,0:T(8,128)S(1)}, u32[]{:S(2)}, u32[]{:S(2)}) collective-permute-start(f32[2,1,1,384,64]{3,4,2,1,0:T(8,128)S(1)} %pad_maximum_fusion.5), channel_id=1, source_target_pairs={{0,2},{1,3},{2,0},{3,1},{4,6},{5,7},{6,4},{7,5},{8,10},{9,11},{10,... | collective-permute-start | bytes 589832 | tf_op jit(solution)/shard_map/ppermute | solution.py:11
  195.6 17.2 %collective-permute-start.34 = (f32[1536,128]{1,0:T(8,128)}, f32[1536,128]{1,0:T(8,128)}, u32[]{:S(2)}, u32[]{:S(2)}) collective-permute-start(f32[1536,128]{1,0:T(8,128)} %bitcast.25), channel_id=1, source_target_pairs={{0,1},{1,0},{2,3},{3,2},{4,5},{5,4},{6,7},{7,6},{8,9},{9,8},{10,11... | collective-permute-start | bytes 2359304 | tf_op jit(solution)/shard_map/ppermute | solution.py:11
  (20 other events, 228.0 us)

commit v17 on v15

--- a/solution.py
+++ b/solution.py
@@ -105,12 +105,21 @@
                 "rows", 1, row_count,
             )
         gathered = coef_a[None]
-        step = 1
-        while step < row_count:
-            low = (row_index & step) == 0
-            gathered = in_order(low, gathered, exchange(gathered, "rows", step), 0)
-            step *= 2
-        chains_a.append(gathered)
+        for k in range(row_bits):
+            pairs = []
+            for i in range(row_count * col_count):
+                r, c = divmod(i, col_count)
+                pairs.append((i, (r ^ (1 << (row_bits - 1 - k if c % 2 else k))) * col_count + c))
+            bit = jnp.where(first, k, row_bits - 1 - k)
+            low = (row_index >> bit) % 2 == 0
+            gathered = in_order(low, gathered, lax.ppermute(gathered, ("rows", "cols"), pairs), 0)
+        rest = gathered.shape[1:]
+        swapped = (
+            gathered.reshape((2,) * row_bits + rest)
+            .transpose(tuple(range(row_bits - 1, -1, -1)) + tuple(range(row_bits, row_bits + len(rest))))
+            .reshape(gathered.shape)
+        )
+        chains_a.append(jnp.where(first, gathered, swapped))
         gathered = coef_d.reshape((1,) * col_bits + coef_d.shape)
         for bit in range(col_bits - 1, -1, -1):
             low = (col_index >> bit) % 2 == 0

time: 226 us -> 232 us (1.027)
  other arithmetic: 17.5 us -> 22.2 us
  local copies, waits for them, and re-layouts: 17.8 us -> 22.5 us
  waiting for transfers between devices: 91 us -> 88.4 us
    ppermute x25 -> x21, starting transfers between devices: 23.2 us -> 18 us  [exchange(): return lax.ppermute(x, axis, [(i, i ^ step) for i in range(count)])]
    ppermute x0 -> x4, starting transfers between devices: none -> 4.22 us  [shards(): lax.ppermute(gathered, ('rows', 'cols'), pairs)]
    concatenate x1 -> x4, local copies, waits for them, and re-layouts: 0.26 us -> 3.68 us  [in_order(): jnp.concatenate([jnp.where(first, mine, theirs), jnp.where(first, theirs,...]
    select_n x12, other arithmetic: 3.82 us -> 6.74 us  [in_order(): jnp.where(first, mine, theirs)]
    ppermute x25 -> x21, waiting for transfers between devices: 56.2 us -> 53.5 us  [exchange(): return lax.ppermute(x, axis, [(i, i ^ step) for i in range(count)])]
    unnamed x20 -> x22, local copies, waits for them, and re-layouts: 5.75 us -> 5.75 us
  transfers between devices with their start and end apart: 35 -> 35, of which waited for: 23 -> 21; matrix products, arithmetic and copies ran while one was open for 21% -> 25% of each run, Pallas kernels for 0% -> 0%
where the time goes in v17:
time: 232 us; the launch traced here: 231 us
  waiting for transfers between devices  88.4 us (38%)
  matrix products  58.9 us (25%)
  starting transfers between devices  38.2 us (16%)
  local copies, waits for them, and re-layouts  22.5 us (10%)
  other arithmetic  22.2 us (10%)
    ppermute x21, waiting for transfers between devices, exchange(): return lax.ppermute(x, axis, [(i, i ^ step) for i in range(count)])  53.5 us
    dot_general x2, matrix products, partial_rows(): jnp.dot(columns.T, direct, precision=fast, preferred_element_type=jnp.flo...  32.4 us
    ppermute x2, waiting for transfers between devices, shards(): strip = kept + lax.ppermute(sent, 'cols', pairs)  21.6 us
    ppermute x21, starting transfers between devices, exchange(): return lax.ppermute(x, axis, [(i, i ^ step) for i in range(count)])  18 us
    ppermute x8, waiting for transfers between devices, shards(): coef_a = coef_a + lax.ppermute(coef_a, 'cols', pairs)  13.2 us
    ppermute x8, starting transfers between devices, shards(): coef_a = coef_a + lax.ppermute(coef_a, 'cols', pairs)  11.5 us
    dot_general x1, matrix products, shards(): jnp.dot(adjoint, full_a, precision=fast, preferred_element_type=jnp.float32)  10.7 us
    dot_general x1, matrix products, shards(): jnp.dot(direct, full_d, precision=fast, preferred_element_type=jnp.float32)  10.6 us
  transfers between devices with their start and end apart: 35, of which 21 were waited for; matrix products, arithmetic and copies ran while one was open for 25% of the time, Pallas kernels for 0%

profile of v17, /device:TPU:0, one launch (start us, length us, event | category | flops | bytes accessed | tf_op | source)
XLA Modules:
  0.0 231.3 jit_solution(2914310948117303023)
XLA Ops:
  0.7 16.2 %fusion.7 = f32[768,1536]{1,0:T(8,128)} fusion(f32[1536,1536]{1,0:T(8,128)} %param.3, f32[1536,1536]{1,0:T(8,128)} %param.4, s32[]{:T(128)S(6)} %select_n.305), kind=kOutput, calls=%fused_computation.5 | convolution fusion | flops 10872815616 | bytes 18874372 | tf_op jit(solution)/shard_map/dot_general | solution.py:47
  17.4 16.2 %fusion.4 = f32[768,1536]{1,0:T(8,128)} fusion(f32[1536,1536]{1,0:T(8,128)} %param.3, f32[1536,1536]{1,0:T(8,128)} %param.4, s32[]{:T(128)S(6)} %select_n.304), kind=kOutput, calls=%fused_computation.4 | convolution fusion | flops 10872815616 | bytes 18874372 | tf_op jit(solution)/shard_map/dot_general | solution.py:47
  33.5 4.8 %add.172 = f32[768,1536]{1,0:T(8,128)S(1)} add(f32[768,1536]{1,0:T(8,128)} %fusion.4, f32[768,1536]{1,0:T(8,128)} %collective-permute-done) | non-fusion elementwise | flops 1179648 | bytes 14155776 | tf_op jit(solution)/shard_map/add | solution.py:51
  41.5 2.6 %collective-permute-start.1 = (f32[2,192,768]{2,1,0:T(8,128)S(1)}, f32[2,192,768]{2,1,0:T(8,128)}, u32[]{:S(2)}, u32[]{:S(2)}) collective-permute-start(f32[2,192,768]{2,1,0:T(8,128)S(1)} %dynamic-slice_bitcast_fusion.1), channel_id=1, source_target_pairs={{0,8},{8,0},{16,24},{24,16},{1,9},{9,1},{17,25},{25,17},{2,10},{10... | collective-permute-start | bytes 3538952 | tf_op jit(solution)/shard_map/ppermute | solution.py:11
  44.1 2.4 %dynamic-slice_bitcast_fusion = f32[2,192,768]{2,1,0:T(8,128)} fusion(f32[2,2,192,768]{3,2,1,0:T(8,128)} %bitcast.83, s32[]{:T(128)S(6)} %select_n.311), kind=kLoop, calls=%fused_computation.19 | loop fusion | bytes 2359300 | tf_op jit(solution)/shard_map/jit(dynamic_index_in_dim)/squeeze | solution.py:65
  48.0 22.9 %collective-permute-done.1 = f32[2,192,768]{2,1,0:T(8,128)} collective-permute-done((f32[2,192,768]{2,1,0:T(8,128)S(1)}, f32[2,192,768]{2,1,0:T(8,128)}, u32[]{:S(2)}, u32[]{:S(2)}) %collective-permute-start.1) | collective-permute-done | bytes 1179680 | tf_op jit(solution)/shard_map/ppermute | solution.py:11
  79.3 8.7 %collective-permute-done.2 = f32[192,768]{1,0:T(8,128)} collective-permute-done((f32[192,768]{1,0:T(8,128)S(1)}, f32[192,768]{1,0:T(8,128)}, u32[]{:S(2)}, u32[]{:S(2)}) %collective-permute-start.2) | collective-permute-done | bytes 589856 | tf_op jit(solution)/shard_map/ppermute | solution.py:11
  89.1 4.0 %collective-permute-done.4 = f32[192,768]{1,0:T(8,128)} collective-permute-done((f32[192,768]{1,0:T(8,128)}, f32[192,768]{1,0:T(8,128)}, u32[]{:S(2)}, u32[]{:S(2)}) %collective-permute-start.4) | collective-permute-done | bytes 589856 | tf_op jit(solution)/shard_map/ppermute | solution.py:11
  95.4 2.2 reshape.55
  100.8 13.5 %collective-permute-done.5 = f32[192,2,384]{2,0,1:T(8,128)S(1)} collective-permute-done((f32[192,2,384]{2,0,1:T(8,128)S(1)}, f32[192,2,384]{2,0,1:T(8,128)S(1)}, u32[]{:S(2)}, u32[]{:S(2)}) %collective-permute-start.5) | collective-permute-done | bytes 589856 | tf_op jit(solution)/shard_map/ppermute | solution.py:88
  114.5 2.8 %collective-permute-start.6 = (f32[192,384]{1,0:T(8,128)S(1)}, f32[192,384]{1,0:T(8,128)S(1)}, u32[]{:S(2)}, u32[]{:S(2)}) collective-permute-start(f32[192,384]{1,0:T(8,128)S(1)} %select_bitcast_fusion), channel_id=1, source_target_pairs={{0,4},{1,3},{2,6},{3,1},{4,0},{5,7},{6,2},{7,5},{8,12},{9,11},{10,... | collective-permute-start | bytes 884744 | tf_op jit(solution)/shard_map/ppermute | solution.py:88
  117.3 8.1 %collective-permute-done.6 = f32[192,384]{1,0:T(8,128)S(1)} collective-permute-done((f32[192,384]{1,0:T(8,128)S(1)}, f32[192,384]{1,0:T(8,128)S(1)}, u32[]{:S(2)}, u32[]{:S(2)}) %collective-permute-start.6) | collective-permute-done | bytes 294944 | tf_op jit(solution)/shard_map/ppermute | solution.py:88
  131.0 3.1 %collective-permute-done.19 = f32[384,64]{0,1:T(8,128)S(1)} collective-permute-done((f32[384,64]{0,1:T(8,128)S(1)}, f32[384,64]{0,1:T(8,128)S(1)}, u32[]{:S(2)}, u32[]{:S(2)}) %collective-permute-start.19) | collective-permute-done | bytes 98336 | tf_op jit(solution)/shard_map/ppermute | solution.py:102
  135.9 2.9 %collective-permute-start.9 = (f32[384,64]{0,1:T(8,128)S(1)}, f32[384,64]{0,1:T(8,128)S(1)}, u32[]{:S(2)}, u32[]{:S(2)}) collective-permute-start(f32[384,64]{0,1:T(8,128)S(1)} %add.193), channel_id=1, source_target_pairs={{0,4},{1,3},{2,6},{3,1},{4,0},{5,7},{6,2},{7,5},{8,12},{9,11},{10,... | collective-permute-start | bytes 294920 | tf_op jit(solution)/shard_map/ppermute | solution.py:102
  143.8 1.9 collective-permute-done.21
  154.8 2.8 %collective-permute-done.23 = f32[384,64]{0,1:T(8,128)S(1)} collective-permute-done((f32[384,64]{0,1:T(8,128)S(1)}, f32[384,64]{0,1:T(8,128)S(1)}, u32[]{:S(2)}, u32[]{:S(2)}) %collective-permute-start.23) | collective-permute-done | bytes 98336 | tf_op jit(solution)/shard_map/ppermute | solution.py:102
  160.8 3.5 %collective-permute-done.24 = f32[384,64]{0,1:T(8,128)S(1)} collective-permute-done((f32[384,64]{0,1:T(8,128)S(1)}, f32[384,64]{0,1:T(8,128)S(1)}, u32[]{:S(2)}, u32[]{:S(2)}) %collective-permute-start.24) | collective-permute-done | bytes 98336 | tf_op jit(solution)/shard_map/ppermute | solution.py:102
  171.7 2.1 collective-permute-done.14
  178.6 3.1 %collective-permute-done.26 = f32[384,64]{0,1:T(8,128)S(1)} collective-permute-done((f32[384,64]{0,1:T(8,128)S(1)}, f32[384,64]{0,1:T(8,128)S(1)}, u32[]{:S(2)}, u32[]{:S(2)}) %collective-permute-start.26) | collective-permute-done | bytes 98336 | tf_op jit(solution)/shard_map/ppermute | solution.py:11
  181.9 3.1 %collective-permute-done.16 = f32[1,1,1,384,64]{3,4,2,1,0:T(8,128)S(1)} collective-permute-done((f32[1,1,1,384,64]{3,4,2,1,0:T(8,128)S(1)}, f32[1,1,1,384,64]{3,4,2,1,0:T(8,128)S(1)}, u32[]{:S(2)}, u32[]{:S(2)}) %collective-permute-start.16) | collective-permute-done | bytes 98336 | tf_op jit(solution)/shard_map/ppermute | solution.py:11
  185.7 2.5 %collective-permute-done.27 = f32[1,1,1,384,64]{3,4,2,1,0:T(8,128)S(1)} collective-permute-done((f32[1,1,1,384,64]{3,4,2,1,0:T(8,128)S(1)}, f32[1,1,1,384,64]{3,4,2,1,0:T(8,128)S(1)}, u32[]{:S(2)}, u32[]{:S(2)}) %collective-permute-start.27) | collective-permute-done | bytes 98336 | tf_op jit(solution)/shard_map/ppermute | solution.py:11
  203.1 2.1 copy.21
  205.2 10.6 %fusion.10 = f32[1536,256]{0,1:T(8,128)S(1)} fusion(f32[1536,1536]{1,0:T(8,128)} %param.3, f32[192,8,2,128]{3,2,1,0:T(2,128)} %bitcast.88), kind=kOutput, calls=%fused_computation.8 | convolution fusion | flops 3624271872 | bytes 12582912 | tf_op jit(solution)/shard_map/dot_general | solution.py:141
  219.0 10.7 %fusion.11 = f32[1536,256]{0,1:T(8,128)S(1)} fusion(f32[1536,1536]{1,0:T(8,128)} %param.4, f32[1536,128]{1,0:T(8,128)S(1)} %get-tuple-element.11, f32[1536,128]{1,0:T(8,128)S(1)} %get-tuple-element.10), kind=kOutput, calls=%fused_computation.9 | convolution fusion | flops 3624665088 | bytes 12582912 | tf_op jit(solution)/shard_map/dot_general | solution.py:142
  (143 shorter events, 77.5 us)
Async XLA Ops:
  16.9 16.6 %collective-permute-start = (f32[768,1536]{1,0:T(8,128)}, f32[768,1536]{1,0:T(8,128)}, u32[]{:S(2)}, u32[]{:S(2)}) collective-permute-start(f32[768,1536]{1,0:T(8,128)} %fusion.7), channel_id=1, source_target_pairs={{0,1},{1,0},{2,3},{3,2},{4,5},{5,4},{6,7},{7,6},{8,9},{9,8},{10,11... | collective-permute-start | bytes 14155784 | tf_op jit(solution)/shard_map/ppermute | solution.py:11
  41.5 29.3 %collective-permute-start.1 = (f32[2,192,768]{2,1,0:T(8,128)S(1)}, f32[2,192,768]{2,1,0:T(8,128)}, u32[]{:S(2)}, u32[]{:S(2)}) collective-permute-start(f32[2,192,768]{2,1,0:T(8,128)S(1)} %dynamic-slice_bitcast_fusion.1), channel_id=1, source_target_pairs={{0,8},{8,0},{16,24},{24,16},{1,9},{9,1},{17,25},{25,17},{2,10},{10... | collective-permute-start | bytes 3538952 | tf_op jit(solution)/shard_map/ppermute | solution.py:11
  46.5 28.4 %collective-permute-start.3 = (f32[2,192,768]{2,1,0:T(8,128)}, f32[2,192,768]{2,1,0:T(8,128)}, u32[]{:S(2)}, u32[]{:S(2)}) collective-permute-start(f32[2,192,768]{2,1,0:T(8,128)} %dynamic-slice_bitcast_fusion), channel_id=1, source_target_pairs={{0,16},{8,24},{16,0},{24,8},{1,17},{9,25},{17,1},{25,9},{2,18},{10... | collective-permute-start | bytes 3538952 | tf_op jit(solution)/shard_map/ppermute | solution.py:11
  72.7 15.3 %collective-permute-start.2 = (f32[192,768]{1,0:T(8,128)S(1)}, f32[192,768]{1,0:T(8,128)}, u32[]{:S(2)}, u32[]{:S(2)}) collective-permute-start(f32[192,768]{1,0:T(8,128)S(1)} %dynamic-slice_bitcast_fusion.3), channel_id=1, source_target_pairs={{0,16},{8,24},{16,0},{24,8},{1,17},{9,25},{17,1},{25,9},{2,18},{10... | collective-permute-start | bytes 1769480 | tf_op jit(solution)/shard_map/ppermute | solution.py:11
  78.2 14.9 %collective-permute-start.4 = (f32[192,768]{1,0:T(8,128)}, f32[192,768]{1,0:T(8,128)}, u32[]{:S(2)}, u32[]{:S(2)}) collective-permute-start(f32[192,768]{1,0:T(8,128)} %dynamic-slice_bitcast_fusion.2), channel_id=1, source_target_pairs={{0,8},{8,0},{16,24},{24,16},{1,9},{9,1},{17,25},{25,17},{2,10},{10... | collective-permute-start | bytes 1769480 | tf_op jit(solution)/shard_map/ppermute | solution.py:11
  99.2 15.2 %collective-permute-start.5 = (f32[192,2,384]{2,0,1:T(8,128)S(1)}, f32[192,2,384]{2,0,1:T(8,128)S(1)}, u32[]{:S(2)}, u32[]{:S(2)}) collective-permute-start(f32[192,2,384]{2,0,1:T(8,128)S(1)} %bitcast_select_fusion), channel_id=1, source_target_pairs={{0,2},{1,5},{2,0},{3,7},{4,6},{5,1},{6,4},{7,3},{8,10},{9,13},{10,... | collective-permute-start | bytes 1769480 | tf_op jit(solution)/shard_map/ppermute | solution.py:88
  114.5 10.9 %collective-permute-start.6 = (f32[192,384]{1,0:T(8,128)S(1)}, f32[192,384]{1,0:T(8,128)S(1)}, u32[]{:S(2)}, u32[]{:S(2)}) collective-permute-start(f32[192,384]{1,0:T(8,128)S(1)} %select_bitcast_fusion), channel_id=1, source_target_pairs={{0,4},{1,3},{2,6},{3,1},{4,0},{5,7},{6,2},{7,5},{8,12},{9,11},{10,... | collective-permute-start | bytes 884744 | tf_op jit(solution)/shard_map/ppermute | solution.py:88
  128.0 6.1 %collective-permute-start.19 = (f32[384,64]{0,1:T(8,128)S(1)}, f32[384,64]{0,1:T(8,128)S(1)}, u32[]{:S(2)}, u32[]{:S(2)}) collective-permute-start(f32[384,64]{0,1:T(8,128)S(1)} %fusion.18), channel_id=1, source_target_pairs={{0,2},{1,5},{2,0},{3,7},{4,6},{5,1},{6,4},{7,3},{8,10},{9,13},{10,... | collective-permute-start | bytes 294920 | tf_op jit(solution)/shard_map/ppermute | solution.py:102
  129.6 6.3 %collective-permute-start.8 = (f32[384,64]{0,1:T(8,128)S(1)}, f32[384,64]{0,1:T(8,128)S(1)}, u32[]{:S(2)}, u32[]{:S(2)}) collective-permute-start(f32[384,64]{0,1:T(8,128)S(1)} %fusion.20), channel_id=1, source_target_pairs={{0,2},{1,5},{2,0},{3,7},{4,6},{5,1},{6,4},{7,3},{8,10},{9,13},{10,... | collective-permute-start | bytes 294920 | tf_op jit(solution)/shard_map/ppermute | solution.py:102
  135.9 6.2 %collective-permute-start.9 = (f32[384,64]{0,1:T(8,128)S(1)}, f32[384,64]{0,1:T(8,128)S(1)}, u32[]{:S(2)}, u32[]{:S(2)}) collective-permute-start(f32[384,64]{0,1:T(8,128)S(1)} %add.193), channel_id=1, source_target_pairs={{0,4},{1,3},{2,6},{3,1},{4,0},{5,7},{6,2},{7,5},{8,12},{9,11},{10,... | collective-permute-start | bytes 294920 | tf_op jit(solution)/shard_map/ppermute | solution.py:102
  151.4 6.2 %collective-permute-start.23 = (f32[384,64]{0,1:T(8,128)S(1)}, f32[384,64]{0,1:T(8,128)S(1)}, u32[]{:S(2)}, u32[]{:S(2)}) collective-permute-start(f32[384,64]{0,1:T(8,128)S(1)} %fusion.22), channel_id=1, source_target_pairs={{0,2},{1,5},{2,0},{3,7},{4,6},{5,1},{6,4},{7,3},{8,10},{9,13},{10,... | collective-permute-start | bytes 294920 | tf_op jit(solution)/shard_map/ppermute | solution.py:102
  153.5 6.0 %collective-permute-start.12 = (f32[384,64]{0,1:T(8,128)S(1)}, f32[384,64]{0,1:T(8,128)S(1)}, u32[]{:S(2)}, u32[]{:S(2)}) collective-permute-start(f32[384,64]{0,1:T(8,128)S(1)} %fusion.26), channel_id=1, source_target_pairs={{0,2},{1,5},{2,0},{3,7},{4,6},{5,1},{6,4},{7,3},{8,10},{9,13},{10,... | collective-permute-start | bytes 294920 | tf_op jit(solution)/shard_map/ppermute | solution.py:102
  157.6 6.6 %collective-permute-start.24 = (f32[384,64]{0,1:T(8,128)S(1)}, f32[384,64]{0,1:T(8,128)S(1)}, u32[]{:S(2)}, u32[]{:S(2)}) collective-permute-start(f32[384,64]{0,1:T(8,128)S(1)} %add.205), channel_id=1, source_target_pairs={{0,4},{1,3},{2,6},{3,1},{4,0},{5,7},{6,2},{7,5},{8,12},{9,11},{10,... | collective-permute-start | bytes 294920 | tf_op jit(solution)/shard_map/ppermute | solution.py:102
  159.5 6.9 %collective-permute-start.13 = (f32[384,64]{0,1:T(8,128)S(1)}, f32[384,64]{0,1:T(8,128)S(1)}, u32[]{:S(2)}, u32[]{:S(2)}) collective-permute-start(f32[384,64]{0,1:T(8,128)S(1)} %add.197), channel_id=1, source_target_pairs={{0,4},{1,3},{2,6},{3,1},{4,0},{5,7},{6,2},{7,5},{8,12},{9,11},{10,... | collective-permute-start | bytes 294920 | tf_op jit(solution)/shard_map/ppermute | solution.py:102
  164.3 6.2 %collective-permute-start.32 = (f32[1,384,64]{1,2,0:T(8,128)S(1)}, f32[1,384,64]{1,2,0:T(8,128)S(1)}, u32[]{:S(2)}, u32[]{:S(2)}) collective-permute-start(f32[1,384,64]{1,2,0:T(8,128)S(1)} %add_bitcast_fusion.2), channel_id=1, source_target_pairs={{0,8},{1,17},{2,10},{3,19},{4,12},{5,21},{6,14},{7,23},{8,0},{9,25... | collective-permute-start | bytes 294920 | tf_op jit(solution)/shard_map/ppermute | solution.py:115
  166.4 8.4 %collective-permute-start.30 = (f32[1,384,64]{1,2,0:T(8,128)S(1)}, f32[1,384,64]{1,2,0:T(8,128)S(1)}, u32[]{:S(2)}, u32[]{:S(2)}) collective-permute-start(f32[1,384,64]{1,2,0:T(8,128)S(1)} %add_bitcast_fusion.3), channel_id=1, source_target_pairs={{0,8},{1,17},{2,10},{3,19},{4,12},{5,21},{6,14},{7,23},{8,0},{9,25... | collective-permute-start | bytes 294920 | tf_op jit(solution)/shard_map/ppermute | solution.py:115
  169.5 6.5 %collective-permute-start.25 = (f32[384,64]{0,1:T(8,128)S(1)}, f32[384,64]{0,1:T(8,128)S(1)}, u32[]{:S(2)}, u32[]{:S(2)}) collective-permute-start(f32[384,64]{0,1:T(8,128)S(1)} %fusion.30), channel_id=1, source_target_pairs={{0,8},{8,0},{16,24},{24,16},{1,9},{9,1},{17,25},{25,17},{2,10},{10... | collective-permute-start | bytes 294920 | tf_op jit(solution)/shard_map/ppermute | solution.py:11
  170.6 17.8 %collective-permute-start.33 = (f32[2,384,64]{1,2,0:T(8,128)S(1)}, f32[2,384,64]{1,2,0:T(8,128)S(1)}, u32[]{:S(2)}, u32[]{:S(2)}) collective-permute-start(f32[2,384,64]{1,2,0:T(8,128)S(1)} %pad_maximum_fusion.9), channel_id=1, source_target_pairs={{0,16},{1,9},{2,18},{3,11},{4,20},{5,13},{6,22},{7,15},{8,24},{9,1... | collective-permute-start | bytes 589832 | tf_op jit(solution)/shard_map/ppermute | solution.py:115
  174.8 15.4 %collective-permute-start.31 = (f32[2,384,64]{1,2,0:T(8,128)S(1)}, f32[2,384,64]{1,2,0:T(8,128)}, u32[]{:S(2)}, u32[]{:S(2)}) collective-permute-start(f32[2,384,64]{1,2,0:T(8,128)S(1)} %pad_maximum_fusion.8), channel_id=1, source_target_pairs={{0,16},{1,9},{2,18},{3,11},{4,20},{5,13},{6,22},{7,15},{8,24},{9,1... | collective-permute-start | bytes 589832 | tf_op jit(solution)/shard_map/ppermute | solution.py:115
  178.5 6.4 %collective-permute-start.16 = (f32[1,1,1,384,64]{3,4,2,1,0:T(8,128)S(1)}, f32[1,1,1,384,64]{3,4,2,1,0:T(8,128)S(1)}, u32[]{:S(2)}, u32[]{:S(2)}) collective-permute-start(f32[1,1,1,384,64]{3,4,2,1,0:T(8,128)S(1)} %add_bitcast_fusion.1), channel_id=1, source_target_pairs={{0,4},{1,5},{2,6},{3,7},{4,0},{5,1},{6,2},{7,3},{8,12},{9,13},{10,... | collective-permute-start | bytes 294920 | tf_op jit(solution)/shard_map/ppermute | solution.py:11
  181.7 6.5 %collective-permute-start.27 = (f32[1,1,1,384,64]{3,4,2,1,0:T(8,128)S(1)}, f32[1,1,1,384,64]{3,4,2,1,0:T(8,128)S(1)}, u32[]{:S(2)}, u32[]{:S(2)}) collective-permute-start(f32[1,1,1,384,64]{3,4,2,1,0:T(8,128)S(1)} %add_bitcast_fusion), channel_id=1, source_target_pairs={{0,4},{1,5},{2,6},{3,7},{4,0},{5,1},{6,2},{7,3},{8,12},{9,13},{10,... | collective-permute-start | bytes 294920 | tf_op jit(solution)/shard_map/ppermute | solution.py:11
  185.7 8.3 %collective-permute-start.17 = (f32[2,1,1,384,64]{3,4,2,1,0:T(8,128)}, f32[2,1,1,384,64]{3,4,2,1,0:T(8,128)}, u32[]{:S(2)}, u32[]{:S(2)}) collective-permute-start(f32[2,1,1,384,64]{3,4,2,1,0:T(8,128)} %pad_maximum_fusion.6), channel_id=1, source_target_pairs={{0,2},{1,3},{2,0},{3,1},{4,6},{5,7},{6,4},{7,5},{8,10},{9,11},{10,... | collective-permute-start | bytes 589832 | tf_op jit(solution)/shard_map/ppermute | solution.py:11
  188.2 7.6 %collective-permute-start.28 = (f32[2,1,1,384,64]{3,4,2,1,0:T(8,128)S(1)}, f32[2,1,1,384,64]{3,4,2,1,0:T(8,128)}, u32[]{:S(2)}, u32[]{:S(2)}) collective-permute-start(f32[2,1,1,384,64]{3,4,2,1,0:T(8,128)S(1)} %pad_maximum_fusion.7), channel_id=1, source_target_pairs={{0,2},{1,3},{2,0},{3,1},{4,6},{5,7},{6,4},{7,5},{8,10},{9,11},{10,... | collective-permute-start | bytes 589832 | tf_op jit(solution)/shard_map/ppermute | solution.py:11
  200.9 16.6 %collective-permute-start.34 = (f32[1536,128]{1,0:T(8,128)}, f32[1536,128]{1,0:T(8,128)}, u32[]{:S(2)}, u32[]{:S(2)}) collective-permute-start(f32[1536,128]{1,0:T(8,128)} %bitcast.28), channel_id=1, source_target_pairs={{0,1},{1,0},{2,3},{3,2},{4,5},{5,4},{6,7},{7,6},{8,9},{9,8},{10,11... | collective-permute-start | bytes 2359304 | tf_op jit(solution)/shard_map/ppermute | solution.py:11
  (21 other events, 241.9 us)
